TPU v7x, 256 devices: a whole 4x4x8 slice. The times are simulated.
256 devices in a mesh: gx: 64 (over y, x, z_lo, core), gy: 4 (over z_hi).
Axes of the slice: x: 4, y: 4, z: 8 (z_hi: 4, z_lo: 2; z = z_hi * 2 + z_lo), core: 2. Of those that a mesh axis runs over, the one named last changes fastest.
Arguments:
- state: float32 [4, 4, 512, 8192], P(None, None, 'gx', 'gy'), may hold values from -6 to 6
- start: float32 [4, 4, 512, 8192], P(None, None, 'gx', 'gy'), may hold values from -6 to 6
- eddy: float32 [4, 512, 8192], P(None, 'gx', 'gy'), may hold values from 0.05 to 0.5
- solid: int32 [4, 512, 8192], P(None, 'gx', 'gy'), may hold values 0 or 1
- facet_wall: float32 [4, 524288], P(None, ('gx', 'gy')), may hold values from -6 to 6
- facet_dist: float32 [524288], P(('gx', 'gy')), may hold values from 0.1 to 1
- facet_area: float32 [524288], P(('gx', 'gy')), may hold values from 0.1 to 1
- facet_owner: int32 [524288, 1], P(('gx', 'gy')), may hold values from 0 to 63; in each aligned block of 2048 rows (0 to 2047, 2048 to 4095, ...) at most 64 rows name the same one
- facet_cell: int32 [524288], P(('gx', 'gy')), may hold values from 0 to 65535
Outputs:
- new_state: float32 [4, 4, 512, 8192], P(None, None, 'gx', 'gy')
- facet_flux: float32 [4, 524288], P(None, ('gx', 'gy'))
Inputs may be any that keep to these rules, and one draw needn't show every extreme that they name: `facet_owner`: among the 2048 facets of one device at most 64 share one owner, and that many do in some devices.
All inputs are finite; a program needn't handle non-finite values. No bound on the sum of `solid` on one device may be relied on, other than what follows from the above.
Results may differ from a plain program's by a relative error of at most 0.0003.
Values sent between devices are 32-bit elements; how exact they have to be, the bound alone decides.
No kernel may reach another device: no remote copies, remote signals or barrier semaphores. Data moves between devices by JAX's collectives and lax.ppermute only.
A program may use at most 64 MiB of HBM per device.

v0:
```python
import math

import jax
import jax.numpy as jnp
from jax import lax
from jax.sharding import PartitionSpec as P

dt_step = 0.2
exact = lax.Precision.HIGHEST


def padded(shard, sides, width):
    for axis, dim in sides:
        peers, length = (lax.axis_size(axis), shard.shape[dim])
        up = [(i, (i + 1) % peers) for i in range(peers)]
        down = [(j, i) for i, j in up]
        last = lax.slice_in_dim(shard, length - width, length, axis=dim)
        leading = lax.slice_in_dim(shard, 0, width, axis=dim)
        before = lax.ppermute(last, axis, up)
        after = lax.ppermute(leading, axis, down)
        shard = jnp.concatenate([before, shard, after], axis=dim)
    return shard


def upwind_derivative(shifted, velocity):
    forward = (
        -2.0 * shifted(-3)
        + 15.0 * shifted(-2)
        - 60.0 * shifted(-1)
        + 20.0 * shifted(0)
        + 30.0 * shifted(1)
        - 3.0 * shifted(2)
    ) / 60.0
    backward = (
        3.0 * shifted(-2)
        - 30.0 * shifted(-1)
        - 20.0 * shifted(0)
        + 60.0 * shifted(1)
        - 15.0 * shifted(2)
        + 2.0 * shifted(3)
    ) / 60.0
    return jnp.where(velocity > 0, forward, backward)


def vertical_terms(fields, eddy):
    lower = jnp.concatenate([fields[:, :1], fields[:, :-1]], axis=1)
    upper = jnp.concatenate([fields[:, 1:], fields[:, -1:]], axis=1)
    derz = (upper - lower) * 0.5
    face_eddy = 0.5 * (eddy[:-1] + eddy[1:])
    no_face = jnp.zeros_like(eddy[:1])
    eddy_up = jnp.concatenate([face_eddy, no_face], axis=0)
    eddy_down = jnp.concatenate([no_face, face_eddy], axis=0)
    zdiffuse = eddy_up * (upper - fields) - eddy_down * (fields - lower)
    return (derz, zdiffuse)


def tendency(field_x, field_y, eddy_x, eddy_y, fields, eddy, forcing, solid):
    derx = upwind_derivative(field_x, fields[0])
    dery = upwind_derivative(field_y, fields[1])
    derz, zdiffuse = vertical_terms(fields, eddy)
    advect = fields[0] * derx + fields[1] * dery + fields[2] * derz
    east_eddy = 0.5 * (eddy + eddy_x(1))
    west_eddy = 0.5 * (eddy_x(-1) + eddy)
    north_eddy = 0.5 * (eddy + eddy_y(1))
    south_eddy = 0.5 * (eddy_y(-1) + eddy)
    diff_x = east_eddy * (field_x(1) - fields) - west_eddy * (fields - field_x(-1))
    diff_y = north_eddy * (field_y(1) - fields) - south_eddy * (fields - field_y(-1))
    diffuse = diff_x + diff_y + zdiffuse
    return (diffuse - advect - forcing) * (1.0 - solid.astype(jnp.float32))


def local(state, start, eddy, solid, facet_wall, facet_dist, facet_area, facet_owner, facet_cell):
    levels = state.shape[1]
    cells_x = state.shape[2]
    cells_y = state.shape[3]
    packed = jnp.concatenate([state, eddy[None]], axis=0)
    padded_all = padded(packed, (("gx", 2), ("gy", 3)), 3)
    fields_pad = padded_all[:4]
    eddy_pad = padded_all[4]
    pad_width = 3

    def field_x(offset):
        return fields_pad[:, :, 3 + offset : 3 + offset + cells_x, 3 : 3 + cells_y]

    def field_y(offset):
        return fields_pad[:, :, 3 : 3 + cells_x, 3 + offset : 3 + offset + cells_y]

    def eddy_x(offset):
        return eddy_pad[
            :, pad_width + offset : pad_width + offset + cells_x, pad_width : pad_width + cells_y
        ]

    def eddy_y(offset):
        return eddy_pad[
            :, pad_width : pad_width + cells_x, pad_width + offset : pad_width + offset + cells_y
        ]

    facet_count = facet_cell.shape[0]
    owners_gx = lax.axis_size("gx")
    capacity = 2 * facet_count // owners_gx
    slots = owners_gx * capacity
    owner_gx = facet_owner[:, 0]
    owner_hot = (owner_gx[:, None] == jnp.arange(owners_gx, dtype=jnp.int32)[None, :]).astype(
        jnp.bfloat16
    )
    positions = jnp.arange(facet_count, dtype=jnp.int32)
    earlier = (positions[:, None] > positions[None, :]).astype(jnp.bfloat16)
    before = jnp.dot(earlier, owner_hot, preferred_element_type=jnp.float32)
    owner_float = owner_hot.astype(jnp.float32)
    slot_rank = jnp.sum(before * owner_float, axis=1)
    rank_hot = (slot_rank[:, None] == jnp.arange(capacity, dtype=jnp.float32)[None, :]).astype(
        jnp.float32
    )
    payload = jnp.concatenate(
        [facet_wall, facet_dist[None], facet_area[None], facet_cell[None].astype(jnp.float32)],
        axis=0,
    )
    spread = payload[:, None, :] * owner_float.T[None]
    outgoing = jnp.einsum("cof,fk->cok", spread, rank_hot, precision=exact)
    filled = jnp.dot(owner_float.T, rank_hot, precision=exact)
    unit_dist = (jnp.arange(7, dtype=jnp.int32) == 4).astype(jnp.float32)[:, None, None]
    outgoing = outgoing + unit_dist * (1.0 - filled)[None]
    received = lax.all_to_all(outgoing, "gx", split_axis=1, concat_axis=1, tiled=True).reshape(
        7, slots
    )
    block_rows = math.gcd(slots, 1024)
    block_count = slots // block_rows
    row_count = levels * cells_x
    grid_rows = state.reshape(4, row_count, cells_y)
    pieces = received.reshape(7, block_count, block_rows).transpose(1, 0, 2)
    column_ids = jnp.arange(cells_y, dtype=jnp.int32)
    row_ids = jnp.arange(row_count, dtype=jnp.int32)

    def visit(forcing_sum, piece):
        cell_index = (piece[6] + 0.5).astype(jnp.int32)
        row_index = cell_index // cells_y
        col_index = cell_index % cells_y
        col_hot = (col_index[:, None] == column_ids[None, :]).astype(jnp.float32)
        row_hot = (row_index[:, None] == row_ids[None, :]).astype(jnp.float32)
        picked = jnp.einsum("cry,sy->csr", grid_rows, col_hot, precision=exact)
        cell_values = jnp.sum(picked * row_hot[None], axis=2)
        wall_flux = piece[5] * (cell_values - piece[:4]) / piece[4]
        weighted = wall_flux[:, :, None] * row_hot[None]
        added = jnp.einsum("csr,sy->cry", weighted, col_hot, precision=exact)
        return (forcing_sum + added, wall_flux)

    forcing_rows, flux_blocks = lax.scan(
        visit, jnp.zeros((4, row_count, cells_y), jnp.float32), pieces
    )
    forcing = forcing_rows.reshape(state.shape)
    wall_flux = flux_blocks.transpose(1, 0, 2).reshape(4, owners_gx, capacity)
    returned = lax.all_to_all(wall_flux, "gx", split_axis=1, concat_axis=1, tiled=True)
    through = jnp.einsum("cok,fk->cof", returned, rank_hot, precision=exact)
    facet_flux = jnp.sum(through * owner_float.T[None], axis=1)
    change = tendency(field_x, field_y, eddy_x, eddy_y, state, eddy, forcing, solid)
    new_state = start + dt_step * change
    return (new_state, facet_flux)


def solution(mesh):
    in_specs = (
        P(None, None, "gx", "gy"),
        P(None, None, "gx", "gy"),
        P(None, "gx", "gy"),
        P(None, "gx", "gy"),
        P(None, ("gx", "gy")),
        P(("gx", "gy")),
        P(("gx", "gy")),
        P(("gx", "gy"), None),
        P(("gx", "gy")),
    )
    out_specs = (P(None, None, "gx", "gy"), P(None, ("gx", "gy")))
    return jax.shard_map(local, mesh=mesh, in_specs=in_specs, out_specs=out_specs, check_vma=False)
```

profile of v0, /device:TPU:1, one launch (start us, length us, event | category | flops | bytes accessed | tf_op | source)
XLA Modules:
  0.0 143.7 jit_solution(9958243106326014654)
XLA Ops:
  0.7 2.4 %fusion.41 = f32[2048]{0:T(1024)S(1)} fusion(s32[2048]{0:T(1024)} %bitcast.110), kind=kOutput, calls=%fused_computation.49 | convolution fusion | flops 541849600 | bytes 16384 | tf_op jit(solution)/shard_map/dot_general | solution.py:108
  3.3 0.3 convolution_subtract_fusion
  3.6 0.4 copy-done.10
  4.1 1.9 %fusion.38 = f32[7,64,64]{2,1,0:T(8,128)S(1)} fusion(f32[64,2048]{1,0:T(8,128)S(1)} %fusion.76, f32[7,2048]{1,0:T(8,128)S(1)} %pad_maximum_fusion.17, f32[2048]{0:T(1024)S(1)} %fusion.41, f32[64,64]{1,0:T(8,128)S(1)} %convolution_subtract_fusion, f32[7]{0:T(128)S(1)} %compare_convert_fusion), kind=kOutput, calls=%fused_computation.48 | convolution fusion | flops 705748992 | bytes 720924 | tf_op jit(solution)/shard_map/cof,fk->cok/dot_general | solution.py:119
  6.0 0.1 copy.118
  6.2 0.9 reshape.205
  7.0 10.3 %all-to-all-start = ((f32[64,1,448]{2,1,0:T(1,128)}), f32[64,1,448]{2,1,0:T(1,128)S(1)}, u32[]{:S(2)}, u32[]{:S(2)}) async-start(f32[64,1,448]{2,1,0:T(1,128)} %reshape.205), calls=%async_computation | async-start | bytes 262144 | tf_op jit(solution)/shard_map/all_to_all | solution.py:123
  17.4 0.3 copy.62
  17.7 0.7 copy.61
  18.3 1.5 %pad_maximum_fusion.16 = (f32[5,4,3,2048]{3,0,2,1:T(8,128)}, f32[5,4,3,2048]{3,0,2,1:T(8,128)}) fusion(f32[1,4,8,2048]{3,0,2,1:T(1,128)S(1)} %copy.62, f32[4,4,8,2048]{3,0,2,1:T(4,128)S(1)} %copy.61), kind=kLoop, calls=%fused_computation.100 | loop fusion | flops 245760 | bytes 2293760 | tf_op jit(solution)/shard_map/slice | solution.py:17
  19.8 1.6 %collective-permute-start = (f32[5,4,3,2048]{3,0,2,1:T(8,128)}, f32[5,4,3,2048]{3,0,2,1:T(8,128)S(1)}, u32[]{:S(2)}, u32[]{:S(2)}) collective-permute-start(f32[5,4,3,2048]{3,0,2,1:T(8,128)} %get-tuple-element.153), channel_id=1, source_target_pairs={{0,4},{4,8},{8,12},{12,16},{16,20},{20,24},{24,28},{28,32},{32,36}... | collective-permute-start | bytes 1474568 | tf_op jit(solution)/shard_map/ppermute | solution.py:19
  21.5 2.0 %slice_bitcast_fusion.1 = (f32[4,8,2048]{2,1,0:T(8,128)}, f32[4,8,2048]{2,1,0:T(8,128)}, f32[4,8,2048]{2,1,0:T(8,128)}) fusion(f32[4,4,8,2048]{3,2,1,0:T(8,128)} %param.11), kind=kLoop, calls=%fused_computation.125 | loop fusion | flops 65536 | bytes 1572864 | tf_op jit(solution)/shard_map/mul | solution.py:61
  23.5 1.5 %fusion.88 = (f32[4,3,8,2048]{3,0,2,1:T(4,128)}, f32[4,3,8,2048]{3,0,2,1:T(4,128)}) fusion(f32[4,4,8,2048]{3,0,2,1:T(4,128)S(1)} %copy.61), kind=kLoop, calls=%fused_computation.133 | loop fusion | bytes 3145728 | tf_op jit(solution)/shard_map/slice | solution.py:47
  25.0 0.9 fusion.91
  25.9 0.9 fusion.89
  26.7 0.7 copy-done.11
  27.4 0.5 broadcast.278
  27.9 1.8 %reduce.1 = f32[64,448]{1,0:T(8,128)S(1)} reduce(f32[64,1,448]{2,1,0:T(1,128)} %copy-done.11, f32[]{:T(128)} %broadcast.278), dimensions={1}, to_apply=%all_to_all.6.reduce_sub_computation | reduce | bytes 229380 | tf_op jit(solution)/shard_map/all_to_all | solution.py:123
  29.7 0.1 reshape.206
  29.8 0.7 copy.80
  30.6 1.1 reshape_reshape.3
  31.6 45.3 %while.15 = (s32[]{:T(128)}, f32[4,32,2048]{2,1,0:T(8,128)}, f32[4,4,1024]{2,1,0:T(4,128)}, f32[4,7,1024]{2,0,1:T(4,128)S(1)}, f32[4,32,2048]{2,1,0:T(8,128)}, /*index=5*/s32[]{:T(128)}, s32[]{:T(128)}, s32[]{}, s32[]{}, s32[]{}) while((s32[]{:T(128)}, f32[4,32,2048]{2,1,0:T(8,128)}, f32[4,4,1024]{2,1,0:T(4,128)}, ...), condition=%wide.region_3.4_spmd.clone, body=%wide.region_1.3_spmd.clone.sunk | while | flops 6447670272 | bytes 12157167 | solution.py:147
  31.8 6.0 %fusion.108 = f32[1024,4]{0,1:T(4,128)S(1)} fusion(f32[4,32,2048]{2,1,0:T(8,128)} %get-tuple-element.238, s32[1024]{0:T(1024)S(1)} %get-tuple-element.210, f32[1024,32]{0,1:T(8,128)S(1)} %fusion.107), kind=kOutput, calls=%fused_computation.10.clone.1 | convolution fusion | flops 3223580672 | bytes 1200128 | tf_op jit(solution)/shard_map/while/body/eval_jaxpr/cry,sy->csr/dot_general | solution.py:140
  37.8 0.6 divide_dynamic-update-slice_fusion.2
  38.5 3.5 %fusion.110 = f32[4,32,2048]{2,1,0:T(8,128)S(1)} fusion(s32[1024]{0:T(1024)S(1)} %get-tuple-element.210, f32[4,32,2048]{2,1,0:T(8,128)S(1)} %copy-done.7, pred[]{:T(512)S(6)} %compare.17, f32[1024,32]{0,1:T(8,128)S(1)} %fusion.107, f32[4,1024]{1,0:T(4,128)S(1)} %fusion.109), kind=kOutput, calls=%fused_computation.8.clone.1 | convolution fusion | flops 3223977984 | bytes 2248705 | tf_op jit(solution)/shard_map/while/body/eval_jaxpr/csr,sy->cry/dot_general | solution.py:144
  42.0 1.0 copy-done.8
  43.1 6.0 %fusion.108 = f32[1024,4]{0,1:T(4,128)S(1)} fusion(f32[4,32,2048]{2,1,0:T(8,128)} %get-tuple-element.238, s32[1024]{0:T(1024)S(1)} %get-tuple-element.210, f32[1024,32]{0,1:T(8,128)S(1)} %fusion.107), kind=kOutput, calls=%fused_computation.10.clone.1 | convolution fusion | flops 3223580672 | bytes 1200128 | tf_op jit(solution)/shard_map/while/body/eval_jaxpr/cry,sy->csr/dot_general | solution.py:140
  49.1 0.6 divide_dynamic-update-slice_fusion.2
  49.8 3.5 %fusion.110 = f32[4,32,2048]{2,1,0:T(8,128)S(1)} fusion(s32[1024]{0:T(1024)S(1)} %get-tuple-element.210, f32[4,32,2048]{2,1,0:T(8,128)S(1)} %copy-done.7, pred[]{:T(512)S(6)} %compare.17, f32[1024,32]{0,1:T(8,128)S(1)} %fusion.107, f32[4,1024]{1,0:T(4,128)S(1)} %fusion.109), kind=kOutput, calls=%fused_computation.8.clone.1 | convolution fusion | flops 3223977984 | bytes 2248705 | tf_op jit(solution)/shard_map/while/body/eval_jaxpr/csr,sy->cry/dot_general | solution.py:144
  53.3 1.0 copy-done.8
  54.4 6.0 %fusion.108 = f32[1024,4]{0,1:T(4,128)S(1)} fusion(f32[4,32,2048]{2,1,0:T(8,128)} %get-tuple-element.238, s32[1024]{0:T(1024)S(1)} %get-tuple-element.210, f32[1024,32]{0,1:T(8,128)S(1)} %fusion.107), kind=kOutput, calls=%fused_computation.10.clone.1 | convolution fusion | flops 3223580672 | bytes 1200128 | tf_op jit(solution)/shard_map/while/body/eval_jaxpr/cry,sy->csr/dot_general | solution.py:140
  60.5 0.6 divide_dynamic-update-slice_fusion.2
  61.1 3.5 %fusion.110 = f32[4,32,2048]{2,1,0:T(8,128)S(1)} fusion(s32[1024]{0:T(1024)S(1)} %get-tuple-element.210, f32[4,32,2048]{2,1,0:T(8,128)S(1)} %copy-done.7, pred[]{:T(512)S(6)} %compare.17, f32[1024,32]{0,1:T(8,128)S(1)} %fusion.107, f32[4,1024]{1,0:T(4,128)S(1)} %fusion.109), kind=kOutput, calls=%fused_computation.8.clone.1 | convolution fusion | flops 3223977984 | bytes 2248705 | tf_op jit(solution)/shard_map/while/body/eval_jaxpr/csr,sy->cry/dot_general | solution.py:144
  64.6 1.0 copy-done.8
  65.7 6.0 %fusion.108 = f32[1024,4]{0,1:T(4,128)S(1)} fusion(f32[4,32,2048]{2,1,0:T(8,128)} %get-tuple-element.238, s32[1024]{0:T(1024)S(1)} %get-tuple-element.210, f32[1024,32]{0,1:T(8,128)S(1)} %fusion.107), kind=kOutput, calls=%fused_computation.10.clone.1 | convolution fusion | flops 3223580672 | bytes 1200128 | tf_op jit(solution)/shard_map/while/body/eval_jaxpr/cry,sy->csr/dot_general | solution.py:140
  71.8 0.6 divide_dynamic-update-slice_fusion.2
  72.4 3.5 %fusion.110 = f32[4,32,2048]{2,1,0:T(8,128)S(1)} fusion(s32[1024]{0:T(1024)S(1)} %get-tuple-element.210, f32[4,32,2048]{2,1,0:T(8,128)S(1)} %copy-done.7, pred[]{:T(512)S(6)} %compare.17, f32[1024,32]{0,1:T(8,128)S(1)} %fusion.107, f32[4,1024]{1,0:T(4,128)S(1)} %fusion.109), kind=kOutput, calls=%fused_computation.8.clone.1 | convolution fusion | flops 3223977984 | bytes 2248705 | tf_op jit(solution)/shard_map/while/body/eval_jaxpr/csr,sy->cry/dot_general | solution.py:144
  75.9 1.0 copy-done.8
  76.9 0.9 copy.84
  77.8 0.1 reshape.202
  77.9 0.1 copy.119
  78.0 0.8 reshape.207
  78.7 9.0 %all-to-all-start.1 = ((f32[64,1,256]{2,1,0:T(1,128)}), f32[64,1,256]{2,1,0:T(1,128)S(1)}, u32[]{:S(2)}, u32[]{:S(2)}) async-start(f32[64,1,256]{2,1,0:T(1,128)} %reshape.207), calls=%async_computation.1 | async-start | bytes 131072 | tf_op jit(solution)/shard_map/all_to_all | solution.py:152
  87.7 1.1 broadcast_compare_fusion.1
  88.8 2.9 %copy.82 = f32[4,32,2048]{2,0,1:T(4,128)} copy(f32[4,32,2048]{2,1,0:T(8,128)} %get-tuple-element.95) | data formatting | bytes 2097152 | tf_op jit(solution)/shard_map/while | solution.py:147
  91.7 4.1 %all-to-all-done.1 = f32[64,1,256]{2,1,0:T(1,128)S(1)} async-done(((f32[64,1,256]{2,1,0:T(1,128)}), f32[64,1,256]{2,1,0:T(1,128)S(1)}, u32[]{:S(2)}, u32[]{:S(2)}) %all-to-all-start.1) | async-done | bytes 65568 | tf_op jit(solution)/shard_map/all_to_all | solution.py:152
  95.8 0.7 reduce.2
  96.5 0.1 reshape.208
  96.6 2.7 %fusion.37 = f32[4,2048]{1,0:T(4,128)} fusion(f32[64,2048]{1,0:T(8,128)} %copy-done.10, f32[2048]{0:T(1024)S(1)} %fusion.41, f32[4,64,64]{2,0,1:T(4,128)S(1)} %bitcast.107), kind=kOutput, calls=%fused_computation.47 | convolution fusion | flops 403824640 | bytes 630784 | tf_op jit(solution)/shard_map/cok,fk->cof/dot_general | solution.py:153
  99.4 0.6 pad_maximum_fusion
  100.0 1.8 %copy-done = f32[5,4,14,2048]{3,0,2,1:T(8,128)} copy-done((f32[5,4,14,2048]{3,0,2,1:T(8,128)}, f32[5,4,14,2048]{3,0,2,1:T(8,128)S(1)}, u32[]{:S(2)}) %copy-start) | copy-done | bytes 2293784
  101.8 0.1 fusion.87
  101.9 3.1 %collective-permute-start.2 = (f32[5,4,14,3]{3,0,2,1:T(8,128)S(1)}, f32[5,4,14,3]{3,0,2,1:T(8,128)S(1)}, u32[]{:S(2)}, u32[]{:S(2)}) collective-permute-start(f32[5,4,14,3]{3,0,2,1:T(8,128)S(1)} %get-tuple-element.149), channel_id=1, source_target_pairs={{0,1},{1,2},{2,3},{3,0},{4,5},{5,6},{6,7},{7,4},{8,9},{9,10},{10,1... | collective-permute-start | bytes 10088 | tf_op jit(solution)/shard_map/ppermute | solution.py:19
  105.0 2.2 %collective-permute-start.3 = (f32[5,4,14,3]{3,0,2,1:T(8,128)S(1)}, f32[5,4,14,3]{3,0,2,1:T(8,128)}, u32[]{:S(2)}, u32[]{:S(2)}) collective-permute-start(f32[5,4,14,3]{3,0,2,1:T(8,128)S(1)} %get-tuple-element.150), channel_id=1, source_target_pairs={{1,0},{2,1},{3,2},{0,3},{5,4},{6,5},{7,6},{4,7},{9,8},{10,9},{11,1... | collective-permute-start | bytes 10088 | tf_op jit(solution)/shard_map/ppermute | solution.py:20
  107.2 3.4 %maximum_maximum_fusion = (f32[5,4,11,2048]{3,0,2,1:T(8,128)}, f32[5,4,11,2048]{3,0,2,1:T(8,128)}) fusion(f32[1,4,8,2048]{3,0,2,1:T(1,128)S(1)} %copy.62, f32[4,4,8,2048]{3,0,2,1:T(4,128)S(1)} %copy.61, f32[5,4,3,2048]{3,0,2,1:T(8,128)S(1)} %collective-permute-done, f32[5,4,3,2048]{3,0,2,1:T(8,128)S(1)} %collective-permute-done.1), kind=kLoop, calls=%fused_computation.42 | loop fusion | flops 1802240 | bytes 5898240 | tf_op jit(solution)/shard_map/concatenate | solution.py:21
  110.6 5.7 %collective-permute-done.2 = f32[5,4,14,3]{3,0,2,1:T(8,128)S(1)} collective-permute-done((f32[5,4,14,3]{3,0,2,1:T(8,128)S(1)}, f32[5,4,14,3]{3,0,2,1:T(8,128)S(1)}, u32[]{:S(2)}, u32[]{:S(2)}) %collective-permute-start.2) | collective-permute-done | bytes 3392 | tf_op jit(solution)/shard_map/ppermute | solution.py:19
  116.3 3.0 %collective-permute-done.3 = f32[5,4,14,3]{3,0,2,1:T(8,128)} collective-permute-done((f32[5,4,14,3]{3,0,2,1:T(8,128)S(1)}, f32[5,4,14,3]{3,0,2,1:T(8,128)}, u32[]{:S(2)}, u32[]{:S(2)}) %collective-permute-start.3) | collective-permute-done | bytes 3392 | tf_op jit(solution)/shard_map/ppermute | solution.py:20
  119.3 5.1 %concatenate.46 = f32[5,4,14,2054]{3,0,2,1:T(8,128)} concatenate(f32[5,4,14,3]{3,0,2,1:T(8,128)S(1)} %collective-permute-done.2, f32[5,4,14,2048]{3,0,2,1:T(8,128)} %copy-done, f32[5,4,14,3]{3,0,2,1:T(8,128)} %collective-permute-done.3), dimensions={3} | concatenate | bytes 4600960 | tf_op jit(solution)/shard_map/concatenate | solution.py:21
  124.4 2.8 %slice.209 = f32[1,4,14,2054]{3,0,2,1:T(1,128)S(1)} slice(f32[5,4,14,2054]{3,0,2,1:T(8,128)} %concatenate.46), slice={[4:5], [0:4], [0:14], [0:2054]} | slice | bytes 920192 | tf_op jit(solution)/shard_map/slice | solution.py:79
  127.1 0.1 copy.117
  127.2 0.6 fusion.90
  127.9 0.7 fusion.80
  128.6 13.5 %copy_add_fusion = f32[4,4,8,2048]{3,0,2,1:T(4,128)S(1)} fusion(f32[4,4,8,2048]{3,2,1,0:T(8,128)} %param.12, f32[4,4,8,2048]{3,0,2,1:T(4,128)} %bitcast.96, f32[5,4,14,3]{3,0,2,1:T(8,128)} %collective-permute-done.3, f32[5,4,3,2048]{3,0,2,1:T(8,128)S(1)} %collective-permute-done.1, f32[1,4,8,2048]{3,0,2,1:T(1,128)S(1)} %copy.62, ...), kind=kLoop, calls=%fused_computation.98 | loop fusion | flops 26476544 | bytes 16587328 | tf_op jit(solution)/shard_map/add | solution.py:156
  142.1 1.6 %copy.87 = f32[4,4,8,2048]{3,2,1,0:T(8,128)} copy(f32[4,4,8,2048]{3,0,2,1:T(4,128)S(1)} %copy_add_fusion) | data formatting | bytes 2097152
  (76 shorter events, 0.6 us)
Async XLA Ops:
  0.6 2.5 %copy-start.14 = (s32[2048,1]{0,1:T(1,128)S(1)}, s32[2048,1]{0,1:T(1,128)}, u32[]{:S(2)}) copy-start(s32[2048,1]{0,1:T(1,128)} %param.18) | copy-start | bytes 24580
  0.7 2.6 %copy-start.15 = (s32[2048]{0:T(1024)S(1)}, s32[2048]{0:T(1024)}, u32[]{:S(2)}) copy-start(s32[2048]{0:T(1024)} %param.19) | copy-start | bytes 24580
  0.7 2.9 %copy-start.13 = (f32[4,2048]{1,0:T(4,128)S(1)}, f32[4,2048]{1,0:T(4,128)}, u32[]{:S(2)}) copy-start(f32[4,2048]{1,0:T(4,128)} %param.15) | copy-start | bytes 98308
  0.7 2.9 %copy-start.16 = (f32[2048]{0:T(1024)S(1)}, f32[2048]{0:T(1024)}, u32[]{:S(2)}) copy-start(f32[2048]{0:T(1024)} %param.17) | copy-start | bytes 24580
  0.7 2.9 %copy-start.17 = (f32[2048]{0:T(1024)S(1)}, f32[2048]{0:T(1024)}, u32[]{:S(2)}) copy-start(f32[2048]{0:T(1024)} %param.16) | copy-start | bytes 24580
  3.2 14.2 %copy-start.4 = (f32[4,8,2048]{2,1,0:T(8,128)S(1)}, f32[4,8,2048]{2,1,0:T(8,128)}, u32[]{:S(2)}) copy-start(f32[4,8,2048]{2,1,0:T(8,128)} %param.13) | copy-start | bytes 786436
  3.2 14.5 %copy-start.3 = (f32[4,4,8,2048]{3,2,1,0:T(8,128)S(1)}, f32[4,4,8,2048]{3,2,1,0:T(8,128)}, u32[]{:S(2)}) copy-start(f32[4,4,8,2048]{3,2,1,0:T(8,128)} %param.11) | copy-start | bytes 3145732
  3.2 0.8 copy-start.10
  7.0 19.7 %all-to-all-start = ((f32[64,1,448]{2,1,0:T(1,128)}), f32[64,1,448]{2,1,0:T(1,128)S(1)}, u32[]{:S(2)}, u32[]{:S(2)}) async-start(f32[64,1,448]{2,1,0:T(1,128)} %reshape.205), calls=%async_computation | async-start | bytes 262144 | tf_op jit(solution)/shard_map/all_to_all | solution.py:123
  18.3 6.6 %copy-start.12 = (s32[4,8,2048]{2,1,0:T(8,128)S(1)}, s32[4,8,2048]{2,1,0:T(8,128)}, u32[]{:S(2)}) copy-start(s32[4,8,2048]{2,1,0:T(8,128)} %param.14) | copy-start | bytes 786436
  19.8 79.5 %collective-permute-start = (f32[5,4,3,2048]{3,0,2,1:T(8,128)}, f32[5,4,3,2048]{3,0,2,1:T(8,128)S(1)}, u32[]{:S(2)}, u32[]{:S(2)}) collective-permute-start(f32[5,4,3,2048]{3,0,2,1:T(8,128)} %get-tuple-element.153), channel_id=1, source_target_pairs={{0,4},{4,8},{8,12},{12,16},{16,20},{20,24},{24,28},{28,32},{32,36}... | collective-permute-start | bytes 1474568 | tf_op jit(solution)/shard_map/ppermute | solution.py:19
  21.5 77.9 %collective-permute-start.1 = (f32[5,4,3,2048]{3,0,2,1:T(8,128)}, f32[5,4,3,2048]{3,0,2,1:T(8,128)S(1)}, u32[]{:S(2)}, u32[]{:S(2)}) collective-permute-start(f32[5,4,3,2048]{3,0,2,1:T(8,128)} %get-tuple-element.154), channel_id=1, source_target_pairs={{4,0},{8,4},{12,8},{16,12},{20,16},{24,20},{28,24},{32,28},{36,32}... | collective-permute-start | bytes 1474568 | tf_op jit(solution)/shard_map/ppermute | solution.py:20
  26.7 0.7 copy-start.11
  31.8 6.7 %copy-start.7 = (f32[4,32,2048]{2,1,0:T(8,128)S(1)}, f32[4,32,2048]{2,1,0:T(8,128)}, u32[]{:S(2)}) copy-start(f32[4,32,2048]{2,1,0:T(8,128)} %get-tuple-element.225) | copy-start | bytes 3145732 | tf_op jit(solution)/shard_map/while
  42.0 1.0 copy-start.8
  43.1 6.7 %copy-start.7 = (f32[4,32,2048]{2,1,0:T(8,128)S(1)}, f32[4,32,2048]{2,1,0:T(8,128)}, u32[]{:S(2)}) copy-start(f32[4,32,2048]{2,1,0:T(8,128)} %get-tuple-element.225) | copy-start | bytes 3145732 | tf_op jit(solution)/shard_map/while
  53.3 1.0 copy-start.8
  54.4 6.7 %copy-start.7 = (f32[4,32,2048]{2,1,0:T(8,128)S(1)}, f32[4,32,2048]{2,1,0:T(8,128)}, u32[]{:S(2)}) copy-start(f32[4,32,2048]{2,1,0:T(8,128)} %get-tuple-element.225) | copy-start | bytes 3145732 | tf_op jit(solution)/shard_map/while
  64.6 1.0 copy-start.8
  65.7 6.7 %copy-start.7 = (f32[4,32,2048]{2,1,0:T(8,128)S(1)}, f32[4,32,2048]{2,1,0:T(8,128)}, u32[]{:S(2)}) copy-start(f32[4,32,2048]{2,1,0:T(8,128)} %get-tuple-element.225) | copy-start | bytes 3145732 | tf_op jit(solution)/shard_map/while
  75.9 1.0 copy-start.8
  78.7 17.0 %all-to-all-start.1 = ((f32[64,1,256]{2,1,0:T(1,128)}), f32[64,1,256]{2,1,0:T(1,128)S(1)}, u32[]{:S(2)}, u32[]{:S(2)}) async-start(f32[64,1,256]{2,1,0:T(1,128)} %reshape.207), calls=%async_computation.1 | async-start | bytes 131072 | tf_op jit(solution)/shard_map/all_to_all | solution.py:152
  100.0 1.8 %copy-start = (f32[5,4,14,2048]{3,0,2,1:T(8,128)}, f32[5,4,14,2048]{3,0,2,1:T(8,128)S(1)}, u32[]{:S(2)}) copy-start(f32[5,4,14,2048]{3,0,2,1:T(8,128)S(1)} %pad_maximum_fusion) | copy-start | bytes 6881284
  101.9 14.4 %collective-permute-start.2 = (f32[5,4,14,3]{3,0,2,1:T(8,128)S(1)}, f32[5,4,14,3]{3,0,2,1:T(8,128)S(1)}, u32[]{:S(2)}, u32[]{:S(2)}) collective-permute-start(f32[5,4,14,3]{3,0,2,1:T(8,128)S(1)} %get-tuple-element.149), channel_id=1, source_target_pairs={{0,1},{1,2},{2,3},{3,0},{4,5},{5,6},{6,7},{7,4},{8,9},{9,10},{10,1... | collective-permute-start | bytes 10088 | tf_op jit(solution)/shard_map/ppermute | solution.py:19
  105.0 14.3 %collective-permute-start.3 = (f32[5,4,14,3]{3,0,2,1:T(8,128)S(1)}, f32[5,4,14,3]{3,0,2,1:T(8,128)}, u32[]{:S(2)}, u32[]{:S(2)}) collective-permute-start(f32[5,4,14,3]{3,0,2,1:T(8,128)S(1)} %get-tuple-element.150), channel_id=1, source_target_pairs={{1,0},{2,1},{3,2},{0,3},{5,4},{6,5},{7,6},{4,7},{9,8},{10,9},{11,1... | collective-permute-start | bytes 10088 | tf_op jit(solution)/shard_map/ppermute | solution.py:20
  116.3 3.0 %copy-start.9 = (f32[5,4,14,3]{3,0,2,1:T(8,128)}, f32[5,4,14,3]{3,0,2,1:T(8,128)S(1)}, u32[]{:S(2)}) copy-start(f32[5,4,14,3]{3,0,2,1:T(8,128)S(1)} %collective-permute-done.2) | copy-start | bytes 10084
  124.3 4.2 %copy-start.1 = (f32[5,4,11,2048]{3,0,2,1:T(8,128)S(1)}, f32[5,4,11,2048]{3,0,2,1:T(8,128)}, u32[]{:S(2)}) copy-start(f32[5,4,11,2048]{3,0,2,1:T(8,128)} %get-tuple-element.151) | copy-start | bytes 5406724
  124.3 4.2 %copy-start.2 = (f32[5,4,11,2048]{3,0,2,1:T(8,128)S(1)}, f32[5,4,11,2048]{3,0,2,1:T(8,128)}, u32[]{:S(2)}) copy-start(f32[5,4,11,2048]{3,0,2,1:T(8,128)} %get-tuple-element.152) | copy-start | bytes 5406724
  124.3 4.2 %copy-start.5 = (f32[4,8,2048]{2,1,0:T(8,128)S(1)}, f32[4,8,2048]{2,1,0:T(8,128)}, u32[]{:S(2)}) copy-start(f32[4,8,2048]{2,1,0:T(8,128)} %get-tuple-element.172) | copy-start | bytes 786436
  124.3 4.2 %copy-start.6 = (f32[4,8,2048]{2,1,0:T(8,128)S(1)}, f32[4,8,2048]{2,1,0:T(8,128)}, u32[]{:S(2)}) copy-start(f32[4,8,2048]{2,1,0:T(8,128)} %get-tuple-element.173) | copy-start | bytes 786436
where the time goes:
time: 144 us
  matrix products  45.6 us (32%)
  other arithmetic  29 us (20%)
  local copies, waits for them, and re-layouts  28.8 us (20%)
  starting transfers between devices  26.2 us (18%)
  waiting for transfers between devices  12.7 us (9%)
    dot_general x4, matrix products, visit(): picked = jnp.einsum('cry,sy->csr', grid_rows, col_hot, precision=exact)  24.2 us
    dot_general x4, matrix products, visit(): added = jnp.einsum('csr,sy->cry', weighted, col_hot, precision=exact)  14.1 us
    add x1, other arithmetic, local(): new_state = start + dt_step * change  13.5 us
    all_to_all x1, starting transfers between devices, local(): lax.all_to_all(outgoing, 'gx', split_axis=1, concat_axis=1, tiled=True)  10.3 us
    all_to_all x1, starting transfers between devices, local(): lax.all_to_all(wall_flux, 'gx', split_axis=1, concat_axis=1, tiled=True)  8.95 us
    unnamed x38, local copies, waits for them, and re-layouts  7.06 us
    ppermute x2, waiting for transfers between devices, padded(): before = lax.ppermute(last, axis, up)  5.71 us
    concatenate x1, local copies, waits for them, and re-layouts, padded(): shard = jnp.concatenate([before, shard, after], axis=dim)  5.07 us
  transfers between devices with their start and end apart: 6, of which 3 were waited for; matrix products, arithmetic and copies ran while one was open for 46% of the time, Pallas kernels for 0%

commit v1 on v0

--- a/solution.py
+++ b/solution.py
@@ -3,6 +3,8 @@
 import jax
 import jax.numpy as jnp
 from jax import lax
+from jax.experimental import pallas as pl
+from jax.experimental.pallas import tpu as pltpu
 from jax.sharding import PartitionSpec as P
 
 dt_step = 0.2
@@ -69,6 +71,76 @@
     return (diffuse - advect - forcing) * (1.0 - solid.astype(jnp.float32))
 
 
+def _pieces(x, n):
+    out = []
+    rest = x
+    for _ in range(n):
+        p = rest.astype(jnp.bfloat16)
+        out.append(p)
+        rest = rest - p.astype(jnp.float32)
+    return out
+
+
+def owner_kernel(x_ref, cell_ref, wall_ref, area_ref, dist_ref, forcing_ref, flux_ref, pieces_ref):
+    rows, cols = x_ref.shape
+    fields = wall_ref.shape[0]
+    per_field = rows // fields
+    block = cell_ref.shape[1]
+
+    @pl.when(pl.program_id(0) == 0)
+    def _():
+        parts = _pieces(x_ref[...], 3)
+        for i, p in enumerate(parts):
+            pieces_ref[i * rows:(i + 1) * rows, :] = p
+        forcing_ref[...] = jnp.zeros_like(forcing_ref)
+
+    cell = cell_ref[...]
+    col = cell % cols
+    row = cell // cols
+    hot = (lax.broadcasted_iota(jnp.int32, (cols, block), 0) == col).astype(jnp.bfloat16)
+    picked = jnp.dot(pieces_ref[...], hot, preferred_element_type=jnp.float32)
+    value = (picked[0:rows] + picked[rows:2 * rows]) + picked[2 * rows:3 * rows]
+    pick_row = lax.broadcasted_iota(jnp.int32, (per_field, block), 0) == row
+    gathered = jnp.concatenate(
+        [jnp.sum(jnp.where(pick_row, value[f * per_field:(f + 1) * per_field], 0.0), axis=0, keepdims=True)
+         for f in range(fields)], axis=0)
+    flux = area_ref[...] * (gathered - wall_ref[...]) / dist_ref[...]
+    flux_ref[...] = flux
+    spread = jnp.concatenate(
+        [jnp.where(pick_row, flux[f:f + 1], 0.0) for f in range(fields)], axis=0)
+    w_hi, w_lo = _pieces(spread, 2)
+    w = jnp.concatenate([w_hi, w_lo], axis=0)
+    added = lax.dot_general(w, hot, (((1,), (1,)), ((), ())), preferred_element_type=jnp.float32)
+    forcing_ref[...] += added[0:rows] + added[rows:2 * rows]
+
+
+def owner_side(x, cell, wall, area, dist, block=256):
+    rows, cols = x.shape
+    fields, slots = wall.shape
+    steps = slots // block
+    return pl.pallas_call(
+        owner_kernel,
+        grid=(steps,),
+        in_specs=[
+            pl.BlockSpec((rows, cols), lambda j: (0, 0)),
+            pl.BlockSpec((1, block), lambda j: (0, j)),
+            pl.BlockSpec((fields, block), lambda j: (0, j)),
+            pl.BlockSpec((1, block), lambda j: (0, j)),
+            pl.BlockSpec((1, block), lambda j: (0, j)),
+        ],
+        out_specs=[
+            pl.BlockSpec((rows, cols), lambda j: (0, 0)),
+            pl.BlockSpec((fields, block), lambda j: (0, j)),
+        ],
+        out_shape=[
+            jax.ShapeDtypeStruct((rows, cols), jnp.float32),
+            jax.ShapeDtypeStruct((fields, slots), jnp.float32),
+        ],
+        scratch_shapes=[pltpu.VMEM((3 * rows, cols), jnp.bfloat16)],
+        compiler_params=pltpu.CompilerParams(dimension_semantics=("arbitrary",)),
+    )(x, cell, wall, area, dist)
+
+
 def local(state, start, eddy, solid, facet_wall, facet_dist, facet_area, facet_owner, facet_cell):
     levels = state.shape[1]
     cells_x = state.shape[2]
@@ -123,32 +195,14 @@
     received = lax.all_to_all(outgoing, "gx", split_axis=1, concat_axis=1, tiled=True).reshape(
         7, slots
     )
-    block_rows = math.gcd(slots, 1024)
-    block_count = slots // block_rows
     row_count = levels * cells_x
-    grid_rows = state.reshape(4, row_count, cells_y)
-    pieces = received.reshape(7, block_count, block_rows).transpose(1, 0, 2)
-    column_ids = jnp.arange(cells_y, dtype=jnp.int32)
-    row_ids = jnp.arange(row_count, dtype=jnp.int32)
-
-    def visit(forcing_sum, piece):
-        cell_index = (piece[6] + 0.5).astype(jnp.int32)
-        row_index = cell_index // cells_y
-        col_index = cell_index % cells_y
-        col_hot = (col_index[:, None] == column_ids[None, :]).astype(jnp.float32)
-        row_hot = (row_index[:, None] == row_ids[None, :]).astype(jnp.float32)
-        picked = jnp.einsum("cry,sy->csr", grid_rows, col_hot, precision=exact)
-        cell_values = jnp.sum(picked * row_hot[None], axis=2)
-        wall_flux = piece[5] * (cell_values - piece[:4]) / piece[4]
-        weighted = wall_flux[:, :, None] * row_hot[None]
-        added = jnp.einsum("csr,sy->cry", weighted, col_hot, precision=exact)
-        return (forcing_sum + added, wall_flux)
-
-    forcing_rows, flux_blocks = lax.scan(
-        visit, jnp.zeros((4, row_count, cells_y), jnp.float32), pieces
+    grid_rows = state.reshape(4 * row_count, cells_y)
+    cell_index = (received[6:7] + 0.5).astype(jnp.int32)
+    forcing_rows, flux_slots = owner_side(
+        grid_rows, cell_index, received[:4], received[5:6], received[4:5]
     )
     forcing = forcing_rows.reshape(state.shape)
-    wall_flux = flux_blocks.transpose(1, 0, 2).reshape(4, owners_gx, capacity)
+    wall_flux = flux_slots.reshape(4, owners_gx, capacity)
     returned = lax.all_to_all(wall_flux, "gx", split_axis=1, concat_axis=1, tiled=True)
     through = jnp.einsum("cok,fk->cof", returned, rank_hot, precision=exact)
     facet_flux = jnp.sum(through * owner_float.T[None], axis=1)

time: 144 us -> 142 us (0.986)
  matrix products: 45.6 us -> 7.39 us
  Pallas kernels: 0 us -> 27.9 us
  local copies, waits for them, and re-layouts: 28.8 us -> 32.6 us
  waiting for transfers between devices: 12.7 us -> 15.2 us
    dot_general x8 -> x0, matrix products: 38.2 us -> none  [the longest x4 24.2 us: visit(): picked = jnp.einsum('cry,sy->csr', grid_rows, col_hot, precision=exact)]
    pallas_call x0 -> x1, Pallas kernels: none -> 27.9 us  [owner_side(): pl.pallas_call(owner_kernel, grid=(steps,), in_specs=[pl.BlockSpec((rows,...]
    slice x8 -> x6, local copies, waits for them, and re-layouts: 0.15 us -> 8 us  [the longest x2 3.29 us: local(): received[4:5]]
    while x17 -> x0, local copies, waits for them, and re-layouts: 6.77 us -> none
    all_to_all x1, waiting for transfers between devices: 4.08 us -> 8.13 us  [local(): lax.all_to_all(wall_flux, 'gx', split_axis=1, concat_axis=1, tiled=True)]
    dynamic_update_slice x4 -> x0, other arithmetic: 2.48 us -> none  [local(): lax.scan(visit, jnp.zeros((4, row_count, cells_y), jnp.float32), pieces)]
    concatenate x2, other arithmetic: 4 us -> 6.32 us  [padded(): shard = jnp.concatenate([before, shard, after], axis=dim)]
    unnamed x38 -> x44, local copies, waits for them, and re-layouts: 7.06 us -> 9.37 us
  transfers between devices with their start and end apart: 6 -> 6, of which waited for: 3 -> 4; matrix products, arithmetic and copies ran while one was open for 46% -> 24% of each run, Pallas kernels for 0% -> 20%
where the time goes in v1:
time: 142 us; the launch traced here: 141 us
  local copies, waits for them, and re-layouts  32.6 us (23%)
  other arithmetic  29.9 us (21%)
  Pallas kernels  27.9 us (20%)
  starting transfers between devices  26.6 us (19%)
  waiting for transfers between devices  15.2 us (11%)
  matrix products  7.39 us (5%)
    pallas_call x1, Pallas kernels, owner_side(): pl.pallas_call(owner_kernel, grid=(steps,), in_specs=[pl.BlockSpec((rows,...  27.9 us
    add x1, other arithmetic, local(): new_state = start + dt_step * change  14.1 us
    all_to_all x1, starting transfers between devices, local(): lax.all_to_all(outgoing, 'gx', split_axis=1, concat_axis=1, tiled=True)  10.3 us
    unnamed x44, local copies, waits for them, and re-layouts  9.37 us
    all_to_all x1, starting transfers between devices, local(): lax.all_to_all(wall_flux, 'gx', split_axis=1, concat_axis=1, tiled=True)  9.34 us
    all_to_all x1, waiting for transfers between devices, local(): lax.all_to_all(wall_flux, 'gx', split_axis=1, concat_axis=1, tiled=True)  8.13 us
    concatenate x2, other arithmetic, padded(): shard = jnp.concatenate([before, shard, after], axis=dim)  6.32 us
    concatenate x1, local copies, waits for them, and re-layouts, padded(): shard = jnp.concatenate([before, shard, after], axis=dim)  5.16 us
  transfers between devices with their start and end apart: 6, of which 4 were waited for; matrix products, arithmetic and copies ran while one was open for 24% of the time, Pallas kernels for 20%

profile of v1, /device:TPU:1, one launch (start us, length us, event | category | flops | bytes accessed | tf_op | source)
XLA Modules:
  0.0 140.6 jit_solution(14225684786452791873)
XLA Ops:
  0.6 0.0 copy-start.15
  0.7 0.0 copy-start.16
  0.7 0.0 copy-start.14
  0.7 0.0 copy-start.17
  0.7 0.0 copy-start.18
  0.7 2.4 %fusion.10 = f32[2048]{0:T(1024)S(1)} fusion(s32[2048]{0:T(1024)} %bitcast.43), kind=kOutput, calls=%fused_computation.13 | convolution fusion | flops 541849600 | bytes 16384 | tf_op jit(solution)/shard_map/dot_general | solution.py:180
  3.2 0.0 copy-start.5
  3.2 0.0 copy-start.3
  3.3 0.3 convolution_subtract_fusion
  3.6 0.4 copy-done.11
  4.1 1.9 %fusion.7 = f32[7,64,64]{2,1,0:T(8,128)S(1)} fusion(f32[64,2048]{1,0:T(8,128)S(1)} %fusion.45, f32[7,2048]{1,0:T(8,128)S(1)} %pad_maximum_fusion.17, f32[2048]{0:T(1024)S(1)} %fusion.10, f32[64,64]{1,0:T(8,128)S(1)} %convolution_subtract_fusion, f32[7]{0:T(128)S(1)} %compare_convert_fusion), kind=kOutput, calls=%fused_computation.12 | convolution fusion | flops 705748992 | bytes 720924 | tf_op jit(solution)/shard_map/cof,fk->cok/dot_general | solution.py:191
  6.0 0.1 copy.110
  6.2 0.8 reshape.103
  7.0 10.3 %all-to-all-start = ((f32[64,1,448]{2,1,0:T(1,128)}), f32[64,1,448]{2,1,0:T(1,128)S(1)}, u32[]{:S(2)}, u32[]{:S(2)}) async-start(f32[64,1,448]{2,1,0:T(1,128)} %reshape.103), calls=%async_computation | async-start | bytes 262144 | tf_op jit(solution)/shard_map/all_to_all | solution.py:195
  17.4 0.3 copy.60
  17.6 0.7 copy.59
  18.3 0.0 copy-start.13
  18.3 1.5 %pad_maximum_fusion.16 = (f32[5,4,3,2048]{3,0,2,1:T(8,128)}, f32[5,4,3,2048]{3,0,2,1:T(8,128)}) fusion(f32[1,4,8,2048]{3,0,2,1:T(1,128)S(1)} %copy.60, f32[4,4,8,2048]{3,0,2,1:T(4,128)S(1)} %copy.59), kind=kLoop, calls=%fused_computation.64 | loop fusion | flops 245760 | bytes 2293760 | tf_op jit(solution)/shard_map/slice | solution.py:19
  19.8 1.6 %collective-permute-start = (f32[5,4,3,2048]{3,0,2,1:T(8,128)}, f32[5,4,3,2048]{3,0,2,1:T(8,128)S(1)}, u32[]{:S(2)}, u32[]{:S(2)}) collective-permute-start(f32[5,4,3,2048]{3,0,2,1:T(8,128)} %get-tuple-element.18), channel_id=1, source_target_pairs={{0,4},{4,8},{8,12},{12,16},{16,20},{20,24},{24,28},{28,32},{32,36}... | collective-permute-start | bytes 1474568 | tf_op jit(solution)/shard_map/ppermute | solution.py:21
  21.5 0.0 collective-permute-start.1
  21.5 0.9 slice_bitcast_fusion.1
  22.4 1.5 %fusion.59 = (f32[4,3,8,2048]{3,0,2,1:T(4,128)}, f32[4,3,8,2048]{3,0,2,1:T(4,128)}) fusion(f32[4,4,8,2048]{3,0,2,1:T(4,128)S(1)} %copy.59), kind=kLoop, calls=%fused_computation.102 | loop fusion | bytes 3145728 | tf_op jit(solution)/shard_map/slice | solution.py:49
  23.9 0.9 fusion.62
  24.8 0.8 fusion.60
  25.6 0.2 all-to-all-done
  25.8 0.7 copy-done.12
  26.5 0.6 broadcast.122
  27.1 1.9 %reduce.12 = f32[64,448]{1,0:T(8,128)S(1)} reduce(f32[64,1,448]{2,1,0:T(1,128)} %copy-done.12, f32[]{:T(128)} %broadcast.122), dimensions={1}, to_apply=%all_to_all.6.reduce_sub_computation | reduce | bytes 229380 | tf_op jit(solution)/shard_map/all_to_all | solution.py:195
  29.0 0.8 reshape.104
  29.8 1.7 %fusion.57 = s32[64,64]{1,0:T(8,128)} fusion(f32[7,64,64]{2,0,1:T(8,128)} %bitcast.37), kind=kLoop, calls=%fused_computation.99 | loop fusion | flops 8192 | bytes 32768 | tf_op jit(solution)/shard_map/convert_element_type | solution.py:200
  31.5 1.8 %slice_reduce_fusion = (f32[64,64]{1,0:T(8,128)}, f32[64,64]{1,0:T(8,128)}) fusion(f32[7,64,64]{2,0,1:T(8,128)} %bitcast.38), kind=kLoop, calls=%fused_computation.95 | loop fusion | bytes 65536 | tf_op jit(solution)/shard_map/slice | solution.py:202
  33.3 1.0 slice.219
  34.3 1.4 %convert_element_type.51.cell_ref = s32[1,4096]{1,0:T(1,128)} reshape(s32[64,64]{1,0:T(8,128)} %fusion.57) | data formatting | bytes 32768 | tf_op jit(solution)/shard_map/convert_element_type | solution.py:200
  35.7 0.7 copy.78
  36.4 1.6 %slice.196.wall_ref = f32[4,4096]{1,0:T(4,128)} reshape(f32[4,64,64]{2,1,0:T(8,128)} %copy.78) | data formatting | bytes 131072 | tf_op jit(solution)/shard_map/slice | solution.py:202
  38.0 1.4 %slice.200.dist_ref = f32[1,4096]{1,0:T(1,128)} reshape(f32[64,64]{1,0:T(8,128)} %get-tuple-element.12) | data formatting | bytes 32768 | tf_op jit(solution)/shard_map/slice | solution.py:202
  39.5 1.4 %slice.198.area_ref = f32[1,4096]{1,0:T(1,128)} reshape(f32[64,64]{1,0:T(8,128)} %get-tuple-element.13) | data formatting | bytes 32768 | tf_op jit(solution)/shard_map/slice | solution.py:202
  40.9 27.9 %shard_map.104 = (f32[128,2048]{1,0:T(8,128)}, f32[4,4096]{1,0:T(4,128)}) custom-call(f32[128,2048]{1,0:T(8,128)} %bitcast.32, s32[1,4096]{1,0:T(1,128)} %convert_element_type.51.cell_ref, f32[4,4096]{1,0:T(4,128)} %slice.196.wall_ref, f32[1,4096]{1,0:T(1,128)} %slice.198.area_ref, f32[1,4096]{1,0:T(1,128)} %slice.200.dist_ref), custom_call_target="tpu_custom_call" | custom-call | tf_op jit(solution)/shard_map/pallas_call | solution.py:121
  68.8 1.0 reshape.82
  69.8 0.7 copy.111
  70.5 1.7 %reshape.105 = f32[64,1,256]{2,1,0:T(1,128)} reshape(f32[64,4,64]{2,1,0:T(4,128)} %bitcast.40) | data formatting | bytes 131072
  72.2 9.3 %all-to-all-start.1 = ((f32[64,1,256]{2,1,0:T(1,128)}), f32[64,1,256]{2,1,0:T(1,128)}, u32[]{:S(2)}, u32[]{:S(2)}) async-start(f32[64,1,256]{2,1,0:T(1,128)} %reshape.105), calls=%async_computation.1 | async-start | bytes 131072 | tf_op jit(solution)/shard_map/all_to_all | solution.py:206
  81.5 0.1 broadcast_compare_fusion.1
  81.6 8.1 %all-to-all-done.1 = f32[64,1,256]{2,1,0:T(1,128)} async-done(((f32[64,1,256]{2,1,0:T(1,128)}), f32[64,1,256]{2,1,0:T(1,128)}, u32[]{:S(2)}, u32[]{:S(2)}) %all-to-all-start.1) | async-done | bytes 65568 | tf_op jit(solution)/shard_map/all_to_all | solution.py:206
  89.8 1.7 %reduce.13 = f32[64,256]{1,0:T(8,128)S(1)} reduce(f32[64,1,256]{2,1,0:T(1,128)} %all-to-all-done.1, f32[]{:T(128)} %broadcast.122), dimensions={1}, to_apply=%all_to_all.7.reduce_sub_computation | reduce | bytes 131076 | tf_op jit(solution)/shard_map/all_to_all | solution.py:206
  91.4 0.1 reshape.106
  91.6 2.7 %fusion.6 = f32[4,2048]{1,0:T(4,128)} fusion(f32[64,2048]{1,0:T(8,128)} %copy-done.11, f32[2048]{0:T(1024)S(1)} %fusion.10, f32[4,64,64]{2,0,1:T(4,128)S(1)} %bitcast.41), kind=kOutput, calls=%fused_computation.11 | convolution fusion | flops 403824640 | bytes 630784 | tf_op jit(solution)/shard_map/cok,fk->cof/dot_general | solution.py:207
  94.3 0.0 collective-permute-done
  94.3 1.7 %pad_maximum_fusion = f32[5,4,14,2048]{3,0,2,1:T(8,128)S(1)} fusion(f32[5,4,3,2048]{3,0,2,1:T(8,128)} %collective-permute-done.1, f32[1,4,8,2048]{3,0,2,1:T(1,128)S(1)} %copy.60, f32[4,4,8,2048]{3,0,2,1:T(4,128)S(1)} %copy.59, f32[5,4,3,2048]{3,0,2,1:T(8,128)S(1)} %collective-permute-done), kind=kLoop, calls=%fused_computation.2 | loop fusion | flops 1720320 | bytes 4587520 | tf_op jit(solution)/shard_map/concatenate | solution.py:23
  96.1 1.8 %copy-done = f32[5,4,14,2048]{3,0,2,1:T(8,128)} copy-done((f32[5,4,14,2048]{3,0,2,1:T(8,128)}, f32[5,4,14,2048]{3,0,2,1:T(8,128)S(1)}, u32[]{:S(2)}) %copy-start) | copy-done | bytes 2293784
  97.9 0.1 fusion.58
  98.0 3.1 %collective-permute-start.2 = (f32[5,4,14,3]{3,0,2,1:T(8,128)S(1)}, f32[5,4,14,3]{3,0,2,1:T(8,128)S(1)}, u32[]{:S(2)}, u32[]{:S(2)}) collective-permute-start(f32[5,4,14,3]{3,0,2,1:T(8,128)S(1)} %get-tuple-element.14), channel_id=1, source_target_pairs={{0,1},{1,2},{2,3},{3,0},{4,5},{5,6},{6,7},{7,4},{8,9},{9,10},{10,1... | collective-permute-start | bytes 10088 | tf_op jit(solution)/shard_map/ppermute | solution.py:21
  101.1 2.2 %collective-permute-start.3 = (f32[5,4,14,3]{3,0,2,1:T(8,128)S(1)}, f32[5,4,14,3]{3,0,2,1:T(8,128)}, u32[]{:S(2)}, u32[]{:S(2)}) collective-permute-start(f32[5,4,14,3]{3,0,2,1:T(8,128)S(1)} %get-tuple-element.15), channel_id=1, source_target_pairs={{1,0},{2,1},{3,2},{0,3},{5,4},{6,5},{7,6},{4,7},{9,8},{10,9},{11,1... | collective-permute-start | bytes 10088 | tf_op jit(solution)/shard_map/ppermute | solution.py:22
  103.3 4.6 %maximum_maximum_fusion = (f32[5,4,11,2048]{3,0,2,1:T(8,128)}, f32[5,4,11,2048]{3,0,2,1:T(8,128)}) fusion(f32[1,4,8,2048]{3,0,2,1:T(1,128)S(1)} %copy.60, f32[4,4,8,2048]{3,0,2,1:T(4,128)S(1)} %copy.59, f32[5,4,3,2048]{3,0,2,1:T(8,128)S(1)} %collective-permute-done, f32[5,4,3,2048]{3,0,2,1:T(8,128)} %collective-permute-done.1), kind=kLoop, calls=%fused_computation.6 | loop fusion | flops 1802240 | bytes 5898240 | tf_op jit(solution)/shard_map/concatenate | solution.py:23
  107.9 4.8 %collective-permute-done.2 = f32[5,4,14,3]{3,0,2,1:T(8,128)S(1)} collective-permute-done((f32[5,4,14,3]{3,0,2,1:T(8,128)S(1)}, f32[5,4,14,3]{3,0,2,1:T(8,128)S(1)}, u32[]{:S(2)}, u32[]{:S(2)}) %collective-permute-start.2) | collective-permute-done | bytes 3392 | tf_op jit(solution)/shard_map/ppermute | solution.py:21
  112.7 0.7 copy-done.10
  113.4 2.0 %collective-permute-done.3 = f32[5,4,14,3]{3,0,2,1:T(8,128)} collective-permute-done((f32[5,4,14,3]{3,0,2,1:T(8,128)S(1)}, f32[5,4,14,3]{3,0,2,1:T(8,128)}, u32[]{:S(2)}, u32[]{:S(2)}) %collective-permute-start.3) | collective-permute-done | bytes 3392 | tf_op jit(solution)/shard_map/ppermute | solution.py:22
  115.4 5.2 %concatenate.46 = f32[5,4,14,2054]{3,0,2,1:T(8,128)} concatenate(f32[5,4,14,3]{3,0,2,1:T(8,128)} %copy-done.10, f32[5,4,14,2048]{3,0,2,1:T(8,128)} %copy-done, f32[5,4,14,3]{3,0,2,1:T(8,128)} %collective-permute-done.3), dimensions={3} | concatenate | bytes 4600960 | tf_op jit(solution)/shard_map/concatenate | solution.py:23
  120.6 2.8 %slice.203 = f32[1,4,14,2054]{3,0,2,1:T(1,128)S(1)} slice(f32[5,4,14,2054]{3,0,2,1:T(8,128)} %concatenate.46), slice={[4:5], [0:4], [0:14], [0:2054]} | slice | bytes 920192 | tf_op jit(solution)/shard_map/slice | solution.py:151
  123.4 0.1 copy.109
  123.5 0.6 fusion.61
  124.1 0.7 fusion.49
  124.9 14.1 %copy_add_fusion = f32[4,4,8,2048]{3,0,2,1:T(4,128)S(1)} fusion(f32[4,4,8,2048]{3,2,1,0:T(8,128)} %param.10, f32[4,4,8,2048]{3,2,1,0:T(8,128)} %bitcast.35, f32[5,4,14,3]{3,0,2,1:T(8,128)} %collective-permute-done.3, f32[5,4,3,2048]{3,0,2,1:T(8,128)} %collective-permute-done.1, f32[1,4,8,2048]{3,0,2,1:T(1,128)S(1)} %copy.60, f32[4,4,8,2048]{3,0,2,1:T(4,128)S(1)} %copy.59, ...), kind=kLoop, calls=%fused_computation.62 | loop fusion | flops 26476544 | bytes 16587328 | tf_op jit(solution)/shard_map/add | solution.py:210
  139.0 1.6 %copy.83 = f32[4,4,8,2048]{3,2,1,0:T(8,128)} copy(f32[4,4,8,2048]{3,0,2,1:T(4,128)S(1)} %copy_add_fusion) | data formatting | bytes 2097152
  (32 shorter events, 0.2 us)
Async XLA Ops:
  0.6 2.5 %copy-start.15 = (s32[2048,1]{0,1:T(1,128)S(1)}, s32[2048,1]{0,1:T(1,128)}, u32[]{:S(2)}) copy-start(s32[2048,1]{0,1:T(1,128)} %param.16) | copy-start | bytes 24580
  0.7 2.6 %copy-start.16 = (s32[2048]{0:T(1024)S(1)}, s32[2048]{0:T(1024)}, u32[]{:S(2)}) copy-start(s32[2048]{0:T(1024)} %param.17) | copy-start | bytes 24580
  0.7 2.9 %copy-start.14 = (f32[4,2048]{1,0:T(4,128)S(1)}, f32[4,2048]{1,0:T(4,128)}, u32[]{:S(2)}) copy-start(f32[4,2048]{1,0:T(4,128)} %param.13) | copy-start | bytes 98308
  0.7 2.9 %copy-start.17 = (f32[2048]{0:T(1024)S(1)}, f32[2048]{0:T(1024)}, u32[]{:S(2)}) copy-start(f32[2048]{0:T(1024)} %param.15) | copy-start | bytes 24580
  0.7 2.9 %copy-start.18 = (f32[2048]{0:T(1024)S(1)}, f32[2048]{0:T(1024)}, u32[]{:S(2)}) copy-start(f32[2048]{0:T(1024)} %param.14) | copy-start | bytes 24580
  3.2 14.2 %copy-start.5 = (f32[4,8,2048]{2,1,0:T(8,128)S(1)}, f32[4,8,2048]{2,1,0:T(8,128)}, u32[]{:S(2)}) copy-start(f32[4,8,2048]{2,1,0:T(8,128)} %param.11) | copy-start | bytes 786436
  3.2 14.5 %copy-start.3 = (f32[4,4,8,2048]{3,2,1,0:T(8,128)S(1)}, f32[4,4,8,2048]{3,2,1,0:T(8,128)}, u32[]{:S(2)}) copy-start(f32[4,4,8,2048]{3,2,1,0:T(8,128)} %param.9) | copy-start | bytes 3145732
  3.2 0.8 copy-start.11
  7.0 18.8 %all-to-all-start = ((f32[64,1,448]{2,1,0:T(1,128)}), f32[64,1,448]{2,1,0:T(1,128)S(1)}, u32[]{:S(2)}, u32[]{:S(2)}) async-start(f32[64,1,448]{2,1,0:T(1,128)} %reshape.103), calls=%async_computation | async-start | bytes 262144 | tf_op jit(solution)/shard_map/all_to_all | solution.py:195
  18.3 5.5 %copy-start.13 = (s32[4,8,2048]{2,1,0:T(8,128)S(1)}, s32[4,8,2048]{2,1,0:T(8,128)}, u32[]{:S(2)}) copy-start(s32[4,8,2048]{2,1,0:T(8,128)} %param.12) | copy-start | bytes 786436
  19.8 74.5 %collective-permute-start = (f32[5,4,3,2048]{3,0,2,1:T(8,128)}, f32[5,4,3,2048]{3,0,2,1:T(8,128)S(1)}, u32[]{:S(2)}, u32[]{:S(2)}) collective-permute-start(f32[5,4,3,2048]{3,0,2,1:T(8,128)} %get-tuple-element.18), channel_id=1, source_target_pairs={{0,4},{4,8},{8,12},{12,16},{16,20},{20,24},{24,28},{28,32},{32,36}... | collective-permute-start | bytes 1474568 | tf_op jit(solution)/shard_map/ppermute | solution.py:21
  21.5 72.8 %collective-permute-start.1 = (f32[5,4,3,2048]{3,0,2,1:T(8,128)}, f32[5,4,3,2048]{3,0,2,1:T(8,128)}, u32[]{:S(2)}, u32[]{:S(2)}) collective-permute-start(f32[5,4,3,2048]{3,0,2,1:T(8,128)} %get-tuple-element.19), channel_id=1, source_target_pairs={{4,0},{8,4},{12,8},{16,12},{20,16},{24,20},{28,24},{32,28},{36,32}... | collective-permute-start | bytes 1474568 | tf_op jit(solution)/shard_map/ppermute | solution.py:22
  23.9 57.7 %copy-start.4 = (f32[4,4,8,2048]{3,2,1,0:T(8,128)S(1)}, f32[4,4,8,2048]{3,2,1,0:T(8,128)}, u32[]{:S(2)}) copy-start(f32[4,4,8,2048]{3,2,1,0:T(8,128)} %param.9) | copy-start | bytes 3145732
  25.8 0.7 copy-start.12
  72.2 17.6 %all-to-all-start.1 = ((f32[64,1,256]{2,1,0:T(1,128)}), f32[64,1,256]{2,1,0:T(1,128)}, u32[]{:S(2)}, u32[]{:S(2)}) async-start(f32[64,1,256]{2,1,0:T(1,128)} %reshape.105), calls=%async_computation.1 | async-start | bytes 131072 | tf_op jit(solution)/shard_map/all_to_all | solution.py:206
  96.0 1.8 %copy-start = (f32[5,4,14,2048]{3,0,2,1:T(8,128)}, f32[5,4,14,2048]{3,0,2,1:T(8,128)S(1)}, u32[]{:S(2)}) copy-start(f32[5,4,14,2048]{3,0,2,1:T(8,128)S(1)} %pad_maximum_fusion) | copy-start | bytes 6881284
  98.0 14.7 %collective-permute-start.2 = (f32[5,4,14,3]{3,0,2,1:T(8,128)S(1)}, f32[5,4,14,3]{3,0,2,1:T(8,128)S(1)}, u32[]{:S(2)}, u32[]{:S(2)}) collective-permute-start(f32[5,4,14,3]{3,0,2,1:T(8,128)S(1)} %get-tuple-element.14), channel_id=1, source_target_pairs={{0,1},{1,2},{2,3},{3,0},{4,5},{5,6},{6,7},{7,4},{8,9},{9,10},{10,1... | collective-permute-start | bytes 10088 | tf_op jit(solution)/shard_map/ppermute | solution.py:21
  101.1 14.4 %collective-permute-start.3 = (f32[5,4,14,3]{3,0,2,1:T(8,128)S(1)}, f32[5,4,14,3]{3,0,2,1:T(8,128)}, u32[]{:S(2)}, u32[]{:S(2)}) collective-permute-start(f32[5,4,14,3]{3,0,2,1:T(8,128)S(1)} %get-tuple-element.15), channel_id=1, source_target_pairs={{1,0},{2,1},{3,2},{0,3},{5,4},{6,5},{7,6},{4,7},{9,8},{10,9},{11,1... | collective-permute-start | bytes 10088 | tf_op jit(solution)/shard_map/ppermute | solution.py:22
  112.7 0.7 copy-start.10
  115.4 9.4 %copy-start.6 = (f32[4,3,8,2048]{3,0,2,1:T(4,128)S(1)}, f32[4,3,8,2048]{3,0,2,1:T(4,128)}, u32[]{:S(2)}) copy-start(f32[4,3,8,2048]{3,0,2,1:T(4,128)} %get-tuple-element.25) | copy-start | bytes 2359300
  115.4 9.4 %copy-start.9 = (f32[4,8,2048]{2,1,0:T(8,128)S(1)}, f32[4,8,2048]{2,1,0:T(8,128)}, u32[]{:S(2)}) copy-start(f32[4,8,2048]{2,1,0:T(8,128)} %get-tuple-element.39) | copy-start | bytes 786436
  120.6 4.2 %copy-start.1 = (f32[5,4,11,2048]{3,0,2,1:T(8,128)S(1)}, f32[5,4,11,2048]{3,0,2,1:T(8,128)}, u32[]{:S(2)}) copy-start(f32[5,4,11,2048]{3,0,2,1:T(8,128)} %get-tuple-element.16) | copy-start | bytes 5406724
  120.6 4.3 %copy-start.2 = (f32[5,4,11,2048]{3,0,2,1:T(8,128)S(1)}, f32[5,4,11,2048]{3,0,2,1:T(8,128)}, u32[]{:S(2)}) copy-start(f32[5,4,11,2048]{3,0,2,1:T(8,128)} %get-tuple-element.17) | copy-start | bytes 5406724
  120.6 4.3 %copy-start.7 = (f32[4,8,2048]{2,1,0:T(8,128)S(1)}, f32[4,8,2048]{2,1,0:T(8,128)}, u32[]{:S(2)}) copy-start(f32[4,8,2048]{2,1,0:T(8,128)} %get-tuple-element.37) | copy-start | bytes 786436
  120.6 4.3 %copy-start.8 = (f32[4,8,2048]{2,1,0:T(8,128)S(1)}, f32[4,8,2048]{2,1,0:T(8,128)}, u32[]{:S(2)}) copy-start(f32[4,8,2048]{2,1,0:T(8,128)} %get-tuple-element.38) | copy-start | bytes 786436

commit v2 on v1

v2 whole, which is shorter than its diff:
```python
import math

import jax
import jax.numpy as jnp
from jax import lax
from jax.experimental import pallas as pl
from jax.experimental.pallas import tpu as pltpu
from jax.sharding import PartitionSpec as P

dt_step = 0.2
exact = lax.Precision.HIGHEST


def _upwind(s, c):
    forward = (((((-2.0 * s(-3) + 15.0 * s(-2)) - 60.0 * s(-1)) + 20.0 * s(0)) + 30.0 * s(1)) - 3.0 * s(2))
    backward = (((((3.0 * s(-2) - 30.0 * s(-1)) - 20.0 * s(0)) + 60.0 * s(1)) - 15.0 * s(2)) + 2.0 * s(3))
    return jnp.where(c > 0, forward, backward) / 60.0


def _x_shifter(f, lo, hi):
    rows = f.shape[0]
    row = lax.broadcasted_iota(jnp.int32, f.shape, 0)
    width = lo.shape[0]
    lo_b = [jnp.broadcast_to(lo[i:i + 1], f.shape) for i in range(width)]
    hi_b = [jnp.broadcast_to(hi[i:i + 1], f.shape) for i in range(width)]
    cache = {0: f}

    def s(k):
        if k in cache:
            return cache[k]
        if k > 0:
            r = pltpu.roll(f, rows - k, 0)
            patch = hi_b[k - 1]
            for i in range(k - 2, -1, -1):
                patch = jnp.where(row == rows - k + i, hi_b[i], patch)
            out = jnp.where(row < rows - k, r, patch)
        else:
            m = -k
            r = pltpu.roll(f, m, 0)
            patch = lo_b[width - 1]
            for i in range(m - 1):
                patch = jnp.where(row == i, lo_b[width - m + i], patch)
            out = jnp.where(row >= m, r, patch)
        cache[k] = out
        return out
    return s


def _y_shifter(f, lo, hi):
    cols = f.shape[1]
    edge = lo.shape[1]
    lane = lax.broadcasted_iota(jnp.int32, lo.shape, 1)
    cache = {0: f}

    def s(k):
        if k in cache:
            return cache[k]
        if k > 0:
            r = pltpu.roll(f, cols - k, 1)
            patch = pltpu.roll(hi, edge - k, 1)
            last = jnp.where(lane >= edge - k, patch, r[:, cols - edge:])
            out = jnp.concatenate([r[:, :cols - edge], last], axis=1)
        else:
            m = -k
            r = pltpu.roll(f, m, 1)
            patch = pltpu.roll(lo, m, 1)
            first = jnp.where(lane < m, patch, r[:, :edge])
            out = jnp.concatenate([first, r[:, edge:]], axis=1)
        cache[k] = out
        return out
    return s


def stencil_kernel(sc_ref, sd_ref, su_ref, xl_ref, xh_ref, yl_ref, yh_ref, out_ref):
    level = pl.program_id(0)
    levels = pl.num_programs(0)
    fields = sc_ref.shape[0] - 1
    e = sc_ref[fields, 0]
    ed = sd_ref[fields, 0]
    eu = su_ref[fields, 0]
    up_w = jnp.where(level < levels - 1, 1.0, 0.0)
    down_w = jnp.where(level > 0, 1.0, 0.0)
    eddy_up = (0.5 * (e + eu)) * up_w
    eddy_down = (0.5 * (ed + e)) * down_w
    ex = _x_shifter(e, xl_ref[fields, 0, 2:3], xh_ref[fields, 0, 0:1])
    ey = _y_shifter(e, yl_ref[fields, 0], yh_ref[fields, 0])
    east = 0.5 * (e + ex(1))
    west = 0.5 * (ex(-1) + e)
    north = 0.5 * (e + ey(1))
    south = 0.5 * (ey(-1) + e)
    u = sc_ref[0, 0]
    v = sc_ref[1, 0]
    w = sc_ref[2, 0]
    for f in range(fields):
        fv = sc_ref[f, 0]
        lower = sd_ref[f, 0]
        upper = su_ref[f, 0]
        sx = _x_shifter(fv, xl_ref[f, 0], xh_ref[f, 0])
        sy = _y_shifter(fv, yl_ref[f, 0], yh_ref[f, 0])
        derx = _upwind(sx, u)
        dery = _upwind(sy, v)
        derz = (upper - lower) * 0.5
        zdiffuse = eddy_up * (upper - fv) - eddy_down * (fv - lower)
        advect = (u * derx + v * dery) + w * derz
        diff_x = east * (sx(1) - fv) - west * (fv - sx(-1))
        diff_y = north * (sy(1) - fv) - south * (fv - sy(-1))
        diffuse = (diff_x + diff_y) + zdiffuse
        out_ref[f, 0] = diffuse - advect


def stencil(packed, xl, xh, yl, yh):
    nf, levels, cx, cy = packed.shape
    w = xl.shape[2]
    edge = yl.shape[3]
    fields = nf - 1
    return pl.pallas_call(
        stencil_kernel,
        grid=(levels,),
        in_specs=[
            pl.BlockSpec((nf, 1, cx, cy), lambda l: (0, l, 0, 0)),
            pl.BlockSpec((nf, 1, cx, cy), lambda l: (0, jnp.maximum(l - 1, 0), 0, 0)),
            pl.BlockSpec((nf, 1, cx, cy), lambda l: (0, jnp.minimum(l + 1, levels - 1), 0, 0)),
            pl.BlockSpec((nf, 1, w, cy), lambda l: (0, l, 0, 0)),
            pl.BlockSpec((nf, 1, w, cy), lambda l: (0, l, 0, 0)),
            pl.BlockSpec((nf, 1, cx, edge), lambda l: (0, l, 0, 0)),
            pl.BlockSpec((nf, 1, cx, edge), lambda l: (0, l, 0, 0)),
        ],
        out_specs=pl.BlockSpec((fields, 1, cx, cy), lambda l: (0, l, 0, 0)),
        out_shape=jax.ShapeDtypeStruct((fields, levels, cx, cy), jnp.float32),
        compiler_params=pltpu.CompilerParams(dimension_semantics=("arbitrary",)),
        cost_estimate=pl.CostEstimate(flops=200 * fields * levels * cx * cy, transcendentals=0,
                                      bytes_accessed=4 * (4 * nf + fields) * levels * cx * cy),
    )(packed, packed, packed, xl, xh, yl, yh)


def _pieces(x, n):
    out = []
    rest = x
    for _ in range(n):
        p = rest.astype(jnp.bfloat16)
        out.append(p)
        rest = rest - p.astype(jnp.float32)
    return out


def owner_kernel(x_ref, pay_ref, forcing_ref, flux_ref, pieces_ref, iota_ref):
    rows, cols = x_ref.shape
    fields = 4
    per_field = rows // fields
    block = pay_ref.shape[1]
    sub = 256
    nsub = cols // sub

    @pl.when(pl.program_id(0) == 0)
    def _():
        parts = _pieces(x_ref[...], 3)
        for i, p in enumerate(parts):
            pieces_ref[i * rows:(i + 1) * rows, :] = p
        forcing_ref[...] = jnp.zeros_like(forcing_ref)
        iota_ref[...] = lax.broadcasted_iota(jnp.int32, (sub, block), 0).astype(jnp.bfloat16)

    pay = pay_ref[...]
    cell = (pay[6:7] + 0.5).astype(jnp.int32)
    col = cell % cols
    row = cell // cols
    hi = col // sub
    lo = (col % sub).astype(jnp.float32)
    iota = iota_ref[...]
    hots = []
    for a in range(nsub):
        sel = jnp.where(hi == a, lo, -1.0).astype(jnp.bfloat16)
        hots.append(jnp.where(iota == sel, jnp.bfloat16(1), jnp.bfloat16(0)))
    hot = jnp.concatenate(hots, axis=0)
    picked = jnp.dot(pieces_ref[...], hot, preferred_element_type=jnp.float32)
    value = (picked[0:rows] + picked[rows:2 * rows]) + picked[2 * rows:3 * rows]
    pick_row = lax.broadcasted_iota(jnp.int32, (per_field, block), 0) == row
    gathered = jnp.concatenate(
        [jnp.sum(jnp.where(pick_row, value[f * per_field:(f + 1) * per_field], 0.0), axis=0, keepdims=True)
         for f in range(fields)], axis=0)
    flux = pay[5:6] * (gathered - pay[0:4]) / pay[4:5]
    flux_ref[...] = flux
    spread = jnp.concatenate(
        [jnp.where(pick_row, flux[f:f + 1], 0.0) for f in range(fields)], axis=0)
    w = jnp.concatenate(_pieces(spread, 2), axis=0)
    added = lax.dot_general(w, hot, (((1,), (1,)), ((), ())), preferred_element_type=jnp.float32)
    forcing_ref[...] += added[0:rows] + added[rows:2 * rows]


def owner_side(x, pay, block=1024):
    rows, cols = x.shape
    slots = pay.shape[1]
    steps = slots // block
    return pl.pallas_call(
        owner_kernel,
        grid=(steps,),
        in_specs=[
            pl.BlockSpec((rows, cols), lambda j: (0, 0)),
            pl.BlockSpec((8, block), lambda j: (0, j)),
        ],
        out_specs=[
            pl.BlockSpec((rows, cols), lambda j: (0, 0)),
            pl.BlockSpec((4, block), lambda j: (0, j)),
        ],
        out_shape=[
            jax.ShapeDtypeStruct((rows, cols), jnp.float32),
            jax.ShapeDtypeStruct((4, slots), jnp.float32),
        ],
        scratch_shapes=[pltpu.VMEM((3 * rows, cols), jnp.bfloat16),
                        pltpu.VMEM((256, block), jnp.bfloat16)],
        compiler_params=pltpu.CompilerParams(dimension_semantics=("arbitrary",),
                                             vmem_limit_bytes=48 * 1024 * 1024),
        cost_estimate=pl.CostEstimate(flops=2 * (5 * rows) * cols * slots, transcendentals=0,
                                      bytes_accessed=4 * (2 * rows * cols + 12 * slots)),
    )(x, pay)


def exchange(shard, axis, dim, low, high):
    peers = lax.axis_size(axis)
    length = shard.shape[dim]
    up = [(i, (i + 1) % peers) for i in range(peers)]
    down = [(j, i) for i, j in up]
    last = lax.slice_in_dim(shard, length - low, length, axis=dim)
    leading = lax.slice_in_dim(shard, 0, high, axis=dim)
    before = lax.ppermute(last, axis, up)
    after = lax.ppermute(leading, axis, down)
    return before, after


def local(state, start, eddy, solid, facet_wall, facet_dist, facet_area, facet_owner, facet_cell):
    levels = state.shape[1]
    cells_x = state.shape[2]
    cells_y = state.shape[3]
    packed = jnp.concatenate([state, eddy[None]], axis=0)
    x_low, x_high = exchange(packed, "gx", 2, 3, 3)
    y_low, y_high = exchange(packed, "gy", 3, 128, 128)

    facet_count = facet_cell.shape[0]
    owners_gx = lax.axis_size("gx")
    capacity = 2 * facet_count // owners_gx
    slots = owners_gx * capacity
    owner_gx = facet_owner[:, 0]
    owner_hot = (owner_gx[:, None] == jnp.arange(owners_gx, dtype=jnp.int32)[None, :]).astype(
        jnp.bfloat16
    )
    positions = jnp.arange(facet_count, dtype=jnp.int32)
    earlier = (positions[:, None] > positions[None, :]).astype(jnp.bfloat16)
    before = jnp.dot(earlier, owner_hot, preferred_element_type=jnp.float32)
    owner_float = owner_hot.astype(jnp.float32)
    slot_rank = jnp.sum(before * owner_float, axis=1)
    rank_hot = (slot_rank[:, None] == jnp.arange(capacity, dtype=jnp.float32)[None, :]).astype(
        jnp.float32
    )
    payload = jnp.concatenate(
        [facet_wall, facet_dist[None], facet_area[None], facet_cell[None].astype(jnp.float32)],
        axis=0,
    )
    spread = payload[:, None, :] * owner_float.T[None]
    outgoing = jnp.einsum("cof,fk->cok", spread, rank_hot, precision=exact)
    filled = jnp.dot(owner_float.T, rank_hot, precision=exact)
    unit_dist = (jnp.arange(7, dtype=jnp.int32) == 4).astype(jnp.float32)[:, None, None]
    outgoing = outgoing + unit_dist * (1.0 - filled)[None]
    received = lax.all_to_all(outgoing, "gx", split_axis=1, concat_axis=1, tiled=True).reshape(
        7, slots
    )
    tend = stencil(packed, x_low, x_high, y_low, y_high)
    pay = jnp.concatenate([received, jnp.zeros((1, slots), jnp.float32)], axis=0)
    forcing_rows, flux_slots = owner_side(state.reshape(4 * levels * cells_x, cells_y), pay)
    forcing = forcing_rows.reshape(state.shape)
    wall_flux = flux_slots.reshape(4, owners_gx, capacity)
    returned = lax.all_to_all(wall_flux, "gx", split_axis=1, concat_axis=1, tiled=True)
    through = jnp.einsum("cok,fk->cof", returned, rank_hot, precision=exact)
    facet_flux = jnp.sum(through * owner_float.T[None], axis=1)
    change = (tend - forcing) * (1.0 - solid.astype(jnp.float32))
    new_state = start + dt_step * change
    return (new_state, facet_flux)


def solution(mesh):
    in_specs = (
        P(None, None, "gx", "gy"),
        P(None, None, "gx", "gy"),
        P(None, "gx", "gy"),
        P(None, "gx", "gy"),
        P(None, ("gx", "gy")),
        P(("gx", "gy")),
        P(("gx", "gy")),
        P(("gx", "gy"), None),
        P(("gx", "gy")),
    )
    out_specs = (P(None, None, "gx", "gy"), P(None, ("gx", "gy")))
    return jax.shard_map(local, mesh=mesh, in_specs=in_specs, out_specs=out_specs, check_vma=False)
```

time: 142 us -> 81.4 us (0.57)
  local copies, waits for them, and re-layouts: 32.6 us -> 9.6 us
  other arithmetic: 29.9 us -> 8.25 us
  Pallas kernels: 27.9 us -> 18.7 us
  starting transfers between devices: 26.6 us -> 22.5 us
  matrix products: 7.39 us -> 5.56 us
    pallas_call x1, Pallas kernels: 27.9 us -> 12.1 us  [owner_side(): pl.pallas_call(owner_kernel, grid=(steps,), in_specs=[pl.BlockSpec((rows,...]
    add x1, other arithmetic: 14.1 us -> 2.42 us  [local(): new_state = start + dt_step * change]
    slice x12 -> x2, local copies, waits for them, and re-layouts: 13.9 us -> 2.21 us  [the longest x1 1.11 us: exchange(): leading = lax.slice_in_dim(shard, 0, high, axis=dim)]
    all_to_all x1, waiting for transfers between devices: 0.2 us -> 8.45 us  [local(): lax.all_to_all(outgoing, 'gx', split_axis=1, concat_axis=1, tiled=True)]
    unnamed x44 -> x26, local copies, waits for them, and re-layouts: 9.37 us -> 1.88 us
    ppermute x4, waiting for transfers between devices: 6.86 us -> 0.01 us  [the longest x2 0.01 us: exchange(): before = lax.ppermute(last, axis, up)]
    pallas_call x0 -> x1, Pallas kernels: none -> 6.65 us  [stencil(): pl.pallas_call(stencil_kernel, grid=(levels,), in_specs=[pl.BlockSpec((nf...]
    concatenate x1, local copies, waits for them, and re-layouts: 5.16 us -> 0.01 us  [local(): jnp.concatenate([received, jnp.zeros((1, slots), jnp.float32)], axis=0)]
  transfers between devices with their start and end apart: 6 -> 6, of which waited for: 4 -> 2; matrix products, arithmetic and copies ran while one was open for 24% -> 22% of each run, Pallas kernels for 20% -> 15%
where the time goes in v2:
time: 81.4 us; the launch traced here: 81 us
  starting transfers between devices  22.5 us (28%)
  Pallas kernels  18.7 us (23%)
  waiting for transfers between devices  15.5 us (19%)
  local copies, waits for them, and re-layouts  9.6 us (12%)
  other arithmetic  8.25 us (10%)
  matrix products  5.56 us (7%)
  between operations  0.91 us (1%)
    pallas_call x1, Pallas kernels, owner_side(): pl.pallas_call(owner_kernel, grid=(steps,), in_specs=[pl.BlockSpec((rows,...  12.1 us
    all_to_all x1, starting transfers between devices, local(): lax.all_to_all(outgoing, 'gx', split_axis=1, concat_axis=1, tiled=True)  9.79 us
    all_to_all x1, waiting for transfers between devices, local(): lax.all_to_all(outgoing, 'gx', split_axis=1, concat_axis=1, tiled=True)  8.45 us
    all_to_all x1, waiting for transfers between devices, local(): lax.all_to_all(wall_flux, 'gx', split_axis=1, concat_axis=1, tiled=True)  6.99 us
    pallas_call x1, Pallas kernels, stencil(): pl.pallas_call(stencil_kernel, grid=(levels,), in_specs=[pl.BlockSpec((nf...  6.65 us
    ppermute x2, starting transfers between devices, exchange(): before = lax.ppermute(last, axis, up)  5.82 us
    all_to_all x1, starting transfers between devices, local(): lax.all_to_all(wall_flux, 'gx', split_axis=1, concat_axis=1, tiled=True)  4.55 us
    concatenate x3, other arithmetic, local(): packed = jnp.concatenate([state, eddy[None]], axis=0)  4.17 us
  transfers between devices with their start and end apart: 6, of which 2 were waited for; matrix products, arithmetic and copies ran while one was open for 22% of the time, Pallas kernels for 15%

profile of v2, /device:TPU:1, one launch (start us, length us, event | category | flops | bytes accessed | tf_op | source)
XLA Modules:
  0.0 81.0 jit_solution(16264037893269476123)
XLA Ops:
  0.6 2.4 %fusion.12 = (f32[5,4,3,2048]{3,2,1,0:T(4,128)S(1)}, f32[5,4,3,2048]{3,2,1,0:T(4,128)S(1)}) fusion(f32[4,4,8,2048]{3,2,1,0:T(8,128)} %param.9, f32[1,4,8,2048]{3,2,1,0:T(8,128)} %bitcast.21), kind=kLoop, calls=%fused_computation.23 | loop fusion | flops 245760 | bytes 2293760 | tf_op jit(solution)/shard_map/concatenate | solution.py:233
  3.0 0.0 copy-start
  3.0 0.0 copy-start.1
  3.0 1.1 %copy.11 = f32[5,4,3,2048]{3,1,2,0:T(4,128)} copy(f32[5,4,3,2048]{3,2,1,0:T(4,128)S(1)} %get-tuple-element.9) | data formatting | bytes 983040 | tf_op jit(solution)/shard_map/slice | solution.py:222
  4.1 3.0 %collective-permute-start = (f32[5,4,3,2048]{3,1,2,0:T(4,128)}, f32[5,4,3,2048]{3,1,2,0:T(4,128)}, u32[]{:S(2)}, u32[]{:S(2)}) collective-permute-start(f32[5,4,3,2048]{3,1,2,0:T(4,128)} %copy.11), channel_id=1, source_target_pairs={{0,4},{4,8},{8,12},{12,16},{16,20},{20,24},{24,28},{28,32},{32,36}... | collective-permute-start | bytes 1474568 | tf_op jit(solution)/shard_map/ppermute | solution.py:224
  7.1 0.0 copy-start.5
  7.1 1.1 %copy.12 = f32[5,4,3,2048]{3,1,2,0:T(4,128)} copy(f32[5,4,3,2048]{3,2,1,0:T(4,128)S(1)} %get-tuple-element.8) | data formatting | bytes 983040 | tf_op jit(solution)/shard_map/slice | solution.py:223
  8.2 0.2 collective-permute-start.1
  8.4 0.0 copy-done
  8.4 0.0 copy-done.1
  8.4 0.6 fusion.26
  9.1 2.8 %collective-permute-start.2 = (f32[5,4,8,128]{3,2,1,0:T(8,128)}, f32[5,4,8,128]{3,2,1,0:T(8,128)}, u32[]{:S(2)}, u32[]{:S(2)}) collective-permute-start(f32[5,4,8,128]{3,2,1,0:T(8,128)} %get-tuple-element.7), channel_id=1, source_target_pairs={{0,1},{1,2},{2,3},{3,0},{4,5},{5,6},{6,7},{7,4},{8,9},{9,10},{10,1... | collective-permute-start | bytes 245768 | tf_op jit(solution)/shard_map/ppermute | solution.py:224
  11.9 2.1 %collective-permute-start.3 = (f32[5,4,8,128]{3,2,1,0:T(8,128)S(1)}, f32[5,4,8,128]{3,2,1,0:T(8,128)}, u32[]{:S(2)}, u32[]{:S(2)}) collective-permute-start(f32[5,4,8,128]{3,2,1,0:T(8,128)S(1)} %get-tuple-element.6), channel_id=1, source_target_pairs={{1,0},{2,1},{3,2},{0,3},{5,4},{6,5},{7,6},{4,7},{9,8},{10,9},{11,1... | collective-permute-start | bytes 245768 | tf_op jit(solution)/shard_map/ppermute | solution.py:225
  14.0 0.0 copy-done.5
  14.1 0.0 copy-start.6
  14.1 0.0 copy-start.4
  14.1 0.0 copy-start.7
  14.1 0.0 copy-start.8
  14.1 1.7 %fusion.10 = f32[2048]{0:T(1024)S(1)} fusion(s32[2048]{0:T(1024)S(1)} %bitcast.30), kind=kOutput, calls=%fused_computation.19 | convolution fusion | flops 541849600 | bytes 16384 | tf_op jit(solution)/shard_map/dot_general | solution.py:247
  15.8 0.0 copy-start.9
  15.8 0.0 copy-done.6
  15.8 0.3 convolution_subtract_fusion
  16.1 0.0 copy-done.4
  16.1 0.0 copy-done.7
  16.1 0.0 copy-done.8
  16.2 0.0 copy-start.3
  16.2 1.9 %fusion.7 = f32[7,64,64]{2,1,0:T(8,128)S(1)} fusion(f32[64,2048]{1,0:T(8,128)S(1)} %fusion.18, f32[7,2048]{1,0:T(8,128)S(1)} %pad_maximum_fusion.1, f32[2048]{0:T(1024)S(1)} %fusion.10, f32[64,64]{1,0:T(8,128)S(1)} %convolution_subtract_fusion, f32[7]{0:T(128)S(1)} %compare_convert_fusion), kind=kOutput, calls=%fused_computation.18 | convolution fusion | flops 705748992 | bytes 720924 | tf_op jit(solution)/shard_map/cof,fk->cok/dot_general | solution.py:258
  18.1 0.1 copy.23
  18.3 0.0 copy-done.9
  18.3 0.8 %reshape.56 = f32[64,1,448]{2,1,0:T(1,128)} reshape(f32[64,7,64]{2,1,0:T(8,128)S(1)} %bitcast.24) | data formatting | bytes 229376
  19.1 9.8 %all-to-all-start = ((f32[64,1,448]{2,1,0:T(1,128)}), f32[64,1,448]{2,1,0:T(1,128)S(1)}, u32[]{:S(2)}, u32[]{:S(2)}) async-start(f32[64,1,448]{2,1,0:T(1,128)} %reshape.56), calls=%async_computation | async-start | bytes 262144 | tf_op jit(solution)/shard_map/all_to_all | solution.py:262
  28.9 0.0 copy-done.3
  29.0 8.4 %all-to-all-done = f32[64,1,448]{2,1,0:T(1,128)S(1)} async-done(((f32[64,1,448]{2,1,0:T(1,128)}), f32[64,1,448]{2,1,0:T(1,128)S(1)}, u32[]{:S(2)}, u32[]{:S(2)}) %all-to-all-start) | async-done | bytes 114720 | tf_op jit(solution)/shard_map/all_to_all | solution.py:262
  37.4 0.5 broadcast.30
  37.9 0.9 %reduce = f32[64,448]{1,0:T(8,128)S(1)} reduce(f32[64,1,448]{2,1,0:T(1,128)S(1)} %all-to-all-done, f32[]{:T(128)} %broadcast.30), dimensions={1}, to_apply=%all_to_all.6.reduce_sub_computation | reduce | bytes 229380 | tf_op jit(solution)/shard_map/all_to_all | solution.py:262
  38.8 0.1 reshape.57
  38.9 0.1 reshape.52
  39.1 12.1 %shard_map.105 = (f32[128,2048]{1,0:T(8,128)S(1)}, f32[4,4096]{1,0:T(4,128)S(1)}) custom-call(f32[128,2048]{1,0:T(8,128)S(1)} %bitcast.19, f32[8,4096]{1,0:T(8,128)S(1)} %concatenate.11.pay_ref), custom_call_target="tpu_custom_call" | custom-call | flops 10737418240 | bytes 2293760 | tf_op jit(solution)/shard_map/pallas_call | solution.py:193
  51.2 0.1 reshape.54
  51.3 0.1 copy.24
  51.4 0.8 reshape.58
  52.1 4.5 %all-to-all-start.1 = ((f32[64,1,256]{2,1,0:T(1,128)}), f32[64,1,256]{2,1,0:T(1,128)S(1)}, u32[]{:S(2)}, u32[]{:S(2)}) async-start(f32[64,1,256]{2,1,0:T(1,128)} %reshape.58), calls=%async_computation.1 | async-start | bytes 131072 | tf_op jit(solution)/shard_map/all_to_all | solution.py:270
  56.7 0.0 copy-start.10
  56.7 1.2 %pad_maximum_fusion.sc_ref.sd_ref.su_ref = f32[5,4,8,2048]{3,2,1,0:T(8,128)} fusion(f32[1,4,8,2048]{3,2,1,0:T(8,128)S(1)} %bitcast.23, f32[4,4,8,2048]{3,2,1,0:T(8,128)S(1)} %copy-done), kind=kLoop, calls=%fused_computation.8 | loop fusion | flops 327680 | bytes 2621440 | tf_op jit(solution)/shard_map/concatenate | solution.py:233
  57.9 7.0 %all-to-all-done.1 = f32[64,1,256]{2,1,0:T(1,128)S(1)} async-done(((f32[64,1,256]{2,1,0:T(1,128)}), f32[64,1,256]{2,1,0:T(1,128)S(1)}, u32[]{:S(2)}, u32[]{:S(2)}) %all-to-all-start.1) | async-done | bytes 65568 | tf_op jit(solution)/shard_map/all_to_all | solution.py:270
  64.9 0.7 reduce.1
  65.6 0.1 reshape.59
  65.7 0.0 copy-done.10
  65.7 1.7 %fusion.6 = f32[4,2048]{1,0:T(4,128)} fusion(f32[64,2048]{1,0:T(8,128)S(1)} %fusion.18, f32[2048]{0:T(1024)S(1)} %copy-done.10, f32[4,64,64]{2,0,1:T(4,128)S(1)} %bitcast.27), kind=kOutput, calls=%fused_computation.17 | convolution fusion | flops 403824640 | bytes 630784 | tf_op jit(solution)/shard_map/cok,fk->cof/dot_general | solution.py:271
  67.4 0.0 collective-permute-done
  67.4 2.2 %copy.13.xl_ref = f32[5,4,3,2048]{3,2,1,0:T(4,128)} copy(f32[5,4,3,2048]{3,1,2,0:T(4,128)} %collective-permute-done) | data formatting | bytes 983040 | tf_op jit(solution)/shard_map/ppermute | solution.py:224
  69.6 0.0 collective-permute-done.1
  69.6 2.3 %copy.14.xh_ref = f32[5,4,3,2048]{3,2,1,0:T(4,128)} copy(f32[5,4,3,2048]{3,1,2,0:T(4,128)} %collective-permute-done.1) | data formatting | bytes 983040 | tf_op jit(solution)/shard_map/ppermute | solution.py:225
  71.9 0.0 copy-start.2
  71.9 0.0 collective-permute-done.2.yl_ref
  71.9 0.0 collective-permute-done.3.yh_ref
  71.9 6.7 %shard_map.104 = f32[4,4,8,2048]{3,2,1,0:T(8,128)} custom-call(f32[5,4,8,2048]{3,2,1,0:T(8,128)} %pad_maximum_fusion.sc_ref.sd_ref.su_ref, f32[5,4,8,2048]{3,2,1,0:T(8,128)} %pad_maximum_fusion.sc_ref.sd_ref.su_ref, f32[5,4,8,2048]{3,2,1,0:T(8,128)} %pad_maximum_fusion.sc_ref.sd_ref.su_ref, f32[5,4,3,2048]{3,2,1,0:T(4,128)} %copy.13.xl_ref, ...), custom_call_target="tpu_custom_call" | custom-call | flops 52428800 | bytes 6291456 | tf_op jit(solution)/shard_map/pallas_call | solution.py:116
  78.6 0.0 copy-done.2
  78.6 2.4 %multiply_add_fusion = f32[4,4,8,2048]{3,2,1,0:T(8,128)} fusion(f32[4,4,8,2048]{3,2,1,0:T(8,128)S(1)} %copy-done.2, f32[4,4,8,2048]{3,2,1,0:T(8,128)} %shard_map.104, f32[4,4,8,2048]{3,2,1,0:T(8,128)S(1)} %bitcast.20, f32[4,8,2048]{2,1,0:T(8,128)S(1)} %convert_subtract_fusion), kind=kLoop, calls=%fused_computation.21 | loop fusion | flops 1048576 | bytes 4456448 | tf_op jit(solution)/shard_map/add | solution.py:274
  (7 shorter events, 0.2 us)
Async XLA Ops:
  3.0 5.4 %copy-start = (f32[4,4,8,2048]{3,2,1,0:T(8,128)S(1)}, f32[4,4,8,2048]{3,2,1,0:T(8,128)}, u32[]{:S(2)}) copy-start(f32[4,4,8,2048]{3,2,1,0:T(8,128)} %param.9) | copy-start | bytes 3145732
  3.0 5.4 %copy-start.1 = (f32[4,8,2048]{2,1,0:T(8,128)S(1)}, f32[4,8,2048]{2,1,0:T(8,128)}, u32[]{:S(2)}) copy-start(f32[4,8,2048]{2,1,0:T(8,128)} %param.11) | copy-start | bytes 786436
  4.1 63.3 %collective-permute-start = (f32[5,4,3,2048]{3,1,2,0:T(4,128)}, f32[5,4,3,2048]{3,1,2,0:T(4,128)}, u32[]{:S(2)}, u32[]{:S(2)}) collective-permute-start(f32[5,4,3,2048]{3,1,2,0:T(4,128)} %copy.11), channel_id=1, source_target_pairs={{0,4},{4,8},{8,12},{12,16},{16,20},{20,24},{24,28},{28,32},{32,36}... | collective-permute-start | bytes 1474568 | tf_op jit(solution)/shard_map/ppermute | solution.py:224
  7.1 6.9 %copy-start.5 = (s32[2048,1]{0,1:T(1,128)S(1)}, s32[2048,1]{0,1:T(1,128)}, u32[]{:S(2)}) copy-start(s32[2048,1]{0,1:T(1,128)} %param.16) | copy-start | bytes 24580
  8.2 61.4 %collective-permute-start.1 = (f32[5,4,3,2048]{3,1,2,0:T(4,128)}, f32[5,4,3,2048]{3,1,2,0:T(4,128)}, u32[]{:S(2)}, u32[]{:S(2)}) collective-permute-start(f32[5,4,3,2048]{3,1,2,0:T(4,128)} %copy.12), channel_id=1, source_target_pairs={{4,0},{8,4},{12,8},{16,12},{20,16},{24,20},{28,24},{32,28},{36,32}... | collective-permute-start | bytes 1474568 | tf_op jit(solution)/shard_map/ppermute | solution.py:225
  9.1 62.8 %collective-permute-start.2 = (f32[5,4,8,128]{3,2,1,0:T(8,128)}, f32[5,4,8,128]{3,2,1,0:T(8,128)}, u32[]{:S(2)}, u32[]{:S(2)}) collective-permute-start(f32[5,4,8,128]{3,2,1,0:T(8,128)} %get-tuple-element.7), channel_id=1, source_target_pairs={{0,1},{1,2},{2,3},{3,0},{4,5},{5,6},{6,7},{7,4},{8,9},{9,10},{10,1... | collective-permute-start | bytes 245768 | tf_op jit(solution)/shard_map/ppermute | solution.py:224
  11.9 60.0 %collective-permute-start.3 = (f32[5,4,8,128]{3,2,1,0:T(8,128)S(1)}, f32[5,4,8,128]{3,2,1,0:T(8,128)}, u32[]{:S(2)}, u32[]{:S(2)}) collective-permute-start(f32[5,4,8,128]{3,2,1,0:T(8,128)S(1)} %get-tuple-element.6), channel_id=1, source_target_pairs={{1,0},{2,1},{3,2},{0,3},{5,4},{6,5},{7,6},{4,7},{9,8},{10,9},{11,1... | collective-permute-start | bytes 245768 | tf_op jit(solution)/shard_map/ppermute | solution.py:225
  14.1 1.7 %copy-start.6 = (s32[2048]{0:T(1024)S(1)}, s32[2048]{0:T(1024)}, u32[]{:S(2)}) copy-start(s32[2048]{0:T(1024)} %param.17) | copy-start | bytes 24580
  14.1 2.0 %copy-start.4 = (f32[4,2048]{1,0:T(4,128)S(1)}, f32[4,2048]{1,0:T(4,128)}, u32[]{:S(2)}) copy-start(f32[4,2048]{1,0:T(4,128)} %param.13) | copy-start | bytes 98308
  14.1 2.0 %copy-start.7 = (f32[2048]{0:T(1024)S(1)}, f32[2048]{0:T(1024)}, u32[]{:S(2)}) copy-start(f32[2048]{0:T(1024)} %param.15) | copy-start | bytes 24580
  14.1 2.0 %copy-start.8 = (f32[2048]{0:T(1024)S(1)}, f32[2048]{0:T(1024)}, u32[]{:S(2)}) copy-start(f32[2048]{0:T(1024)} %param.14) | copy-start | bytes 24580
  15.8 2.5 %copy-start.9 = (f32[2048]{0:T(1024)}, f32[2048]{0:T(1024)S(1)}, u32[]{:S(2)}) copy-start(f32[2048]{0:T(1024)S(1)} %fusion.10) | copy-start | bytes 24580
  16.2 12.8 %copy-start.3 = (s32[4,8,2048]{2,1,0:T(8,128)S(1)}, s32[4,8,2048]{2,1,0:T(8,128)}, u32[]{:S(2)}) copy-start(s32[4,8,2048]{2,1,0:T(8,128)} %param.12) | copy-start | bytes 786436
  19.1 18.3 %all-to-all-start = ((f32[64,1,448]{2,1,0:T(1,128)}), f32[64,1,448]{2,1,0:T(1,128)S(1)}, u32[]{:S(2)}, u32[]{:S(2)}) async-start(f32[64,1,448]{2,1,0:T(1,128)} %reshape.56), calls=%async_computation | async-start | bytes 262144 | tf_op jit(solution)/shard_map/all_to_all | solution.py:262
  52.1 12.7 %all-to-all-start.1 = ((f32[64,1,256]{2,1,0:T(1,128)}), f32[64,1,256]{2,1,0:T(1,128)S(1)}, u32[]{:S(2)}, u32[]{:S(2)}) async-start(f32[64,1,256]{2,1,0:T(1,128)} %reshape.58), calls=%async_computation.1 | async-start | bytes 131072 | tf_op jit(solution)/shard_map/all_to_all | solution.py:270
  56.7 9.0 %copy-start.10 = (f32[2048]{0:T(1024)S(1)}, f32[2048]{0:T(1024)}, u32[]{:S(2)}) copy-start(f32[2048]{0:T(1024)} %copy-done.9) | copy-start | bytes 24580
  71.9 6.7 %copy-start.2 = (f32[4,4,8,2048]{3,2,1,0:T(8,128)S(1)}, f32[4,4,8,2048]{3,2,1,0:T(8,128)}, u32[]{:S(2)}) copy-start(f32[4,4,8,2048]{3,2,1,0:T(8,128)} %param.10) | copy-start | bytes 3145732

commit v3 on v2

--- a/solution.py
+++ b/solution.py
@@ -17,12 +17,12 @@
     return jnp.where(c > 0, forward, backward) / 60.0
 
 
-def _x_shifter(f, lo, hi):
+def _x_shifter(f, lo_rows, hi_rows):
     rows = f.shape[0]
     row = lax.broadcasted_iota(jnp.int32, f.shape, 0)
-    width = lo.shape[0]
-    lo_b = [jnp.broadcast_to(lo[i:i + 1], f.shape) for i in range(width)]
-    hi_b = [jnp.broadcast_to(hi[i:i + 1], f.shape) for i in range(width)]
+    width = len(lo_rows)
+    lo_b = [jnp.broadcast_to(r, f.shape) for r in lo_rows]
+    hi_b = [jnp.broadcast_to(r, f.shape) for r in hi_rows]
     cache = {0: f}
 
     def s(k):
@@ -82,7 +82,8 @@
     down_w = jnp.where(level > 0, 1.0, 0.0)
     eddy_up = (0.5 * (e + eu)) * up_w
     eddy_down = (0.5 * (ed + e)) * down_w
-    ex = _x_shifter(e, xl_ref[fields, 0, 2:3], xh_ref[fields, 0, 0:1])
+    width = xl_ref.shape[1] // (fields + 1)
+    ex = _x_shifter(e, [xl_ref[0, pl.ds(fields * width + width - 1, 1), :]], [xh_ref[0, pl.ds(fields * width, 1), :]])
     ey = _y_shifter(e, yl_ref[fields, 0], yh_ref[fields, 0])
     east = 0.5 * (e + ex(1))
     west = 0.5 * (ex(-1) + e)
@@ -95,7 +96,8 @@
         fv = sc_ref[f, 0]
         lower = sd_ref[f, 0]
         upper = su_ref[f, 0]
-        sx = _x_shifter(fv, xl_ref[f, 0], xh_ref[f, 0])
+        sx = _x_shifter(fv, [xl_ref[0, pl.ds(f * width + i, 1), :] for i in range(width)],
+                        [xh_ref[0, pl.ds(f * width + i, 1), :] for i in range(width)])
         sy = _y_shifter(fv, yl_ref[f, 0], yh_ref[f, 0])
         derx = _upwind(sx, u)
         dery = _upwind(sy, v)
@@ -110,7 +112,7 @@
 
 def stencil(packed, xl, xh, yl, yh):
     nf, levels, cx, cy = packed.shape
-    w = xl.shape[2]
+    w = xl.shape[1]
     edge = yl.shape[3]
     fields = nf - 1
     return pl.pallas_call(
@@ -120,8 +122,8 @@
             pl.BlockSpec((nf, 1, cx, cy), lambda l: (0, l, 0, 0)),
             pl.BlockSpec((nf, 1, cx, cy), lambda l: (0, jnp.maximum(l - 1, 0), 0, 0)),
             pl.BlockSpec((nf, 1, cx, cy), lambda l: (0, jnp.minimum(l + 1, levels - 1), 0, 0)),
-            pl.BlockSpec((nf, 1, w, cy), lambda l: (0, l, 0, 0)),
-            pl.BlockSpec((nf, 1, w, cy), lambda l: (0, l, 0, 0)),
+            pl.BlockSpec((1, w, cy), lambda l: (l, 0, 0)),
+            pl.BlockSpec((1, w, cy), lambda l: (l, 0, 0)),
             pl.BlockSpec((nf, 1, cx, edge), lambda l: (0, l, 0, 0)),
             pl.BlockSpec((nf, 1, cx, edge), lambda l: (0, l, 0, 0)),
         ],
@@ -214,6 +216,13 @@
     )(x, pay)
 
 
+def shift_pair(last, leading, axis):
+    peers = lax.axis_size(axis)
+    up = [(i, (i + 1) % peers) for i in range(peers)]
+    down = [(j, i) for i, j in up]
+    return lax.ppermute(last, axis, up), lax.ppermute(leading, axis, down)
+
+
 def exchange(shard, axis, dim, low, high):
     peers = lax.axis_size(axis)
     length = shard.shape[dim]
@@ -231,7 +240,10 @@
     cells_x = state.shape[2]
     cells_y = state.shape[3]
     packed = jnp.concatenate([state, eddy[None]], axis=0)
-    x_low, x_high = exchange(packed, "gx", 2, 3, 3)
+    x_rows = jnp.transpose(packed, (1, 0, 2, 3))
+    x_last = x_rows[:, :, cells_x - 3:].reshape(levels, -1, cells_y)
+    x_first = x_rows[:, :, :3].reshape(levels, -1, cells_y)
+    x_low, x_high = shift_pair(x_last, x_first, "gx")
     y_low, y_high = exchange(packed, "gy", 3, 128, 128)
 
     facet_count = facet_cell.shape[0]
@@ -259,19 +271,24 @@
     filled = jnp.dot(owner_float.T, rank_hot, precision=exact)
     unit_dist = (jnp.arange(7, dtype=jnp.int32) == 4).astype(jnp.float32)[:, None, None]
     outgoing = outgoing + unit_dist * (1.0 - filled)[None]
+    x_low, x_high, y_low, y_high, outgoing = lax.optimization_barrier(
+        (x_low, x_high, y_low, y_high, outgoing)
+    )
     received = lax.all_to_all(outgoing, "gx", split_axis=1, concat_axis=1, tiled=True).reshape(
         7, slots
     )
     tend = stencil(packed, x_low, x_high, y_low, y_high)
+    tend, received = lax.optimization_barrier((tend, received))
     pay = jnp.concatenate([received, jnp.zeros((1, slots), jnp.float32)], axis=0)
     forcing_rows, flux_slots = owner_side(state.reshape(4 * levels * cells_x, cells_y), pay)
     forcing = forcing_rows.reshape(state.shape)
     wall_flux = flux_slots.reshape(4, owners_gx, capacity)
     returned = lax.all_to_all(wall_flux, "gx", split_axis=1, concat_axis=1, tiled=True)
+    change = (tend - forcing) * (1.0 - solid.astype(jnp.float32))
+    new_state = start + dt_step * change
+    new_state, returned = lax.optimization_barrier((new_state, returned))
     through = jnp.einsum("cok,fk->cof", returned, rank_hot, precision=exact)
     facet_flux = jnp.sum(through * owner_float.T[None], axis=1)
-    change = (tend - forcing) * (1.0 - solid.astype(jnp.float32))
-    new_state = start + dt_step * change
     return (new_state, facet_flux)
 
 

time: 81.4 us -> 78.7 us (0.967)
  starting transfers between devices: 22.5 us -> 28 us
  local copies, waits for them, and re-layouts: 9.6 us -> 4.41 us
  waiting for transfers between devices: 15.5 us -> 13.7 us
  other arithmetic: 8.25 us -> 6.95 us
    all_to_all x1, waiting for transfers between devices: 8.45 us -> 1.71 us  [local(): lax.all_to_all(outgoing, 'gx', split_axis=1, concat_axis=1, tiled=True)]
    ppermute x2 -> x1, waiting for transfers between devices: 0.01 us -> 6.45 us  [exchange(): before = lax.ppermute(last, axis, up)]
    ppermute x2 -> x0, local copies, waits for them, and re-layouts: 4.5 us -> none  [the longest x1 2.25 us: exchange(): after = lax.ppermute(leading, axis, down)]
    concatenate x3 -> x1, other arithmetic: 4.17 us -> 0.01 us  [local(): packed = jnp.concatenate([state, eddy[None]], axis=0)]
    ppermute x0 -> x2, starting transfers between devices: none -> 3.37 us  [shift_pair(): return (lax.ppermute(last, axis, up), lax.ppermute(leading, axis, down))]
    ppermute x2 -> x1, starting transfers between devices: 5.82 us -> 2.9 us  [exchange(): before = lax.ppermute(last, axis, up)]
    transpose x0 -> x1, other arithmetic: none -> 2.6 us  [local(): x_rows = jnp.transpose(packed, (1, 0, 2, 3))]
    all_to_all x1, starting transfers between devices: 4.55 us -> 7.13 us  [local(): lax.all_to_all(wall_flux, 'gx', split_axis=1, concat_axis=1, tiled=True)]
  transfers between devices with their start and end apart: 6 -> 6, of which waited for: 2 -> 3; matrix products, arithmetic and copies ran while one was open for 22% -> 9% of each run, Pallas kernels for 15% -> 9%
where the time goes in v3:
time: 78.7 us; the launch traced here: 78.4 us
  starting transfers between devices  28 us (36%)
  Pallas kernels  18.8 us (24%)
  waiting for transfers between devices  13.7 us (17%)
  other arithmetic  6.95 us (9%)
  matrix products  5.57 us (7%)
  local copies, waits for them, and re-layouts  4.41 us (6%)
  between operations  1.01 us (1%)
    all_to_all x1, starting transfers between devices, local(): lax.all_to_all(outgoing, 'gx', split_axis=1, concat_axis=1, tiled=True)  12.4 us
    pallas_call x1, Pallas kernels, owner_side(): pl.pallas_call(owner_kernel, grid=(steps,), in_specs=[pl.BlockSpec((rows,...  12.1 us
    all_to_all x1, starting transfers between devices, local(): lax.all_to_all(wall_flux, 'gx', split_axis=1, concat_axis=1, tiled=True)  7.13 us
    pallas_call x1, Pallas kernels, stencil(): pl.pallas_call(stencil_kernel, grid=(levels,), in_specs=[pl.BlockSpec((nf...  6.7 us
    ppermute x1, waiting for transfers between devices, exchange(): before = lax.ppermute(last, axis, up)  6.45 us
    all_to_all x1, waiting for transfers between devices, local(): lax.all_to_all(wall_flux, 'gx', split_axis=1, concat_axis=1, tiled=True)  5.56 us
    ppermute x2, starting transfers between devices, shift_pair(): return (lax.ppermute(last, axis, up), lax.ppermute(leading, axis, down))  3.37 us
    ppermute x1, starting transfers between devices, exchange(): before = lax.ppermute(last, axis, up)  2.9 us
  transfers between devices with their start and end apart: 6, of which 3 were waited for; matrix products, arithmetic and copies ran while one was open for 9% of the time, Pallas kernels for 9%

profile of v3, /device:TPU:1, one launch (start us, length us, event | category | flops | bytes accessed | tf_op | source)
XLA Modules:
  0.0 78.4 jit_solution(13533816329036359356)
XLA Ops:
  0.6 2.6 %fusion.25 = (f32[4,5,8,2048]{3,2,0,1:T(8,128)S(1)}, f32[5,4,8,2048]{3,2,1,0:T(8,128)}) fusion(f32[1,4,8,2048]{3,2,1,0:T(8,128)} %bitcast.29, f32[4,4,8,2048]{3,2,1,0:T(8,128)} %param.9), kind=kLoop, calls=%fused_computation.36 | loop fusion | flops 327680 | bytes 3932160 | tf_op jit(solution)/shard_map/transpose | solution.py:243
  3.2 0.2 fusion.26
  3.4 0.3 copy.15
  3.8 0.3 copy.16
  4.1 0.0 copy-start
  4.1 0.0 copy-start.2
  4.1 3.1 %collective-permute-start = (f32[4,15,2048]{2,1,0:T(8,128)S(1)}, f32[4,15,2048]{2,1,0:T(8,128)S(1)}, u32[]{:S(2)}, u32[]{:S(2)}) collective-permute-start(f32[4,15,2048]{2,1,0:T(8,128)S(1)} %copy.16), channel_id=1, source_target_pairs={{0,4},{4,8},{8,12},{12,16},{16,20},{20,24},{24,28},{28,32},{32,36}... | collective-permute-start | bytes 1474568 | tf_op jit(solution)/shard_map/ppermute | solution.py:223
  7.2 0.3 copy.17
  7.5 0.0 copy-start.11
  7.5 0.3 copy.18
  7.8 0.3 collective-permute-start.1
  8.1 0.0 copy-done
  8.1 0.0 copy-done.2
  8.1 2.9 %collective-permute-start.2 = (f32[5,4,8,128]{3,2,1,0:T(8,128)S(1)}, f32[5,4,8,128]{3,2,1,0:T(8,128)S(1)}, u32[]{:S(2)}, u32[]{:S(2)}) collective-permute-start(f32[5,4,8,128]{3,2,1,0:T(8,128)S(1)} %get-tuple-element.25), channel_id=1, source_target_pairs={{0,1},{1,2},{2,3},{3,0},{4,5},{5,6},{6,7},{7,4},{8,9},{9,10},{10,1... | collective-permute-start | bytes 245768 | tf_op jit(solution)/shard_map/ppermute | solution.py:233
  11.0 2.2 %collective-permute-start.3 = (f32[5,4,8,128]{3,2,1,0:T(8,128)S(1)}, f32[5,4,8,128]{3,2,1,0:T(8,128)S(1)}, u32[]{:S(2)}, u32[]{:S(2)}) collective-permute-start(f32[5,4,8,128]{3,2,1,0:T(8,128)S(1)} %get-tuple-element.24), channel_id=1, source_target_pairs={{1,0},{2,1},{3,2},{0,3},{5,4},{6,5},{7,6},{4,7},{9,8},{10,9},{11,1... | collective-permute-start | bytes 245768 | tf_op jit(solution)/shard_map/ppermute | solution.py:234
  13.2 0.0 copy-done.11
  13.3 0.0 copy-start.5
  13.3 0.0 copy-start.12
  13.3 0.0 copy-start.10
  13.3 0.0 copy-start.13
  13.3 0.0 copy-start.14
  13.4 1.7 %fusion.10 = f32[2048]{0:T(1024)S(1)} fusion(s32[2048]{0:T(1024)S(1)} %bitcast.35), kind=kOutput, calls=%fused_computation.15 | convolution fusion | flops 541849600 | bytes 16384 | tf_op jit(solution)/shard_map/dot_general | solution.py:259
  15.0 0.3 convolution_subtract_fusion
  15.3 0.0 copy-done.12
  15.3 0.0 copy-done.10
  15.3 0.0 copy-done.13
  15.4 0.0 copy-done.14
  15.4 0.0 copy-done.5
  15.4 0.0 copy-start.7
  15.4 1.9 %fusion.7 = f32[7,64,64]{2,1,0:T(8,128)S(1)} fusion(f32[64,2048]{1,0:T(8,128)S(1)} %fusion.16, f32[7,2048]{1,0:T(8,128)S(1)} %pad_maximum_fusion.1, f32[2048]{0:T(1024)S(1)} %fusion.10, f32[64,64]{1,0:T(8,128)S(1)} %convolution_subtract_fusion, f32[7]{0:T(128)S(1)} %compare_convert_fusion), kind=kOutput, calls=%fused_computation.14 | convolution fusion | flops 705748992 | bytes 720924 | tf_op jit(solution)/shard_map/cof,fk->cok/dot_general | solution.py:270
  17.4 6.4 %collective-permute-done.2.yl_ref = f32[5,4,8,128]{3,2,1,0:T(8,128)S(1)} collective-permute-done((f32[5,4,8,128]{3,2,1,0:T(8,128)S(1)}, f32[5,4,8,128]{3,2,1,0:T(8,128)S(1)}, u32[]{:S(2)}, u32[]{:S(2)}) %collective-permute-start.2) | collective-permute-done | bytes 81952 | tf_op jit(solution)/shard_map/ppermute | solution.py:233
  23.8 0.0 collective-permute-done.3.yh_ref
  23.8 0.0 collective-permute-done.xl_ref
  23.8 0.0 copy-start.3
  23.9 0.0 collective-permute-done.1.xh_ref
  23.9 0.0 copy-start.4
  23.9 0.1 copy.27
  24.0 0.9 %reshape.64 = f32[64,1,448]{2,1,0:T(1,128)} reshape(f32[64,7,64]{2,1,0:T(8,128)S(1)} %bitcast.27) | data formatting | bytes 229376
  24.9 12.4 %all-to-all-start = ((f32[64,1,448]{2,1,0:T(1,128)}), f32[64,1,448]{2,1,0:T(1,128)S(1)}, u32[]{:S(2)}, u32[]{:S(2)}) async-start(f32[64,1,448]{2,1,0:T(1,128)} %reshape.64), calls=%async_computation | async-start | bytes 262144 | tf_op jit(solution)/shard_map/all_to_all | solution.py:277
  37.3 0.0 copy-done.7
  37.3 0.0 copy-done.8
  37.3 0.0 copy-done.9
  37.3 0.0 copy-done.3
  37.4 0.0 copy-done.4
  37.4 6.7 %shard_map.104 = f32[4,4,8,2048]{3,2,1,0:T(8,128)} custom-call(f32[5,4,8,2048]{3,2,1,0:T(8,128)} %get-tuple-element.29.sc_ref.sd_ref.su_ref, f32[5,4,8,2048]{3,2,1,0:T(8,128)} %get-tuple-element.29.sc_ref.sd_ref.su_ref, f32[5,4,8,2048]{3,2,1,0:T(8,128)} %get-tuple-element.29.sc_ref.sd_ref.su_ref, f32[4,15,2048]{2,1,0:T(8,128)} %copy-done.3, ...), custom_call_target="tpu_custom_call" | custom-call | flops 52428800 | bytes 6291456 | tf_op jit(solution)/shard_map/pallas_call | solution.py:118
  44.1 1.7 %all-to-all-done = f32[64,1,448]{2,1,0:T(1,128)S(1)} async-done(((f32[64,1,448]{2,1,0:T(1,128)}), f32[64,1,448]{2,1,0:T(1,128)S(1)}, u32[]{:S(2)}, u32[]{:S(2)}) %all-to-all-start) | async-done | bytes 114720 | tf_op jit(solution)/shard_map/all_to_all | solution.py:277
  45.8 0.5 broadcast.30
  46.3 1.0 %reduce = f32[64,448]{1,0:T(8,128)S(1)} reduce(f32[64,1,448]{2,1,0:T(1,128)S(1)} %all-to-all-done, f32[]{:T(128)} %broadcast.30), dimensions={1}, to_apply=%all_to_all.6.reduce_sub_computation | reduce | bytes 229380 | tf_op jit(solution)/shard_map/all_to_all | solution.py:277
  47.2 0.1 reshape.65
  47.4 0.1 reshape.59
  47.5 0.0 copy-start.1
  47.5 12.1 %shard_map.105 = (f32[128,2048]{1,0:T(8,128)S(1)}, f32[4,4096]{1,0:T(4,128)S(1)}) custom-call(f32[128,2048]{1,0:T(8,128)S(1)} %bitcast.23, f32[8,4096]{1,0:T(8,128)S(1)} %concatenate.11.pay_ref), custom_call_target="tpu_custom_call" | custom-call | flops 10737418240 | bytes 2293760 | tf_op jit(solution)/shard_map/pallas_call | solution.py:195
  59.6 0.1 reshape.62
  59.8 0.1 copy.28
  59.8 0.8 reshape.66
  60.6 7.1 %all-to-all-start.1 = ((f32[64,1,256]{2,1,0:T(1,128)}), f32[64,1,256]{2,1,0:T(1,128)S(1)}, u32[]{:S(2)}, u32[]{:S(2)}) async-start(f32[64,1,256]{2,1,0:T(1,128)} %reshape.66), calls=%async_computation.1 | async-start | bytes 131072 | tf_op jit(solution)/shard_map/all_to_all | solution.py:286
  67.7 0.0 copy-done.1
  67.7 0.0 copy-start.6
  67.8 2.5 %multiply_add_fusion = f32[4,4,8,2048]{3,2,1,0:T(8,128)} fusion(f32[4,4,8,2048]{3,2,1,0:T(8,128)} %param.10, f32[4,4,8,2048]{3,2,1,0:T(8,128)S(1)} %copy-done.1, f32[4,4,8,2048]{3,2,1,0:T(8,128)S(1)} %bitcast.24, f32[4,8,2048]{2,1,0:T(8,128)S(1)} %convert_subtract_fusion), kind=kLoop, calls=%fused_computation.17 | loop fusion | flops 1048576 | bytes 4456448 | tf_op jit(solution)/shard_map/add | solution.py:288
  70.2 5.6 %all-to-all-done.1 = f32[64,1,256]{2,1,0:T(1,128)S(1)} async-done(((f32[64,1,256]{2,1,0:T(1,128)}), f32[64,1,256]{2,1,0:T(1,128)S(1)}, u32[]{:S(2)}, u32[]{:S(2)}) %all-to-all-start.1) | async-done | bytes 65568 | tf_op jit(solution)/shard_map/all_to_all | solution.py:286
  75.8 0.8 %reduce.1 = f32[64,256]{1,0:T(8,128)S(1)} reduce(f32[64,1,256]{2,1,0:T(1,128)S(1)} %all-to-all-done.1, f32[]{:T(128)} %broadcast.30), dimensions={1}, to_apply=%all_to_all.7.reduce_sub_computation | reduce | bytes 131076 | tf_op jit(solution)/shard_map/all_to_all | solution.py:286
  76.6 0.1 reshape.67
  76.7 0.0 copy-done.6
  76.7 1.7 %fusion.6 = f32[4,2048]{1,0:T(4,128)} fusion(f32[64,2048]{1,0:T(8,128)S(1)} %copy-done.6, f32[2048]{0:T(1024)S(1)} %fusion.10, f32[4,64,64]{2,0,1:T(4,128)S(1)} %bitcast.32), kind=kOutput, calls=%fused_computation.13 | convolution fusion | flops 403824640 | bytes 630784 | tf_op jit(solution)/shard_map/cok,fk->cof/dot_general | solution.py:290
  (10 shorter events, 0.2 us)
Async XLA Ops:
  4.1 4.0 %copy-start = (f32[4,4,8,2048]{3,2,1,0:T(8,128)S(1)}, f32[4,4,8,2048]{3,2,1,0:T(8,128)}, u32[]{:S(2)}) copy-start(f32[4,4,8,2048]{3,2,1,0:T(8,128)} %param.9) | copy-start | bytes 3145732
  4.1 4.0 %copy-start.2 = (f32[4,8,2048]{2,1,0:T(8,128)S(1)}, f32[4,8,2048]{2,1,0:T(8,128)}, u32[]{:S(2)}) copy-start(f32[4,8,2048]{2,1,0:T(8,128)} %param.11) | copy-start | bytes 786436
  4.1 19.7 %collective-permute-start = (f32[4,15,2048]{2,1,0:T(8,128)S(1)}, f32[4,15,2048]{2,1,0:T(8,128)S(1)}, u32[]{:S(2)}, u32[]{:S(2)}) collective-permute-start(f32[4,15,2048]{2,1,0:T(8,128)S(1)} %copy.16), channel_id=1, source_target_pairs={{0,4},{4,8},{8,12},{12,16},{16,20},{20,24},{24,28},{28,32},{32,36}... | collective-permute-start | bytes 1474568 | tf_op jit(solution)/shard_map/ppermute | solution.py:223
  7.5 5.7 %copy-start.11 = (s32[2048,1]{0,1:T(1,128)S(1)}, s32[2048,1]{0,1:T(1,128)}, u32[]{:S(2)}) copy-start(s32[2048,1]{0,1:T(1,128)} %param.16) | copy-start | bytes 24580
  7.8 16.0 %collective-permute-start.1 = (f32[4,15,2048]{2,1,0:T(8,128)S(1)}, f32[4,15,2048]{2,1,0:T(8,128)S(1)}, u32[]{:S(2)}, u32[]{:S(2)}) collective-permute-start(f32[4,15,2048]{2,1,0:T(8,128)S(1)} %copy.18), channel_id=1, source_target_pairs={{4,0},{8,4},{12,8},{16,12},{20,16},{24,20},{28,24},{32,28},{36,32}... | collective-permute-start | bytes 1474568 | tf_op jit(solution)/shard_map/ppermute | solution.py:223
  8.1 15.7 %collective-permute-start.2 = (f32[5,4,8,128]{3,2,1,0:T(8,128)S(1)}, f32[5,4,8,128]{3,2,1,0:T(8,128)S(1)}, u32[]{:S(2)}, u32[]{:S(2)}) collective-permute-start(f32[5,4,8,128]{3,2,1,0:T(8,128)S(1)} %get-tuple-element.25), channel_id=1, source_target_pairs={{0,1},{1,2},{2,3},{3,0},{4,5},{5,6},{6,7},{7,4},{8,9},{9,10},{10,1... | collective-permute-start | bytes 245768 | tf_op jit(solution)/shard_map/ppermute | solution.py:233
  11.0 12.8 %collective-permute-start.3 = (f32[5,4,8,128]{3,2,1,0:T(8,128)S(1)}, f32[5,4,8,128]{3,2,1,0:T(8,128)S(1)}, u32[]{:S(2)}, u32[]{:S(2)}) collective-permute-start(f32[5,4,8,128]{3,2,1,0:T(8,128)S(1)} %get-tuple-element.24), channel_id=1, source_target_pairs={{1,0},{2,1},{3,2},{0,3},{5,4},{6,5},{7,6},{4,7},{9,8},{10,9},{11,1... | collective-permute-start | bytes 245768 | tf_op jit(solution)/shard_map/ppermute | solution.py:234
  13.3 2.1 %copy-start.5 = (f32[64,2048]{1,0:T(8,128)}, f32[64,2048]{1,0:T(8,128)S(1)}, u32[]{:S(2)}) copy-start(f32[64,2048]{1,0:T(8,128)S(1)} %fusion.16) | copy-start | bytes 1572868
  13.3 2.0 %copy-start.12 = (s32[2048]{0:T(1024)S(1)}, s32[2048]{0:T(1024)}, u32[]{:S(2)}) copy-start(s32[2048]{0:T(1024)} %param.17) | copy-start | bytes 24580
  13.3 2.0 %copy-start.10 = (f32[4,2048]{1,0:T(4,128)S(1)}, f32[4,2048]{1,0:T(4,128)}, u32[]{:S(2)}) copy-start(f32[4,2048]{1,0:T(4,128)} %param.13) | copy-start | bytes 98308
  13.3 2.0 %copy-start.13 = (f32[2048]{0:T(1024)S(1)}, f32[2048]{0:T(1024)}, u32[]{:S(2)}) copy-start(f32[2048]{0:T(1024)} %param.15) | copy-start | bytes 24580
  13.3 2.0 %copy-start.14 = (f32[2048]{0:T(1024)S(1)}, f32[2048]{0:T(1024)}, u32[]{:S(2)}) copy-start(f32[2048]{0:T(1024)} %param.14) | copy-start | bytes 24580
  15.4 21.9 %copy-start.7 = (s32[4,8,2048]{2,1,0:T(8,128)S(1)}, s32[4,8,2048]{2,1,0:T(8,128)}, u32[]{:S(2)}) copy-start(s32[4,8,2048]{2,1,0:T(8,128)} %param.12) | copy-start | bytes 786436
  23.8 13.5 %copy-start.8 = (f32[5,4,8,128]{3,2,1,0:T(8,128)}, f32[5,4,8,128]{3,2,1,0:T(8,128)S(1)}, u32[]{:S(2)}) copy-start(f32[5,4,8,128]{3,2,1,0:T(8,128)S(1)} %collective-permute-done.2.yl_ref) | copy-start | bytes 245764
  23.8 13.5 %copy-start.9 = (f32[5,4,8,128]{3,2,1,0:T(8,128)}, f32[5,4,8,128]{3,2,1,0:T(8,128)S(1)}, u32[]{:S(2)}) copy-start(f32[5,4,8,128]{3,2,1,0:T(8,128)S(1)} %collective-permute-done.3.yh_ref) | copy-start | bytes 245764
  23.8 13.5 %copy-start.3 = (f32[4,15,2048]{2,1,0:T(8,128)}, f32[4,15,2048]{2,1,0:T(8,128)S(1)}, u32[]{:S(2)}) copy-start(f32[4,15,2048]{2,1,0:T(8,128)S(1)} %collective-permute-done.xl_ref) | copy-start | bytes 1474564
  23.9 13.5 %copy-start.4 = (f32[4,15,2048]{2,1,0:T(8,128)}, f32[4,15,2048]{2,1,0:T(8,128)S(1)}, u32[]{:S(2)}) copy-start(f32[4,15,2048]{2,1,0:T(8,128)S(1)} %collective-permute-done.1.xh_ref) | copy-start | bytes 1474564
  24.9 20.9 %all-to-all-start = ((f32[64,1,448]{2,1,0:T(1,128)}), f32[64,1,448]{2,1,0:T(1,128)S(1)}, u32[]{:S(2)}, u32[]{:S(2)}) async-start(f32[64,1,448]{2,1,0:T(1,128)} %reshape.64), calls=%async_computation | async-start | bytes 262144 | tf_op jit(solution)/shard_map/all_to_all | solution.py:277
  47.5 20.2 %copy-start.1 = (f32[4,4,8,2048]{3,2,1,0:T(8,128)S(1)}, f32[4,4,8,2048]{3,2,1,0:T(8,128)}, u32[]{:S(2)}) copy-start(f32[4,4,8,2048]{3,2,1,0:T(8,128)} %shard_map.104) | copy-start | bytes 3145732
  60.6 15.2 %all-to-all-start.1 = ((f32[64,1,256]{2,1,0:T(1,128)}), f32[64,1,256]{2,1,0:T(1,128)S(1)}, u32[]{:S(2)}, u32[]{:S(2)}) async-start(f32[64,1,256]{2,1,0:T(1,128)} %reshape.66), calls=%async_computation.1 | async-start | bytes 131072 | tf_op jit(solution)/shard_map/all_to_all | solution.py:286
  67.7 9.0 %copy-start.6 = (f32[64,2048]{1,0:T(8,128)S(1)}, f32[64,2048]{1,0:T(8,128)}, u32[]{:S(2)}) copy-start(f32[64,2048]{1,0:T(8,128)} %copy-done.5) | copy-start | bytes 1572868

commit v4 on v3

--- a/solution.py
+++ b/solution.py
@@ -71,19 +71,19 @@
     return s
 
 
-def stencil_kernel(sc_ref, sd_ref, su_ref, xl_ref, xh_ref, yl_ref, yh_ref, out_ref):
+def stencil_kernel(sc_ref, sd_ref, su_ref, ec_ref, ed_ref, eu_ref, xl_ref, xh_ref, yl_ref, yh_ref, out_ref):
     level = pl.program_id(0)
     levels = pl.num_programs(0)
-    fields = sc_ref.shape[0] - 1
-    e = sc_ref[fields, 0]
-    ed = sd_ref[fields, 0]
-    eu = su_ref[fields, 0]
+    fields = sc_ref.shape[0]
+    width = (xl_ref.shape[1] - 1) // fields
+    e = ec_ref[0]
+    ed = ed_ref[0]
+    eu = eu_ref[0]
     up_w = jnp.where(level < levels - 1, 1.0, 0.0)
     down_w = jnp.where(level > 0, 1.0, 0.0)
     eddy_up = (0.5 * (e + eu)) * up_w
     eddy_down = (0.5 * (ed + e)) * down_w
-    width = xl_ref.shape[1] // (fields + 1)
-    ex = _x_shifter(e, [xl_ref[0, pl.ds(fields * width + width - 1, 1), :]], [xh_ref[0, pl.ds(fields * width, 1), :]])
+    ex = _x_shifter(e, [xl_ref[0, pl.ds(fields * width, 1), :]], [xh_ref[0, pl.ds(fields * width, 1), :]])
     ey = _y_shifter(e, yl_ref[fields, 0], yh_ref[fields, 0])
     east = 0.5 * (e + ex(1))
     west = 0.5 * (ex(-1) + e)
@@ -110,18 +110,23 @@
         out_ref[f, 0] = diffuse - advect
 
 
-def stencil(packed, xl, xh, yl, yh):
-    nf, levels, cx, cy = packed.shape
+def stencil(state, eddy, xl, xh, yl, yh):
+    fields, levels, cx, cy = state.shape
     w = xl.shape[1]
+    nf = yl.shape[0]
     edge = yl.shape[3]
-    fields = nf - 1
+    below = lambda l: jnp.maximum(l - 1, 0)
+    above = lambda l: jnp.minimum(l + 1, levels - 1)
     return pl.pallas_call(
         stencil_kernel,
         grid=(levels,),
         in_specs=[
-            pl.BlockSpec((nf, 1, cx, cy), lambda l: (0, l, 0, 0)),
-            pl.BlockSpec((nf, 1, cx, cy), lambda l: (0, jnp.maximum(l - 1, 0), 0, 0)),
-            pl.BlockSpec((nf, 1, cx, cy), lambda l: (0, jnp.minimum(l + 1, levels - 1), 0, 0)),
+            pl.BlockSpec((fields, 1, cx, cy), lambda l: (0, l, 0, 0)),
+            pl.BlockSpec((fields, 1, cx, cy), lambda l: (0, below(l), 0, 0)),
+            pl.BlockSpec((fields, 1, cx, cy), lambda l: (0, above(l), 0, 0)),
+            pl.BlockSpec((1, cx, cy), lambda l: (l, 0, 0)),
+            pl.BlockSpec((1, cx, cy), lambda l: (below(l), 0, 0)),
+            pl.BlockSpec((1, cx, cy), lambda l: (above(l), 0, 0)),
             pl.BlockSpec((1, w, cy), lambda l: (l, 0, 0)),
             pl.BlockSpec((1, w, cy), lambda l: (l, 0, 0)),
             pl.BlockSpec((nf, 1, cx, edge), lambda l: (0, l, 0, 0)),
@@ -132,7 +137,7 @@
         compiler_params=pltpu.CompilerParams(dimension_semantics=("arbitrary",)),
         cost_estimate=pl.CostEstimate(flops=200 * fields * levels * cx * cy, transcendentals=0,
                                       bytes_accessed=4 * (4 * nf + fields) * levels * cx * cy),
-    )(packed, packed, packed, xl, xh, yl, yh)
+    )(state, state, state, eddy, eddy, eddy, xl, xh, yl, yh)
 
 
 def _pieces(x, n):
@@ -155,7 +160,7 @@
 
     @pl.when(pl.program_id(0) == 0)
     def _():
-        parts = _pieces(x_ref[...], 3)
+        parts = _pieces(x_ref[...], 2)
         for i, p in enumerate(parts):
             pieces_ref[i * rows:(i + 1) * rows, :] = p
         forcing_ref[...] = jnp.zeros_like(forcing_ref)
@@ -174,7 +179,7 @@
         hots.append(jnp.where(iota == sel, jnp.bfloat16(1), jnp.bfloat16(0)))
     hot = jnp.concatenate(hots, axis=0)
     picked = jnp.dot(pieces_ref[...], hot, preferred_element_type=jnp.float32)
-    value = (picked[0:rows] + picked[rows:2 * rows]) + picked[2 * rows:3 * rows]
+    value = picked[0:rows] + picked[rows:2 * rows]
     pick_row = lax.broadcasted_iota(jnp.int32, (per_field, block), 0) == row
     gathered = jnp.concatenate(
         [jnp.sum(jnp.where(pick_row, value[f * per_field:(f + 1) * per_field], 0.0), axis=0, keepdims=True)
@@ -207,11 +212,11 @@
             jax.ShapeDtypeStruct((rows, cols), jnp.float32),
             jax.ShapeDtypeStruct((4, slots), jnp.float32),
         ],
-        scratch_shapes=[pltpu.VMEM((3 * rows, cols), jnp.bfloat16),
+        scratch_shapes=[pltpu.VMEM((2 * rows, cols), jnp.bfloat16),
                         pltpu.VMEM((256, block), jnp.bfloat16)],
         compiler_params=pltpu.CompilerParams(dimension_semantics=("arbitrary",),
                                              vmem_limit_bytes=48 * 1024 * 1024),
-        cost_estimate=pl.CostEstimate(flops=2 * (5 * rows) * cols * slots, transcendentals=0,
+        cost_estimate=pl.CostEstimate(flops=2 * (4 * rows) * cols * slots, transcendentals=0,
                                       bytes_accessed=4 * (2 * rows * cols + 12 * slots)),
     )(x, pay)
 
@@ -239,12 +244,19 @@
     levels = state.shape[1]
     cells_x = state.shape[2]
     cells_y = state.shape[3]
-    packed = jnp.concatenate([state, eddy[None]], axis=0)
-    x_rows = jnp.transpose(packed, (1, 0, 2, 3))
-    x_last = x_rows[:, :, cells_x - 3:].reshape(levels, -1, cells_y)
-    x_first = x_rows[:, :, :3].reshape(levels, -1, cells_y)
-    x_low, x_high = shift_pair(x_last, x_first, "gx")
-    y_low, y_high = exchange(packed, "gy", 3, 128, 128)
+    width = 3
+    edge = 128
+
+    def x_rows(lo, hi):
+        rows = jnp.transpose(state[:, :, lo:hi], (1, 0, 2, 3)).reshape(levels, -1, cells_y)
+        return jnp.concatenate([rows, eddy[:, lo:hi][:, -1:] if lo else eddy[:, 0:1]], axis=1)
+
+    x_low, x_high = shift_pair(x_rows(cells_x - width, cells_x), x_rows(0, width), "gx")
+
+    def y_cols(lo, hi):
+        return jnp.concatenate([state[..., lo:hi], eddy[None, ..., lo:hi]], axis=0)
+
+    y_low, y_high = shift_pair(y_cols(cells_y - edge, cells_y), y_cols(0, edge), "gy")
 
     facet_count = facet_cell.shape[0]
     owners_gx = lax.axis_size("gx")
@@ -271,22 +283,23 @@
     filled = jnp.dot(owner_float.T, rank_hot, precision=exact)
     unit_dist = (jnp.arange(7, dtype=jnp.int32) == 4).astype(jnp.float32)[:, None, None]
     outgoing = outgoing + unit_dist * (1.0 - filled)[None]
+    outgoing = jnp.concatenate([outgoing, jnp.zeros((1, owners_gx, capacity), jnp.float32)], axis=0)
+    outgoing = jnp.transpose(outgoing, (1, 0, 2)).reshape(owners_gx, -1)
     x_low, x_high, y_low, y_high, outgoing = lax.optimization_barrier(
         (x_low, x_high, y_low, y_high, outgoing)
     )
-    received = lax.all_to_all(outgoing, "gx", split_axis=1, concat_axis=1, tiled=True).reshape(
-        7, slots
-    )
-    tend = stencil(packed, x_low, x_high, y_low, y_high)
+    received = lax.all_to_all(outgoing, "gx", 0, 0, tiled=True)
+    tend = stencil(state, eddy, x_low, x_high, y_low, y_high)
     tend, received = lax.optimization_barrier((tend, received))
-    pay = jnp.concatenate([received, jnp.zeros((1, slots), jnp.float32)], axis=0)
+    pay = jnp.transpose(received.reshape(owners_gx, 8, capacity), (1, 0, 2)).reshape(8, slots)
     forcing_rows, flux_slots = owner_side(state.reshape(4 * levels * cells_x, cells_y), pay)
     forcing = forcing_rows.reshape(state.shape)
-    wall_flux = flux_slots.reshape(4, owners_gx, capacity)
-    returned = lax.all_to_all(wall_flux, "gx", split_axis=1, concat_axis=1, tiled=True)
+    wall_flux = jnp.transpose(flux_slots.reshape(4, owners_gx, capacity), (1, 0, 2)).reshape(owners_gx, -1)
+    returned = lax.all_to_all(wall_flux, "gx", 0, 0, tiled=True)
     change = (tend - forcing) * (1.0 - solid.astype(jnp.float32))
     new_state = start + dt_step * change
     new_state, returned = lax.optimization_barrier((new_state, returned))
+    returned = jnp.transpose(returned.reshape(owners_gx, 4, capacity), (1, 0, 2))
     through = jnp.einsum("cok,fk->cof", returned, rank_hot, precision=exact)
     facet_flux = jnp.sum(through * owner_float.T[None], axis=1)
     return (new_state, facet_flux)

time: 78.7 us -> 75.6 us (0.961)
  local copies, waits for them, and re-layouts: 4.41 us -> 8.28 us
  other arithmetic: 6.95 us -> 3.47 us
  starting transfers between devices: 28 us -> 25 us
  Pallas kernels: 18.8 us -> 16.6 us
  waiting for transfers between devices: 13.7 us -> 15.2 us
    ppermute x2 -> x4, waiting for transfers between devices: 0.01 us -> 8.75 us  [shift_pair(): return (lax.ppermute(last, axis, up), lax.ppermute(leading, axis, down))]
    ppermute x2 -> x0, waiting for transfers between devices: 6.45 us -> none  [the longest x1 6.45 us: exchange(): before = lax.ppermute(last, axis, up)]
    ppermute x2 -> x4, starting transfers between devices: 3.37 us -> 8.75 us  [shift_pair(): return (lax.ppermute(last, axis, up), lax.ppermute(leading, axis, down))]
    ppermute x2 -> x0, starting transfers between devices: 5.12 us -> none  [the longest x1 2.9 us: exchange(): before = lax.ppermute(last, axis, up)]
    all_to_all x2, starting transfers between devices: 19.5 us -> 16.3 us  [the longest x1 8.79 us: local(): returned = lax.all_to_all(wall_flux, 'gx', 0, 0, tiled=True)]
    transpose x1 -> x0, other arithmetic: 2.6 us -> none  [local(): x_rows = jnp.transpose(packed, (1, 0, 2, 3))]
    transpose x0 -> x6, local copies, waits for them, and re-layouts: none -> 2.49 us  [the longest x3 2.26 us: x_rows(): jnp.transpose(state[:, :, lo:hi], (1, 0, 2, 3)).reshape(levels, -1, cells_y)]
    pallas_call x1, Pallas kernels: 12.1 us -> 9.8 us  [owner_side(): pl.pallas_call(owner_kernel, grid=(steps,), in_specs=[pl.BlockSpec((rows,...]
  transfers between devices with their start and end apart: 6 -> 6, of which waited for: 3 -> 4; matrix products, arithmetic and copies ran while one was open for 9% -> 15% of each run, Pallas kernels for 9% -> 9%
where the time goes in v4:
time: 75.6 us; the launch traced here: 75.1 us
  starting transfers between devices  25 us (33%)
  Pallas kernels  16.6 us (22%)
  waiting for transfers between devices  15.2 us (20%)
  local copies, waits for them, and re-layouts  8.28 us (11%)
  matrix products  5.56 us (7%)
  other arithmetic  3.47 us (5%)
  between operations  0.95 us (1%)
    pallas_call x1, Pallas kernels, owner_side(): pl.pallas_call(owner_kernel, grid=(steps,), in_specs=[pl.BlockSpec((rows,...  9.8 us
    all_to_all x1, starting transfers between devices, local(): returned = lax.all_to_all(wall_flux, 'gx', 0, 0, tiled=True)  8.79 us
    ppermute x4, starting transfers between devices, shift_pair(): return (lax.ppermute(last, axis, up), lax.ppermute(leading, axis, down))  8.75 us
    ppermute x4, waiting for transfers between devices, shift_pair(): return (lax.ppermute(last, axis, up), lax.ppermute(leading, axis, down))  8.75 us
    all_to_all x1, starting transfers between devices, local(): received = lax.all_to_all(outgoing, 'gx', 0, 0, tiled=True)  7.47 us
    pallas_call x1, Pallas kernels, stencil(): pl.pallas_call(stencil_kernel, grid=(levels,), in_specs=[pl.BlockSpec((fi...  6.81 us
    all_to_all x1, waiting for transfers between devices, local(): returned = lax.all_to_all(wall_flux, 'gx', 0, 0, tiled=True)  5.52 us
    add x1, other arithmetic, local(): new_state = start + dt_step * change  2.52 us
  transfers between devices with their start and end apart: 6, of which 4 were waited for; matrix products, arithmetic and copies ran while one was open for 15% of the time, Pallas kernels for 9%

profile of v4, /device:TPU:1, one launch (start us, length us, event | category | flops | bytes accessed | tf_op | source)
XLA Modules:
  0.0 75.1 jit_solution(9940304008269164811)
XLA Ops:
  0.6 0.7 slice_bitcast_fusion.2
  1.4 0.9 %fusion.23 = (f32[4,4,8,128]{3,2,1,0:T(8,128)S(1)}, f32[4,4,8,128]{3,2,1,0:T(8,128)S(1)}) fusion(f32[4,4,8,2048]{3,2,1,0:T(8,128)} %su_ref.1), kind=kLoop, calls=%fused_computation.41 | loop fusion | bytes 262144 | tf_op jit(solution)/shard_map/slice | solution.py:257
  2.3 3.9 %collective-permute-start.2 = (f32[5,4,8,128]{3,2,1,0:T(8,128)S(1)}, f32[5,4,8,128]{3,2,1,0:T(8,128)S(1)}, u32[]{:S(2)}, u32[]{:S(2)}) collective-permute-start(f32[5,4,8,128]{3,2,1,0:T(8,128)S(1)} %pad_maximum_fusion.2), channel_id=1, source_target_pairs={{0,1},{1,2},{2,3},{3,0},{4,5},{5,6},{6,7},{7,4},{8,9},{9,10},{10,1... | collective-permute-start | bytes 245768 | tf_op jit(solution)/shard_map/ppermute | solution.py:228
  6.2 3.1 %collective-permute-start.3 = (f32[5,4,8,128]{3,2,1,0:T(8,128)S(1)}, f32[5,4,8,128]{3,2,1,0:T(8,128)S(1)}, u32[]{:S(2)}, u32[]{:S(2)}) collective-permute-start(f32[5,4,8,128]{3,2,1,0:T(8,128)S(1)} %pad_maximum_fusion.3), channel_id=1, source_target_pairs={{1,0},{2,1},{3,2},{0,3},{5,4},{6,5},{7,6},{4,7},{9,8},{10,9},{11,1... | collective-permute-start | bytes 245768 | tf_op jit(solution)/shard_map/ppermute | solution.py:228
  9.3 1.1 %fusion.24 = (f32[4,1,2048]{2,1,0:T(1,128)S(1)}, f32[4,1,2048]{2,1,0:T(1,128)S(1)}) fusion(f32[4,8,2048]{2,1,0:T(8,128)} %eu_ref.1), kind=kLoop, calls=%fused_computation.42 | loop fusion | bytes 131072 | tf_op jit(solution)/shard_map/slice | solution.py:252
  10.4 1.7 %slice_bitcast_fusion = (f32[4,4,3,2048]{3,2,0,1:T(4,128)S(1)}, f32[4,4,3,2048]{3,2,0,1:T(4,128)S(1)}) fusion(f32[4,4,8,2048]{3,2,1,0:T(8,128)} %su_ref.1), kind=kLoop, calls=%fused_computation.20 | loop fusion | bytes 1572864 | tf_op jit(solution)/shard_map/transpose | solution.py:251
  12.1 0.3 copy.21
  12.4 0.2 copy.22
  12.6 0.1 pad_maximum_fusion
  12.7 1.7 %collective-permute-start = (f32[4,13,2048]{2,1,0:T(8,128)S(1)}, f32[4,13,2048]{2,1,0:T(8,128)S(1)}, u32[]{:S(2)}, u32[]{:S(2)}) collective-permute-start(f32[4,13,2048]{2,1,0:T(8,128)S(1)} %pad_maximum_fusion), channel_id=1, source_target_pairs={{0,4},{4,8},{8,12},{12,16},{16,20},{20,24},{24,28},{28,32},{32,36}... | collective-permute-start | bytes 1277960 | tf_op jit(solution)/shard_map/ppermute | solution.py:228
  14.4 0.3 copy.23
  14.6 0.0 copy-start.10
  14.6 0.2 copy.24
  14.9 0.1 pad_maximum_fusion.1
  14.9 0.1 collective-permute-start.1
  15.0 0.3 copy-done.10
  15.3 0.0 copy-start.11
  15.3 0.0 copy-start.9
  15.3 0.0 copy-start.12
  15.3 1.7 %fusion.10 = f32[2048]{0:T(1024)S(1)} fusion(s32[2048]{0:T(1024)S(1)} %bitcast.45), kind=kOutput, calls=%fused_computation.10 | convolution fusion | flops 541849600 | bytes 16384 | tf_op jit(solution)/shard_map/dot_general | solution.py:271
  17.0 0.0 copy-done.11
  17.0 0.0 copy-start.4
  17.1 0.3 convolution_subtract_fusion
  17.3 0.0 copy-done.9
  17.4 0.0 copy-done.12
  17.4 0.0 copy-done.13
  17.4 1.9 %fusion.7 = f32[7,64,64]{2,1,0:T(8,128)S(1)} fusion(f32[64,2048]{1,0:T(8,128)S(1)} %fusion.16, f32[7,2048]{1,0:T(8,128)S(1)} %pad_maximum_fusion.4, f32[2048]{0:T(1024)S(1)} %fusion.10, f32[64,64]{1,0:T(8,128)S(1)} %convolution_subtract_fusion, f32[7]{0:T(128)S(1)} %compare_convert_fusion), kind=kOutput, calls=%fused_computation.9 | convolution fusion | flops 705748992 | bytes 720924 | tf_op jit(solution)/shard_map/cof,fk->cok/dot_general | solution.py:282
  19.4 0.0 copy-done.4
  19.4 0.0 copy-start.6
  19.4 0.2 copy.25
  19.6 0.1 reshape.74
  19.7 0.0 collective-permute-done.2.yl_ref
  19.7 0.0 copy-start.7
  19.7 0.0 collective-permute-done.3.yh_ref
  19.7 0.0 copy-start.8
  19.7 0.7 collective-permute-done.xl_ref
  20.5 8.0 %collective-permute-done.1.xh_ref = f32[4,13,2048]{2,1,0:T(8,128)S(1)} collective-permute-done((f32[4,13,2048]{2,1,0:T(8,128)S(1)}, f32[4,13,2048]{2,1,0:T(8,128)S(1)}, u32[]{:S(2)}, u32[]{:S(2)}) %collective-permute-start.1) | collective-permute-done | bytes 426016 | tf_op jit(solution)/shard_map/ppermute | solution.py:228
  28.5 0.8 %copy.26 = f32[64,1,512]{2,1,0:T(1,128)} copy(f32[64,1,512]{2,0,1:T(8,128)S(1)} %bitcast.39) | data formatting | bytes 262144 | tf_op jit(solution)/shard_map/all_to_all | solution.py:291
  29.3 7.5 %all-to-all-start = ((f32[64,1,512]{2,1,0:T(1,128)}), f32[64,1,512]{2,1,0:T(1,128)S(1)}, u32[]{:S(2)}, u32[]{:S(2)}) async-start(f32[64,1,512]{2,1,0:T(1,128)} %copy.26), calls=%async_computation | async-start | bytes 262144 | tf_op jit(solution)/shard_map/all_to_all | solution.py:291
  36.8 0.0 copy-done.6
  36.8 0.7 convert_subtract_fusion
  37.5 0.0 copy-done.7
  37.5 0.0 copy-done.8
  37.5 0.0 copy-done.2
  37.5 0.0 copy-done.3
  37.6 6.8 %shard_map.104 = f32[4,4,8,2048]{3,2,1,0:T(8,128)} custom-call(f32[4,4,8,2048]{3,2,1,0:T(8,128)} %su_ref.1, f32[4,4,8,2048]{3,2,1,0:T(8,128)} %su_ref.1, f32[4,4,8,2048]{3,2,1,0:T(8,128)} %su_ref.1, f32[4,8,2048]{2,1,0:T(8,128)} %eu_ref.1, f32[4,8,2048]{2,1,0:T(8,128)} %eu_ref.1, f32[4,8,2048]{2,1,0:T(8,128)} %eu_ref.1, f32[4,13,2048]{2,1,0:T(8,128)} %copy-done.2, ...), custom_call_target="tpu_custom_call" | custom-call | flops 52428800 | bytes 6291456 | tf_op jit(solution)/shard_map/pallas_call | solution.py:120
  44.4 0.9 %all-to-all-done = f32[64,1,512]{2,1,0:T(1,128)S(1)} async-done(((f32[64,1,512]{2,1,0:T(1,128)}), f32[64,1,512]{2,1,0:T(1,128)S(1)}, u32[]{:S(2)}, u32[]{:S(2)}) %all-to-all-start) | async-done | bytes 131104 | tf_op jit(solution)/shard_map/all_to_all | solution.py:291
  45.3 0.1 reshape.76
  45.4 0.1 copy.27
  45.5 0.1 reshape.77.pay_ref
  45.6 0.0 copy-done
  45.6 0.0 copy-start.1
  45.6 9.8 %shard_map.105 = (f32[128,2048]{1,0:T(8,128)S(1)}, f32[4,4096]{1,0:T(4,128)S(1)}) custom-call(f32[128,2048]{1,0:T(8,128)S(1)} %bitcast.34, f32[8,4096]{1,0:T(8,128)S(1)} %reshape.77.pay_ref), custom_call_target="tpu_custom_call" | custom-call | flops 8589934592 | bytes 2293760 | tf_op jit(solution)/shard_map/pallas_call | solution.py:200
  55.4 0.1 reshape.79
  55.6 0.1 copy.39
  55.6 0.8 %all_to_all.22 = f32[64,1,256]{2,1,0:T(1,128)} reshape(f32[64,4,64]{2,1,0:T(4,128)S(1)} %bitcast.41) | data formatting | bytes 131072 | tf_op jit(solution)/shard_map/all_to_all | solution.py:298
  56.4 8.8 %all-to-all-start.1 = ((f32[64,1,256]{2,1,0:T(1,128)}), f32[64,1,256]{2,1,0:T(1,128)S(1)}, u32[]{:S(2)}, u32[]{:S(2)}) async-start(f32[64,1,256]{2,1,0:T(1,128)} %all_to_all.22), calls=%async_computation.1 | async-start | bytes 131072 | tf_op jit(solution)/shard_map/all_to_all | solution.py:298
  65.2 0.0 copy-done.1
  65.2 0.0 copy-start.5
  65.2 2.5 %multiply_add_fusion = f32[4,4,8,2048]{3,2,1,0:T(8,128)} fusion(f32[4,4,8,2048]{3,2,1,0:T(8,128)} %param.10, f32[4,4,8,2048]{3,2,1,0:T(8,128)S(1)} %copy-done.1, f32[4,4,8,2048]{3,2,1,0:T(8,128)S(1)} %bitcast.35, f32[4,8,2048]{2,1,0:T(8,128)} %convert_subtract_fusion), kind=kLoop, calls=%fused_computation.12 | loop fusion | flops 1048576 | bytes 4456448 | tf_op jit(solution)/shard_map/add | solution.py:300
  67.7 5.5 %all-to-all-done.1 = f32[64,1,256]{2,1,0:T(1,128)S(1)} async-done(((f32[64,1,256]{2,1,0:T(1,128)}), f32[64,1,256]{2,1,0:T(1,128)S(1)}, u32[]{:S(2)}, u32[]{:S(2)}) %all-to-all-start.1) | async-done | bytes 65568 | tf_op jit(solution)/shard_map/all_to_all | solution.py:298
  73.3 0.1 reshape.80
  73.4 0.0 copy-done.5
  73.4 1.7 %fusion.6 = f32[4,2048]{1,0:T(4,128)} fusion(f32[64,2048]{1,0:T(8,128)S(1)} %copy-done.5, f32[2048]{0:T(1024)S(1)} %fusion.10, f32[4,64,64]{2,0,1:T(4,128)S(1)} %bitcast.43), kind=kOutput, calls=%fused_computation.8 | convolution fusion | flops 403824640 | bytes 630784 | tf_op jit(solution)/shard_map/cok,fk->cof/dot_general | solution.py:303
  (13 shorter events, 0.1 us)
Async XLA Ops:
  2.3 17.4 %collective-permute-start.2 = (f32[5,4,8,128]{3,2,1,0:T(8,128)S(1)}, f32[5,4,8,128]{3,2,1,0:T(8,128)S(1)}, u32[]{:S(2)}, u32[]{:S(2)}) collective-permute-start(f32[5,4,8,128]{3,2,1,0:T(8,128)S(1)} %pad_maximum_fusion.2), channel_id=1, source_target_pairs={{0,1},{1,2},{2,3},{3,0},{4,5},{5,6},{6,7},{7,4},{8,9},{9,10},{10,1... | collective-permute-start | bytes 245768 | tf_op jit(solution)/shard_map/ppermute | solution.py:228
  6.2 13.6 %collective-permute-start.3 = (f32[5,4,8,128]{3,2,1,0:T(8,128)S(1)}, f32[5,4,8,128]{3,2,1,0:T(8,128)S(1)}, u32[]{:S(2)}, u32[]{:S(2)}) collective-permute-start(f32[5,4,8,128]{3,2,1,0:T(8,128)S(1)} %pad_maximum_fusion.3), channel_id=1, source_target_pairs={{1,0},{2,1},{3,2},{0,3},{5,4},{6,5},{7,6},{4,7},{9,8},{10,9},{11,1... | collective-permute-start | bytes 245768 | tf_op jit(solution)/shard_map/ppermute | solution.py:228
  12.7 7.8 %collective-permute-start = (f32[4,13,2048]{2,1,0:T(8,128)S(1)}, f32[4,13,2048]{2,1,0:T(8,128)S(1)}, u32[]{:S(2)}, u32[]{:S(2)}) collective-permute-start(f32[4,13,2048]{2,1,0:T(8,128)S(1)} %pad_maximum_fusion), channel_id=1, source_target_pairs={{0,4},{4,8},{8,12},{12,16},{16,20},{20,24},{24,28},{28,32},{32,36}... | collective-permute-start | bytes 1277960 | tf_op jit(solution)/shard_map/ppermute | solution.py:228
  14.6 0.7 copy-start.10
  14.9 13.6 %collective-permute-start.1 = (f32[4,13,2048]{2,1,0:T(8,128)S(1)}, f32[4,13,2048]{2,1,0:T(8,128)S(1)}, u32[]{:S(2)}, u32[]{:S(2)}) collective-permute-start(f32[4,13,2048]{2,1,0:T(8,128)S(1)} %pad_maximum_fusion.1), channel_id=1, source_target_pairs={{4,0},{8,4},{12,8},{16,12},{20,16},{24,20},{28,24},{32,28},{36,32}... | collective-permute-start | bytes 1277960 | tf_op jit(solution)/shard_map/ppermute | solution.py:228
  15.3 1.7 %copy-start.11 = (s32[2048]{0:T(1024)S(1)}, s32[2048]{0:T(1024)}, u32[]{:S(2)}) copy-start(s32[2048]{0:T(1024)} %param.17) | copy-start | bytes 24580
  15.3 2.0 %copy-start.9 = (f32[4,2048]{1,0:T(4,128)S(1)}, f32[4,2048]{1,0:T(4,128)}, u32[]{:S(2)}) copy-start(f32[4,2048]{1,0:T(4,128)} %param.13) | copy-start | bytes 98308
  15.3 2.0 %copy-start.12 = (f32[2048]{0:T(1024)S(1)}, f32[2048]{0:T(1024)}, u32[]{:S(2)}) copy-start(f32[2048]{0:T(1024)} %param.15) | copy-start | bytes 24580
  15.3 2.0 %copy-start.13 = (f32[2048]{0:T(1024)S(1)}, f32[2048]{0:T(1024)}, u32[]{:S(2)}) copy-start(f32[2048]{0:T(1024)} %param.14) | copy-start | bytes 24580
  17.0 2.3 %copy-start.4 = (f32[64,2048]{1,0:T(8,128)}, f32[64,2048]{1,0:T(8,128)S(1)}, u32[]{:S(2)}) copy-start(f32[64,2048]{1,0:T(8,128)S(1)} %fusion.16) | copy-start | bytes 1572868
  19.4 17.4 %copy-start.6 = (s32[4,8,2048]{2,1,0:T(8,128)S(1)}, s32[4,8,2048]{2,1,0:T(8,128)}, u32[]{:S(2)}) copy-start(s32[4,8,2048]{2,1,0:T(8,128)} %param.12) | copy-start | bytes 786436
  19.7 17.8 %copy-start.7 = (f32[5,4,8,128]{3,2,1,0:T(8,128)}, f32[5,4,8,128]{3,2,1,0:T(8,128)S(1)}, u32[]{:S(2)}) copy-start(f32[5,4,8,128]{3,2,1,0:T(8,128)S(1)} %collective-permute-done.2.yl_ref) | copy-start | bytes 245764
  19.7 17.8 %copy-start.8 = (f32[5,4,8,128]{3,2,1,0:T(8,128)}, f32[5,4,8,128]{3,2,1,0:T(8,128)S(1)}, u32[]{:S(2)}) copy-start(f32[5,4,8,128]{3,2,1,0:T(8,128)S(1)} %collective-permute-done.3.yh_ref) | copy-start | bytes 245764
  20.5 17.1 %copy-start.2 = (f32[4,13,2048]{2,1,0:T(8,128)}, f32[4,13,2048]{2,1,0:T(8,128)S(1)}, u32[]{:S(2)}) copy-start(f32[4,13,2048]{2,1,0:T(8,128)S(1)} %collective-permute-done.xl_ref) | copy-start | bytes 1277956
  28.5 9.1 %copy-start.3 = (f32[4,13,2048]{2,1,0:T(8,128)}, f32[4,13,2048]{2,1,0:T(8,128)S(1)}, u32[]{:S(2)}) copy-start(f32[4,13,2048]{2,1,0:T(8,128)S(1)} %collective-permute-done.1.xh_ref) | copy-start | bytes 1277956
  29.3 16.0 %all-to-all-start = ((f32[64,1,512]{2,1,0:T(1,128)}), f32[64,1,512]{2,1,0:T(1,128)S(1)}, u32[]{:S(2)}, u32[]{:S(2)}) async-start(f32[64,1,512]{2,1,0:T(1,128)} %copy.26), calls=%async_computation | async-start | bytes 262144 | tf_op jit(solution)/shard_map/all_to_all | solution.py:291
  44.4 1.2 %copy-start = (f32[4,4,8,2048]{3,2,1,0:T(8,128)S(1)}, f32[4,4,8,2048]{3,2,1,0:T(8,128)}, u32[]{:S(2)}) copy-start(f32[4,4,8,2048]{3,2,1,0:T(8,128)} %su_ref.1) | copy-start | bytes 3145732
  45.6 19.6 %copy-start.1 = (f32[4,4,8,2048]{3,2,1,0:T(8,128)S(1)}, f32[4,4,8,2048]{3,2,1,0:T(8,128)}, u32[]{:S(2)}) copy-start(f32[4,4,8,2048]{3,2,1,0:T(8,128)} %shard_map.104) | copy-start | bytes 3145732
  56.4 16.9 %all-to-all-start.1 = ((f32[64,1,256]{2,1,0:T(1,128)}), f32[64,1,256]{2,1,0:T(1,128)S(1)}, u32[]{:S(2)}, u32[]{:S(2)}) async-start(f32[64,1,256]{2,1,0:T(1,128)} %all_to_all.22), calls=%async_computation.1 | async-start | bytes 131072 | tf_op jit(solution)/shard_map/all_to_all | solution.py:298
  65.2 8.2 %copy-start.5 = (f32[64,2048]{1,0:T(8,128)S(1)}, f32[64,2048]{1,0:T(8,128)}, u32[]{:S(2)}) copy-start(f32[64,2048]{1,0:T(8,128)} %copy-done.4) | copy-start | bytes 1572868

commit v5 on v4

--- a/solution.py
+++ b/solution.py
@@ -221,6 +221,16 @@
     )(x, pay)
 
 
+def two_stage_all_to_all(x):
+    outer = lax.axis_size("ga")
+    inner = lax.axis_size("gb")
+    rest = x.shape[1:]
+    y = x.reshape((outer, inner) + rest)
+    y = lax.all_to_all(y, "gb", 1, 1, tiled=True)
+    y = lax.all_to_all(y, "ga", 0, 0, tiled=True)
+    return y.reshape((outer * inner,) + rest)
+
+
 def shift_pair(last, leading, axis):
     peers = lax.axis_size(axis)
     up = [(i, (i + 1) % peers) for i in range(peers)]
@@ -251,7 +261,7 @@
         rows = jnp.transpose(state[:, :, lo:hi], (1, 0, 2, 3)).reshape(levels, -1, cells_y)
         return jnp.concatenate([rows, eddy[:, lo:hi][:, -1:] if lo else eddy[:, 0:1]], axis=1)
 
-    x_low, x_high = shift_pair(x_rows(cells_x - width, cells_x), x_rows(0, width), "gx")
+    x_low, x_high = shift_pair(x_rows(cells_x - width, cells_x), x_rows(0, width), ("ga", "gb"))
 
     def y_cols(lo, hi):
         return jnp.concatenate([state[..., lo:hi], eddy[None, ..., lo:hi]], axis=0)
@@ -259,7 +269,7 @@
     y_low, y_high = shift_pair(y_cols(cells_y - edge, cells_y), y_cols(0, edge), "gy")
 
     facet_count = facet_cell.shape[0]
-    owners_gx = lax.axis_size("gx")
+    owners_gx = lax.axis_size(("ga", "gb"))
     capacity = 2 * facet_count // owners_gx
     slots = owners_gx * capacity
     owner_gx = facet_owner[:, 0]
@@ -288,14 +298,14 @@
     x_low, x_high, y_low, y_high, outgoing = lax.optimization_barrier(
         (x_low, x_high, y_low, y_high, outgoing)
     )
-    received = lax.all_to_all(outgoing, "gx", 0, 0, tiled=True)
+    received = two_stage_all_to_all(outgoing)
     tend = stencil(state, eddy, x_low, x_high, y_low, y_high)
     tend, received = lax.optimization_barrier((tend, received))
     pay = jnp.transpose(received.reshape(owners_gx, 8, capacity), (1, 0, 2)).reshape(8, slots)
     forcing_rows, flux_slots = owner_side(state.reshape(4 * levels * cells_x, cells_y), pay)
     forcing = forcing_rows.reshape(state.shape)
     wall_flux = jnp.transpose(flux_slots.reshape(4, owners_gx, capacity), (1, 0, 2)).reshape(owners_gx, -1)
-    returned = lax.all_to_all(wall_flux, "gx", 0, 0, tiled=True)
+    returned = two_stage_all_to_all(wall_flux)
     change = (tend - forcing) * (1.0 - solid.astype(jnp.float32))
     new_state = start + dt_step * change
     new_state, returned = lax.optimization_barrier((new_state, returned))
@@ -306,16 +316,22 @@
 
 
 def solution(mesh):
+    devices = mesh.devices
+    groups = 8
+    split = jax.sharding.Mesh(
+        devices.reshape(groups, devices.shape[0] // groups, devices.shape[1]), ("ga", "gb", "gy")
+    )
+    gx = ("ga", "gb")
     in_specs = (
-        P(None, None, "gx", "gy"),
-        P(None, None, "gx", "gy"),
-        P(None, "gx", "gy"),
-        P(None, "gx", "gy"),
-        P(None, ("gx", "gy")),
-        P(("gx", "gy")),
-        P(("gx", "gy")),
-        P(("gx", "gy"), None),
-        P(("gx", "gy")),
-    )
-    out_specs = (P(None, None, "gx", "gy"), P(None, ("gx", "gy")))
-    return jax.shard_map(local, mesh=mesh, in_specs=in_specs, out_specs=out_specs, check_vma=False)
+        P(None, None, gx, "gy"),
+        P(None, None, gx, "gy"),
+        P(None, gx, "gy"),
+        P(None, gx, "gy"),
+        P(None, (*gx, "gy")),
+        P((*gx, "gy")),
+        P((*gx, "gy")),
+        P((*gx, "gy"), None),
+        P((*gx, "gy")),
+    )
+    out_specs = (P(None, None, gx, "gy"), P(None, (*gx, "gy")))
+    return jax.shard_map(local, mesh=split, in_specs=in_specs, out_specs=out_specs, check_vma=False)

time: 75.6 us -> 88.1 us (1.17)
  blocking collectives: 0 us -> 8.22 us
  waiting for transfers between devices: 15.2 us -> 17.7 us
  local copies, waits for them, and re-layouts: 8.28 us -> 9.62 us
  other arithmetic: 3.47 us -> 2.41 us
  matrix products: 5.56 us -> 6.6 us
    all_to_all x0 -> x1, blocking collectives: none -> 8.22 us  [two_stage_all_to_all(): y = lax.all_to_all(y, 'gb', 1, 1, tiled=True)]
    all_to_all x2 -> x3, waiting for transfers between devices: 6.45 us -> 8.9 us  [the longest x2 5.69 us: two_stage_all_to_all(): y = lax.all_to_all(y, 'ga', 0, 0, tiled=True)]
    add x1, other arithmetic: 2.52 us -> 1.2 us  [local(): new_state = start + dt_step * change]
    dot_general x1, matrix products: 1.69 us -> 2.72 us  [local(): through = jnp.einsum('cok,fk->cof', returned, rank_hot, precision=exact)]
    all_to_all x2 -> x3, starting transfers between devices: 16.3 us -> 16.6 us  [the longest x2 11.7 us: two_stage_all_to_all(): y = lax.all_to_all(y, 'ga', 0, 0, tiled=True)]
  transfers between devices with their start and end apart: 6 -> 7, of which waited for: 4 -> 5; matrix products, arithmetic and copies ran while one was open for 15% -> 12% of each run, Pallas kernels for 9% -> 8%
where the time goes in v5:
time: 88.1 us; the launch traced here: 87.4 us
  starting transfers between devices  25.4 us (29%)
  waiting for transfers between devices  17.7 us (20%)
  Pallas kernels  16.6 us (19%)
  local copies, waits for them, and re-layouts  9.62 us (11%)
  blocking collectives  8.22 us (9%)
  matrix products  6.6 us (7%)
  other arithmetic  2.41 us (3%)
  between operations  0.93 us (1%)
    all_to_all x2, starting transfers between devices, two_stage_all_to_all(): y = lax.all_to_all(y, 'ga', 0, 0, tiled=True)  11.7 us
    pallas_call x1, Pallas kernels, owner_side(): pl.pallas_call(owner_kernel, grid=(steps,), in_specs=[pl.BlockSpec((rows,...  9.78 us
    ppermute x4, waiting for transfers between devices, shift_pair(): return (lax.ppermute(last, axis, up), lax.ppermute(leading, axis, down))  8.76 us
    ppermute x4, starting transfers between devices, shift_pair(): return (lax.ppermute(last, axis, up), lax.ppermute(leading, axis, down))  8.75 us
    all_to_all x1, blocking collectives, two_stage_all_to_all(): y = lax.all_to_all(y, 'gb', 1, 1, tiled=True)  8.22 us
    pallas_call x1, Pallas kernels, stencil(): pl.pallas_call(stencil_kernel, grid=(levels,), in_specs=[pl.BlockSpec((fi...  6.81 us
    all_to_all x2, waiting for transfers between devices, two_stage_all_to_all(): y = lax.all_to_all(y, 'ga', 0, 0, tiled=True)  5.69 us
    all_to_all x1, starting transfers between devices, two_stage_all_to_all(): y = lax.all_to_all(y, 'gb', 1, 1, tiled=True)  4.95 us
  transfers between devices with their start and end apart: 7, of which 5 were waited for; matrix products, arithmetic and copies ran while one was open for 12% of the time, Pallas kernels for 8%

profile of v5, /device:TPU:1, one launch (start us, length us, event | category | flops | bytes accessed | tf_op | source)
XLA Modules:
  0.0 87.4 jit_solution(8954830579004338388)
XLA Ops:
  0.6 0.7 slice_bitcast_fusion.2
  1.4 0.9 %fusion.23 = (f32[4,4,8,128]{3,2,1,0:T(8,128)S(1)}, f32[4,4,8,128]{3,2,1,0:T(8,128)S(1)}) fusion(f32[4,4,8,2048]{3,2,1,0:T(8,128)} %su_ref.1), kind=kLoop, calls=%fused_computation.39 | loop fusion | bytes 262144 | tf_op jit(solution)/shard_map/slice | solution.py:267
  2.3 3.9 %collective-permute-start.2 = (f32[5,4,8,128]{3,2,1,0:T(8,128)S(1)}, f32[5,4,8,128]{3,2,1,0:T(8,128)S(1)}, u32[]{:S(2)}, u32[]{:S(2)}) collective-permute-start(f32[5,4,8,128]{3,2,1,0:T(8,128)S(1)} %pad_maximum_fusion.2), channel_id=1, source_target_pairs={{0,1},{1,2},{2,3},{3,0},{4,5},{5,6},{6,7},{7,4},{8,9},{9,10},{10,1... | collective-permute-start | bytes 245768 | tf_op jit(solution)/shard_map/ppermute | solution.py:238
  6.2 3.1 %collective-permute-start.3 = (f32[5,4,8,128]{3,2,1,0:T(8,128)S(1)}, f32[5,4,8,128]{3,2,1,0:T(8,128)S(1)}, u32[]{:S(2)}, u32[]{:S(2)}) collective-permute-start(f32[5,4,8,128]{3,2,1,0:T(8,128)S(1)} %pad_maximum_fusion.3), channel_id=1, source_target_pairs={{1,0},{2,1},{3,2},{0,3},{5,4},{6,5},{7,6},{4,7},{9,8},{10,9},{11,1... | collective-permute-start | bytes 245768 | tf_op jit(solution)/shard_map/ppermute | solution.py:238
  9.3 1.1 %fusion.24 = (f32[4,1,2048]{2,1,0:T(1,128)S(1)}, f32[4,1,2048]{2,1,0:T(1,128)S(1)}) fusion(f32[4,8,2048]{2,1,0:T(8,128)} %eu_ref.1), kind=kLoop, calls=%fused_computation.40 | loop fusion | bytes 131072 | tf_op jit(solution)/shard_map/slice | solution.py:262
  10.4 1.7 %slice_bitcast_fusion = (f32[4,4,3,2048]{3,2,0,1:T(4,128)S(1)}, f32[4,4,3,2048]{3,2,0,1:T(4,128)S(1)}) fusion(f32[4,4,8,2048]{3,2,1,0:T(8,128)} %su_ref.1), kind=kLoop, calls=%fused_computation.20 | loop fusion | bytes 1572864 | tf_op jit(solution)/shard_map/transpose | solution.py:261
  12.1 0.3 copy.31
  12.4 0.2 copy.32
  12.6 0.1 pad_maximum_fusion
  12.7 1.7 %collective-permute-start = (f32[4,13,2048]{2,1,0:T(8,128)S(1)}, f32[4,13,2048]{2,1,0:T(8,128)S(1)}, u32[]{:S(2)}, u32[]{:S(2)}) collective-permute-start(f32[4,13,2048]{2,1,0:T(8,128)S(1)} %pad_maximum_fusion), channel_id=1, source_target_pairs={{0,4},{4,8},{8,12},{12,16},{16,20},{20,24},{24,28},{28,32},{32,36}... | collective-permute-start | bytes 1277960 | tf_op jit(solution)/shard_map/ppermute | solution.py:238
  14.3 0.3 copy.33
  14.6 0.0 copy-start.9
  14.6 0.2 copy.34
  14.9 0.1 pad_maximum_fusion.1
  14.9 0.1 collective-permute-start.1
  15.0 0.3 copy-done.9
  15.3 1.7 %fusion.10 = f32[2048]{0:T(1024)S(1)} fusion(s32[2048]{0:T(1024)S(1)} %bitcast.41), kind=kOutput, calls=%fused_computation.10 | convolution fusion | flops 541849600 | bytes 16384 | tf_op jit(solution)/shard_map/dot_general | solution.py:281
  17.0 0.0 copy-done.10
  17.0 0.0 copy-start.5
  17.1 0.3 convolution_subtract_fusion
  17.3 0.0 copy-done.8
  17.3 0.0 copy-done.11
  17.4 0.0 copy-done.12
  17.4 1.9 %fusion.7 = f32[7,64,64]{2,1,0:T(8,128)S(1)} fusion(f32[64,2048]{1,0:T(8,128)S(1)} %fusion.16, f32[7,2048]{1,0:T(8,128)S(1)} %pad_maximum_fusion.4, f32[2048]{0:T(1024)S(1)} %fusion.10, f32[64,64]{1,0:T(8,128)S(1)} %convolution_subtract_fusion, f32[7]{0:T(128)S(1)} %compare_convert_fusion), kind=kOutput, calls=%fused_computation.9 | convolution fusion | flops 705748992 | bytes 720924 | tf_op jit(solution)/shard_map/cof,fk->cok/dot_general | solution.py:292
  19.4 0.0 copy-done.5
  19.4 0.2 copy.35
  19.6 0.1 reshape.77
  19.7 0.0 collective-permute-done.2.yl_ref
  19.7 0.0 copy-start.6
  19.7 0.0 collective-permute-done.3.yh_ref
  19.7 0.0 copy-start.7
  19.7 0.7 collective-permute-done.xl_ref
  20.5 8.0 %collective-permute-done.1.xh_ref = f32[4,13,2048]{2,1,0:T(8,128)S(1)} collective-permute-done((f32[4,13,2048]{2,1,0:T(8,128)S(1)}, f32[4,13,2048]{2,1,0:T(8,128)S(1)}, u32[]{:S(2)}, u32[]{:S(2)}) %collective-permute-start.1) | collective-permute-done | bytes 426016 | tf_op jit(solution)/shard_map/ppermute | solution.py:238
  28.5 0.1 copy.36
  28.6 8.2 %all_to_all.20 = f32[8,8,512]{2,0,1:T(8,128)S(1)} all-to-all(f32[8,8,512]{2,0,1:T(8,128)S(1)} %copy.36), channel_id=1, replica_groups=mesh['ga'=8,'gb'=8,'gy'=4] {'gb'}, dimensions={1} | all-to-all | bytes 262144 | tf_op jit(solution)/shard_map/all_to_all | solution.py:229
  36.8 0.7 copy.37
  37.5 5.2 %all-to-all-start.1 = ((f32[8,8,512]{2,1,0:T(8,128)}), f32[8,8,512]{2,1,0:T(8,128)S(1)}, u32[]{:S(2)}, u32[]{:S(2)}) async-start(f32[8,8,512]{2,1,0:T(8,128)} %copy.37), calls=%async_computation.1 | async-start | bytes 262144 | tf_op jit(solution)/shard_map/all_to_all | solution.py:230
  42.7 0.0 copy-done.6
  42.7 0.0 copy-done.7
  42.8 0.0 copy-done.3
  42.8 0.0 copy-done.4
  42.8 6.8 %shard_map.104 = f32[4,4,8,2048]{3,2,1,0:T(8,128)} custom-call(f32[4,4,8,2048]{3,2,1,0:T(8,128)} %su_ref.1, f32[4,4,8,2048]{3,2,1,0:T(8,128)} %su_ref.1, f32[4,4,8,2048]{3,2,1,0:T(8,128)} %su_ref.1, f32[4,8,2048]{2,1,0:T(8,128)} %eu_ref.1, f32[4,8,2048]{2,1,0:T(8,128)} %eu_ref.1, f32[4,8,2048]{2,1,0:T(8,128)} %eu_ref.1, f32[4,13,2048]{2,1,0:T(8,128)} %copy-done.3, ...), custom_call_target="tpu_custom_call" | custom-call | flops 52428800 | bytes 6291456 | tf_op jit(solution)/shard_map/pallas_call | solution.py:120
  49.6 0.2 all-to-all-done.1
  49.8 0.1 reshape.81
  49.9 0.1 copy.38
  50.0 0.1 reshape.82.pay_ref
  50.1 0.7 copy-done
  50.8 9.8 %shard_map.105 = (f32[128,2048]{1,0:T(8,128)S(1)}, f32[4,4096]{1,0:T(4,128)S(1)}) custom-call(f32[128,2048]{1,0:T(8,128)S(1)} %bitcast.30, f32[8,4096]{1,0:T(8,128)S(1)} %reshape.82.pay_ref), custom_call_target="tpu_custom_call" | custom-call | flops 8589934592 | bytes 2293760 | tf_op jit(solution)/shard_map/pallas_call | solution.py:200
  60.6 0.0 copy-start.1
  60.6 0.1 reshape.84
  60.7 0.1 copy.46
  60.8 0.1 reshape_reshape.3
  61.0 0.6 copy.40
  61.6 4.9 %all-to-all-start.2 = ((f32[8,8,256]{2,0,1:T(8,128)}), f32[8,8,256]{2,0,1:T(8,128)S(1)}, u32[]{:S(2)}, u32[]{:S(2)}) async-start(f32[8,8,256]{2,0,1:T(8,128)} %copy.40), calls=%async_computation.2 | async-start | bytes 131072 | tf_op jit(solution)/shard_map/all_to_all | solution.py:229
  66.6 1.0 %convert_subtract_fusion = f32[4,8,2048]{2,1,0:T(8,128)S(1)} fusion(s32[4,8,2048]{2,1,0:T(8,128)} %param.12), kind=kLoop, calls=%fused_computation.24 | loop fusion | flops 131072 | bytes 524288 | tf_op jit(solution)/shard_map/sub | solution.py:309
  67.5 3.2 %all-to-all-done.2 = f32[8,8,256]{2,0,1:T(8,128)S(1)} async-done(((f32[8,8,256]{2,0,1:T(8,128)}), f32[8,8,256]{2,0,1:T(8,128)S(1)}, u32[]{:S(2)}, u32[]{:S(2)}) %all-to-all-start.2) | async-done | bytes 65568 | tf_op jit(solution)/shard_map/all_to_all | solution.py:229
  70.8 0.6 copy.41
  71.4 6.5 %all-to-all-start.3 = ((f32[8,8,256]{2,1,0:T(8,128)}), f32[8,8,256]{2,1,0:T(8,128)S(1)}, u32[]{:S(2)}, u32[]{:S(2)}) async-start(f32[8,8,256]{2,1,0:T(8,128)} %copy.41), calls=%async_computation.3 | async-start | bytes 131072 | tf_op jit(solution)/shard_map/all_to_all | solution.py:230
  77.9 0.0 copy-done.2
  77.9 0.0 copy-done.1
  77.9 1.2 %multiply_add_fusion = f32[4,4,8,2048]{3,2,1,0:T(8,128)} fusion(f32[4,4,8,2048]{3,2,1,0:T(8,128)S(1)} %copy-done.2, f32[4,4,8,2048]{3,2,1,0:T(8,128)S(1)} %copy-done.1, f32[4,4,8,2048]{3,2,1,0:T(8,128)S(1)} %bitcast.31, f32[4,8,2048]{2,1,0:T(8,128)S(1)} %convert_subtract_fusion), kind=kLoop, calls=%fused_computation.12 | loop fusion | flops 1048576 | bytes 4456448 | tf_op jit(solution)/shard_map/add | solution.py:310
  79.1 5.5 %all-to-all-done.3 = f32[8,8,256]{2,1,0:T(8,128)S(1)} async-done(((f32[8,8,256]{2,1,0:T(8,128)}), f32[8,8,256]{2,1,0:T(8,128)S(1)}, u32[]{:S(2)}, u32[]{:S(2)}) %all-to-all-start.3) | async-done | bytes 65568 | tf_op jit(solution)/shard_map/all_to_all | solution.py:230
  84.6 0.1 reshape.86
  84.7 2.7 %fusion.6 = f32[4,2048]{1,0:T(4,128)} fusion(f32[64,2048]{1,0:T(8,128)} %copy-done.5, f32[2048]{0:T(1024)S(1)} %fusion.10, f32[4,64,64]{2,0,1:T(4,128)S(1)} %bitcast.39), kind=kOutput, calls=%fused_computation.8 | convolution fusion | flops 403824640 | bytes 630784 | tf_op jit(solution)/shard_map/cok,fk->cof/dot_general | solution.py:313
  (15 shorter events, 0.1 us)
Async XLA Ops:
  2.3 17.4 %collective-permute-start.2 = (f32[5,4,8,128]{3,2,1,0:T(8,128)S(1)}, f32[5,4,8,128]{3,2,1,0:T(8,128)S(1)}, u32[]{:S(2)}, u32[]{:S(2)}) collective-permute-start(f32[5,4,8,128]{3,2,1,0:T(8,128)S(1)} %pad_maximum_fusion.2), channel_id=1, source_target_pairs={{0,1},{1,2},{2,3},{3,0},{4,5},{5,6},{6,7},{7,4},{8,9},{9,10},{10,1... | collective-permute-start | bytes 245768 | tf_op jit(solution)/shard_map/ppermute | solution.py:238
  6.2 13.5 %collective-permute-start.3 = (f32[5,4,8,128]{3,2,1,0:T(8,128)S(1)}, f32[5,4,8,128]{3,2,1,0:T(8,128)S(1)}, u32[]{:S(2)}, u32[]{:S(2)}) collective-permute-start(f32[5,4,8,128]{3,2,1,0:T(8,128)S(1)} %pad_maximum_fusion.3), channel_id=1, source_target_pairs={{1,0},{2,1},{3,2},{0,3},{5,4},{6,5},{7,6},{4,7},{9,8},{10,9},{11,1... | collective-permute-start | bytes 245768 | tf_op jit(solution)/shard_map/ppermute | solution.py:238
  12.7 7.8 %collective-permute-start = (f32[4,13,2048]{2,1,0:T(8,128)S(1)}, f32[4,13,2048]{2,1,0:T(8,128)S(1)}, u32[]{:S(2)}, u32[]{:S(2)}) collective-permute-start(f32[4,13,2048]{2,1,0:T(8,128)S(1)} %pad_maximum_fusion), channel_id=1, source_target_pairs={{0,4},{4,8},{8,12},{12,16},{16,20},{20,24},{24,28},{28,32},{32,36}... | collective-permute-start | bytes 1277960 | tf_op jit(solution)/shard_map/ppermute | solution.py:238
  14.6 0.7 copy-start.9
  14.9 13.6 %collective-permute-start.1 = (f32[4,13,2048]{2,1,0:T(8,128)S(1)}, f32[4,13,2048]{2,1,0:T(8,128)S(1)}, u32[]{:S(2)}, u32[]{:S(2)}) collective-permute-start(f32[4,13,2048]{2,1,0:T(8,128)S(1)} %pad_maximum_fusion.1), channel_id=1, source_target_pairs={{4,0},{8,4},{12,8},{16,12},{20,16},{24,20},{28,24},{32,28},{36,32}... | collective-permute-start | bytes 1277960 | tf_op jit(solution)/shard_map/ppermute | solution.py:238
  15.3 1.7 %copy-start.10 = (s32[2048]{0:T(1024)S(1)}, s32[2048]{0:T(1024)}, u32[]{:S(2)}) copy-start(s32[2048]{0:T(1024)} %param.17) | copy-start | bytes 24580
  15.3 2.0 %copy-start.8 = (f32[4,2048]{1,0:T(4,128)S(1)}, f32[4,2048]{1,0:T(4,128)}, u32[]{:S(2)}) copy-start(f32[4,2048]{1,0:T(4,128)} %param.13) | copy-start | bytes 98308
  15.3 2.0 %copy-start.11 = (f32[2048]{0:T(1024)S(1)}, f32[2048]{0:T(1024)}, u32[]{:S(2)}) copy-start(f32[2048]{0:T(1024)} %param.15) | copy-start | bytes 24580
  15.3 2.1 %copy-start.12 = (f32[2048]{0:T(1024)S(1)}, f32[2048]{0:T(1024)}, u32[]{:S(2)}) copy-start(f32[2048]{0:T(1024)} %param.14) | copy-start | bytes 24580
  17.0 2.3 %copy-start.5 = (f32[64,2048]{1,0:T(8,128)}, f32[64,2048]{1,0:T(8,128)S(1)}, u32[]{:S(2)}) copy-start(f32[64,2048]{1,0:T(8,128)S(1)} %fusion.16) | copy-start | bytes 1572868
  19.7 23.1 %copy-start.6 = (f32[5,4,8,128]{3,2,1,0:T(8,128)}, f32[5,4,8,128]{3,2,1,0:T(8,128)S(1)}, u32[]{:S(2)}) copy-start(f32[5,4,8,128]{3,2,1,0:T(8,128)S(1)} %collective-permute-done.2.yl_ref) | copy-start | bytes 245764
  19.7 23.0 %copy-start.7 = (f32[5,4,8,128]{3,2,1,0:T(8,128)}, f32[5,4,8,128]{3,2,1,0:T(8,128)S(1)}, u32[]{:S(2)}) copy-start(f32[5,4,8,128]{3,2,1,0:T(8,128)S(1)} %collective-permute-done.3.yh_ref) | copy-start | bytes 245764
  20.5 22.3 %copy-start.3 = (f32[4,13,2048]{2,1,0:T(8,128)}, f32[4,13,2048]{2,1,0:T(8,128)S(1)}, u32[]{:S(2)}) copy-start(f32[4,13,2048]{2,1,0:T(8,128)S(1)} %collective-permute-done.xl_ref) | copy-start | bytes 1277956
  28.5 14.3 %copy-start.4 = (f32[4,13,2048]{2,1,0:T(8,128)}, f32[4,13,2048]{2,1,0:T(8,128)S(1)}, u32[]{:S(2)}) copy-start(f32[4,13,2048]{2,1,0:T(8,128)S(1)} %collective-permute-done.1.xh_ref) | copy-start | bytes 1277956
  37.5 12.3 %all-to-all-start.1 = ((f32[8,8,512]{2,1,0:T(8,128)}), f32[8,8,512]{2,1,0:T(8,128)S(1)}, u32[]{:S(2)}, u32[]{:S(2)}) async-start(f32[8,8,512]{2,1,0:T(8,128)} %copy.37), calls=%async_computation.1 | async-start | bytes 262144 | tf_op jit(solution)/shard_map/all_to_all | solution.py:230
  49.6 1.2 %copy-start = (f32[4,4,8,2048]{3,2,1,0:T(8,128)S(1)}, f32[4,4,8,2048]{3,2,1,0:T(8,128)}, u32[]{:S(2)}) copy-start(f32[4,4,8,2048]{3,2,1,0:T(8,128)} %su_ref.1) | copy-start | bytes 3145732
  50.8 27.1 %copy-start.2 = (f32[4,4,8,2048]{3,2,1,0:T(8,128)S(1)}, f32[4,4,8,2048]{3,2,1,0:T(8,128)}, u32[]{:S(2)}) copy-start(f32[4,4,8,2048]{3,2,1,0:T(8,128)} %param.10) | copy-start | bytes 3145732
  60.6 17.3 %copy-start.1 = (f32[4,4,8,2048]{3,2,1,0:T(8,128)S(1)}, f32[4,4,8,2048]{3,2,1,0:T(8,128)}, u32[]{:S(2)}) copy-start(f32[4,4,8,2048]{3,2,1,0:T(8,128)} %shard_map.104) | copy-start | bytes 3145732
  61.6 9.1 %all-to-all-start.2 = ((f32[8,8,256]{2,0,1:T(8,128)}), f32[8,8,256]{2,0,1:T(8,128)S(1)}, u32[]{:S(2)}, u32[]{:S(2)}) async-start(f32[8,8,256]{2,0,1:T(8,128)} %copy.40), calls=%async_computation.2 | async-start | bytes 131072 | tf_op jit(solution)/shard_map/all_to_all | solution.py:229
  71.4 13.2 %all-to-all-start.3 = ((f32[8,8,256]{2,1,0:T(8,128)}), f32[8,8,256]{2,1,0:T(8,128)S(1)}, u32[]{:S(2)}, u32[]{:S(2)}) async-start(f32[8,8,256]{2,1,0:T(8,128)} %copy.41), calls=%async_computation.3 | async-start | bytes 131072 | tf_op jit(solution)/shard_map/all_to_all | solution.py:230

commit v6 on v4

--- a/solution.py
+++ b/solution.py
@@ -150,42 +150,61 @@
     return out
 
 
-def owner_kernel(x_ref, pay_ref, forcing_ref, flux_ref, pieces_ref, iota_ref):
+def _one_hot(cell, cols, iota):
+    sub = iota.shape[0]
+    col = cell % cols
+    hi = col // sub
+    lo = (col % sub).astype(jnp.float32)
+    hots = []
+    for a in range(cols // sub):
+        sel = jnp.where(hi == a, lo, -1.0).astype(jnp.bfloat16)
+        hots.append(jnp.where(iota == sel, jnp.bfloat16(1), jnp.bfloat16(0)))
+    return jnp.concatenate(hots, axis=0)
+
+
+def gather_kernel(x_ref, pay_ref, flux_ref, pieces_ref, iota_ref):
     rows, cols = x_ref.shape
     fields = 4
     per_field = rows // fields
     block = pay_ref.shape[1]
-    sub = 256
-    nsub = cols // sub
 
     @pl.when(pl.program_id(0) == 0)
     def _():
         parts = _pieces(x_ref[...], 2)
         for i, p in enumerate(parts):
             pieces_ref[i * rows:(i + 1) * rows, :] = p
-        forcing_ref[...] = jnp.zeros_like(forcing_ref)
-        iota_ref[...] = lax.broadcasted_iota(jnp.int32, (sub, block), 0).astype(jnp.bfloat16)
+        iota_ref[...] = lax.broadcasted_iota(jnp.int32, iota_ref.shape, 0).astype(jnp.bfloat16)
 
     pay = pay_ref[...]
     cell = (pay[6:7] + 0.5).astype(jnp.int32)
-    col = cell % cols
     row = cell // cols
-    hi = col // sub
-    lo = (col % sub).astype(jnp.float32)
-    iota = iota_ref[...]
-    hots = []
-    for a in range(nsub):
-        sel = jnp.where(hi == a, lo, -1.0).astype(jnp.bfloat16)
-        hots.append(jnp.where(iota == sel, jnp.bfloat16(1), jnp.bfloat16(0)))
-    hot = jnp.concatenate(hots, axis=0)
+    hot = _one_hot(cell, cols, iota_ref[...])
     picked = jnp.dot(pieces_ref[...], hot, preferred_element_type=jnp.float32)
     value = picked[0:rows] + picked[rows:2 * rows]
     pick_row = lax.broadcasted_iota(jnp.int32, (per_field, block), 0) == row
     gathered = jnp.concatenate(
         [jnp.sum(jnp.where(pick_row, value[f * per_field:(f + 1) * per_field], 0.0), axis=0, keepdims=True)
          for f in range(fields)], axis=0)
-    flux = pay[5:6] * (gathered - pay[0:4]) / pay[4:5]
-    flux_ref[...] = flux
+    flux_ref[...] = pay[5:6] * (gathered - pay[0:4]) / pay[4:5]
+
+
+def scatter_kernel(pay_ref, flux_ref, forcing_ref, iota_ref):
+    rows, cols = forcing_ref.shape
+    fields = 4
+    per_field = rows // fields
+    block = pay_ref.shape[1]
+
+    @pl.when(pl.program_id(0) == 0)
+    def _():
+        forcing_ref[...] = jnp.zeros_like(forcing_ref)
+        iota_ref[...] = lax.broadcasted_iota(jnp.int32, iota_ref.shape, 0).astype(jnp.bfloat16)
+
+    pay = pay_ref[...]
+    cell = (pay[6:7] + 0.5).astype(jnp.int32)
+    row = cell // cols
+    hot = _one_hot(cell, cols, iota_ref[...])
+    flux = flux_ref[...]
+    pick_row = lax.broadcasted_iota(jnp.int32, (per_field, block), 0) == row
     spread = jnp.concatenate(
         [jnp.where(pick_row, flux[f:f + 1], 0.0) for f in range(fields)], axis=0)
     w = jnp.concatenate(_pieces(spread, 2), axis=0)
@@ -193,32 +212,43 @@
     forcing_ref[...] += added[0:rows] + added[rows:2 * rows]
 
 
-def owner_side(x, pay, block=1024):
+def owner_gather(x, pay, block=1024):
     rows, cols = x.shape
     slots = pay.shape[1]
-    steps = slots // block
     return pl.pallas_call(
-        owner_kernel,
-        grid=(steps,),
+        gather_kernel,
+        grid=(slots // block,),
         in_specs=[
             pl.BlockSpec((rows, cols), lambda j: (0, 0)),
             pl.BlockSpec((8, block), lambda j: (0, j)),
         ],
-        out_specs=[
-            pl.BlockSpec((rows, cols), lambda j: (0, 0)),
-            pl.BlockSpec((4, block), lambda j: (0, j)),
-        ],
-        out_shape=[
-            jax.ShapeDtypeStruct((rows, cols), jnp.float32),
-            jax.ShapeDtypeStruct((4, slots), jnp.float32),
-        ],
+        out_specs=pl.BlockSpec((4, block), lambda j: (0, j)),
+        out_shape=jax.ShapeDtypeStruct((4, slots), jnp.float32),
         scratch_shapes=[pltpu.VMEM((2 * rows, cols), jnp.bfloat16),
                         pltpu.VMEM((256, block), jnp.bfloat16)],
         compiler_params=pltpu.CompilerParams(dimension_semantics=("arbitrary",),
                                              vmem_limit_bytes=48 * 1024 * 1024),
-        cost_estimate=pl.CostEstimate(flops=2 * (4 * rows) * cols * slots, transcendentals=0,
-                                      bytes_accessed=4 * (2 * rows * cols + 12 * slots)),
+        cost_estimate=pl.CostEstimate(flops=2 * (2 * rows) * cols * slots, transcendentals=0,
+                                      bytes_accessed=4 * (rows * cols + 12 * slots)),
     )(x, pay)
+
+
+def owner_scatter(pay, flux, rows, cols, block=1024):
+    slots = pay.shape[1]
+    return pl.pallas_call(
+        scatter_kernel,
+        grid=(slots // block,),
+        in_specs=[
+            pl.BlockSpec((8, block), lambda j: (0, j)),
+            pl.BlockSpec((4, block), lambda j: (0, j)),
+        ],
+        out_specs=pl.BlockSpec((rows, cols), lambda j: (0, 0)),
+        out_shape=jax.ShapeDtypeStruct((rows, cols), jnp.float32),
+        scratch_shapes=[pltpu.VMEM((256, block), jnp.bfloat16)],
+        compiler_params=pltpu.CompilerParams(dimension_semantics=("arbitrary",),
+                                             vmem_limit_bytes=48 * 1024 * 1024),
+        cost_estimate=pl.CostEstimate(flops=rows * cols, transcendentals=0, bytes_accessed=4 * rows * cols),
+    )(pay, flux)
 
 
 def shift_pair(last, leading, axis):
@@ -251,7 +281,8 @@
         rows = jnp.transpose(state[:, :, lo:hi], (1, 0, 2, 3)).reshape(levels, -1, cells_y)
         return jnp.concatenate([rows, eddy[:, lo:hi][:, -1:] if lo else eddy[:, 0:1]], axis=1)
 
-    x_low, x_high = shift_pair(x_rows(cells_x - width, cells_x), x_rows(0, width), "gx")
+    x_last, x_first = x_rows(cells_x - width, cells_x), x_rows(0, width)
+    x_low, x_high = shift_pair(x_last, x_first, "gx")
 
     def y_cols(lo, hi):
         return jnp.concatenate([state[..., lo:hi], eddy[None, ..., lo:hi]], axis=0)
@@ -292,9 +323,10 @@
     tend = stencil(state, eddy, x_low, x_high, y_low, y_high)
     tend, received = lax.optimization_barrier((tend, received))
     pay = jnp.transpose(received.reshape(owners_gx, 8, capacity), (1, 0, 2)).reshape(8, slots)
-    forcing_rows, flux_slots = owner_side(state.reshape(4 * levels * cells_x, cells_y), pay)
-    forcing = forcing_rows.reshape(state.shape)
+    flux_slots = owner_gather(state.reshape(4 * levels * cells_x, cells_y), pay)
     wall_flux = jnp.transpose(flux_slots.reshape(4, owners_gx, capacity), (1, 0, 2)).reshape(owners_gx, -1)
+    wall_flux, pay, flux_slots = lax.optimization_barrier((wall_flux, pay, flux_slots))
+    forcing = owner_scatter(pay, flux_slots, 4 * levels * cells_x, cells_y).reshape(state.shape)
     returned = lax.all_to_all(wall_flux, "gx", 0, 0, tiled=True)
     change = (tend - forcing) * (1.0 - solid.astype(jnp.float32))
     new_state = start + dt_step * change

time: 75.6 us -> 70.8 us (0.937)
  waiting for transfers between devices: 15.2 us -> 11.7 us
  other arithmetic: 3.47 us -> 1.45 us
  Pallas kernels: 16.6 us -> 17.8 us
    all_to_all x1, waiting for transfers between devices: 5.52 us -> 1.4 us  [local(): returned = lax.all_to_all(wall_flux, 'gx', 0, 0, tiled=True)]
    add x1, other arithmetic: 2.52 us -> 1.2 us  [local(): new_state = start + dt_step * change]
    pallas_call x1 -> x2, Pallas kernels: 9.8 us -> 10.9 us  [the longest x1 5.44 us: owner_gather(): pl.pallas_call(gather_kernel, grid=(slots // block,), in_specs=[pl.BlockS...]
  transfers between devices with their start and end apart: 6 -> 6, of which waited for: 4 -> 4; matrix products, arithmetic and copies ran while one was open for 15% -> 13% of each run, Pallas kernels for 9% -> 18%
where the time goes in v6:
time: 70.8 us; the launch traced here: 70.4 us
  starting transfers between devices  24.5 us (35%)
  Pallas kernels  17.8 us (25%)
  waiting for transfers between devices  11.7 us (17%)
  local copies, waits for them, and re-layouts  8.41 us (12%)
  matrix products  5.56 us (8%)
  other arithmetic  1.45 us (2%)
  between operations  0.95 us (1%)
    ppermute x4, waiting for transfers between devices, shift_pair(): return (lax.ppermute(last, axis, up), lax.ppermute(leading, axis, down))  8.79 us
    ppermute x4, starting transfers between devices, shift_pair(): return (lax.ppermute(last, axis, up), lax.ppermute(leading, axis, down))  8.75 us
    all_to_all x1, starting transfers between devices, local(): returned = lax.all_to_all(wall_flux, 'gx', 0, 0, tiled=True)  8.28 us
    all_to_all x1, starting transfers between devices, local(): received = lax.all_to_all(outgoing, 'gx', 0, 0, tiled=True)  7.47 us
    pallas_call x1, Pallas kernels, stencil(): pl.pallas_call(stencil_kernel, grid=(levels,), in_specs=[pl.BlockSpec((fi...  6.94 us
    pallas_call x1, Pallas kernels, owner_gather(): pl.pallas_call(gather_kernel, grid=(slots // block,), in_specs=[pl.BlockS...  5.44 us
    pallas_call x1, Pallas kernels, owner_scatter(): pl.pallas_call(scatter_kernel, grid=(slots // block,), in_specs=[pl.Block...  5.44 us
    transpose x3, local copies, waits for them, and re-layouts, x_rows(): jnp.transpose(state[:, :, lo:hi], (1, 0, 2, 3)).reshape(levels, -1, cells_y)  2.28 us
  transfers between devices with their start and end apart: 6, of which 4 were waited for; matrix products, arithmetic and copies ran while one was open for 13% of the time, Pallas kernels for 18%

profile of v6, /device:TPU:1, one launch (start us, length us, event | category | flops | bytes accessed | tf_op | source)
XLA Modules:
  0.0 70.4 jit_solution(1104527760022122248)
XLA Ops:
  0.6 0.7 %slice_bitcast_fusion.2 = (f32[1,4,8,128]{3,2,1,0:T(8,128)S(1)}, f32[1,4,8,128]{3,2,1,0:T(8,128)S(1)}) fusion(f32[4,8,2048]{2,1,0:T(8,128)} %eu_ref.1), kind=kLoop, calls=%fused_computation.38 | loop fusion | bytes 65536 | tf_op jit(solution)/shard_map/broadcast_in_dim | solution.py:288
  1.4 0.9 %fusion.23 = (f32[4,4,8,128]{3,2,1,0:T(8,128)S(1)}, f32[4,4,8,128]{3,2,1,0:T(8,128)S(1)}) fusion(f32[4,4,8,2048]{3,2,1,0:T(8,128)} %su_ref.1), kind=kLoop, calls=%fused_computation.41 | loop fusion | bytes 262144 | tf_op jit(solution)/shard_map/slice | solution.py:288
  2.3 3.9 %collective-permute-start.2 = (f32[5,4,8,128]{3,2,1,0:T(8,128)S(1)}, f32[5,4,8,128]{3,2,1,0:T(8,128)}, u32[]{:S(2)}, u32[]{:S(2)}) collective-permute-start(f32[5,4,8,128]{3,2,1,0:T(8,128)S(1)} %pad_maximum_fusion.2), channel_id=1, source_target_pairs={{0,1},{1,2},{2,3},{3,0},{4,5},{5,6},{6,7},{7,4},{8,9},{9,10},{10,1... | collective-permute-start | bytes 245768 | tf_op jit(solution)/shard_map/ppermute | solution.py:258
  6.2 3.1 %collective-permute-start.3 = (f32[5,4,8,128]{3,2,1,0:T(8,128)S(1)}, f32[5,4,8,128]{3,2,1,0:T(8,128)}, u32[]{:S(2)}, u32[]{:S(2)}) collective-permute-start(f32[5,4,8,128]{3,2,1,0:T(8,128)S(1)} %pad_maximum_fusion.3), channel_id=1, source_target_pairs={{1,0},{2,1},{3,2},{0,3},{5,4},{6,5},{7,6},{4,7},{9,8},{10,9},{11,1... | collective-permute-start | bytes 245768 | tf_op jit(solution)/shard_map/ppermute | solution.py:258
  9.3 1.1 %fusion.24 = (f32[4,1,2048]{2,1,0:T(1,128)S(1)}, f32[4,1,2048]{2,1,0:T(1,128)S(1)}) fusion(f32[4,8,2048]{2,1,0:T(8,128)} %eu_ref.1), kind=kLoop, calls=%fused_computation.42 | loop fusion | bytes 131072 | tf_op jit(solution)/shard_map/slice | solution.py:282
  10.4 1.8 %slice_bitcast_fusion = (f32[4,4,3,2048]{3,2,0,1:T(4,128)S(1)}, f32[4,4,3,2048]{3,2,0,1:T(4,128)S(1)}) fusion(f32[4,4,8,2048]{3,2,1,0:T(8,128)} %su_ref.1), kind=kLoop, calls=%fused_computation.20 | loop fusion | bytes 1572864 | tf_op jit(solution)/shard_map/transpose | solution.py:281
  12.2 0.3 copy.21
  12.5 0.2 copy.22
  12.7 0.1 pad_maximum_fusion
  12.8 1.7 %collective-permute-start = (f32[4,13,2048]{2,1,0:T(8,128)S(1)}, f32[4,13,2048]{2,1,0:T(8,128)S(1)}, u32[]{:S(2)}, u32[]{:S(2)}) collective-permute-start(f32[4,13,2048]{2,1,0:T(8,128)S(1)} %pad_maximum_fusion), channel_id=1, source_target_pairs={{0,4},{4,8},{8,12},{12,16},{16,20},{20,24},{24,28},{28,32},{32,36}... | collective-permute-start | bytes 1277960 | tf_op jit(solution)/shard_map/ppermute | solution.py:258
  14.4 0.3 copy.23
  14.7 0.0 copy-start.7
  14.7 0.2 copy.24
  14.9 0.1 pad_maximum_fusion.1
  15.0 0.1 collective-permute-start.1
  15.1 0.3 copy-done.7
  15.4 0.0 copy-start.8
  15.4 0.0 copy-start.6
  15.4 0.0 copy-start.9
  15.4 0.0 copy-start.10
  15.4 1.7 %fusion.10 = f32[2048]{0:T(1024)S(1)} fusion(s32[2048]{0:T(1024)S(1)} %bitcast.47), kind=kOutput, calls=%fused_computation.10 | convolution fusion | flops 541849600 | bytes 16384 | tf_op jit(solution)/shard_map/dot_general | solution.py:302
  17.1 0.0 copy-done.8
  17.1 0.3 convolution_subtract_fusion
  17.4 0.0 copy-done.6
  17.4 0.0 copy-done.9
  17.4 0.0 copy-done.10
  17.5 1.9 %fusion.7 = f32[7,64,64]{2,1,0:T(8,128)S(1)} fusion(f32[64,2048]{1,0:T(8,128)S(1)} %fusion.16, f32[7,2048]{1,0:T(8,128)S(1)} %pad_maximum_fusion.4, f32[2048]{0:T(1024)S(1)} %fusion.10, f32[64,64]{1,0:T(8,128)S(1)} %convolution_subtract_fusion, f32[7]{0:T(128)S(1)} %compare_convert_fusion), kind=kOutput, calls=%fused_computation.9 | convolution fusion | flops 705748992 | bytes 720924 | tf_op jit(solution)/shard_map/cof,fk->cok/dot_general | solution.py:313
  19.4 0.0 copy-start.5
  19.5 0.2 copy.25
  19.6 0.1 reshape.75
  19.8 0.0 collective-permute-done.2.yl_ref
  19.8 0.0 collective-permute-done.3.yh_ref
  19.8 0.8 %collective-permute-done.xl_ref = f32[4,13,2048]{2,1,0:T(8,128)S(1)} collective-permute-done((f32[4,13,2048]{2,1,0:T(8,128)S(1)}, f32[4,13,2048]{2,1,0:T(8,128)S(1)}, u32[]{:S(2)}, u32[]{:S(2)}) %collective-permute-start) | collective-permute-done | bytes 426016 | tf_op jit(solution)/shard_map/ppermute | solution.py:258
  20.5 0.0 copy-start.3
  20.5 8.0 %collective-permute-done.1.xh_ref = f32[4,13,2048]{2,1,0:T(8,128)S(1)} collective-permute-done((f32[4,13,2048]{2,1,0:T(8,128)S(1)}, f32[4,13,2048]{2,1,0:T(8,128)S(1)}, u32[]{:S(2)}, u32[]{:S(2)}) %collective-permute-start.1) | collective-permute-done | bytes 426016 | tf_op jit(solution)/shard_map/ppermute | solution.py:258
  28.6 0.0 copy-start.4
  28.6 0.8 %copy.26 = f32[64,1,512]{2,1,0:T(1,128)} copy(f32[64,1,512]{2,0,1:T(8,128)S(1)} %bitcast.40) | data formatting | bytes 262144 | tf_op jit(solution)/shard_map/all_to_all | solution.py:322
  29.4 7.5 %all-to-all-start = ((f32[64,1,512]{2,1,0:T(1,128)}), f32[64,1,512]{2,1,0:T(1,128)S(1)}, u32[]{:S(2)}, u32[]{:S(2)}) async-start(f32[64,1,512]{2,1,0:T(1,128)} %copy.26), calls=%async_computation | async-start | bytes 262144 | tf_op jit(solution)/shard_map/all_to_all | solution.py:322
  36.9 0.0 copy-done.5
  36.9 0.0 copy-done.3
  36.9 0.0 copy-done.4
  36.9 6.9 %shard_map.104 = f32[4,4,8,2048]{3,2,1,0:T(8,128)} custom-call(f32[4,4,8,2048]{3,2,1,0:T(8,128)} %su_ref.1, f32[4,4,8,2048]{3,2,1,0:T(8,128)} %su_ref.1, f32[4,4,8,2048]{3,2,1,0:T(8,128)} %su_ref.1, f32[4,8,2048]{2,1,0:T(8,128)} %eu_ref.1, f32[4,8,2048]{2,1,0:T(8,128)} %eu_ref.1, f32[4,8,2048]{2,1,0:T(8,128)} %eu_ref.1, f32[4,13,2048]{2,1,0:T(8,128)} %copy-done.3, ...), custom_call_target="tpu_custom_call" | custom-call | flops 52428800 | bytes 6291456 | tf_op jit(solution)/shard_map/pallas_call | solution.py:120
  43.9 0.0 copy-start
  43.9 1.5 %all-to-all-done = f32[64,1,512]{2,1,0:T(1,128)S(1)} async-done(((f32[64,1,512]{2,1,0:T(1,128)}), f32[64,1,512]{2,1,0:T(1,128)S(1)}, u32[]{:S(2)}, u32[]{:S(2)}) %all-to-all-start) | async-done | bytes 131104 | tf_op jit(solution)/shard_map/all_to_all | solution.py:322
  45.4 0.1 reshape.77
  45.5 0.1 copy.27
  45.5 0.1 reshape.78.pay_ref
  45.7 0.0 copy-done
  45.7 5.4 %shard_map.105.flux_ref = f32[4,4096]{1,0:T(4,128)S(1)} custom-call(f32[128,2048]{1,0:T(8,128)S(1)} %bitcast.35, f32[8,4096]{1,0:T(8,128)S(1)} %reshape.78.pay_ref), custom_call_target="tpu_custom_call" | custom-call | flops 4294967296 | bytes 1245184 | tf_op jit(solution)/shard_map/pallas_call | solution.py:218
  51.1 0.0 copy-start.1
  51.1 0.0 copy-start.2
  51.1 0.1 reshape.79
  51.3 0.1 copy.39
  51.4 0.1 reshape.80
  51.5 0.7 copy.29
  52.2 8.3 %all-to-all-start.1 = ((f32[64,1,256]{2,1,0:T(1,128)}), f32[64,1,256]{2,1,0:T(1,128)S(1)}, u32[]{:S(2)}, u32[]{:S(2)}) async-start(f32[64,1,256]{2,1,0:T(1,128)} %copy.29), calls=%async_computation.1 | async-start | bytes 131072 | tf_op jit(solution)/shard_map/all_to_all | solution.py:330
  60.5 5.4 %shard_map.106 = f32[128,2048]{1,0:T(8,128)S(1)} custom-call(f32[8,4096]{1,0:T(8,128)S(1)} %reshape.78.pay_ref, f32[4,4096]{1,0:T(4,128)S(1)} %shard_map.105.flux_ref), custom_call_target="tpu_custom_call" | custom-call | flops 262144 | bytes 1048576 | tf_op jit(solution)/shard_map/pallas_call | solution.py:238
  65.9 0.0 copy-done.1
  65.9 0.0 copy-done.2
  65.9 1.2 %multiply_add_fusion = f32[4,4,8,2048]{3,2,1,0:T(8,128)} fusion(f32[4,4,8,2048]{3,2,1,0:T(8,128)S(1)} %copy-done.2, f32[4,4,8,2048]{3,2,1,0:T(8,128)S(1)} %copy-done.1, f32[4,4,8,2048]{3,2,1,0:T(8,128)S(1)} %bitcast.36, f32[4,8,2048]{2,1,0:T(8,128)S(1)} %convert_subtract_fusion), kind=kLoop, calls=%fused_computation.12 | loop fusion | flops 1048576 | bytes 4456448 | tf_op jit(solution)/shard_map/add | solution.py:332
  67.1 1.4 %all-to-all-done.1 = f32[64,1,256]{2,1,0:T(1,128)S(1)} async-done(((f32[64,1,256]{2,1,0:T(1,128)}), f32[64,1,256]{2,1,0:T(1,128)S(1)}, u32[]{:S(2)}, u32[]{:S(2)}) %all-to-all-start.1) | async-done | bytes 65568 | tf_op jit(solution)/shard_map/all_to_all | solution.py:330
  68.5 0.1 reshape.82
  68.7 1.7 %fusion.6 = f32[4,2048]{1,0:T(4,128)} fusion(f32[64,2048]{1,0:T(8,128)S(1)} %fusion.16, f32[2048]{0:T(1024)S(1)} %fusion.10, f32[4,64,64]{2,0,1:T(4,128)S(1)} %bitcast.45), kind=kOutput, calls=%fused_computation.8 | convolution fusion | flops 403824640 | bytes 630784 | tf_op jit(solution)/shard_map/cok,fk->cof/dot_general | solution.py:335
  (10 shorter events, 0.2 us)
Async XLA Ops:
  2.3 17.5 %collective-permute-start.2 = (f32[5,4,8,128]{3,2,1,0:T(8,128)S(1)}, f32[5,4,8,128]{3,2,1,0:T(8,128)}, u32[]{:S(2)}, u32[]{:S(2)}) collective-permute-start(f32[5,4,8,128]{3,2,1,0:T(8,128)S(1)} %pad_maximum_fusion.2), channel_id=1, source_target_pairs={{0,1},{1,2},{2,3},{3,0},{4,5},{5,6},{6,7},{7,4},{8,9},{9,10},{10,1... | collective-permute-start | bytes 245768 | tf_op jit(solution)/shard_map/ppermute | solution.py:258
  6.2 13.6 %collective-permute-start.3 = (f32[5,4,8,128]{3,2,1,0:T(8,128)S(1)}, f32[5,4,8,128]{3,2,1,0:T(8,128)}, u32[]{:S(2)}, u32[]{:S(2)}) collective-permute-start(f32[5,4,8,128]{3,2,1,0:T(8,128)S(1)} %pad_maximum_fusion.3), channel_id=1, source_target_pairs={{1,0},{2,1},{3,2},{0,3},{5,4},{6,5},{7,6},{4,7},{9,8},{10,9},{11,1... | collective-permute-start | bytes 245768 | tf_op jit(solution)/shard_map/ppermute | solution.py:258
  12.8 7.8 %collective-permute-start = (f32[4,13,2048]{2,1,0:T(8,128)S(1)}, f32[4,13,2048]{2,1,0:T(8,128)S(1)}, u32[]{:S(2)}, u32[]{:S(2)}) collective-permute-start(f32[4,13,2048]{2,1,0:T(8,128)S(1)} %pad_maximum_fusion), channel_id=1, source_target_pairs={{0,4},{4,8},{8,12},{12,16},{16,20},{20,24},{24,28},{28,32},{32,36}... | collective-permute-start | bytes 1277960 | tf_op jit(solution)/shard_map/ppermute | solution.py:258
  14.7 0.7 copy-start.7
  15.0 13.6 %collective-permute-start.1 = (f32[4,13,2048]{2,1,0:T(8,128)S(1)}, f32[4,13,2048]{2,1,0:T(8,128)S(1)}, u32[]{:S(2)}, u32[]{:S(2)}) collective-permute-start(f32[4,13,2048]{2,1,0:T(8,128)S(1)} %pad_maximum_fusion.1), channel_id=1, source_target_pairs={{4,0},{8,4},{12,8},{16,12},{20,16},{24,20},{28,24},{32,28},{36,32}... | collective-permute-start | bytes 1277960 | tf_op jit(solution)/shard_map/ppermute | solution.py:258
  15.4 1.7 %copy-start.8 = (s32[2048]{0:T(1024)S(1)}, s32[2048]{0:T(1024)}, u32[]{:S(2)}) copy-start(s32[2048]{0:T(1024)} %param.17) | copy-start | bytes 24580
  15.4 2.0 %copy-start.6 = (f32[4,2048]{1,0:T(4,128)S(1)}, f32[4,2048]{1,0:T(4,128)}, u32[]{:S(2)}) copy-start(f32[4,2048]{1,0:T(4,128)} %param.13) | copy-start | bytes 98308
  15.4 2.0 %copy-start.9 = (f32[2048]{0:T(1024)S(1)}, f32[2048]{0:T(1024)}, u32[]{:S(2)}) copy-start(f32[2048]{0:T(1024)} %param.15) | copy-start | bytes 24580
  15.4 2.0 %copy-start.10 = (f32[2048]{0:T(1024)S(1)}, f32[2048]{0:T(1024)}, u32[]{:S(2)}) copy-start(f32[2048]{0:T(1024)} %param.14) | copy-start | bytes 24580
  19.4 17.5 %copy-start.5 = (s32[4,8,2048]{2,1,0:T(8,128)S(1)}, s32[4,8,2048]{2,1,0:T(8,128)}, u32[]{:S(2)}) copy-start(s32[4,8,2048]{2,1,0:T(8,128)} %param.12) | copy-start | bytes 786436
  20.5 16.4 %copy-start.3 = (f32[4,13,2048]{2,1,0:T(8,128)}, f32[4,13,2048]{2,1,0:T(8,128)S(1)}, u32[]{:S(2)}) copy-start(f32[4,13,2048]{2,1,0:T(8,128)S(1)} %collective-permute-done.xl_ref) | copy-start | bytes 1277956
  28.6 8.4 %copy-start.4 = (f32[4,13,2048]{2,1,0:T(8,128)}, f32[4,13,2048]{2,1,0:T(8,128)S(1)}, u32[]{:S(2)}) copy-start(f32[4,13,2048]{2,1,0:T(8,128)S(1)} %collective-permute-done.1.xh_ref) | copy-start | bytes 1277956
  29.4 16.0 %all-to-all-start = ((f32[64,1,512]{2,1,0:T(1,128)}), f32[64,1,512]{2,1,0:T(1,128)S(1)}, u32[]{:S(2)}, u32[]{:S(2)}) async-start(f32[64,1,512]{2,1,0:T(1,128)} %copy.26), calls=%async_computation | async-start | bytes 262144 | tf_op jit(solution)/shard_map/all_to_all | solution.py:322
  43.9 1.8 %copy-start = (f32[4,4,8,2048]{3,2,1,0:T(8,128)S(1)}, f32[4,4,8,2048]{3,2,1,0:T(8,128)}, u32[]{:S(2)}) copy-start(f32[4,4,8,2048]{3,2,1,0:T(8,128)} %su_ref.1) | copy-start | bytes 3145732
  51.1 14.8 %copy-start.1 = (f32[4,4,8,2048]{3,2,1,0:T(8,128)S(1)}, f32[4,4,8,2048]{3,2,1,0:T(8,128)}, u32[]{:S(2)}) copy-start(f32[4,4,8,2048]{3,2,1,0:T(8,128)} %shard_map.104) | copy-start | bytes 3145732
  51.1 14.8 %copy-start.2 = (f32[4,4,8,2048]{3,2,1,0:T(8,128)S(1)}, f32[4,4,8,2048]{3,2,1,0:T(8,128)}, u32[]{:S(2)}) copy-start(f32[4,4,8,2048]{3,2,1,0:T(8,128)} %param.10) | copy-start | bytes 3145732
  52.2 16.3 %all-to-all-start.1 = ((f32[64,1,256]{2,1,0:T(1,128)}), f32[64,1,256]{2,1,0:T(1,128)S(1)}, u32[]{:S(2)}, u32[]{:S(2)}) async-start(f32[64,1,256]{2,1,0:T(1,128)} %copy.29), calls=%async_computation.1 | async-start | bytes 131072 | tf_op jit(solution)/shard_map/all_to_all | solution.py:330

commit v7 on v6

--- a/solution.py
+++ b/solution.py
@@ -284,11 +284,6 @@
     x_last, x_first = x_rows(cells_x - width, cells_x), x_rows(0, width)
     x_low, x_high = shift_pair(x_last, x_first, "gx")
 
-    def y_cols(lo, hi):
-        return jnp.concatenate([state[..., lo:hi], eddy[None, ..., lo:hi]], axis=0)
-
-    y_low, y_high = shift_pair(y_cols(cells_y - edge, cells_y), y_cols(0, edge), "gy")
-
     facet_count = facet_cell.shape[0]
     owners_gx = lax.axis_size("gx")
     capacity = 2 * facet_count // owners_gx
@@ -316,6 +311,12 @@
     outgoing = outgoing + unit_dist * (1.0 - filled)[None]
     outgoing = jnp.concatenate([outgoing, jnp.zeros((1, owners_gx, capacity), jnp.float32)], axis=0)
     outgoing = jnp.transpose(outgoing, (1, 0, 2)).reshape(owners_gx, -1)
+    outgoing, y_state, y_eddy = lax.optimization_barrier((outgoing, state, eddy))
+
+    def y_cols(lo, hi):
+        return jnp.concatenate([y_state[..., lo:hi], y_eddy[None, ..., lo:hi]], axis=0)
+
+    y_low, y_high = shift_pair(y_cols(cells_y - edge, cells_y), y_cols(0, edge), "gy")
     x_low, x_high, y_low, y_high, outgoing = lax.optimization_barrier(
         (x_low, x_high, y_low, y_high, outgoing)
     )

time: 70.8 us -> 71.1 us (level)
  starting transfers between devices: 24.5 us -> 30.5 us
  waiting for transfers between devices: 11.7 us -> 6.05 us
    all_to_all x1, starting transfers between devices: 7.47 us -> 13.6 us  [local(): received = lax.all_to_all(outgoing, 'gx', 0, 0, tiled=True)]
    ppermute x4, waiting for transfers between devices: 8.79 us -> 3.2 us  [shift_pair(): return (lax.ppermute(last, axis, up), lax.ppermute(leading, axis, down))]
  transfers between devices with their start and end apart: 6 -> 6, of which waited for: 4 -> 4; matrix products, arithmetic and copies ran while one was open for 13% -> 11% of each run, Pallas kernels for 18% -> 18%
where the time goes in v7:
time: 71.1 us; the launch traced here: 70.7 us
  starting transfers between devices  30.5 us (43%)
  Pallas kernels  17.9 us (25%)
  local copies, waits for them, and re-layouts  8.34 us (12%)
  waiting for transfers between devices  6.05 us (9%)
  matrix products  5.56 us (8%)
  other arithmetic  1.45 us (2%)
  between operations  0.94 us (1%)
    all_to_all x1, starting transfers between devices, local(): received = lax.all_to_all(outgoing, 'gx', 0, 0, tiled=True)  13.6 us
    ppermute x4, starting transfers between devices, shift_pair(): return (lax.ppermute(last, axis, up), lax.ppermute(leading, axis, down))  8.67 us
    all_to_all x1, starting transfers between devices, local(): returned = lax.all_to_all(wall_flux, 'gx', 0, 0, tiled=True)  8.24 us
    pallas_call x1, Pallas kernels, stencil(): pl.pallas_call(stencil_kernel, grid=(levels,), in_specs=[pl.BlockSpec((fi...  6.94 us
    pallas_call x1, Pallas kernels, owner_gather(): pl.pallas_call(gather_kernel, grid=(slots // block,), in_specs=[pl.BlockS...  5.48 us
    pallas_call x1, Pallas kernels, owner_scatter(): pl.pallas_call(scatter_kernel, grid=(slots // block,), in_specs=[pl.Block...  5.44 us
    ppermute x4, waiting for transfers between devices, shift_pair(): return (lax.ppermute(last, axis, up), lax.ppermute(leading, axis, down))  3.2 us
    transpose x3, local copies, waits for them, and re-layouts, x_rows(): jnp.transpose(state[:, :, lo:hi], (1, 0, 2, 3)).reshape(levels, -1, cells_y)  2.28 us
  transfers between devices with their start and end apart: 6, of which 4 were waited for; matrix products, arithmetic and copies ran while one was open for 11% of the time, Pallas kernels for 18%

profile of v7, /device:TPU:1, one launch (start us, length us, event | category | flops | bytes accessed | tf_op | source)
XLA Modules:
  0.0 70.7 jit_solution(5038784373938295528)
XLA Ops:
  0.6 1.1 %fusion.24 = (f32[4,1,2048]{2,1,0:T(1,128)S(1)}, f32[4,1,2048]{2,1,0:T(1,128)S(1)}) fusion(f32[4,8,2048]{2,1,0:T(8,128)} %eu_ref.1), kind=kLoop, calls=%fused_computation.42 | loop fusion | bytes 131072 | tf_op jit(solution)/shard_map/slice | solution.py:282
  1.8 1.8 %slice_bitcast_fusion = (f32[4,4,3,2048]{3,2,0,1:T(4,128)S(1)}, f32[4,4,3,2048]{3,2,0,1:T(4,128)S(1)}) fusion(f32[4,4,8,2048]{3,2,1,0:T(8,128)} %su_ref.1), kind=kLoop, calls=%fused_computation.20 | loop fusion | bytes 1572864 | tf_op jit(solution)/shard_map/transpose | solution.py:281
  3.5 0.3 copy.21
  3.8 0.2 copy.22
  4.0 0.1 pad_maximum_fusion
  4.1 3.1 %collective-permute-start = (f32[4,13,2048]{2,1,0:T(8,128)S(1)}, f32[4,13,2048]{2,1,0:T(8,128)S(1)}, u32[]{:S(2)}, u32[]{:S(2)}) collective-permute-start(f32[4,13,2048]{2,1,0:T(8,128)S(1)} %pad_maximum_fusion), channel_id=1, source_target_pairs={{0,4},{4,8},{8,12},{12,16},{16,20},{20,24},{24,28},{28,32},{32,36}... | collective-permute-start | bytes 1277960 | tf_op jit(solution)/shard_map/ppermute | solution.py:258
  7.2 0.3 copy.23
  7.5 0.0 copy-start.9
  7.5 0.2 copy.24
  7.7 0.1 pad_maximum_fusion.1
  7.8 0.3 collective-permute-start.1
  8.1 0.1 copy-done.9
  8.2 0.0 copy-start.10
  8.2 0.0 copy-start.8
  8.2 0.0 copy-start.11
  8.2 0.0 copy-start.12
  8.2 1.7 %fusion.10 = f32[2048]{0:T(1024)S(1)} fusion(s32[2048]{0:T(1024)S(1)} %bitcast.47), kind=kOutput, calls=%fused_computation.10 | convolution fusion | flops 541849600 | bytes 16384 | tf_op jit(solution)/shard_map/dot_general | solution.py:297
  9.9 0.0 copy-done.10
  9.9 0.3 convolution_subtract_fusion
  10.2 0.0 copy-done.8
  10.2 0.0 copy-done.11
  10.2 0.0 copy-done.12
  10.2 1.9 %fusion.7 = f32[7,64,64]{2,1,0:T(8,128)S(1)} fusion(f32[64,2048]{1,0:T(8,128)S(1)} %fusion.16, f32[7,2048]{1,0:T(8,128)S(1)} %pad_maximum_fusion.4, f32[2048]{0:T(1024)S(1)} %fusion.10, f32[64,64]{1,0:T(8,128)S(1)} %convolution_subtract_fusion, f32[7]{0:T(128)S(1)} %compare_convert_fusion), kind=kOutput, calls=%fused_computation.9 | convolution fusion | flops 705748992 | bytes 720924 | tf_op jit(solution)/shard_map/cof,fk->cok/dot_general | solution.py:308
  12.2 0.0 copy-start.5
  12.2 0.2 copy.25
  12.4 0.1 reshape.75
  12.5 0.9 %fusion.23 = (f32[4,4,8,128]{3,2,1,0:T(8,128)S(1)}, f32[4,4,8,128]{3,2,1,0:T(8,128)S(1)}) fusion(f32[4,4,8,2048]{3,2,1,0:T(8,128)} %su_ref.1), kind=kLoop, calls=%fused_computation.41 | loop fusion | bytes 262144 | tf_op jit(solution)/shard_map/slice | solution.py:317
  13.4 0.7 %slice_bitcast_fusion.2 = (f32[1,4,8,128]{3,2,1,0:T(8,128)S(1)}, f32[1,4,8,128]{3,2,1,0:T(8,128)S(1)}) fusion(f32[4,8,2048]{2,1,0:T(8,128)} %eu_ref.1), kind=kLoop, calls=%fused_computation.38 | loop fusion | bytes 65536 | tf_op jit(solution)/shard_map/broadcast_in_dim | solution.py:317
  14.2 3.1 %collective-permute-start.2 = (f32[5,4,8,128]{3,2,1,0:T(8,128)S(1)}, f32[5,4,8,128]{3,2,1,0:T(8,128)S(1)}, u32[]{:S(2)}, u32[]{:S(2)}) collective-permute-start(f32[5,4,8,128]{3,2,1,0:T(8,128)S(1)} %pad_maximum_fusion.2), channel_id=1, source_target_pairs={{0,1},{1,2},{2,3},{3,0},{4,5},{5,6},{6,7},{7,4},{8,9},{9,10},{10,1... | collective-permute-start | bytes 245768 | tf_op jit(solution)/shard_map/ppermute | solution.py:258
  17.2 2.2 %collective-permute-start.3 = (f32[5,4,8,128]{3,2,1,0:T(8,128)S(1)}, f32[5,4,8,128]{3,2,1,0:T(8,128)S(1)}, u32[]{:S(2)}, u32[]{:S(2)}) collective-permute-start(f32[5,4,8,128]{3,2,1,0:T(8,128)S(1)} %pad_maximum_fusion.3), channel_id=1, source_target_pairs={{1,0},{2,1},{3,2},{0,3},{5,4},{6,5},{7,6},{4,7},{9,8},{10,9},{11,1... | collective-permute-start | bytes 245768 | tf_op jit(solution)/shard_map/ppermute | solution.py:258
  19.5 2.9 %collective-permute-done.2.yl_ref = f32[5,4,8,128]{3,2,1,0:T(8,128)S(1)} collective-permute-done((f32[5,4,8,128]{3,2,1,0:T(8,128)S(1)}, f32[5,4,8,128]{3,2,1,0:T(8,128)S(1)}, u32[]{:S(2)}, u32[]{:S(2)}) %collective-permute-start.2) | collective-permute-done | bytes 81952 | tf_op jit(solution)/shard_map/ppermute | solution.py:258
  22.4 0.0 copy-start.6
  22.4 0.3 collective-permute-done.3.yh_ref
  22.7 0.0 collective-permute-done.xl_ref
  22.7 0.0 collective-permute-done.1.xh_ref
  22.7 0.0 copy-start.4
  22.7 1.0 %copy.26 = f32[64,1,512]{2,1,0:T(1,128)} copy(f32[64,1,512]{2,0,1:T(8,128)S(1)} %bitcast.40) | data formatting | bytes 262144 | tf_op jit(solution)/shard_map/all_to_all | solution.py:323
  23.6 13.6 %all-to-all-start = ((f32[64,1,512]{2,1,0:T(1,128)}), f32[64,1,512]{2,1,0:T(1,128)S(1)}, u32[]{:S(2)}, u32[]{:S(2)}) async-start(f32[64,1,512]{2,1,0:T(1,128)} %copy.26), calls=%async_computation | async-start | bytes 262144 | tf_op jit(solution)/shard_map/all_to_all | solution.py:323
  37.2 0.0 copy-done.5
  37.3 0.0 copy-done.6
  37.3 0.0 copy-done.7
  37.3 0.0 copy-done.3
  37.3 0.0 copy-done.4
  37.3 6.9 %shard_map.104 = f32[4,4,8,2048]{3,2,1,0:T(8,128)} custom-call(f32[4,4,8,2048]{3,2,1,0:T(8,128)} %su_ref.1, f32[4,4,8,2048]{3,2,1,0:T(8,128)} %su_ref.1, f32[4,4,8,2048]{3,2,1,0:T(8,128)} %su_ref.1, f32[4,8,2048]{2,1,0:T(8,128)} %eu_ref.1, f32[4,8,2048]{2,1,0:T(8,128)} %eu_ref.1, f32[4,8,2048]{2,1,0:T(8,128)} %eu_ref.1, f32[4,13,2048]{2,1,0:T(8,128)} %copy-done.3, ...), custom_call_target="tpu_custom_call" | custom-call | flops 52428800 | bytes 6291456 | tf_op jit(solution)/shard_map/pallas_call | solution.py:120
  44.2 1.5 %all-to-all-done = f32[64,1,512]{2,1,0:T(1,128)S(1)} async-done(((f32[64,1,512]{2,1,0:T(1,128)}), f32[64,1,512]{2,1,0:T(1,128)S(1)}, u32[]{:S(2)}, u32[]{:S(2)}) %all-to-all-start) | async-done | bytes 131104 | tf_op jit(solution)/shard_map/all_to_all | solution.py:323
  45.7 0.1 reshape.77
  45.8 0.1 copy.27
  45.9 0.1 reshape.78.pay_ref
  46.0 0.0 copy-done
  46.0 5.5 %shard_map.105.flux_ref = f32[4,4096]{1,0:T(4,128)S(1)} custom-call(f32[128,2048]{1,0:T(8,128)S(1)} %bitcast.35, f32[8,4096]{1,0:T(8,128)S(1)} %reshape.78.pay_ref), custom_call_target="tpu_custom_call" | custom-call | flops 4294967296 | bytes 1245184 | tf_op jit(solution)/shard_map/pallas_call | solution.py:218
  51.5 0.0 copy-start.1
  51.5 0.0 copy-start.2
  51.5 0.1 reshape.79
  51.6 0.1 copy.39
  51.7 0.1 reshape.80
  51.9 0.7 copy.29
  52.6 8.2 %all-to-all-start.1 = ((f32[64,1,256]{2,1,0:T(1,128)}), f32[64,1,256]{2,1,0:T(1,128)S(1)}, u32[]{:S(2)}, u32[]{:S(2)}) async-start(f32[64,1,256]{2,1,0:T(1,128)} %copy.29), calls=%async_computation.1 | async-start | bytes 131072 | tf_op jit(solution)/shard_map/all_to_all | solution.py:331
  60.8 5.4 %shard_map.106 = f32[128,2048]{1,0:T(8,128)S(1)} custom-call(f32[8,4096]{1,0:T(8,128)S(1)} %reshape.78.pay_ref, f32[4,4096]{1,0:T(4,128)S(1)} %shard_map.105.flux_ref), custom_call_target="tpu_custom_call" | custom-call | flops 262144 | bytes 1048576 | tf_op jit(solution)/shard_map/pallas_call | solution.py:238
  66.3 0.0 copy-done.1
  66.3 0.0 copy-done.2
  66.3 1.2 %multiply_add_fusion = f32[4,4,8,2048]{3,2,1,0:T(8,128)} fusion(f32[4,4,8,2048]{3,2,1,0:T(8,128)S(1)} %copy-done.2, f32[4,4,8,2048]{3,2,1,0:T(8,128)S(1)} %copy-done.1, f32[4,4,8,2048]{3,2,1,0:T(8,128)S(1)} %bitcast.36, f32[4,8,2048]{2,1,0:T(8,128)S(1)} %convert_subtract_fusion), kind=kLoop, calls=%fused_computation.12 | loop fusion | flops 1048576 | bytes 4456448 | tf_op jit(solution)/shard_map/add | solution.py:333
  67.5 1.4 %all-to-all-done.1 = f32[64,1,256]{2,1,0:T(1,128)S(1)} async-done(((f32[64,1,256]{2,1,0:T(1,128)}), f32[64,1,256]{2,1,0:T(1,128)S(1)}, u32[]{:S(2)}, u32[]{:S(2)}) %all-to-all-start.1) | async-done | bytes 65568 | tf_op jit(solution)/shard_map/all_to_all | solution.py:331
  68.9 0.1 reshape.82
  69.0 1.7 %fusion.6 = f32[4,2048]{1,0:T(4,128)} fusion(f32[64,2048]{1,0:T(8,128)S(1)} %fusion.16, f32[2048]{0:T(1024)S(1)} %fusion.10, f32[4,64,64]{2,0,1:T(4,128)S(1)} %bitcast.45), kind=kOutput, calls=%fused_computation.8 | convolution fusion | flops 403824640 | bytes 630784 | tf_op jit(solution)/shard_map/cok,fk->cof/dot_general | solution.py:336
  (13 shorter events, 0.2 us)
Async XLA Ops:
  4.1 18.6 %collective-permute-start = (f32[4,13,2048]{2,1,0:T(8,128)S(1)}, f32[4,13,2048]{2,1,0:T(8,128)S(1)}, u32[]{:S(2)}, u32[]{:S(2)}) collective-permute-start(f32[4,13,2048]{2,1,0:T(8,128)S(1)} %pad_maximum_fusion), channel_id=1, source_target_pairs={{0,4},{4,8},{8,12},{12,16},{16,20},{20,24},{24,28},{28,32},{32,36}... | collective-permute-start | bytes 1277960 | tf_op jit(solution)/shard_map/ppermute | solution.py:258
  7.5 0.7 copy-start.9
  7.8 14.9 %collective-permute-start.1 = (f32[4,13,2048]{2,1,0:T(8,128)S(1)}, f32[4,13,2048]{2,1,0:T(8,128)S(1)}, u32[]{:S(2)}, u32[]{:S(2)}) collective-permute-start(f32[4,13,2048]{2,1,0:T(8,128)S(1)} %pad_maximum_fusion.1), channel_id=1, source_target_pairs={{4,0},{8,4},{12,8},{16,12},{20,16},{24,20},{28,24},{32,28},{36,32}... | collective-permute-start | bytes 1277960 | tf_op jit(solution)/shard_map/ppermute | solution.py:258
  8.2 1.7 %copy-start.10 = (s32[2048]{0:T(1024)S(1)}, s32[2048]{0:T(1024)}, u32[]{:S(2)}) copy-start(s32[2048]{0:T(1024)} %param.17) | copy-start | bytes 24580
  8.2 2.0 %copy-start.8 = (f32[4,2048]{1,0:T(4,128)S(1)}, f32[4,2048]{1,0:T(4,128)}, u32[]{:S(2)}) copy-start(f32[4,2048]{1,0:T(4,128)} %param.13) | copy-start | bytes 98308
  8.2 2.0 %copy-start.11 = (f32[2048]{0:T(1024)S(1)}, f32[2048]{0:T(1024)}, u32[]{:S(2)}) copy-start(f32[2048]{0:T(1024)} %param.15) | copy-start | bytes 24580
  8.2 2.0 %copy-start.12 = (f32[2048]{0:T(1024)S(1)}, f32[2048]{0:T(1024)}, u32[]{:S(2)}) copy-start(f32[2048]{0:T(1024)} %param.14) | copy-start | bytes 24580
  12.2 25.0 %copy-start.5 = (s32[4,8,2048]{2,1,0:T(8,128)S(1)}, s32[4,8,2048]{2,1,0:T(8,128)}, u32[]{:S(2)}) copy-start(s32[4,8,2048]{2,1,0:T(8,128)} %param.12) | copy-start | bytes 786436
  14.2 8.2 %collective-permute-start.2 = (f32[5,4,8,128]{3,2,1,0:T(8,128)S(1)}, f32[5,4,8,128]{3,2,1,0:T(8,128)S(1)}, u32[]{:S(2)}, u32[]{:S(2)}) collective-permute-start(f32[5,4,8,128]{3,2,1,0:T(8,128)S(1)} %pad_maximum_fusion.2), channel_id=1, source_target_pairs={{0,1},{1,2},{2,3},{3,0},{4,5},{5,6},{6,7},{7,4},{8,9},{9,10},{10,1... | collective-permute-start | bytes 245768 | tf_op jit(solution)/shard_map/ppermute | solution.py:258
  17.2 5.4 %collective-permute-start.3 = (f32[5,4,8,128]{3,2,1,0:T(8,128)S(1)}, f32[5,4,8,128]{3,2,1,0:T(8,128)S(1)}, u32[]{:S(2)}, u32[]{:S(2)}) collective-permute-start(f32[5,4,8,128]{3,2,1,0:T(8,128)S(1)} %pad_maximum_fusion.3), channel_id=1, source_target_pairs={{1,0},{2,1},{3,2},{0,3},{5,4},{6,5},{7,6},{4,7},{9,8},{10,9},{11,1... | collective-permute-start | bytes 245768 | tf_op jit(solution)/shard_map/ppermute | solution.py:258
  22.4 14.9 %copy-start.6 = (f32[5,4,8,128]{3,2,1,0:T(8,128)}, f32[5,4,8,128]{3,2,1,0:T(8,128)S(1)}, u32[]{:S(2)}) copy-start(f32[5,4,8,128]{3,2,1,0:T(8,128)S(1)} %collective-permute-done.2.yl_ref) | copy-start | bytes 245764
  22.7 14.6 %copy-start.7 = (f32[5,4,8,128]{3,2,1,0:T(8,128)}, f32[5,4,8,128]{3,2,1,0:T(8,128)S(1)}, u32[]{:S(2)}) copy-start(f32[5,4,8,128]{3,2,1,0:T(8,128)S(1)} %collective-permute-done.3.yh_ref) | copy-start | bytes 245764
  22.7 14.6 %copy-start.3 = (f32[4,13,2048]{2,1,0:T(8,128)}, f32[4,13,2048]{2,1,0:T(8,128)S(1)}, u32[]{:S(2)}) copy-start(f32[4,13,2048]{2,1,0:T(8,128)S(1)} %collective-permute-done.xl_ref) | copy-start | bytes 1277956
  22.7 14.6 %copy-start.4 = (f32[4,13,2048]{2,1,0:T(8,128)}, f32[4,13,2048]{2,1,0:T(8,128)S(1)}, u32[]{:S(2)}) copy-start(f32[4,13,2048]{2,1,0:T(8,128)S(1)} %collective-permute-done.1.xh_ref) | copy-start | bytes 1277956
  23.6 22.1 %all-to-all-start = ((f32[64,1,512]{2,1,0:T(1,128)}), f32[64,1,512]{2,1,0:T(1,128)S(1)}, u32[]{:S(2)}, u32[]{:S(2)}) async-start(f32[64,1,512]{2,1,0:T(1,128)} %copy.26), calls=%async_computation | async-start | bytes 262144 | tf_op jit(solution)/shard_map/all_to_all | solution.py:323
  44.2 1.8 %copy-start = (f32[4,4,8,2048]{3,2,1,0:T(8,128)S(1)}, f32[4,4,8,2048]{3,2,1,0:T(8,128)}, u32[]{:S(2)}) copy-start(f32[4,4,8,2048]{3,2,1,0:T(8,128)} %su_ref.1) | copy-start | bytes 3145732
  51.5 14.8 %copy-start.1 = (f32[4,4,8,2048]{3,2,1,0:T(8,128)S(1)}, f32[4,4,8,2048]{3,2,1,0:T(8,128)}, u32[]{:S(2)}) copy-start(f32[4,4,8,2048]{3,2,1,0:T(8,128)} %shard_map.104) | copy-start | bytes 3145732
  51.5 14.8 %copy-start.2 = (f32[4,4,8,2048]{3,2,1,0:T(8,128)S(1)}, f32[4,4,8,2048]{3,2,1,0:T(8,128)}, u32[]{:S(2)}) copy-start(f32[4,4,8,2048]{3,2,1,0:T(8,128)} %param.10) | copy-start | bytes 3145732
  52.6 16.3 %all-to-all-start.1 = ((f32[64,1,256]{2,1,0:T(1,128)}), f32[64,1,256]{2,1,0:T(1,128)S(1)}, u32[]{:S(2)}, u32[]{:S(2)}) async-start(f32[64,1,256]{2,1,0:T(1,128)} %copy.29), calls=%async_computation.1 | async-start | bytes 131072 | tf_op jit(solution)/shard_map/all_to_all | solution.py:331

commit v8 on v7

--- a/solution.py
+++ b/solution.py
@@ -313,10 +313,21 @@
     outgoing = jnp.transpose(outgoing, (1, 0, 2)).reshape(owners_gx, -1)
     outgoing, y_state, y_eddy = lax.optimization_barrier((outgoing, state, eddy))
 
-    def y_cols(lo, hi):
-        return jnp.concatenate([y_state[..., lo:hi], y_eddy[None, ..., lo:hi]], axis=0)
-
-    y_low, y_high = shift_pair(y_cols(cells_y - edge, cells_y), y_cols(0, edge), "gy")
+    def y_cols(lo, hi, one):
+        return jnp.concatenate([y_state[..., lo:hi].reshape(-1), y_eddy[..., one:one + 1].reshape(-1)])
+
+    def y_tile(flat, lanes, one):
+        fields_part = flat[: 4 * levels * cells_x * width].reshape(4, levels, cells_x, width)
+        eddy_part = flat[4 * levels * cells_x * width:].reshape(1, levels, cells_x, 1)
+        pad_f = ((0, 0), (0, 0), (0, 0), (lanes, edge - width - lanes))
+        pad_e = ((0, 0), (0, 0), (0, 0), (one, edge - 1 - one))
+        return jnp.concatenate([jnp.pad(fields_part, pad_f), jnp.pad(eddy_part, pad_e)], axis=0)
+
+    y_low, y_high = shift_pair(
+        y_cols(cells_y - width, cells_y, cells_y - 1), y_cols(0, width, 0), "gy"
+    )
+    y_low = y_tile(y_low, edge - width, edge - 1)
+    y_high = y_tile(y_high, 0, 0)
     x_low, x_high, y_low, y_high, outgoing = lax.optimization_barrier(
         (x_low, x_high, y_low, y_high, outgoing)
     )

time: 71.1 us -> 71.6 us (level)
  starting transfers between devices: 30.5 us -> 27.5 us
  local copies, waits for them, and re-layouts: 8.34 us -> 9.75 us
  waiting for transfers between devices: 6.05 us -> 7.34 us
  other arithmetic: 1.45 us -> 2.19 us
    all_to_all x1, starting transfers between devices: 13.6 us -> 10.6 us  [local(): received = lax.all_to_all(outgoing, 'gx', 0, 0, tiled=True)]
    ppermute x4, waiting for transfers between devices: 3.2 us -> 4.45 us  [shift_pair(): return (lax.ppermute(last, axis, up), lax.ppermute(leading, axis, down))]
    reshape x0 -> x8, local copies, waits for them, and re-layouts: none -> 1.19 us  [the longest x2 0.42 us: y_cols(): y_state[..., lo:hi].reshape(-1)]
    slice x1 -> x4, local copies, waits for them, and re-layouts: 0.88 us -> 1.84 us  [the longest x1 0.95 us: y_cols(): y_state[..., lo:hi].reshape(-1)]
    broadcast_in_dim x1 -> x0, local copies, waits for them, and re-layouts: 0.74 us -> none  [y_cols(): y_eddy[None, ..., lo:hi]]
    concatenate x2 -> x3, other arithmetic: 0.01 us -> 0.75 us  [the longest x1 0.73 us: y_tile(): jnp.concatenate([jnp.pad(fields_part, pad_f), jnp.pad(eddy_part, pad_e)],...]
  transfers between devices with their start and end apart: 6 -> 6, of which waited for: 4 -> 4; matrix products, arithmetic and copies ran while one was open for 11% -> 14% of each run, Pallas kernels for 18% -> 17%
where the time goes in v8:
time: 71.6 us; the launch traced here: 71.2 us
  starting transfers between devices  27.5 us (38%)
  Pallas kernels  17.8 us (25%)
  local copies, waits for them, and re-layouts  9.75 us (14%)
  waiting for transfers between devices  7.34 us (10%)
  matrix products  5.56 us (8%)
  other arithmetic  2.19 us (3%)
  between operations  0.98 us (1%)
    all_to_all x1, starting transfers between devices, local(): received = lax.all_to_all(outgoing, 'gx', 0, 0, tiled=True)  10.6 us
    ppermute x4, starting transfers between devices, shift_pair(): return (lax.ppermute(last, axis, up), lax.ppermute(leading, axis, down))  8.66 us
    all_to_all x1, starting transfers between devices, local(): returned = lax.all_to_all(wall_flux, 'gx', 0, 0, tiled=True)  8.2 us
    pallas_call x1, Pallas kernels, stencil(): pl.pallas_call(stencil_kernel, grid=(levels,), in_specs=[pl.BlockSpec((fi...  6.92 us
    pallas_call x1, Pallas kernels, owner_gather(): pl.pallas_call(gather_kernel, grid=(slots // block,), in_specs=[pl.BlockS...  5.46 us
    pallas_call x1, Pallas kernels, owner_scatter(): pl.pallas_call(scatter_kernel, grid=(slots // block,), in_specs=[pl.Block...  5.44 us
    ppermute x4, waiting for transfers between devices, shift_pair(): return (lax.ppermute(last, axis, up), lax.ppermute(leading, axis, down))  4.45 us
    transpose x3, local copies, waits for them, and re-layouts, x_rows(): jnp.transpose(state[:, :, lo:hi], (1, 0, 2, 3)).reshape(levels, -1, cells_y)  2.28 us
  transfers between devices with their start and end apart: 6, of which 4 were waited for; matrix products, arithmetic and copies ran while one was open for 14% of the time, Pallas kernels for 17%

profile of v8, /device:TPU:1, one launch (start us, length us, event | category | flops | bytes accessed | tf_op | source)
XLA Modules:
  0.0 71.2 jit_solution(4602141842518621525)
XLA Ops:
  0.6 1.1 %fusion.24 = (f32[4,1,2048]{2,1,0:T(1,128)S(1)}, f32[4,1,2048]{2,1,0:T(1,128)S(1)}) fusion(f32[4,8,2048]{2,1,0:T(8,128)} %eu_ref.1), kind=kLoop, calls=%fused_computation.46 | loop fusion | bytes 131072 | tf_op jit(solution)/shard_map/slice | solution.py:282
  1.8 1.8 %slice_bitcast_fusion = (f32[4,4,3,2048]{3,2,0,1:T(4,128)S(1)}, f32[4,4,3,2048]{3,2,0,1:T(4,128)S(1)}) fusion(f32[4,4,8,2048]{3,2,1,0:T(8,128)} %su_ref.1), kind=kLoop, calls=%fused_computation.20 | loop fusion | bytes 1572864 | tf_op jit(solution)/shard_map/transpose | solution.py:281
  3.5 0.3 copy.25
  3.8 0.2 copy.26
  4.0 0.1 pad_maximum_fusion
  4.1 3.1 %collective-permute-start = (f32[4,13,2048]{2,1,0:T(8,128)S(1)}, f32[4,13,2048]{2,1,0:T(8,128)S(1)}, u32[]{:S(2)}, u32[]{:S(2)}) collective-permute-start(f32[4,13,2048]{2,1,0:T(8,128)S(1)} %pad_maximum_fusion), channel_id=1, source_target_pairs={{0,4},{4,8},{8,12},{12,16},{16,20},{20,24},{24,28},{28,32},{32,36}... | collective-permute-start | bytes 1277960 | tf_op jit(solution)/shard_map/ppermute | solution.py:258
  7.2 0.3 copy.27
  7.5 0.0 copy-start.7
  7.5 0.2 copy.28
  7.7 0.1 pad_maximum_fusion.1
  7.8 0.3 collective-permute-start.1
  8.1 0.1 copy-done.7
  8.2 1.7 %fusion.10 = f32[2048]{0:T(1024)S(1)} fusion(s32[2048]{0:T(1024)S(1)} %bitcast.49), kind=kOutput, calls=%fused_computation.10 | convolution fusion | flops 541849600 | bytes 16384 | tf_op jit(solution)/shard_map/dot_general | solution.py:297
  9.9 0.0 copy-done.8
  9.9 0.3 convolution_subtract_fusion
  10.2 0.0 copy-done.6
  10.2 0.0 copy-done.9
  10.2 0.0 copy-done.10
  10.2 1.9 %fusion.7 = f32[7,64,64]{2,1,0:T(8,128)S(1)} fusion(f32[64,2048]{1,0:T(8,128)S(1)} %fusion.16, f32[7,2048]{1,0:T(8,128)S(1)} %pad_maximum_fusion.2, f32[2048]{0:T(1024)S(1)} %fusion.10, f32[64,64]{1,0:T(8,128)S(1)} %convolution_subtract_fusion, f32[7]{0:T(128)S(1)} %compare_convert_fusion), kind=kOutput, calls=%fused_computation.9 | convolution fusion | flops 705748992 | bytes 720924 | tf_op jit(solution)/shard_map/cof,fk->cok/dot_general | solution.py:308
  12.2 0.2 copy.29
  12.4 0.0 copy-start.5
  12.4 0.1 reshape.115
  12.5 1.0 %fusion.23 = (f32[4,4,8,3]{3,2,1,0:T(8,128)S(1)}, f32[4,4,8,3]{3,2,1,0:T(8,128)S(1)}) fusion(f32[4,4,8,2048]{3,2,1,0:T(8,128)} %su_ref.1), kind=kLoop, calls=%fused_computation.45 | loop fusion | bytes 6144 | tf_op jit(solution)/shard_map/slice | solution.py:317
  13.5 0.9 %slice_reduce_fusion = (f32[4,8]{1,0:T(4,128)S(1)}, f32[4,8]{1,0:T(4,128)S(1)}) fusion(f32[4,8,2048]{2,1,0:T(8,128)} %eu_ref.1), kind=kLoop, calls=%fused_computation.40 | loop fusion | bytes 512 | tf_op jit(solution)/shard_map/slice | solution.py:317
  14.3 0.1 reshape.121
  14.4 0.2 reshape.120
  14.7 5.2 %collective-permute-start.3 = (f32[416]{0:T(512)S(1)}, f32[416]{0:T(512)S(1)}, u32[]{:S(2)}, u32[]{:S(2)}) collective-permute-start(f32[416]{0:T(512)S(1)} %pad_maximum_fusion.4), channel_id=1, source_target_pairs={{1,0},{2,1},{3,2},{0,3},{5,4},{6,5},{7,6},{4,7},{9,8},{10,9},{11,1... | collective-permute-start | bytes 5000 | tf_op jit(solution)/shard_map/ppermute | solution.py:258
  19.9 0.1 reshape.117
  20.0 0.2 reshape.116
  20.2 0.1 collective-permute-start.2
  20.3 0.3 collective-permute-done.3
  20.6 0.1 reshape.133
  20.7 4.1 %collective-permute-done.2 = f32[416]{0:T(512)S(1)} collective-permute-done((f32[416]{0:T(512)S(1)}, f32[416]{0:T(512)S(1)}, u32[]{:S(2)}, u32[]{:S(2)}) %collective-permute-start.2) | collective-permute-done | bytes 1696 | tf_op jit(solution)/shard_map/ppermute | solution.py:258
  24.8 0.1 reshape.132
  24.9 0.2 reshape.122
  25.1 0.2 reshape.118
  25.3 0.7 %select_maximum_fusion = (f32[5,4,8,128]{3,2,1,0:T(8,128)}, f32[5,4,8,128]{3,2,1,0:T(8,128)}) fusion(f32[1,4,8,1]{3,2,1,0:T(8,128)S(1)} %reshape.133, f32[4,4,8,3]{3,2,1,0:T(8,128)S(1)} %reshape.122, f32[1,4,8,1]{3,2,1,0:T(8,128)S(1)} %reshape.132, f32[4,4,8,3]{3,2,1,0:T(8,128)S(1)} %reshape.118), kind=kLoop, calls=%fused_computation.34 | loop fusion | flops 163840 | bytes 167168 | tf_op jit(solution)/shard_map/concatenate | solution.py:324
  26.1 0.0 collective-permute-done.xl_ref
  26.1 0.0 collective-permute-done.1.xh_ref
  26.1 0.0 copy-start.4
  26.1 1.0 %copy.32 = f32[64,1,512]{2,1,0:T(1,128)} copy(f32[64,1,512]{2,0,1:T(8,128)S(1)} %bitcast.42) | data formatting | bytes 262144 | tf_op jit(solution)/shard_map/all_to_all | solution.py:334
  27.1 10.6 %all-to-all-start = ((f32[64,1,512]{2,1,0:T(1,128)}), f32[64,1,512]{2,1,0:T(1,128)S(1)}, u32[]{:S(2)}, u32[]{:S(2)}) async-start(f32[64,1,512]{2,1,0:T(1,128)} %copy.32), calls=%async_computation | async-start | bytes 262144 | tf_op jit(solution)/shard_map/all_to_all | solution.py:334
  37.7 0.0 copy-done.5
  37.8 0.0 copy-done.3
  37.8 0.0 copy-done.4
  37.8 6.9 %shard_map.104 = f32[4,4,8,2048]{3,2,1,0:T(8,128)} custom-call(f32[4,4,8,2048]{3,2,1,0:T(8,128)} %su_ref.1, f32[4,4,8,2048]{3,2,1,0:T(8,128)} %su_ref.1, f32[4,4,8,2048]{3,2,1,0:T(8,128)} %su_ref.1, f32[4,8,2048]{2,1,0:T(8,128)} %eu_ref.1, f32[4,8,2048]{2,1,0:T(8,128)} %eu_ref.1, f32[4,8,2048]{2,1,0:T(8,128)} %eu_ref.1, f32[4,13,2048]{2,1,0:T(8,128)} %copy-done.3, ...), custom_call_target="tpu_custom_call" | custom-call | flops 52428800 | bytes 6291456 | tf_op jit(solution)/shard_map/pallas_call | solution.py:120
  44.7 1.5 %all-to-all-done = f32[64,1,512]{2,1,0:T(1,128)S(1)} async-done(((f32[64,1,512]{2,1,0:T(1,128)}), f32[64,1,512]{2,1,0:T(1,128)S(1)}, u32[]{:S(2)}, u32[]{:S(2)}) %all-to-all-start) | async-done | bytes 131104 | tf_op jit(solution)/shard_map/all_to_all | solution.py:334
  46.2 0.1 reshape.125
  46.3 0.1 copy.33
  46.4 0.1 reshape.126.pay_ref
  46.5 0.0 copy-done
  46.5 5.5 %shard_map.105.flux_ref = f32[4,4096]{1,0:T(4,128)S(1)} custom-call(f32[128,2048]{1,0:T(8,128)S(1)} %bitcast.37, f32[8,4096]{1,0:T(8,128)S(1)} %reshape.126.pay_ref), custom_call_target="tpu_custom_call" | custom-call | flops 4294967296 | bytes 1245184 | tf_op jit(solution)/shard_map/pallas_call | solution.py:218
  52.0 0.0 copy-start.1
  52.0 0.0 copy-start.2
  52.0 0.1 reshape.127
  52.1 0.1 copy.45
  52.2 0.1 reshape.128
  52.4 0.7 copy.35
  53.1 8.2 %all-to-all-start.1 = ((f32[64,1,256]{2,1,0:T(1,128)}), f32[64,1,256]{2,1,0:T(1,128)S(1)}, u32[]{:S(2)}, u32[]{:S(2)}) async-start(f32[64,1,256]{2,1,0:T(1,128)} %copy.35), calls=%async_computation.1 | async-start | bytes 131072 | tf_op jit(solution)/shard_map/all_to_all | solution.py:342
  61.3 5.4 %shard_map.106 = f32[128,2048]{1,0:T(8,128)S(1)} custom-call(f32[8,4096]{1,0:T(8,128)S(1)} %reshape.126.pay_ref, f32[4,4096]{1,0:T(4,128)S(1)} %shard_map.105.flux_ref), custom_call_target="tpu_custom_call" | custom-call | flops 262144 | bytes 1048576 | tf_op jit(solution)/shard_map/pallas_call | solution.py:238
  66.8 1.2 %multiply_add_fusion = f32[4,4,8,2048]{3,2,1,0:T(8,128)} fusion(f32[4,4,8,2048]{3,2,1,0:T(8,128)S(1)} %copy-done.2, f32[4,4,8,2048]{3,2,1,0:T(8,128)S(1)} %copy-done.1, f32[4,4,8,2048]{3,2,1,0:T(8,128)S(1)} %bitcast.38, f32[4,8,2048]{2,1,0:T(8,128)S(1)} %convert_subtract_fusion), kind=kLoop, calls=%fused_computation.12 | loop fusion | flops 1048576 | bytes 4456448 | tf_op jit(solution)/shard_map/add | solution.py:344
  68.0 1.4 %all-to-all-done.1 = f32[64,1,256]{2,1,0:T(1,128)S(1)} async-done(((f32[64,1,256]{2,1,0:T(1,128)}), f32[64,1,256]{2,1,0:T(1,128)S(1)}, u32[]{:S(2)}, u32[]{:S(2)}) %all-to-all-start.1) | async-done | bytes 65568 | tf_op jit(solution)/shard_map/all_to_all | solution.py:342
  69.4 0.1 reshape.130
  69.5 1.7 %fusion.6 = f32[4,2048]{1,0:T(4,128)} fusion(f32[64,2048]{1,0:T(8,128)S(1)} %fusion.16, f32[2048]{0:T(1024)S(1)} %fusion.10, f32[4,64,64]{2,0,1:T(4,128)S(1)} %bitcast.47), kind=kOutput, calls=%fused_computation.8 | convolution fusion | flops 403824640 | bytes 630784 | tf_op jit(solution)/shard_map/cok,fk->cof/dot_general | solution.py:347
  (20 shorter events, 0.2 us)
Async XLA Ops:
  4.1 22.0 %collective-permute-start = (f32[4,13,2048]{2,1,0:T(8,128)S(1)}, f32[4,13,2048]{2,1,0:T(8,128)S(1)}, u32[]{:S(2)}, u32[]{:S(2)}) collective-permute-start(f32[4,13,2048]{2,1,0:T(8,128)S(1)} %pad_maximum_fusion), channel_id=1, source_target_pairs={{0,4},{4,8},{8,12},{12,16},{16,20},{20,24},{24,28},{28,32},{32,36}... | collective-permute-start | bytes 1277960 | tf_op jit(solution)/shard_map/ppermute | solution.py:258
  7.5 0.7 copy-start.7
  7.8 18.3 %collective-permute-start.1 = (f32[4,13,2048]{2,1,0:T(8,128)S(1)}, f32[4,13,2048]{2,1,0:T(8,128)S(1)}, u32[]{:S(2)}, u32[]{:S(2)}) collective-permute-start(f32[4,13,2048]{2,1,0:T(8,128)S(1)} %pad_maximum_fusion.1), channel_id=1, source_target_pairs={{4,0},{8,4},{12,8},{16,12},{20,16},{24,20},{28,24},{32,28},{36,32}... | collective-permute-start | bytes 1277960 | tf_op jit(solution)/shard_map/ppermute | solution.py:258
  8.2 1.7 %copy-start.8 = (s32[2048]{0:T(1024)S(1)}, s32[2048]{0:T(1024)}, u32[]{:S(2)}) copy-start(s32[2048]{0:T(1024)} %param.17) | copy-start | bytes 24580
  8.2 2.0 %copy-start.6 = (f32[4,2048]{1,0:T(4,128)S(1)}, f32[4,2048]{1,0:T(4,128)}, u32[]{:S(2)}) copy-start(f32[4,2048]{1,0:T(4,128)} %param.13) | copy-start | bytes 98308
  8.2 2.0 %copy-start.9 = (f32[2048]{0:T(1024)S(1)}, f32[2048]{0:T(1024)}, u32[]{:S(2)}) copy-start(f32[2048]{0:T(1024)} %param.15) | copy-start | bytes 24580
  8.2 2.0 %copy-start.10 = (f32[2048]{0:T(1024)S(1)}, f32[2048]{0:T(1024)}, u32[]{:S(2)}) copy-start(f32[2048]{0:T(1024)} %param.14) | copy-start | bytes 24580
  12.4 25.3 %copy-start.5 = (s32[4,8,2048]{2,1,0:T(8,128)S(1)}, s32[4,8,2048]{2,1,0:T(8,128)}, u32[]{:S(2)}) copy-start(s32[4,8,2048]{2,1,0:T(8,128)} %param.12) | copy-start | bytes 786436
  14.7 5.9 %collective-permute-start.3 = (f32[416]{0:T(512)S(1)}, f32[416]{0:T(512)S(1)}, u32[]{:S(2)}, u32[]{:S(2)}) collective-permute-start(f32[416]{0:T(512)S(1)} %pad_maximum_fusion.4), channel_id=1, source_target_pairs={{1,0},{2,1},{3,2},{0,3},{5,4},{6,5},{7,6},{4,7},{9,8},{10,9},{11,1... | collective-permute-start | bytes 5000 | tf_op jit(solution)/shard_map/ppermute | solution.py:258
  20.2 4.6 %collective-permute-start.2 = (f32[416]{0:T(512)S(1)}, f32[416]{0:T(512)S(1)}, u32[]{:S(2)}, u32[]{:S(2)}) collective-permute-start(f32[416]{0:T(512)S(1)} %pad_maximum_fusion.3), channel_id=1, source_target_pairs={{0,1},{1,2},{2,3},{3,0},{4,5},{5,6},{6,7},{7,4},{8,9},{9,10},{10,1... | collective-permute-start | bytes 5000 | tf_op jit(solution)/shard_map/ppermute | solution.py:258
  26.1 11.7 %copy-start.3 = (f32[4,13,2048]{2,1,0:T(8,128)}, f32[4,13,2048]{2,1,0:T(8,128)S(1)}, u32[]{:S(2)}) copy-start(f32[4,13,2048]{2,1,0:T(8,128)S(1)} %collective-permute-done.xl_ref) | copy-start | bytes 1277956
  26.1 11.7 %copy-start.4 = (f32[4,13,2048]{2,1,0:T(8,128)}, f32[4,13,2048]{2,1,0:T(8,128)S(1)}, u32[]{:S(2)}) copy-start(f32[4,13,2048]{2,1,0:T(8,128)S(1)} %collective-permute-done.1.xh_ref) | copy-start | bytes 1277956
  27.1 19.1 %all-to-all-start = ((f32[64,1,512]{2,1,0:T(1,128)}), f32[64,1,512]{2,1,0:T(1,128)S(1)}, u32[]{:S(2)}, u32[]{:S(2)}) async-start(f32[64,1,512]{2,1,0:T(1,128)} %copy.32), calls=%async_computation | async-start | bytes 262144 | tf_op jit(solution)/shard_map/all_to_all | solution.py:334
  44.7 1.8 %copy-start = (f32[4,4,8,2048]{3,2,1,0:T(8,128)S(1)}, f32[4,4,8,2048]{3,2,1,0:T(8,128)}, u32[]{:S(2)}) copy-start(f32[4,4,8,2048]{3,2,1,0:T(8,128)} %su_ref.1) | copy-start | bytes 3145732
  52.0 14.7 %copy-start.1 = (f32[4,4,8,2048]{3,2,1,0:T(8,128)S(1)}, f32[4,4,8,2048]{3,2,1,0:T(8,128)}, u32[]{:S(2)}) copy-start(f32[4,4,8,2048]{3,2,1,0:T(8,128)} %shard_map.104) | copy-start | bytes 3145732
  52.0 14.7 %copy-start.2 = (f32[4,4,8,2048]{3,2,1,0:T(8,128)S(1)}, f32[4,4,8,2048]{3,2,1,0:T(8,128)}, u32[]{:S(2)}) copy-start(f32[4,4,8,2048]{3,2,1,0:T(8,128)} %param.10) | copy-start | bytes 3145732
  53.1 16.3 %all-to-all-start.1 = ((f32[64,1,256]{2,1,0:T(1,128)}), f32[64,1,256]{2,1,0:T(1,128)S(1)}, u32[]{:S(2)}, u32[]{:S(2)}) async-start(f32[64,1,256]{2,1,0:T(1,128)} %copy.35), calls=%async_computation.1 | async-start | bytes 131072 | tf_op jit(solution)/shard_map/all_to_all | solution.py:342

commit v9 on v8

--- a/solution.py
+++ b/solution.py
@@ -328,9 +328,6 @@
     )
     y_low = y_tile(y_low, edge - width, edge - 1)
     y_high = y_tile(y_high, 0, 0)
-    x_low, x_high, y_low, y_high, outgoing = lax.optimization_barrier(
-        (x_low, x_high, y_low, y_high, outgoing)
-    )
     received = lax.all_to_all(outgoing, "gx", 0, 0, tiled=True)
     tend = stencil(state, eddy, x_low, x_high, y_low, y_high)
     tend, received = lax.optimization_barrier((tend, received))

time: 71.6 us -> 75.1 us (1.049)
  waiting for transfers between devices: 7.34 us -> 12 us
  starting transfers between devices: 27.5 us -> 25.7 us
  local copies, waits for them, and re-layouts: 9.75 us -> 8.81 us
  matrix products: 5.56 us -> 6.35 us
  other arithmetic: 2.19 us -> 2.98 us
    ppermute x4, waiting for transfers between devices: 4.45 us -> 10.6 us  [shift_pair(): return (lax.ppermute(last, axis, up), lax.ppermute(leading, axis, down))]
    unnamed x24 -> x26, local copies, waits for them, and re-layouts: 0.16 us -> 1.8 us
    transpose x3, local copies, waits for them, and re-layouts: 2.28 us -> 0.76 us  [x_rows(): jnp.transpose(state[:, :, lo:hi], (1, 0, 2, 3)).reshape(levels, -1, cells_y)]
    all_to_all x1, waiting for transfers between devices: 1.5 us -> 0.01 us  [local(): received = lax.all_to_all(outgoing, 'gx', 0, 0, tiled=True)]
    ppermute x4, starting transfers between devices: 8.66 us -> 7.29 us  [shift_pair(): return (lax.ppermute(last, axis, up), lax.ppermute(leading, axis, down))]
    slice x1, local copies, waits for them, and re-layouts: 0.95 us -> 0.1 us  [y_cols(): y_state[..., lo:hi].reshape(-1)]
    concatenate x2, other arithmetic: 0.14 us -> 0.93 us  [x_rows(): jnp.concatenate([rows, eddy[:, lo:hi][:, -1:] if lo else eddy[:, 0:1]], a...]
    dot_general x1, matrix products: 1.66 us -> 2.45 us  [local(): before = jnp.dot(earlier, owner_hot, preferred_element_type=jnp.float32)]
  transfers between devices with their start and end apart: 6 -> 6, of which waited for: 4 -> 3; matrix products, arithmetic and copies ran while one was open for 14% -> 10% of each run, Pallas kernels for 17% -> 7%
where the time goes in v9:
time: 75.1 us; the launch traced here: 74.6 us
  starting transfers between devices  25.7 us (34%)
  Pallas kernels  17.8 us (24%)
  waiting for transfers between devices  12 us (16%)
  local copies, waits for them, and re-layouts  8.81 us (12%)
  matrix products  6.35 us (8%)
  other arithmetic  2.98 us (4%)
  between operations  1 us (1%)
    ppermute x4, waiting for transfers between devices, shift_pair(): return (lax.ppermute(last, axis, up), lax.ppermute(leading, axis, down))  10.6 us
    all_to_all x1, starting transfers between devices, local(): received = lax.all_to_all(outgoing, 'gx', 0, 0, tiled=True)  10.3 us
    all_to_all x1, starting transfers between devices, local(): returned = lax.all_to_all(wall_flux, 'gx', 0, 0, tiled=True)  8.11 us
    ppermute x4, starting transfers between devices, shift_pair(): return (lax.ppermute(last, axis, up), lax.ppermute(leading, axis, down))  7.29 us
    pallas_call x1, Pallas kernels, stencil(): pl.pallas_call(stencil_kernel, grid=(levels,), in_specs=[pl.BlockSpec((fi...  6.92 us
    pallas_call x1, Pallas kernels, owner_gather(): pl.pallas_call(gather_kernel, grid=(slots // block,), in_specs=[pl.BlockS...  5.44 us
    pallas_call x1, Pallas kernels, owner_scatter(): pl.pallas_call(scatter_kernel, grid=(slots // block,), in_specs=[pl.Block...  5.44 us
    dot_general x1, matrix products, local(): before = jnp.dot(earlier, owner_hot, preferred_element_type=jnp.float32)  2.45 us
  transfers between devices with their start and end apart: 6, of which 3 were waited for; matrix products, arithmetic and copies ran while one was open for 10% of the time, Pallas kernels for 7%

profile of v9, /device:TPU:1, one launch (start us, length us, event | category | flops | bytes accessed | tf_op | source)
XLA Modules:
  0.0 74.6 jit_solution(16026196170051331768)
XLA Ops:
  0.6 0.0 copy-start.8
  0.7 0.0 copy-start.9
  0.7 0.0 copy-start.7
  0.7 0.0 copy-start.10
  0.7 0.0 copy-start.11
  0.7 2.4 %fusion.10 = f32[2048]{0:T(1024)S(1)} fusion(s32[2048]{0:T(1024)} %bitcast.49), kind=kOutput, calls=%fused_computation.10 | convolution fusion | flops 541849600 | bytes 16384 | tf_op jit(solution)/shard_map/dot_general | solution.py:297
  3.2 0.0 copy-done.8
  3.2 0.3 convolution_subtract_fusion
  3.6 1.9 %fusion.7 = f32[7,64,64]{2,1,0:T(8,128)S(1)} fusion(f32[64,2048]{1,0:T(8,128)S(1)} %fusion.16, f32[7,2048]{1,0:T(8,128)S(1)} %pad_maximum_fusion.2, f32[2048]{0:T(1024)S(1)} %fusion.10, f32[64,64]{1,0:T(8,128)S(1)} %convolution_subtract_fusion, f32[7]{0:T(128)S(1)} %compare_convert_fusion), kind=kOutput, calls=%fused_computation.9 | convolution fusion | flops 705748992 | bytes 720924 | tf_op jit(solution)/shard_map/cof,fk->cok/dot_general | solution.py:308
  5.5 0.0 copy-start
  5.6 0.2 copy.29
  5.7 0.1 reshape.115
  5.9 0.8 %copy.32 = f32[64,1,512]{2,1,0:T(1,128)} copy(f32[64,1,512]{2,0,1:T(8,128)S(1)} %bitcast.43) | data formatting | bytes 262144 | tf_op jit(solution)/shard_map/all_to_all | solution.py:331
  6.6 10.3 %all-to-all-start = ((f32[64,1,512]{2,1,0:T(1,128)}), f32[64,1,512]{2,1,0:T(1,128)S(1)}, u32[]{:S(2)}, u32[]{:S(2)}) async-start(f32[64,1,512]{2,1,0:T(1,128)} %copy.32), calls=%async_computation | async-start | bytes 262144 | tf_op jit(solution)/shard_map/all_to_all | solution.py:331
  17.0 0.9 %slice_reduce_fusion = (f32[4,8]{1,0:T(4,128)S(1)}, f32[4,8]{1,0:T(4,128)S(1)}) fusion(f32[4,8,2048]{2,1,0:T(8,128)} %eu_ref.1), kind=kLoop, calls=%fused_computation.40 | loop fusion | bytes 512 | tf_op jit(solution)/shard_map/slice | solution.py:317
  17.9 0.1 reshape.117
  17.9 0.0 copy-done
  17.9 0.1 fusion.23
  18.0 0.2 reshape.116
  18.3 3.1 %collective-permute-start.2 = (f32[416]{0:T(512)S(1)}, f32[416]{0:T(512)S(1)}, u32[]{:S(2)}, u32[]{:S(2)}) collective-permute-start(f32[416]{0:T(512)S(1)} %pad_maximum_fusion.3), channel_id=1, source_target_pairs={{0,1},{1,2},{2,3},{3,0},{4,5},{5,6},{6,7},{7,4},{8,9},{9,10},{10,1... | collective-permute-start | bytes 5000 | tf_op jit(solution)/shard_map/ppermute | solution.py:258
  21.3 0.1 reshape.121
  21.4 0.2 reshape.120
  21.6 2.2 %collective-permute-start.3 = (f32[416]{0:T(512)S(1)}, f32[416]{0:T(512)S(1)}, u32[]{:S(2)}, u32[]{:S(2)}) collective-permute-start(f32[416]{0:T(512)S(1)} %pad_maximum_fusion.4), channel_id=1, source_target_pairs={{1,0},{2,1},{3,2},{0,3},{5,4},{6,5},{7,6},{4,7},{9,8},{10,9},{11,1... | collective-permute-start | bytes 5000 | tf_op jit(solution)/shard_map/ppermute | solution.py:258
  23.9 1.1 %fusion.24 = (f32[4,1,2048]{2,1,0:T(1,128)S(1)}, f32[4,1,2048]{2,1,0:T(1,128)S(1)}) fusion(f32[4,8,2048]{2,1,0:T(8,128)} %eu_ref.1), kind=kLoop, calls=%fused_computation.46 | loop fusion | bytes 131072 | tf_op jit(solution)/shard_map/slice | solution.py:282
  25.0 0.2 slice_bitcast_fusion
  25.2 0.3 copy.25
  25.5 0.2 copy.26
  25.7 0.1 pad_maximum_fusion
  25.8 2.0 %collective-permute-start = (f32[4,13,2048]{2,1,0:T(8,128)S(1)}, f32[4,13,2048]{2,1,0:T(8,128)S(1)}, u32[]{:S(2)}, u32[]{:S(2)}) collective-permute-start(f32[4,13,2048]{2,1,0:T(8,128)S(1)} %pad_maximum_fusion), channel_id=1, source_target_pairs={{0,4},{4,8},{8,12},{12,16},{16,20},{20,24},{24,28},{28,32},{32,36}... | collective-permute-start | bytes 1277960 | tf_op jit(solution)/shard_map/ppermute | solution.py:258
  27.8 0.3 copy.27
  28.1 0.0 copy-start.6
  28.1 0.2 copy.28
  28.3 0.9 %pad_maximum_fusion.1 = f32[4,13,2048]{2,1,0:T(8,128)} fusion(f32[4,1,2048]{2,1,0:T(1,128)S(1)} %get-tuple-element.28, f32[4,12,2048]{2,1,0:T(8,128)S(1)} %copy.28), kind=kLoop, calls=%fused_computation.14 | loop fusion | flops 106496 | bytes 851968 | tf_op jit(solution)/shard_map/concatenate | solution.py:282
  29.2 0.0 collective-permute-start.1
  29.2 0.0 collective-permute-done.3
  29.2 0.1 reshape.133
  29.3 0.0 collective-permute-done.2
  29.4 0.1 reshape.132
  29.5 0.2 reshape.122
  29.7 0.2 reshape.118
  29.9 0.7 select_maximum_fusion
  30.6 0.0 all-to-all-done
  30.6 3.3 %collective-permute-done.xl_ref = f32[4,13,2048]{2,1,0:T(8,128)S(1)} collective-permute-done((f32[4,13,2048]{2,1,0:T(8,128)S(1)}, f32[4,13,2048]{2,1,0:T(8,128)S(1)}, u32[]{:S(2)}, u32[]{:S(2)}) %collective-permute-start) | collective-permute-done | bytes 426016 | tf_op jit(solution)/shard_map/ppermute | solution.py:258
  33.9 7.2 %collective-permute-done.1.xh_ref = f32[4,13,2048]{2,1,0:T(8,128)S(1)} collective-permute-done((f32[4,13,2048]{2,1,0:T(8,128)}, f32[4,13,2048]{2,1,0:T(8,128)S(1)}, u32[]{:S(2)}, u32[]{:S(2)}) %collective-permute-start.1) | collective-permute-done | bytes 426016 | tf_op jit(solution)/shard_map/ppermute | solution.py:258
  41.2 0.0 copy-done.4
  41.2 0.8 %copy-done.5 = f32[4,13,2048]{2,1,0:T(8,128)} copy-done((f32[4,13,2048]{2,1,0:T(8,128)}, f32[4,13,2048]{2,1,0:T(8,128)S(1)}, u32[]{:S(2)}) %copy-start.5) | copy-done | bytes 426008
  42.0 6.9 %shard_map.104 = f32[4,4,8,2048]{3,2,1,0:T(8,128)} custom-call(f32[4,4,8,2048]{3,2,1,0:T(8,128)} %su_ref.1, f32[4,4,8,2048]{3,2,1,0:T(8,128)} %su_ref.1, f32[4,4,8,2048]{3,2,1,0:T(8,128)} %su_ref.1, f32[4,8,2048]{2,1,0:T(8,128)} %eu_ref.1, f32[4,8,2048]{2,1,0:T(8,128)} %eu_ref.1, f32[4,8,2048]{2,1,0:T(8,128)} %eu_ref.1, f32[4,13,2048]{2,1,0:T(8,128)} %copy-done.4, ...), custom_call_target="tpu_custom_call" | custom-call | flops 52428800 | bytes 6291456 | tf_op jit(solution)/shard_map/pallas_call | solution.py:120
  48.9 0.1 reshape.125
  49.0 0.1 copy.33
  49.1 0.1 reshape.126.pay_ref
  49.2 0.9 %copy-done.1 = f32[4,4,8,2048]{3,2,1,0:T(8,128)S(1)} copy-done((f32[4,4,8,2048]{3,2,1,0:T(8,128)S(1)}, f32[4,4,8,2048]{3,2,1,0:T(8,128)}, u32[]{:S(2)}) %copy-start.1) | copy-done | bytes 1048600
  50.1 5.4 %shard_map.105.flux_ref = f32[4,4096]{1,0:T(4,128)S(1)} custom-call(f32[128,2048]{1,0:T(8,128)S(1)} %bitcast.37, f32[8,4096]{1,0:T(8,128)S(1)} %reshape.126.pay_ref), custom_call_target="tpu_custom_call" | custom-call | flops 4294967296 | bytes 1245184 | tf_op jit(solution)/shard_map/pallas_call | solution.py:218
  55.6 0.0 copy-start.2
  55.6 0.0 copy-start.3
  55.6 0.1 reshape.127
  55.7 0.1 copy.45
  55.8 0.1 reshape.128
  55.9 0.7 copy.35
  56.6 8.1 %all-to-all-start.1 = ((f32[64,1,256]{2,1,0:T(1,128)}), f32[64,1,256]{2,1,0:T(1,128)S(1)}, u32[]{:S(2)}, u32[]{:S(2)}) async-start(f32[64,1,256]{2,1,0:T(1,128)} %copy.35), calls=%async_computation.1 | async-start | bytes 131072 | tf_op jit(solution)/shard_map/all_to_all | solution.py:339
  64.7 5.4 %shard_map.106 = f32[128,2048]{1,0:T(8,128)S(1)} custom-call(f32[8,4096]{1,0:T(8,128)S(1)} %reshape.126.pay_ref, f32[4,4096]{1,0:T(4,128)S(1)} %shard_map.105.flux_ref), custom_call_target="tpu_custom_call" | custom-call | flops 262144 | bytes 1048576 | tf_op jit(solution)/shard_map/pallas_call | solution.py:238
  70.2 1.2 %multiply_add_fusion = f32[4,4,8,2048]{3,2,1,0:T(8,128)} fusion(f32[4,4,8,2048]{3,2,1,0:T(8,128)S(1)} %copy-done.3, f32[4,4,8,2048]{3,2,1,0:T(8,128)S(1)} %copy-done.2, f32[4,4,8,2048]{3,2,1,0:T(8,128)S(1)} %bitcast.38, f32[4,8,2048]{2,1,0:T(8,128)S(1)} %convert_subtract_fusion), kind=kLoop, calls=%fused_computation.12 | loop fusion | flops 1048576 | bytes 4456448 | tf_op jit(solution)/shard_map/add | solution.py:341
  71.4 1.4 %all-to-all-done.1 = f32[64,1,256]{2,1,0:T(1,128)S(1)} async-done(((f32[64,1,256]{2,1,0:T(1,128)}), f32[64,1,256]{2,1,0:T(1,128)S(1)}, u32[]{:S(2)}, u32[]{:S(2)}) %all-to-all-start.1) | async-done | bytes 65568 | tf_op jit(solution)/shard_map/all_to_all | solution.py:339
  72.8 0.1 reshape.130
  72.9 1.7 %fusion.6 = f32[4,2048]{1,0:T(4,128)} fusion(f32[64,2048]{1,0:T(8,128)S(1)} %fusion.16, f32[2048]{0:T(1024)S(1)} %fusion.10, f32[4,64,64]{2,0,1:T(4,128)S(1)} %bitcast.47), kind=kOutput, calls=%fused_computation.8 | convolution fusion | flops 403824640 | bytes 630784 | tf_op jit(solution)/shard_map/cok,fk->cof/dot_general | solution.py:344
  (22 shorter events, 0.2 us)
Async XLA Ops:
  0.6 2.5 %copy-start.8 = (s32[2048,1]{0,1:T(1,128)S(1)}, s32[2048,1]{0,1:T(1,128)}, u32[]{:S(2)}) copy-start(s32[2048,1]{0,1:T(1,128)} %param.16) | copy-start | bytes 24580
  0.7 2.6 %copy-start.9 = (s32[2048]{0:T(1024)S(1)}, s32[2048]{0:T(1024)}, u32[]{:S(2)}) copy-start(s32[2048]{0:T(1024)} %param.17) | copy-start | bytes 24580
  0.7 2.8 %copy-start.7 = (f32[4,2048]{1,0:T(4,128)S(1)}, f32[4,2048]{1,0:T(4,128)}, u32[]{:S(2)}) copy-start(f32[4,2048]{1,0:T(4,128)} %param.13) | copy-start | bytes 98308
  0.7 2.8 %copy-start.10 = (f32[2048]{0:T(1024)S(1)}, f32[2048]{0:T(1024)}, u32[]{:S(2)}) copy-start(f32[2048]{0:T(1024)} %param.15) | copy-start | bytes 24580
  0.7 2.8 %copy-start.11 = (f32[2048]{0:T(1024)S(1)}, f32[2048]{0:T(1024)}, u32[]{:S(2)}) copy-start(f32[2048]{0:T(1024)} %param.14) | copy-start | bytes 24580
  5.5 12.4 %copy-start = (f32[4,4,8,2048]{3,2,1,0:T(8,128)S(1)}, f32[4,4,8,2048]{3,2,1,0:T(8,128)}, u32[]{:S(2)}) copy-start(f32[4,4,8,2048]{3,2,1,0:T(8,128)} %su_ref.1) | copy-start | bytes 3145732
  6.6 24.0 %all-to-all-start = ((f32[64,1,512]{2,1,0:T(1,128)}), f32[64,1,512]{2,1,0:T(1,128)S(1)}, u32[]{:S(2)}, u32[]{:S(2)}) async-start(f32[64,1,512]{2,1,0:T(1,128)} %copy.32), calls=%async_computation | async-start | bytes 262144 | tf_op jit(solution)/shard_map/all_to_all | solution.py:331
  18.3 11.1 %collective-permute-start.2 = (f32[416]{0:T(512)S(1)}, f32[416]{0:T(512)S(1)}, u32[]{:S(2)}, u32[]{:S(2)}) collective-permute-start(f32[416]{0:T(512)S(1)} %pad_maximum_fusion.3), channel_id=1, source_target_pairs={{0,1},{1,2},{2,3},{3,0},{4,5},{5,6},{6,7},{7,4},{8,9},{9,10},{10,1... | collective-permute-start | bytes 5000 | tf_op jit(solution)/shard_map/ppermute | solution.py:258
  21.6 7.6 %collective-permute-start.3 = (f32[416]{0:T(512)S(1)}, f32[416]{0:T(512)S(1)}, u32[]{:S(2)}, u32[]{:S(2)}) collective-permute-start(f32[416]{0:T(512)S(1)} %pad_maximum_fusion.4), channel_id=1, source_target_pairs={{1,0},{2,1},{3,2},{0,3},{5,4},{6,5},{7,6},{4,7},{9,8},{10,9},{11,1... | collective-permute-start | bytes 5000 | tf_op jit(solution)/shard_map/ppermute | solution.py:258
  25.8 8.1 %collective-permute-start = (f32[4,13,2048]{2,1,0:T(8,128)S(1)}, f32[4,13,2048]{2,1,0:T(8,128)S(1)}, u32[]{:S(2)}, u32[]{:S(2)}) collective-permute-start(f32[4,13,2048]{2,1,0:T(8,128)S(1)} %pad_maximum_fusion), channel_id=1, source_target_pairs={{0,4},{4,8},{8,12},{12,16},{16,20},{20,24},{24,28},{28,32},{32,36}... | collective-permute-start | bytes 1277960 | tf_op jit(solution)/shard_map/ppermute | solution.py:258
  28.1 1.1 %copy-start.6 = (s32[4,8,2048]{2,1,0:T(8,128)S(1)}, s32[4,8,2048]{2,1,0:T(8,128)}, u32[]{:S(2)}) copy-start(s32[4,8,2048]{2,1,0:T(8,128)} %param.12) | copy-start | bytes 786436
  29.2 12.0 %collective-permute-start.1 = (f32[4,13,2048]{2,1,0:T(8,128)}, f32[4,13,2048]{2,1,0:T(8,128)S(1)}, u32[]{:S(2)}, u32[]{:S(2)}) collective-permute-start(f32[4,13,2048]{2,1,0:T(8,128)} %pad_maximum_fusion.1), channel_id=1, source_target_pairs={{4,0},{8,4},{12,8},{16,12},{20,16},{24,20},{28,24},{32,28},{36,32}... | collective-permute-start | bytes 1277960 | tf_op jit(solution)/shard_map/ppermute | solution.py:258
  33.9 7.2 %copy-start.4 = (f32[4,13,2048]{2,1,0:T(8,128)}, f32[4,13,2048]{2,1,0:T(8,128)S(1)}, u32[]{:S(2)}) copy-start(f32[4,13,2048]{2,1,0:T(8,128)S(1)} %collective-permute-done.xl_ref) | copy-start | bytes 1277956
  41.2 0.8 %copy-start.5 = (f32[4,13,2048]{2,1,0:T(8,128)}, f32[4,13,2048]{2,1,0:T(8,128)S(1)}, u32[]{:S(2)}) copy-start(f32[4,13,2048]{2,1,0:T(8,128)S(1)} %collective-permute-done.1.xh_ref) | copy-start | bytes 1277956
  48.9 1.2 %copy-start.1 = (f32[4,4,8,2048]{3,2,1,0:T(8,128)S(1)}, f32[4,4,8,2048]{3,2,1,0:T(8,128)}, u32[]{:S(2)}) copy-start(f32[4,4,8,2048]{3,2,1,0:T(8,128)} %su_ref.1) | copy-start | bytes 3145732
  55.6 14.6 %copy-start.2 = (f32[4,4,8,2048]{3,2,1,0:T(8,128)S(1)}, f32[4,4,8,2048]{3,2,1,0:T(8,128)}, u32[]{:S(2)}) copy-start(f32[4,4,8,2048]{3,2,1,0:T(8,128)} %shard_map.104) | copy-start | bytes 3145732
  55.6 14.6 %copy-start.3 = (f32[4,4,8,2048]{3,2,1,0:T(8,128)S(1)}, f32[4,4,8,2048]{3,2,1,0:T(8,128)}, u32[]{:S(2)}) copy-start(f32[4,4,8,2048]{3,2,1,0:T(8,128)} %param.10) | copy-start | bytes 3145732
  56.6 16.2 %all-to-all-start.1 = ((f32[64,1,256]{2,1,0:T(1,128)}), f32[64,1,256]{2,1,0:T(1,128)S(1)}, u32[]{:S(2)}, u32[]{:S(2)}) async-start(f32[64,1,256]{2,1,0:T(1,128)} %copy.35), calls=%async_computation.1 | async-start | bytes 131072 | tf_op jit(solution)/shard_map/all_to_all | solution.py:339

commit v10 on v6

--- a/solution.py
+++ b/solution.py
@@ -282,12 +282,26 @@
         return jnp.concatenate([rows, eddy[:, lo:hi][:, -1:] if lo else eddy[:, 0:1]], axis=1)
 
     x_last, x_first = x_rows(cells_x - width, cells_x), x_rows(0, width)
+    x_last, x_first, y_state, y_eddy = lax.optimization_barrier((x_last, x_first, state, eddy))
     x_low, x_high = shift_pair(x_last, x_first, "gx")
 
-    def y_cols(lo, hi):
-        return jnp.concatenate([state[..., lo:hi], eddy[None, ..., lo:hi]], axis=0)
-
-    y_low, y_high = shift_pair(y_cols(cells_y - edge, cells_y), y_cols(0, edge), "gy")
+    def y_cols(lo, hi, one):
+        return jnp.concatenate([y_state[..., lo:hi].reshape(-1), y_eddy[..., one:one + 1].reshape(-1)])
+
+    def y_tile(flat, lanes, one):
+        fields_part = flat[: 4 * levels * cells_x * width].reshape(4, levels, cells_x, width)
+        eddy_part = flat[4 * levels * cells_x * width:].reshape(1, levels, cells_x, 1)
+        pad_f = ((0, 0), (0, 0), (0, 0), (lanes, edge - width - lanes))
+        pad_e = ((0, 0), (0, 0), (0, 0), (one, edge - 1 - one))
+        return jnp.concatenate([jnp.pad(fields_part, pad_f), jnp.pad(eddy_part, pad_e)], axis=0)
+
+    y_last, y_first = y_cols(cells_y - width, cells_y, cells_y - 1), y_cols(0, width, 0)
+    y_last, y_first, facet_wall, facet_dist, facet_area, facet_owner, facet_cell = lax.optimization_barrier(
+        (y_last, y_first, facet_wall, facet_dist, facet_area, facet_owner, facet_cell)
+    )
+    y_low, y_high = shift_pair(y_last, y_first, "gy")
+    y_low = y_tile(y_low, edge - width, edge - 1)
+    y_high = y_tile(y_high, 0, 0)
 
     facet_count = facet_cell.shape[0]
     owners_gx = lax.axis_size("gx")

time: 70.8 us -> 72.2 us (1.020)
  other arithmetic: 1.45 us -> 2.82 us
  local copies, waits for them, and re-layouts: 8.41 us -> 9.53 us
  waiting for transfers between devices: 11.7 us -> 10.6 us
    concatenate x2 -> x4, other arithmetic: 0.01 us -> 1.39 us  [the longest x2 1.37 us: y_tile(): jnp.concatenate([jnp.pad(fields_part, pad_f), jnp.pad(eddy_part, pad_e)],...]
    reshape x0 -> x8, local copies, waits for them, and re-layouts: none -> 1.18 us  [the longest x2 0.41 us: y_cols(): y_state[..., lo:hi].reshape(-1)]
    ppermute x4, waiting for transfers between devices: 8.79 us -> 7.69 us  [shift_pair(): return (lax.ppermute(last, axis, up), lax.ppermute(leading, axis, down))]
    slice x1 -> x4, local copies, waits for them, and re-layouts: 0.88 us -> 1.85 us  [the longest x1 0.97 us: y_cols(): y_state[..., lo:hi].reshape(-1)]
    broadcast_in_dim x1 -> x0, local copies, waits for them, and re-layouts: 0.74 us -> none  [y_cols(): return jnp.concatenate([state[..., lo:hi], eddy[None, ..., lo:hi]], axis=0)]
  transfers between devices with their start and end apart: 6 -> 6, of which waited for: 4 -> 3; matrix products, arithmetic and copies ran while one was open for 13% -> 10% of each run, Pallas kernels for 18% -> 17%
where the time goes in v10:
time: 72.2 us; the launch traced here: 71.7 us
  starting transfers between devices  24.4 us (34%)
  Pallas kernels  17.8 us (25%)
  waiting for transfers between devices  10.6 us (15%)
  local copies, waits for them, and re-layouts  9.53 us (13%)
  matrix products  5.56 us (8%)
  other arithmetic  2.82 us (4%)
  between operations  1.02 us (1%)
    ppermute x4, starting transfers between devices, shift_pair(): return (lax.ppermute(last, axis, up), lax.ppermute(leading, axis, down))  8.59 us
    all_to_all x1, starting transfers between devices, local(): returned = lax.all_to_all(wall_flux, 'gx', 0, 0, tiled=True)  8.22 us
    ppermute x4, waiting for transfers between devices, shift_pair(): return (lax.ppermute(last, axis, up), lax.ppermute(leading, axis, down))  7.69 us
    all_to_all x1, starting transfers between devices, local(): received = lax.all_to_all(outgoing, 'gx', 0, 0, tiled=True)  7.61 us
    pallas_call x1, Pallas kernels, stencil(): pl.pallas_call(stencil_kernel, grid=(levels,), in_specs=[pl.BlockSpec((fi...  6.92 us
    pallas_call x1, Pallas kernels, owner_gather(): pl.pallas_call(gather_kernel, grid=(slots // block,), in_specs=[pl.BlockS...  5.45 us
    pallas_call x1, Pallas kernels, owner_scatter(): pl.pallas_call(scatter_kernel, grid=(slots // block,), in_specs=[pl.Block...  5.44 us
    transpose x3, local copies, waits for them, and re-layouts, x_rows(): jnp.transpose(state[:, :, lo:hi], (1, 0, 2, 3)).reshape(levels, -1, cells_y)  2.28 us
  transfers between devices with their start and end apart: 6, of which 3 were waited for; matrix products, arithmetic and copies ran while one was open for 10% of the time, Pallas kernels for 17%

profile of v10, /device:TPU:1, one launch (start us, length us, event | category | flops | bytes accessed | tf_op | source)
XLA Modules:
  0.0 71.7 jit_solution(11542080817770070057)
XLA Ops:
  0.6 1.1 %fusion.24 = (f32[4,1,2048]{2,1,0:T(1,128)S(1)}, f32[4,1,2048]{2,1,0:T(1,128)S(1)}) fusion(f32[4,8,2048]{2,1,0:T(8,128)} %eu_ref.1), kind=kLoop, calls=%fused_computation.46 | loop fusion | bytes 131072 | tf_op jit(solution)/shard_map/slice | solution.py:282
  1.8 1.8 %slice_bitcast_fusion = (f32[4,4,3,2048]{3,2,0,1:T(4,128)S(1)}, f32[4,4,3,2048]{3,2,0,1:T(4,128)S(1)}) fusion(f32[4,4,8,2048]{3,2,1,0:T(8,128)} %su_ref.1), kind=kLoop, calls=%fused_computation.20 | loop fusion | bytes 1572864 | tf_op jit(solution)/shard_map/transpose | solution.py:281
  3.5 0.3 copy.27
  3.8 0.2 copy.28
  4.0 0.3 copy.25
  4.3 0.2 copy.26
  4.5 0.0 copy-start.7
  4.5 0.1 pad_maximum_fusion
  4.7 0.9 %slice_reduce_fusion = (f32[4,8]{1,0:T(4,128)S(1)}, f32[4,8]{1,0:T(4,128)S(1)}) fusion(f32[4,8,2048]{2,1,0:T(8,128)} %eu_ref.1), kind=kLoop, calls=%fused_computation.40 | loop fusion | bytes 512 | tf_op jit(solution)/shard_map/slice | solution.py:289
  5.6 0.1 reshape.118
  5.6 0.1 reshape.116
  5.7 1.0 %fusion.23 = (f32[4,4,8,3]{3,2,1,0:T(8,128)S(1)}, f32[4,4,8,3]{3,2,1,0:T(8,128)S(1)}) fusion(f32[4,4,8,2048]{3,2,1,0:T(8,128)} %su_ref.1), kind=kLoop, calls=%fused_computation.45 | loop fusion | bytes 6144 | tf_op jit(solution)/shard_map/slice | solution.py:289
  6.7 0.2 reshape.117
  6.9 0.2 reshape.115
  7.1 3.9 %collective-permute-start.2 = (f32[416]{0:T(512)S(1)}, f32[416]{0:T(512)S(1)}, u32[]{:S(2)}, u32[]{:S(2)}) collective-permute-start(f32[416]{0:T(512)S(1)} %pad_maximum_fusion.3), channel_id=1, source_target_pairs={{0,1},{1,2},{2,3},{3,0},{4,5},{5,6},{6,7},{7,4},{8,9},{9,10},{10,1... | collective-permute-start | bytes 5000 | tf_op jit(solution)/shard_map/ppermute | solution.py:258
  11.0 3.1 %collective-permute-start.3 = (f32[416]{0:T(512)S(1)}, f32[416]{0:T(512)S(1)}, u32[]{:S(2)}, u32[]{:S(2)}) collective-permute-start(f32[416]{0:T(512)S(1)} %pad_maximum_fusion.4), channel_id=1, source_target_pairs={{1,0},{2,1},{3,2},{0,3},{5,4},{6,5},{7,6},{4,7},{9,8},{10,9},{11,1... | collective-permute-start | bytes 5000 | tf_op jit(solution)/shard_map/ppermute | solution.py:258
  14.2 1.6 %collective-permute-start = (f32[4,13,2048]{2,1,0:T(8,128)S(1)}, f32[4,13,2048]{2,1,0:T(8,128)S(1)}, u32[]{:S(2)}, u32[]{:S(2)}) collective-permute-start(f32[4,13,2048]{2,1,0:T(8,128)S(1)} %get-tuple-element.25), channel_id=1, source_target_pairs={{0,4},{4,8},{8,12},{12,16},{16,20},{20,24},{24,28},{28,32},{32,36}... | collective-permute-start | bytes 1277960 | tf_op jit(solution)/shard_map/ppermute | solution.py:258
  15.7 0.0 collective-permute-start.1
  15.7 0.0 copy-done.7
  15.7 0.0 copy-start.8
  15.8 0.0 copy-start.6
  15.8 0.0 copy-start.9
  15.8 0.0 copy-start.10
  15.8 1.7 %fusion.10 = f32[2048]{0:T(1024)S(1)} fusion(s32[2048]{0:T(1024)S(1)} %bitcast.49), kind=kOutput, calls=%fused_computation.10 | convolution fusion | flops 541849600 | bytes 16384 | tf_op jit(solution)/shard_map/dot_general | solution.py:316
  17.5 0.0 copy-done.8
  17.5 0.3 convolution_subtract_fusion
  17.8 0.0 copy-done.6
  17.9 1.9 %fusion.7 = f32[7,64,64]{2,1,0:T(8,128)S(1)} fusion(f32[64,2048]{1,0:T(8,128)S(1)} %fusion.16, f32[7,2048]{1,0:T(8,128)S(1)} %pad_maximum_fusion.2, f32[2048]{0:T(1024)S(1)} %fusion.10, f32[64,64]{1,0:T(8,128)S(1)} %convolution_subtract_fusion, f32[7]{0:T(128)S(1)} %compare_convert_fusion), kind=kOutput, calls=%fused_computation.9 | convolution fusion | flops 705748992 | bytes 720924 | tf_op jit(solution)/shard_map/cof,fk->cok/dot_general | solution.py:327
  19.9 0.0 copy-start.5
  19.9 0.2 copy.31
  20.0 0.1 reshape.123
  20.1 0.0 collective-permute-done.3
  20.2 0.1 reshape.133
  20.3 0.0 collective-permute-done.2
  20.3 0.1 reshape.132
  20.4 0.2 reshape.121
  20.6 0.2 reshape.119
  20.8 0.6 select_maximum_fusion.yh_ref
  21.5 0.7 %select_maximum_fusion.1.yl_ref = f32[5,4,8,128]{3,2,1,0:T(8,128)} fusion(f32[1,4,8,1]{3,2,1,0:T(8,128)S(1)} %reshape.132, f32[4,4,8,3]{3,2,1,0:T(8,128)S(1)} %reshape.119), kind=kLoop, calls=%fused_computation.35 | loop fusion | flops 102400 | bytes 83584 | tf_op jit(solution)/shard_map/concatenate | solution.py:296
  22.2 0.0 collective-permute-done.xl_ref
  22.2 7.7 %collective-permute-done.1.xh_ref = f32[4,13,2048]{2,1,0:T(8,128)S(1)} collective-permute-done((f32[4,13,2048]{2,1,0:T(8,128)S(1)}, f32[4,13,2048]{2,1,0:T(8,128)S(1)}, u32[]{:S(2)}, u32[]{:S(2)}) %collective-permute-start.1) | collective-permute-done | bytes 426016 | tf_op jit(solution)/shard_map/ppermute | solution.py:258
  29.9 0.8 %copy.32 = f32[64,1,512]{2,1,0:T(1,128)} copy(f32[64,1,512]{2,0,1:T(8,128)S(1)} %bitcast.42) | data formatting | bytes 262144 | tf_op jit(solution)/shard_map/all_to_all | solution.py:336
  30.7 7.6 %all-to-all-start = ((f32[64,1,512]{2,1,0:T(1,128)}), f32[64,1,512]{2,1,0:T(1,128)S(1)}, u32[]{:S(2)}, u32[]{:S(2)}) async-start(f32[64,1,512]{2,1,0:T(1,128)} %copy.32), calls=%async_computation | async-start | bytes 262144 | tf_op jit(solution)/shard_map/all_to_all | solution.py:336
  38.4 0.0 copy-done.3
  38.4 0.0 copy-done.4
  38.4 6.9 %shard_map.104 = f32[4,4,8,2048]{3,2,1,0:T(8,128)} custom-call(f32[4,4,8,2048]{3,2,1,0:T(8,128)} %su_ref.1, f32[4,4,8,2048]{3,2,1,0:T(8,128)} %su_ref.1, f32[4,4,8,2048]{3,2,1,0:T(8,128)} %su_ref.1, f32[4,8,2048]{2,1,0:T(8,128)} %eu_ref.1, f32[4,8,2048]{2,1,0:T(8,128)} %eu_ref.1, f32[4,8,2048]{2,1,0:T(8,128)} %eu_ref.1, f32[4,13,2048]{2,1,0:T(8,128)} %copy-done.3, ...), custom_call_target="tpu_custom_call" | custom-call | flops 52428800 | bytes 6291456 | tf_op jit(solution)/shard_map/pallas_call | solution.py:120
  45.3 1.5 %all-to-all-done = f32[64,1,512]{2,1,0:T(1,128)S(1)} async-done(((f32[64,1,512]{2,1,0:T(1,128)}), f32[64,1,512]{2,1,0:T(1,128)S(1)}, u32[]{:S(2)}, u32[]{:S(2)}) %all-to-all-start) | async-done | bytes 131104 | tf_op jit(solution)/shard_map/all_to_all | solution.py:336
  46.8 0.1 reshape.125
  46.9 0.1 copy.33
  47.0 0.1 reshape.126.pay_ref
  47.1 0.0 copy-done
  47.1 5.5 %shard_map.105.flux_ref = f32[4,4096]{1,0:T(4,128)S(1)} custom-call(f32[128,2048]{1,0:T(8,128)S(1)} %bitcast.37, f32[8,4096]{1,0:T(8,128)S(1)} %reshape.126.pay_ref), custom_call_target="tpu_custom_call" | custom-call | flops 4294967296 | bytes 1245184 | tf_op jit(solution)/shard_map/pallas_call | solution.py:218
  52.6 0.0 copy-start.1
  52.6 0.0 copy-start.2
  52.6 0.1 reshape.127
  52.7 0.1 copy.45
  52.8 0.1 reshape.128
  52.9 0.7 copy.35
  53.6 8.2 %all-to-all-start.1 = ((f32[64,1,256]{2,1,0:T(1,128)}), f32[64,1,256]{2,1,0:T(1,128)S(1)}, u32[]{:S(2)}, u32[]{:S(2)}) async-start(f32[64,1,256]{2,1,0:T(1,128)} %copy.35), calls=%async_computation.1 | async-start | bytes 131072 | tf_op jit(solution)/shard_map/all_to_all | solution.py:344
  61.9 5.4 %shard_map.106 = f32[128,2048]{1,0:T(8,128)S(1)} custom-call(f32[8,4096]{1,0:T(8,128)S(1)} %reshape.126.pay_ref, f32[4,4096]{1,0:T(4,128)S(1)} %shard_map.105.flux_ref), custom_call_target="tpu_custom_call" | custom-call | flops 262144 | bytes 1048576 | tf_op jit(solution)/shard_map/pallas_call | solution.py:238
  67.3 1.2 %multiply_add_fusion = f32[4,4,8,2048]{3,2,1,0:T(8,128)} fusion(f32[4,4,8,2048]{3,2,1,0:T(8,128)S(1)} %copy-done.2, f32[4,4,8,2048]{3,2,1,0:T(8,128)S(1)} %copy-done.1, f32[4,4,8,2048]{3,2,1,0:T(8,128)S(1)} %bitcast.38, f32[4,8,2048]{2,1,0:T(8,128)S(1)} %convert_subtract_fusion), kind=kLoop, calls=%fused_computation.12 | loop fusion | flops 1048576 | bytes 4456448 | tf_op jit(solution)/shard_map/add | solution.py:346
  68.5 1.4 %all-to-all-done.1 = f32[64,1,256]{2,1,0:T(1,128)S(1)} async-done(((f32[64,1,256]{2,1,0:T(1,128)}), f32[64,1,256]{2,1,0:T(1,128)S(1)}, u32[]{:S(2)}, u32[]{:S(2)}) %all-to-all-start.1) | async-done | bytes 65568 | tf_op jit(solution)/shard_map/all_to_all | solution.py:344
  69.9 0.1 reshape.130
  70.1 1.7 %fusion.6 = f32[4,2048]{1,0:T(4,128)} fusion(f32[64,2048]{1,0:T(8,128)S(1)} %fusion.16, f32[2048]{0:T(1024)S(1)} %fusion.10, f32[4,64,64]{2,0,1:T(4,128)S(1)} %bitcast.47), kind=kOutput, calls=%fused_computation.8 | convolution fusion | flops 403824640 | bytes 630784 | tf_op jit(solution)/shard_map/cok,fk->cof/dot_general | solution.py:349
  (20 shorter events, 0.2 us)
Async XLA Ops:
  4.5 11.2 %copy-start.7 = (s32[2048,1]{0,1:T(1,128)S(1)}, s32[2048,1]{0,1:T(1,128)}, u32[]{:S(2)}) copy-start(s32[2048,1]{0,1:T(1,128)} %param.16) | copy-start | bytes 24580
  7.1 13.1 %collective-permute-start.2 = (f32[416]{0:T(512)S(1)}, f32[416]{0:T(512)S(1)}, u32[]{:S(2)}, u32[]{:S(2)}) collective-permute-start(f32[416]{0:T(512)S(1)} %pad_maximum_fusion.3), channel_id=1, source_target_pairs={{0,1},{1,2},{2,3},{3,0},{4,5},{5,6},{6,7},{7,4},{8,9},{9,10},{10,1... | collective-permute-start | bytes 5000 | tf_op jit(solution)/shard_map/ppermute | solution.py:258
  11.0 9.1 %collective-permute-start.3 = (f32[416]{0:T(512)S(1)}, f32[416]{0:T(512)S(1)}, u32[]{:S(2)}, u32[]{:S(2)}) collective-permute-start(f32[416]{0:T(512)S(1)} %pad_maximum_fusion.4), channel_id=1, source_target_pairs={{1,0},{2,1},{3,2},{0,3},{5,4},{6,5},{7,6},{4,7},{9,8},{10,9},{11,1... | collective-permute-start | bytes 5000 | tf_op jit(solution)/shard_map/ppermute | solution.py:258
  14.2 8.0 %collective-permute-start = (f32[4,13,2048]{2,1,0:T(8,128)S(1)}, f32[4,13,2048]{2,1,0:T(8,128)S(1)}, u32[]{:S(2)}, u32[]{:S(2)}) collective-permute-start(f32[4,13,2048]{2,1,0:T(8,128)S(1)} %get-tuple-element.25), channel_id=1, source_target_pairs={{0,4},{4,8},{8,12},{12,16},{16,20},{20,24},{24,28},{28,32},{32,36}... | collective-permute-start | bytes 1277960 | tf_op jit(solution)/shard_map/ppermute | solution.py:258
  15.7 14.1 %collective-permute-start.1 = (f32[4,13,2048]{2,1,0:T(8,128)S(1)}, f32[4,13,2048]{2,1,0:T(8,128)S(1)}, u32[]{:S(2)}, u32[]{:S(2)}) collective-permute-start(f32[4,13,2048]{2,1,0:T(8,128)S(1)} %get-tuple-element.26), channel_id=1, source_target_pairs={{4,0},{8,4},{12,8},{16,12},{20,16},{24,20},{28,24},{32,28},{36,32}... | collective-permute-start | bytes 1277960 | tf_op jit(solution)/shard_map/ppermute | solution.py:258
  15.7 1.8 %copy-start.8 = (s32[2048]{0:T(1024)S(1)}, s32[2048]{0:T(1024)}, u32[]{:S(2)}) copy-start(s32[2048]{0:T(1024)} %param.17) | copy-start | bytes 24580
  15.8 2.1 %copy-start.6 = (f32[4,2048]{1,0:T(4,128)S(1)}, f32[4,2048]{1,0:T(4,128)}, u32[]{:S(2)}) copy-start(f32[4,2048]{1,0:T(4,128)} %param.13) | copy-start | bytes 98308
  15.8 2.1 %copy-start.9 = (f32[2048]{0:T(1024)S(1)}, f32[2048]{0:T(1024)}, u32[]{:S(2)}) copy-start(f32[2048]{0:T(1024)} %param.15) | copy-start | bytes 24580
  15.8 2.0 %copy-start.10 = (f32[2048]{0:T(1024)S(1)}, f32[2048]{0:T(1024)}, u32[]{:S(2)}) copy-start(f32[2048]{0:T(1024)} %param.14) | copy-start | bytes 24580
  19.9 18.5 %copy-start.5 = (s32[4,8,2048]{2,1,0:T(8,128)S(1)}, s32[4,8,2048]{2,1,0:T(8,128)}, u32[]{:S(2)}) copy-start(s32[4,8,2048]{2,1,0:T(8,128)} %param.12) | copy-start | bytes 786436
  22.2 16.2 %copy-start.3 = (f32[4,13,2048]{2,1,0:T(8,128)}, f32[4,13,2048]{2,1,0:T(8,128)S(1)}, u32[]{:S(2)}) copy-start(f32[4,13,2048]{2,1,0:T(8,128)S(1)} %collective-permute-done.xl_ref) | copy-start | bytes 1277956
  29.9 8.5 %copy-start.4 = (f32[4,13,2048]{2,1,0:T(8,128)}, f32[4,13,2048]{2,1,0:T(8,128)S(1)}, u32[]{:S(2)}) copy-start(f32[4,13,2048]{2,1,0:T(8,128)S(1)} %collective-permute-done.1.xh_ref) | copy-start | bytes 1277956
  30.7 16.1 %all-to-all-start = ((f32[64,1,512]{2,1,0:T(1,128)}), f32[64,1,512]{2,1,0:T(1,128)S(1)}, u32[]{:S(2)}, u32[]{:S(2)}) async-start(f32[64,1,512]{2,1,0:T(1,128)} %copy.32), calls=%async_computation | async-start | bytes 262144 | tf_op jit(solution)/shard_map/all_to_all | solution.py:336
  45.3 1.8 %copy-start = (f32[4,4,8,2048]{3,2,1,0:T(8,128)S(1)}, f32[4,4,8,2048]{3,2,1,0:T(8,128)}, u32[]{:S(2)}) copy-start(f32[4,4,8,2048]{3,2,1,0:T(8,128)} %su_ref.1) | copy-start | bytes 3145732
  52.6 14.8 %copy-start.1 = (f32[4,4,8,2048]{3,2,1,0:T(8,128)S(1)}, f32[4,4,8,2048]{3,2,1,0:T(8,128)}, u32[]{:S(2)}) copy-start(f32[4,4,8,2048]{3,2,1,0:T(8,128)} %shard_map.104) | copy-start | bytes 3145732
  52.6 14.8 %copy-start.2 = (f32[4,4,8,2048]{3,2,1,0:T(8,128)S(1)}, f32[4,4,8,2048]{3,2,1,0:T(8,128)}, u32[]{:S(2)}) copy-start(f32[4,4,8,2048]{3,2,1,0:T(8,128)} %param.10) | copy-start | bytes 3145732
  53.6 16.3 %all-to-all-start.1 = ((f32[64,1,256]{2,1,0:T(1,128)}), f32[64,1,256]{2,1,0:T(1,128)S(1)}, u32[]{:S(2)}, u32[]{:S(2)}) async-start(f32[64,1,256]{2,1,0:T(1,128)} %copy.35), calls=%async_computation.1 | async-start | bytes 131072 | tf_op jit(solution)/shard_map/all_to_all | solution.py:344

commit v11 on v8

--- a/solution.py
+++ b/solution.py
@@ -251,6 +251,21 @@
     )(pay, flux)
 
 
+def swap_edges(last, leading, axis):
+    peers = lax.axis_size(axis)
+    me = lax.axis_index(axis)
+    target = lax.broadcasted_iota(jnp.int32, (peers, 1), 0)
+    blocks = jnp.where(
+        target == (me + 1) % peers,
+        last[None],
+        jnp.where(target == (me + peers - 1) % peers, leading[None], jnp.zeros_like(last)[None]),
+    )
+    got = lax.all_to_all(blocks, axis, 0, 0, tiled=True)
+    below = lax.dynamic_index_in_dim(got, (me + peers - 1) % peers, 0, keepdims=False)
+    above = lax.dynamic_index_in_dim(got, (me + 1) % peers, 0, keepdims=False)
+    return below, above
+
+
 def shift_pair(last, leading, axis):
     peers = lax.axis_size(axis)
     up = [(i, (i + 1) % peers) for i in range(peers)]
@@ -311,7 +326,7 @@
     outgoing = outgoing + unit_dist * (1.0 - filled)[None]
     outgoing = jnp.concatenate([outgoing, jnp.zeros((1, owners_gx, capacity), jnp.float32)], axis=0)
     outgoing = jnp.transpose(outgoing, (1, 0, 2)).reshape(owners_gx, -1)
-    outgoing, y_state, y_eddy = lax.optimization_barrier((outgoing, state, eddy))
+    y_state, y_eddy = state, eddy
 
     def y_cols(lo, hi, one):
         return jnp.concatenate([y_state[..., lo:hi].reshape(-1), y_eddy[..., one:one + 1].reshape(-1)])
@@ -323,7 +338,7 @@
         pad_e = ((0, 0), (0, 0), (0, 0), (one, edge - 1 - one))
         return jnp.concatenate([jnp.pad(fields_part, pad_f), jnp.pad(eddy_part, pad_e)], axis=0)
 
-    y_low, y_high = shift_pair(
+    y_low, y_high = swap_edges(
         y_cols(cells_y - width, cells_y, cells_y - 1), y_cols(0, width, 0), "gy"
     )
     y_low = y_tile(y_low, edge - width, edge - 1)

time: 71.6 us -> 74.5 us (1.041)
  other arithmetic: 2.19 us -> 4.3 us
  waiting for transfers between devices: 7.34 us -> 9.09 us
  starting transfers between devices: 27.5 us -> 26.6 us
    all_to_all x0 -> x1, starting transfers between devices: none -> 9 us  [swap_edges(): got = lax.all_to_all(blocks, axis, 0, 0, tiled=True)]
    ppermute x4 -> x2, starting transfers between devices: 8.66 us -> 1.66 us  [shift_pair(): return (lax.ppermute(last, axis, up), lax.ppermute(leading, axis, down))]
    all_to_all x1, starting transfers between devices: 10.6 us -> 7.51 us  [local(): received = lax.all_to_all(outgoing, 'gx', 0, 0, tiled=True)]
    ppermute x4 -> x2, waiting for transfers between devices: 4.45 us -> 6.23 us  [shift_pair(): return (lax.ppermute(last, axis, up), lax.ppermute(leading, axis, down))]
    concatenate x2, other arithmetic: 0.14 us -> 0.93 us  [x_rows(): jnp.concatenate([rows, eddy[:, lo:hi][:, -1:] if lo else eddy[:, 0:1]], a...]
  transfers between devices with their start and end apart: 6 -> 5, of which waited for: 4 -> 3; matrix products, arithmetic and copies ran while one was open for 14% -> 17% of each run, Pallas kernels for 17% -> 17%
where the time goes in v11:
time: 74.5 us; the launch traced here: 74 us
  starting transfers between devices  26.6 us (36%)
  Pallas kernels  17.9 us (24%)
  local copies, waits for them, and re-layouts  9.55 us (13%)
  waiting for transfers between devices  9.09 us (12%)
  matrix products  5.57 us (7%)
  other arithmetic  4.3 us (6%)
  between operations  1.07 us (1%)
    all_to_all x1, starting transfers between devices, swap_edges(): got = lax.all_to_all(blocks, axis, 0, 0, tiled=True)  9 us
    all_to_all x1, starting transfers between devices, local(): returned = lax.all_to_all(wall_flux, 'gx', 0, 0, tiled=True)  8.42 us
    all_to_all x1, starting transfers between devices, local(): received = lax.all_to_all(outgoing, 'gx', 0, 0, tiled=True)  7.51 us
    pallas_call x1, Pallas kernels, stencil(): pl.pallas_call(stencil_kernel, grid=(levels,), in_specs=[pl.BlockSpec((fi...  6.96 us
    ppermute x2, waiting for transfers between devices, shift_pair(): return (lax.ppermute(last, axis, up), lax.ppermute(leading, axis, down))  6.23 us
    pallas_call x1, Pallas kernels, owner_gather(): pl.pallas_call(gather_kernel, grid=(slots // block,), in_specs=[pl.BlockS...  5.46 us
    pallas_call x1, Pallas kernels, owner_scatter(): pl.pallas_call(scatter_kernel, grid=(slots // block,), in_specs=[pl.Block...  5.44 us
    transpose x3, local copies, waits for them, and re-layouts, x_rows(): jnp.transpose(state[:, :, lo:hi], (1, 0, 2, 3)).reshape(levels, -1, cells_y)  2.28 us
  transfers between devices with their start and end apart: 5, of which 3 were waited for; matrix products, arithmetic and copies ran while one was open for 17% of the time, Pallas kernels for 17%

profile of v11, /device:TPU:1, one launch (start us, length us, event | category | flops | bytes accessed | tf_op | source)
XLA Modules:
  0.0 74.0 jit_solution(3906350073952298906)
XLA Ops:
  0.7 0.9 %slice_reduce_fusion.1 = (f32[4,8]{1,0:T(4,128)S(1)}, f32[4,8]{1,0:T(4,128)S(1)}) fusion(f32[4,8,2048]{2,1,0:T(8,128)} %eu_ref.1), kind=kLoop, calls=%fused_computation.41 | loop fusion | bytes 512 | tf_op jit(solution)/shard_map/slice | solution.py:332
  1.6 0.1 reshape.203
  1.7 0.1 reshape.205
  1.7 1.0 %fusion.23 = (f32[4,4,8,3]{3,2,1,0:T(8,128)S(1)}, f32[4,4,8,3]{3,2,1,0:T(8,128)S(1)}) fusion(f32[4,4,8,2048]{3,2,1,0:T(8,128)} %su_ref.1), kind=kLoop, calls=%fused_computation.55 | loop fusion | bytes 6144 | tf_op jit(solution)/shard_map/slice | solution.py:332
  2.7 0.2 reshape.202
  2.9 0.2 reshape.204
  3.2 0.7 broadcast_select_fusion
  3.8 9.0 %all-to-all-start = ((f32[4,1,416]{2,1,0:T(1,128)}), f32[4,1,416]{2,1,0:T(1,128)S(1)}, u32[]{:S(2)}, u32[]{:S(2)}) async-start(f32[4,1,416]{2,1,0:T(1,128)} %broadcast_select_fusion), calls=%async_computation | async-start | bytes 16384 | tf_op jit(solution)/shard_map/all_to_all | solution.py:263
  12.8 1.1 %fusion.24 = (f32[4,1,2048]{2,1,0:T(1,128)S(1)}, f32[4,1,2048]{2,1,0:T(1,128)S(1)}) fusion(f32[4,8,2048]{2,1,0:T(8,128)} %eu_ref.1), kind=kLoop, calls=%fused_computation.56 | loop fusion | bytes 131072 | tf_op jit(solution)/shard_map/slice | solution.py:297
  13.9 1.8 %slice_bitcast_fusion = (f32[4,4,3,2048]{3,2,0,1:T(4,128)S(1)}, f32[4,4,3,2048]{3,2,0,1:T(4,128)S(1)}) fusion(f32[4,4,8,2048]{3,2,1,0:T(8,128)} %su_ref.1), kind=kLoop, calls=%fused_computation.20 | loop fusion | bytes 1572864 | tf_op jit(solution)/shard_map/transpose | solution.py:296
  15.7 0.3 copy.25
  16.0 0.2 copy.26
  16.2 0.1 pad_maximum_fusion
  16.3 1.7 %collective-permute-start = (f32[4,13,2048]{2,1,0:T(8,128)S(1)}, f32[4,13,2048]{2,1,0:T(8,128)S(1)}, u32[]{:S(2)}, u32[]{:S(2)}) collective-permute-start(f32[4,13,2048]{2,1,0:T(8,128)S(1)} %pad_maximum_fusion), channel_id=1, source_target_pairs={{0,4},{4,8},{8,12},{12,16},{16,20},{20,24},{24,28},{28,32},{32,36}... | collective-permute-start | bytes 1277960 | tf_op jit(solution)/shard_map/ppermute | solution.py:273
  18.0 0.3 copy.27
  18.2 0.0 copy-start.7
  18.2 0.2 copy.28
  18.5 0.9 %pad_maximum_fusion.1 = f32[4,13,2048]{2,1,0:T(8,128)} fusion(f32[4,1,2048]{2,1,0:T(1,128)S(1)} %get-tuple-element.32, f32[4,12,2048]{2,1,0:T(8,128)S(1)} %copy.28), kind=kLoop, calls=%fused_computation.14 | loop fusion | flops 106496 | bytes 851968 | tf_op jit(solution)/shard_map/concatenate | solution.py:297
  19.3 0.0 collective-permute-start.1
  19.3 0.0 copy-done.7
  19.3 0.0 copy-start.8
  19.4 0.0 copy-start.6
  19.4 0.0 copy-start.9
  19.4 0.0 copy-start.10
  19.4 1.7 %fusion.10 = f32[2048]{0:T(1024)S(1)} fusion(s32[2048]{0:T(1024)S(1)} %bitcast.51), kind=kOutput, calls=%fused_computation.10 | convolution fusion | flops 541849600 | bytes 16384 | tf_op jit(solution)/shard_map/dot_general | solution.py:312
  21.1 0.0 copy-done.8
  21.1 0.3 convolution_subtract_fusion
  21.4 0.0 copy-done.6
  21.4 0.0 copy-done.9
  21.4 0.0 copy-done.10
  21.5 1.9 %fusion.7 = f32[7,64,64]{2,1,0:T(8,128)S(1)} fusion(f32[64,2048]{1,0:T(8,128)S(1)} %fusion.16, f32[7,2048]{1,0:T(8,128)S(1)} %pad_maximum_fusion.2, f32[2048]{0:T(1024)S(1)} %fusion.10, f32[64,64]{1,0:T(8,128)S(1)} %convolution_subtract_fusion, f32[7]{0:T(128)S(1)} %compare_convert_fusion), kind=kOutput, calls=%fused_computation.9 | convolution fusion | flops 705748992 | bytes 720924 | tf_op jit(solution)/shard_map/cof,fk->cok/dot_general | solution.py:323
  23.5 0.0 copy-start.5
  23.5 0.2 copy.31
  23.6 0.1 reshape.210
  23.8 0.0 all-to-all-done
  23.8 0.1 reshape.220
  23.9 0.1 reshape.219
  24.0 0.2 reshape.208
  24.2 0.2 reshape.206
  24.5 0.6 select_maximum_fusion.yh_ref
  25.1 0.7 select_maximum_fusion.1.yl_ref
  25.8 0.0 collective-permute-done.xl_ref
  25.8 6.2 %collective-permute-done.1.xh_ref = f32[4,13,2048]{2,1,0:T(8,128)S(1)} collective-permute-done((f32[4,13,2048]{2,1,0:T(8,128)}, f32[4,13,2048]{2,1,0:T(8,128)S(1)}, u32[]{:S(2)}, u32[]{:S(2)}) %collective-permute-start.1) | collective-permute-done | bytes 426016 | tf_op jit(solution)/shard_map/ppermute | solution.py:273
  32.1 0.8 %copy.32 = f32[64,1,512]{2,1,0:T(1,128)} copy(f32[64,1,512]{2,0,1:T(8,128)S(1)} %bitcast.44) | data formatting | bytes 262144 | tf_op jit(solution)/shard_map/all_to_all | solution.py:349
  32.9 7.5 %all-to-all-start.1 = ((f32[64,1,512]{2,1,0:T(1,128)}), f32[64,1,512]{2,1,0:T(1,128)S(1)}, u32[]{:S(2)}, u32[]{:S(2)}) async-start(f32[64,1,512]{2,1,0:T(1,128)} %copy.32), calls=%async_computation.1 | async-start | bytes 262144 | tf_op jit(solution)/shard_map/all_to_all | solution.py:349
  40.4 0.0 copy-done.5
  40.5 7.0 %shard_map.104 = f32[4,4,8,2048]{3,2,1,0:T(8,128)} custom-call(f32[4,4,8,2048]{3,2,1,0:T(8,128)} %su_ref.1, f32[4,4,8,2048]{3,2,1,0:T(8,128)} %su_ref.1, f32[4,4,8,2048]{3,2,1,0:T(8,128)} %su_ref.1, f32[4,8,2048]{2,1,0:T(8,128)} %eu_ref.1, f32[4,8,2048]{2,1,0:T(8,128)} %eu_ref.1, f32[4,8,2048]{2,1,0:T(8,128)} %eu_ref.1, f32[4,13,2048]{2,1,0:T(8,128)} %copy-done.3, ...), custom_call_target="tpu_custom_call" | custom-call | flops 52428800 | bytes 6291456 | tf_op jit(solution)/shard_map/pallas_call | solution.py:120
  47.4 1.5 %all-to-all-done.1 = f32[64,1,512]{2,1,0:T(1,128)S(1)} async-done(((f32[64,1,512]{2,1,0:T(1,128)}), f32[64,1,512]{2,1,0:T(1,128)S(1)}, u32[]{:S(2)}, u32[]{:S(2)}) %all-to-all-start.1) | async-done | bytes 131104 | tf_op jit(solution)/shard_map/all_to_all | solution.py:349
  48.9 0.1 reshape.212
  49.0 0.1 copy.33
  49.1 0.1 reshape.213.pay_ref
  49.2 5.5 %shard_map.105.flux_ref = f32[4,4096]{1,0:T(4,128)S(1)} custom-call(f32[128,2048]{1,0:T(8,128)S(1)} %bitcast.39, f32[8,4096]{1,0:T(8,128)S(1)} %reshape.213.pay_ref), custom_call_target="tpu_custom_call" | custom-call | flops 4294967296 | bytes 1245184 | tf_op jit(solution)/shard_map/pallas_call | solution.py:218
  54.7 0.0 copy-start.1
  54.7 0.0 copy-start.2
  54.7 0.1 reshape.214
  54.8 0.1 copy.45
  54.9 0.1 reshape.215
  55.0 0.7 copy.35
  55.7 8.4 %all-to-all-start.2 = ((f32[64,1,256]{2,1,0:T(1,128)}), f32[64,1,256]{2,1,0:T(1,128)S(1)}, u32[]{:S(2)}, u32[]{:S(2)}) async-start(f32[64,1,256]{2,1,0:T(1,128)} %copy.35), calls=%async_computation.2 | async-start | bytes 131072 | tf_op jit(solution)/shard_map/all_to_all | solution.py:357
  64.2 5.4 %shard_map.106 = f32[128,2048]{1,0:T(8,128)S(1)} custom-call(f32[8,4096]{1,0:T(8,128)S(1)} %reshape.213.pay_ref, f32[4,4096]{1,0:T(4,128)S(1)} %shard_map.105.flux_ref), custom_call_target="tpu_custom_call" | custom-call | flops 262144 | bytes 1048576 | tf_op jit(solution)/shard_map/pallas_call | solution.py:238
  69.6 1.2 %multiply_add_fusion = f32[4,4,8,2048]{3,2,1,0:T(8,128)} fusion(f32[4,4,8,2048]{3,2,1,0:T(8,128)S(1)} %copy-done.2, f32[4,4,8,2048]{3,2,1,0:T(8,128)S(1)} %copy-done.1, f32[4,4,8,2048]{3,2,1,0:T(8,128)S(1)} %bitcast.40, f32[4,8,2048]{2,1,0:T(8,128)S(1)} %convert_subtract_fusion), kind=kLoop, calls=%fused_computation.12 | loop fusion | flops 1048576 | bytes 4456448 | tf_op jit(solution)/shard_map/add | solution.py:359
  70.8 1.4 %all-to-all-done.2 = f32[64,1,256]{2,1,0:T(1,128)S(1)} async-done(((f32[64,1,256]{2,1,0:T(1,128)}), f32[64,1,256]{2,1,0:T(1,128)S(1)}, u32[]{:S(2)}, u32[]{:S(2)}) %all-to-all-start.2) | async-done | bytes 65568 | tf_op jit(solution)/shard_map/all_to_all | solution.py:357
  72.2 0.1 reshape.217
  72.4 1.7 %fusion.6 = f32[4,2048]{1,0:T(4,128)} fusion(f32[64,2048]{1,0:T(8,128)S(1)} %fusion.16, f32[2048]{0:T(1024)S(1)} %fusion.10, f32[4,64,64]{2,0,1:T(4,128)S(1)} %bitcast.49), kind=kOutput, calls=%fused_computation.8 | convolution fusion | flops 403824640 | bytes 630784 | tf_op jit(solution)/shard_map/cok,fk->cof/dot_general | solution.py:362
  (23 shorter events, 0.2 us)
Async XLA Ops:
  3.8 19.9 %all-to-all-start = ((f32[4,1,416]{2,1,0:T(1,128)}), f32[4,1,416]{2,1,0:T(1,128)S(1)}, u32[]{:S(2)}, u32[]{:S(2)}) async-start(f32[4,1,416]{2,1,0:T(1,128)} %broadcast_select_fusion), calls=%async_computation | async-start | bytes 16384 | tf_op jit(solution)/shard_map/all_to_all | solution.py:263
  16.3 9.5 %collective-permute-start = (f32[4,13,2048]{2,1,0:T(8,128)S(1)}, f32[4,13,2048]{2,1,0:T(8,128)S(1)}, u32[]{:S(2)}, u32[]{:S(2)}) collective-permute-start(f32[4,13,2048]{2,1,0:T(8,128)S(1)} %pad_maximum_fusion), channel_id=1, source_target_pairs={{0,4},{4,8},{8,12},{12,16},{16,20},{20,24},{24,28},{28,32},{32,36}... | collective-permute-start | bytes 1277960 | tf_op jit(solution)/shard_map/ppermute | solution.py:273
  18.2 1.1 %copy-start.7 = (s32[2048,1]{0,1:T(1,128)S(1)}, s32[2048,1]{0,1:T(1,128)}, u32[]{:S(2)}) copy-start(s32[2048,1]{0,1:T(1,128)} %param.16) | copy-start | bytes 24580
  19.3 12.7 %collective-permute-start.1 = (f32[4,13,2048]{2,1,0:T(8,128)}, f32[4,13,2048]{2,1,0:T(8,128)S(1)}, u32[]{:S(2)}, u32[]{:S(2)}) collective-permute-start(f32[4,13,2048]{2,1,0:T(8,128)} %pad_maximum_fusion.1), channel_id=1, source_target_pairs={{4,0},{8,4},{12,8},{16,12},{20,16},{24,20},{28,24},{32,28},{36,32}... | collective-permute-start | bytes 1277960 | tf_op jit(solution)/shard_map/ppermute | solution.py:273
  19.3 1.8 %copy-start.8 = (s32[2048]{0:T(1024)S(1)}, s32[2048]{0:T(1024)}, u32[]{:S(2)}) copy-start(s32[2048]{0:T(1024)} %param.17) | copy-start | bytes 24580
  19.4 2.1 %copy-start.6 = (f32[4,2048]{1,0:T(4,128)S(1)}, f32[4,2048]{1,0:T(4,128)}, u32[]{:S(2)}) copy-start(f32[4,2048]{1,0:T(4,128)} %param.13) | copy-start | bytes 98308
  19.4 2.1 %copy-start.9 = (f32[2048]{0:T(1024)S(1)}, f32[2048]{0:T(1024)}, u32[]{:S(2)}) copy-start(f32[2048]{0:T(1024)} %param.15) | copy-start | bytes 24580
  19.4 2.0 %copy-start.10 = (f32[2048]{0:T(1024)S(1)}, f32[2048]{0:T(1024)}, u32[]{:S(2)}) copy-start(f32[2048]{0:T(1024)} %param.14) | copy-start | bytes 24580
  23.5 17.0 %copy-start.5 = (s32[4,8,2048]{2,1,0:T(8,128)S(1)}, s32[4,8,2048]{2,1,0:T(8,128)}, u32[]{:S(2)}) copy-start(s32[4,8,2048]{2,1,0:T(8,128)} %param.12) | copy-start | bytes 786436
  25.8 14.6 %copy-start.3 = (f32[4,13,2048]{2,1,0:T(8,128)}, f32[4,13,2048]{2,1,0:T(8,128)S(1)}, u32[]{:S(2)}) copy-start(f32[4,13,2048]{2,1,0:T(8,128)S(1)} %collective-permute-done.xl_ref) | copy-start | bytes 1277956
  32.1 8.4 %copy-start.4 = (f32[4,13,2048]{2,1,0:T(8,128)}, f32[4,13,2048]{2,1,0:T(8,128)S(1)}, u32[]{:S(2)}) copy-start(f32[4,13,2048]{2,1,0:T(8,128)S(1)} %collective-permute-done.1.xh_ref) | copy-start | bytes 1277956
  32.9 16.0 %all-to-all-start.1 = ((f32[64,1,512]{2,1,0:T(1,128)}), f32[64,1,512]{2,1,0:T(1,128)S(1)}, u32[]{:S(2)}, u32[]{:S(2)}) async-start(f32[64,1,512]{2,1,0:T(1,128)} %copy.32), calls=%async_computation.1 | async-start | bytes 262144 | tf_op jit(solution)/shard_map/all_to_all | solution.py:349
  47.4 1.8 %copy-start = (f32[4,4,8,2048]{3,2,1,0:T(8,128)S(1)}, f32[4,4,8,2048]{3,2,1,0:T(8,128)}, u32[]{:S(2)}) copy-start(f32[4,4,8,2048]{3,2,1,0:T(8,128)} %su_ref.1) | copy-start | bytes 3145732
  54.7 14.9 %copy-start.1 = (f32[4,4,8,2048]{3,2,1,0:T(8,128)S(1)}, f32[4,4,8,2048]{3,2,1,0:T(8,128)}, u32[]{:S(2)}) copy-start(f32[4,4,8,2048]{3,2,1,0:T(8,128)} %shard_map.104) | copy-start | bytes 3145732
  54.7 14.9 %copy-start.2 = (f32[4,4,8,2048]{3,2,1,0:T(8,128)S(1)}, f32[4,4,8,2048]{3,2,1,0:T(8,128)}, u32[]{:S(2)}) copy-start(f32[4,4,8,2048]{3,2,1,0:T(8,128)} %param.10) | copy-start | bytes 3145732
  55.7 16.5 %all-to-all-start.2 = ((f32[64,1,256]{2,1,0:T(1,128)}), f32[64,1,256]{2,1,0:T(1,128)S(1)}, u32[]{:S(2)}, u32[]{:S(2)}) async-start(f32[64,1,256]{2,1,0:T(1,128)} %copy.35), calls=%async_computation.2 | async-start | bytes 131072 | tf_op jit(solution)/shard_map/all_to_all | solution.py:357

commit v12 on v6

--- a/solution.py
+++ b/solution.py
@@ -332,7 +332,19 @@
     new_state = start + dt_step * change
     new_state, returned = lax.optimization_barrier((new_state, returned))
     returned = jnp.transpose(returned.reshape(owners_gx, 4, capacity), (1, 0, 2))
-    through = jnp.einsum("cok,fk->cof", returned, rank_hot, precision=exact)
+    pieces = []
+    rest = returned
+    for _ in range(3):
+        piece = lax.reduce_precision(rest, exponent_bits=8, mantissa_bits=7)
+        rest = rest - piece
+        pieces.append(piece.astype(jnp.bfloat16))
+    rank_bf16 = rank_hot.astype(jnp.bfloat16)
+    through = jnp.einsum(
+        "cok,fk->cof",
+        jnp.concatenate(pieces, axis=2),
+        jnp.concatenate([rank_bf16] * 3, axis=1),
+        preferred_element_type=jnp.float32,
+    )
     facet_flux = jnp.sum(through * owner_float.T[None], axis=1)
     return (new_state, facet_flux)
 

time: 70.8 us -> 71.4 us (level)
  waiting for transfers between devices: 11.7 us -> 3.78 us
  starting transfers between devices: 24.5 us -> 31.3 us
  other arithmetic: 1.45 us -> 3.04 us
    ppermute x4, waiting for transfers between devices: 8.79 us -> 1.68 us  [shift_pair(): return (lax.ppermute(last, axis, up), lax.ppermute(leading, axis, down))]
    all_to_all x1, starting transfers between devices: 7.47 us -> 14 us  [local(): received = lax.all_to_all(outgoing, 'gx', 0, 0, tiled=True)]
    convert_element_type x0 -> x2, other arithmetic: none -> 0.8 us  [the longest x1 0.76 us: local(): rank_bf16 = rank_hot.astype(jnp.bfloat16)]
    concatenate x2, other arithmetic: 0.14 us -> 0.93 us  [x_rows(): jnp.concatenate([rows, eddy[:, lo:hi][:, -1:] if lo else eddy[:, 0:1]], a...]
    all_to_all x1, waiting for transfers between devices: 1.48 us -> 0.71 us  [local(): received = lax.all_to_all(outgoing, 'gx', 0, 0, tiled=True)]
  transfers between devices with their start and end apart: 6 -> 6, of which waited for: 4 -> 3; matrix products, arithmetic and copies ran while one was open for 13% -> 13% of each run, Pallas kernels for 18% -> 18%
where the time goes in v12:
time: 71.4 us; the launch traced here: 70.9 us
  starting transfers between devices  31.3 us (44%)
  Pallas kernels  17.9 us (25%)
  local copies, waits for them, and re-layouts  9.01 us (13%)
  matrix products  4.99 us (7%)
  waiting for transfers between devices  3.78 us (5%)
  other arithmetic  3.04 us (4%)
  between operations  0.96 us (1%)
    all_to_all x1, starting transfers between devices, local(): received = lax.all_to_all(outgoing, 'gx', 0, 0, tiled=True)  14 us
    all_to_all x1, starting transfers between devices, local(): returned = lax.all_to_all(wall_flux, 'gx', 0, 0, tiled=True)  8.85 us
    ppermute x4, starting transfers between devices, shift_pair(): return (lax.ppermute(last, axis, up), lax.ppermute(leading, axis, down))  8.39 us
    pallas_call x1, Pallas kernels, stencil(): pl.pallas_call(stencil_kernel, grid=(levels,), in_specs=[pl.BlockSpec((fi...  7 us
    pallas_call x1, Pallas kernels, owner_scatter(): pl.pallas_call(scatter_kernel, grid=(slots // block,), in_specs=[pl.Block...  5.44 us
    pallas_call x1, Pallas kernels, owner_gather(): pl.pallas_call(gather_kernel, grid=(slots // block,), in_specs=[pl.BlockS...  5.42 us
    transpose x3, local copies, waits for them, and re-layouts, x_rows(): jnp.transpose(state[:, :, lo:hi], (1, 0, 2, 3)).reshape(levels, -1, cells_y)  2.28 us
    dot_general x1, matrix products, local(): outgoing = jnp.einsum('cof,fk->cok', spread, rank_hot, precision=exact)  1.94 us
  transfers between devices with their start and end apart: 6, of which 3 were waited for; matrix products, arithmetic and copies ran while one was open for 13% of the time, Pallas kernels for 18%

profile of v12, /device:TPU:1, one launch (start us, length us, event | category | flops | bytes accessed | tf_op | source)
XLA Modules:
  0.0 70.9 jit_solution(12278350672761238927)
XLA Ops:
  0.6 1.8 %slice_bitcast_fusion = (f32[4,4,3,2048]{3,2,0,1:T(4,128)S(1)}, f32[4,4,3,2048]{3,2,0,1:T(4,128)S(1)}) fusion(f32[4,4,8,2048]{3,2,1,0:T(8,128)} %su_ref.1), kind=kLoop, calls=%fused_computation.26 | loop fusion | bytes 1572864 | tf_op jit(solution)/shard_map/transpose | solution.py:281
  2.4 0.3 copy.21
  2.7 0.2 copy.22
  2.9 1.1 %fusion.33 = (f32[4,1,2048]{2,1,0:T(1,128)S(1)}, f32[4,1,2048]{2,1,0:T(1,128)S(1)}) fusion(f32[4,8,2048]{2,1,0:T(8,128)} %eu_ref.1), kind=kLoop, calls=%fused_computation.58 | loop fusion | bytes 131072 | tf_op jit(solution)/shard_map/slice | solution.py:282
  4.0 0.1 pad_maximum_fusion
  4.1 3.1 %collective-permute-start = (f32[4,13,2048]{2,1,0:T(8,128)S(1)}, f32[4,13,2048]{2,1,0:T(8,128)S(1)}, u32[]{:S(2)}, u32[]{:S(2)}) collective-permute-start(f32[4,13,2048]{2,1,0:T(8,128)S(1)} %pad_maximum_fusion), channel_id=1, source_target_pairs={{0,4},{4,8},{8,12},{12,16},{16,20},{20,24},{24,28},{28,32},{32,36}... | collective-permute-start | bytes 1277960 | tf_op jit(solution)/shard_map/ppermute | solution.py:258
  7.2 0.3 copy.23
  7.5 0.2 copy.24
  7.7 0.0 copy-start.10
  7.7 0.9 %pad_maximum_fusion.1 = f32[4,13,2048]{2,1,0:T(8,128)} fusion(f32[4,1,2048]{2,1,0:T(1,128)S(1)} %get-tuple-element.32, f32[4,12,2048]{2,1,0:T(8,128)S(1)} %copy.24), kind=kLoop, calls=%fused_computation.19 | loop fusion | flops 106496 | bytes 851968 | tf_op jit(solution)/shard_map/concatenate | solution.py:282
  8.6 0.2 collective-permute-start.1
  8.8 0.9 %fusion.32 = (f32[4,4,8,128]{3,2,1,0:T(8,128)S(1)}, f32[4,4,8,128]{3,2,1,0:T(8,128)S(1)}) fusion(f32[4,4,8,2048]{3,2,1,0:T(8,128)} %su_ref.1), kind=kLoop, calls=%fused_computation.57 | loop fusion | bytes 262144 | tf_op jit(solution)/shard_map/slice | solution.py:288
  9.7 0.7 %slice_bitcast_fusion.2 = (f32[1,4,8,128]{3,2,1,0:T(8,128)S(1)}, f32[1,4,8,128]{3,2,1,0:T(8,128)S(1)}) fusion(f32[4,8,2048]{2,1,0:T(8,128)} %eu_ref.1), kind=kLoop, calls=%fused_computation.53 | loop fusion | bytes 65536 | tf_op jit(solution)/shard_map/broadcast_in_dim | solution.py:288
  10.4 2.9 %collective-permute-start.2 = (f32[5,4,8,128]{3,2,1,0:T(8,128)S(1)}, f32[5,4,8,128]{3,2,1,0:T(8,128)S(1)}, u32[]{:S(2)}, u32[]{:S(2)}) collective-permute-start(f32[5,4,8,128]{3,2,1,0:T(8,128)S(1)} %pad_maximum_fusion.2), channel_id=1, source_target_pairs={{0,1},{1,2},{2,3},{3,0},{4,5},{5,6},{6,7},{7,4},{8,9},{9,10},{10,1... | collective-permute-start | bytes 245768 | tf_op jit(solution)/shard_map/ppermute | solution.py:258
  13.3 2.2 %collective-permute-start.3 = (f32[5,4,8,128]{3,2,1,0:T(8,128)S(1)}, f32[5,4,8,128]{3,2,1,0:T(8,128)S(1)}, u32[]{:S(2)}, u32[]{:S(2)}) collective-permute-start(f32[5,4,8,128]{3,2,1,0:T(8,128)S(1)} %pad_maximum_fusion.3), channel_id=1, source_target_pairs={{1,0},{2,1},{3,2},{0,3},{5,4},{6,5},{7,6},{4,7},{9,8},{10,9},{11,1... | collective-permute-start | bytes 245768 | tf_op jit(solution)/shard_map/ppermute | solution.py:258
  15.5 0.0 copy-done.10
  15.5 1.7 %fusion.10 = f32[2048]{0:T(1024)S(1)} fusion(s32[2048]{0:T(1024)S(1)} %bitcast.54), kind=kOutput, calls=%fused_computation.10 | convolution fusion | flops 541849600 | bytes 16384 | tf_op jit(solution)/shard_map/dot_general | solution.py:302
  17.2 0.0 copy-start.5
  17.2 0.0 copy-start.9
  17.2 0.0 copy-start.12
  17.2 0.0 copy-start.13
  17.3 0.3 convolution_subtract_fusion
  17.6 0.0 copy-done.11
  17.6 0.6 copy-done.5
  18.2 0.0 copy-done.9
  18.2 0.0 copy-done.12
  18.2 0.0 copy-done.13
  18.2 1.9 %fusion.7 = f32[7,64,64]{2,1,0:T(8,128)S(1)} fusion(f32[64,2048]{1,0:T(8,128)S(1)} %fusion.19, f32[7,2048]{1,0:T(8,128)S(1)} %pad_maximum_fusion.4, f32[2048]{0:T(1024)S(1)} %fusion.10, f32[64,64]{1,0:T(8,128)S(1)} %convolution_subtract_fusion, f32[7]{0:T(128)S(1)} %compare_convert_fusion), kind=kOutput, calls=%fused_computation.9 | convolution fusion | flops 705748992 | bytes 720924 | tf_op jit(solution)/shard_map/cof,fk->cok/dot_general | solution.py:313
  20.2 0.2 copy.25
  20.4 0.1 reshape.75
  20.5 1.7 %collective-permute-done.2.yl_ref = f32[5,4,8,128]{3,2,1,0:T(8,128)S(1)} collective-permute-done((f32[5,4,8,128]{3,2,1,0:T(8,128)S(1)}, f32[5,4,8,128]{3,2,1,0:T(8,128)S(1)}, u32[]{:S(2)}, u32[]{:S(2)}) %collective-permute-start.2) | collective-permute-done | bytes 81952 | tf_op jit(solution)/shard_map/ppermute | solution.py:258
  22.2 0.0 collective-permute-done.3.yh_ref
  22.2 0.0 collective-permute-done.xl_ref
  22.2 0.0 copy-start.3
  22.2 0.0 collective-permute-done.1.xh_ref
  22.2 0.0 copy-start.4
  22.2 0.9 %copy.26 = f32[64,1,512]{2,1,0:T(1,128)} copy(f32[64,1,512]{2,0,1:T(8,128)S(1)} %bitcast.48) | data formatting | bytes 262144 | tf_op jit(solution)/shard_map/all_to_all | solution.py:322
  23.2 14.0 %all-to-all-start = ((f32[64,1,512]{2,1,0:T(1,128)}), f32[64,1,512]{2,1,0:T(1,128)S(1)}, u32[]{:S(2)}, u32[]{:S(2)}) async-start(f32[64,1,512]{2,1,0:T(1,128)} %copy.26), calls=%async_computation | async-start | bytes 262144 | tf_op jit(solution)/shard_map/all_to_all | solution.py:322
  37.2 0.8 %convert_convert_fusion = bf16[2048,64]{0,1:T(8,128)(2,1)} fusion(f32[2048]{0:T(1024)S(1)} %fusion.10), kind=kLoop, calls=%fused_computation.20 | loop fusion | flops 393216 | bytes 270336 | tf_op jit(solution)/shard_map/convert_element_type | solution.py:341
  37.9 0.0 copy-done.7
  37.9 0.0 copy-done.8
  37.9 0.0 copy-done.3
  37.9 0.0 copy-done.4
  38.0 7.0 %shard_map.104 = f32[4,4,8,2048]{3,2,1,0:T(8,128)} custom-call(f32[4,4,8,2048]{3,2,1,0:T(8,128)} %su_ref.1, f32[4,4,8,2048]{3,2,1,0:T(8,128)} %su_ref.1, f32[4,4,8,2048]{3,2,1,0:T(8,128)} %su_ref.1, f32[4,8,2048]{2,1,0:T(8,128)} %eu_ref.1, f32[4,8,2048]{2,1,0:T(8,128)} %eu_ref.1, f32[4,8,2048]{2,1,0:T(8,128)} %eu_ref.1, f32[4,13,2048]{2,1,0:T(8,128)} %copy-done.3, ...), custom_call_target="tpu_custom_call" | custom-call | flops 52428800 | bytes 6291456 | tf_op jit(solution)/shard_map/pallas_call | solution.py:120
  45.0 0.7 all-to-all-done
  45.7 0.1 reshape.77
  45.8 0.1 copy.27
  45.8 0.1 reshape.78.pay_ref
  46.0 0.2 copy-done
  46.2 5.4 %shard_map.105.flux_ref = f32[4,4096]{1,0:T(4,128)S(1)} custom-call(f32[128,2048]{1,0:T(8,128)S(1)} %bitcast.43, f32[8,4096]{1,0:T(8,128)S(1)} %reshape.78.pay_ref), custom_call_target="tpu_custom_call" | custom-call | flops 4294967296 | bytes 1245184 | tf_op jit(solution)/shard_map/pallas_call | solution.py:218
  51.6 0.0 copy-start.1
  51.6 0.0 copy-start.2
  51.6 0.1 reshape.79
  51.8 0.1 copy.43
  51.8 0.1 reshape.80
  52.0 0.7 copy.29
  52.7 8.9 %all-to-all-start.1 = ((f32[64,1,256]{2,1,0:T(1,128)}), f32[64,1,256]{2,1,0:T(1,128)S(1)}, u32[]{:S(2)}, u32[]{:S(2)}) async-start(f32[64,1,256]{2,1,0:T(1,128)} %copy.29), calls=%async_computation.1 | async-start | bytes 131072 | tf_op jit(solution)/shard_map/all_to_all | solution.py:330
  61.5 5.4 %shard_map.106 = f32[128,2048]{1,0:T(8,128)S(1)} custom-call(f32[8,4096]{1,0:T(8,128)S(1)} %reshape.78.pay_ref, f32[4,4096]{1,0:T(4,128)S(1)} %shard_map.105.flux_ref), custom_call_target="tpu_custom_call" | custom-call | flops 262144 | bytes 1048576 | tf_op jit(solution)/shard_map/pallas_call | solution.py:238
  67.0 0.0 copy-done.1
  67.0 0.0 copy-done.2
  67.0 1.2 %multiply_add_fusion = f32[4,4,8,2048]{3,2,1,0:T(8,128)} fusion(f32[4,4,8,2048]{3,2,1,0:T(8,128)S(1)} %copy-done.2, f32[4,4,8,2048]{3,2,1,0:T(8,128)S(1)} %copy-done.1, f32[4,4,8,2048]{3,2,1,0:T(8,128)S(1)} %bitcast.44, f32[4,8,2048]{2,1,0:T(8,128)S(1)} %convert_subtract_fusion), kind=kLoop, calls=%fused_computation.12 | loop fusion | flops 1048576 | bytes 4456448 | tf_op jit(solution)/shard_map/add | solution.py:332
  68.2 1.4 %all-to-all-done.1 = f32[64,1,256]{2,1,0:T(1,128)S(1)} async-done(((f32[64,1,256]{2,1,0:T(1,128)}), f32[64,1,256]{2,1,0:T(1,128)S(1)}, u32[]{:S(2)}, u32[]{:S(2)}) %all-to-all-start.1) | async-done | bytes 65568 | tf_op jit(solution)/shard_map/all_to_all | solution.py:330
  69.6 0.1 reshape.82
  69.8 1.1 %fusion.6 = f32[4,2048]{1,0:T(4,128)} fusion(f32[64,2048]{1,0:T(8,128)S(1)} %fusion.19, bf16[2048,64]{0,1:T(8,128)(2,1)S(1)} %copy-done.6, bf16[4,64,64]{2,1,0:T(8,128)(2,1)S(1)} %get-tuple-element.35, bf16[4,64,64]{2,1,0:T(8,128)(2,1)S(1)} %get-tuple-element.36, bf16[4,64,64]{2,1,0:T(8,128)(2,1)S(1)} %get-tuple-element.34), kind=kOutput, calls=%fused_computation.8 | convolution fusion | flops 205021184 | bytes 917504 | tf_op jit(solution)/shard_map/cok,fk->cof/dot_general | solution.py:342
  (17 shorter events, 0.2 us)
Async XLA Ops:
  4.1 18.1 %collective-permute-start = (f32[4,13,2048]{2,1,0:T(8,128)S(1)}, f32[4,13,2048]{2,1,0:T(8,128)S(1)}, u32[]{:S(2)}, u32[]{:S(2)}) collective-permute-start(f32[4,13,2048]{2,1,0:T(8,128)S(1)} %pad_maximum_fusion), channel_id=1, source_target_pairs={{0,4},{4,8},{8,12},{12,16},{16,20},{20,24},{24,28},{28,32},{32,36}... | collective-permute-start | bytes 1277960 | tf_op jit(solution)/shard_map/ppermute | solution.py:258
  7.7 7.8 %copy-start.10 = (s32[2048,1]{0,1:T(1,128)S(1)}, s32[2048,1]{0,1:T(1,128)}, u32[]{:S(2)}) copy-start(s32[2048,1]{0,1:T(1,128)} %param.16) | copy-start | bytes 24580
  8.6 13.6 %collective-permute-start.1 = (f32[4,13,2048]{2,1,0:T(8,128)}, f32[4,13,2048]{2,1,0:T(8,128)S(1)}, u32[]{:S(2)}, u32[]{:S(2)}) collective-permute-start(f32[4,13,2048]{2,1,0:T(8,128)} %pad_maximum_fusion.1), channel_id=1, source_target_pairs={{4,0},{8,4},{12,8},{16,12},{20,16},{24,20},{28,24},{32,28},{36,32}... | collective-permute-start | bytes 1277960 | tf_op jit(solution)/shard_map/ppermute | solution.py:258
  10.4 11.8 %collective-permute-start.2 = (f32[5,4,8,128]{3,2,1,0:T(8,128)S(1)}, f32[5,4,8,128]{3,2,1,0:T(8,128)S(1)}, u32[]{:S(2)}, u32[]{:S(2)}) collective-permute-start(f32[5,4,8,128]{3,2,1,0:T(8,128)S(1)} %pad_maximum_fusion.2), channel_id=1, source_target_pairs={{0,1},{1,2},{2,3},{3,0},{4,5},{5,6},{6,7},{7,4},{8,9},{9,10},{10,1... | collective-permute-start | bytes 245768 | tf_op jit(solution)/shard_map/ppermute | solution.py:258
  13.3 8.9 %collective-permute-start.3 = (f32[5,4,8,128]{3,2,1,0:T(8,128)S(1)}, f32[5,4,8,128]{3,2,1,0:T(8,128)S(1)}, u32[]{:S(2)}, u32[]{:S(2)}) collective-permute-start(f32[5,4,8,128]{3,2,1,0:T(8,128)S(1)} %pad_maximum_fusion.3), channel_id=1, source_target_pairs={{1,0},{2,1},{3,2},{0,3},{5,4},{6,5},{7,6},{4,7},{9,8},{10,9},{11,1... | collective-permute-start | bytes 245768 | tf_op jit(solution)/shard_map/ppermute | solution.py:258
  15.5 2.0 %copy-start.11 = (s32[2048]{0:T(1024)S(1)}, s32[2048]{0:T(1024)}, u32[]{:S(2)}) copy-start(s32[2048]{0:T(1024)} %param.17) | copy-start | bytes 24580
  17.2 1.0 %copy-start.5 = (s32[4,8,2048]{2,1,0:T(8,128)S(1)}, s32[4,8,2048]{2,1,0:T(8,128)}, u32[]{:S(2)}) copy-start(s32[4,8,2048]{2,1,0:T(8,128)} %param.12) | copy-start | bytes 786436
  17.2 1.0 %copy-start.9 = (f32[4,2048]{1,0:T(4,128)S(1)}, f32[4,2048]{1,0:T(4,128)}, u32[]{:S(2)}) copy-start(f32[4,2048]{1,0:T(4,128)} %param.13) | copy-start | bytes 98308
  17.2 1.0 %copy-start.12 = (f32[2048]{0:T(1024)S(1)}, f32[2048]{0:T(1024)}, u32[]{:S(2)}) copy-start(f32[2048]{0:T(1024)} %param.15) | copy-start | bytes 24580
  17.2 1.0 %copy-start.13 = (f32[2048]{0:T(1024)S(1)}, f32[2048]{0:T(1024)}, u32[]{:S(2)}) copy-start(f32[2048]{0:T(1024)} %param.14) | copy-start | bytes 24580
  22.2 15.8 %copy-start.7 = (f32[5,4,8,128]{3,2,1,0:T(8,128)}, f32[5,4,8,128]{3,2,1,0:T(8,128)S(1)}, u32[]{:S(2)}) copy-start(f32[5,4,8,128]{3,2,1,0:T(8,128)S(1)} %collective-permute-done.2.yl_ref) | copy-start | bytes 245764
  22.2 15.8 %copy-start.8 = (f32[5,4,8,128]{3,2,1,0:T(8,128)}, f32[5,4,8,128]{3,2,1,0:T(8,128)S(1)}, u32[]{:S(2)}) copy-start(f32[5,4,8,128]{3,2,1,0:T(8,128)S(1)} %collective-permute-done.3.yh_ref) | copy-start | bytes 245764
  22.2 15.8 %copy-start.3 = (f32[4,13,2048]{2,1,0:T(8,128)}, f32[4,13,2048]{2,1,0:T(8,128)S(1)}, u32[]{:S(2)}) copy-start(f32[4,13,2048]{2,1,0:T(8,128)S(1)} %collective-permute-done.xl_ref) | copy-start | bytes 1277956
  22.2 15.7 %copy-start.4 = (f32[4,13,2048]{2,1,0:T(8,128)}, f32[4,13,2048]{2,1,0:T(8,128)S(1)}, u32[]{:S(2)}) copy-start(f32[4,13,2048]{2,1,0:T(8,128)S(1)} %collective-permute-done.1.xh_ref) | copy-start | bytes 1277956
  23.2 22.5 %all-to-all-start = ((f32[64,1,512]{2,1,0:T(1,128)}), f32[64,1,512]{2,1,0:T(1,128)S(1)}, u32[]{:S(2)}, u32[]{:S(2)}) async-start(f32[64,1,512]{2,1,0:T(1,128)} %copy.26), calls=%async_computation | async-start | bytes 262144 | tf_op jit(solution)/shard_map/all_to_all | solution.py:322
  45.0 1.2 %copy-start = (f32[4,4,8,2048]{3,2,1,0:T(8,128)S(1)}, f32[4,4,8,2048]{3,2,1,0:T(8,128)}, u32[]{:S(2)}) copy-start(f32[4,4,8,2048]{3,2,1,0:T(8,128)} %su_ref.1) | copy-start | bytes 3145732
  51.6 15.4 %copy-start.1 = (f32[4,4,8,2048]{3,2,1,0:T(8,128)S(1)}, f32[4,4,8,2048]{3,2,1,0:T(8,128)}, u32[]{:S(2)}) copy-start(f32[4,4,8,2048]{3,2,1,0:T(8,128)} %shard_map.104) | copy-start | bytes 3145732
  51.6 15.4 %copy-start.2 = (f32[4,4,8,2048]{3,2,1,0:T(8,128)S(1)}, f32[4,4,8,2048]{3,2,1,0:T(8,128)}, u32[]{:S(2)}) copy-start(f32[4,4,8,2048]{3,2,1,0:T(8,128)} %param.10) | copy-start | bytes 3145732
  52.7 16.9 %all-to-all-start.1 = ((f32[64,1,256]{2,1,0:T(1,128)}), f32[64,1,256]{2,1,0:T(1,128)S(1)}, u32[]{:S(2)}, u32[]{:S(2)}) async-start(f32[64,1,256]{2,1,0:T(1,128)} %copy.29), calls=%async_computation.1 | async-start | bytes 131072 | tf_op jit(solution)/shard_map/all_to_all | solution.py:330
  67.0 2.8 %copy-start.6 = (bf16[2048,64]{0,1:T(8,128)(2,1)S(1)}, bf16[2048,64]{0,1:T(8,128)(2,1)}, u32[]{:S(2)}) copy-start(bf16[2048,64]{0,1:T(8,128)(2,1)} %convert_convert_fusion) | copy-start | bytes 786436

commit v13 on v10

--- a/solution.py
+++ b/solution.py
@@ -282,8 +282,8 @@
         return jnp.concatenate([rows, eddy[:, lo:hi][:, -1:] if lo else eddy[:, 0:1]], axis=1)
 
     x_last, x_first = x_rows(cells_x - width, cells_x), x_rows(0, width)
-    x_last, x_first, y_state, y_eddy = lax.optimization_barrier((x_last, x_first, state, eddy))
     x_low, x_high = shift_pair(x_last, x_first, "gx")
+    _, _, y_state, y_eddy = lax.optimization_barrier((x_last, x_first, state, eddy))
 
     def y_cols(lo, hi, one):
         return jnp.concatenate([y_state[..., lo:hi].reshape(-1), y_eddy[..., one:one + 1].reshape(-1)])
@@ -296,10 +296,10 @@
         return jnp.concatenate([jnp.pad(fields_part, pad_f), jnp.pad(eddy_part, pad_e)], axis=0)
 
     y_last, y_first = y_cols(cells_y - width, cells_y, cells_y - 1), y_cols(0, width, 0)
-    y_last, y_first, facet_wall, facet_dist, facet_area, facet_owner, facet_cell = lax.optimization_barrier(
+    y_low, y_high = shift_pair(y_last, y_first, "gy")
+    _, _, facet_wall, facet_dist, facet_area, facet_owner, facet_cell = lax.optimization_barrier(
         (y_last, y_first, facet_wall, facet_dist, facet_area, facet_owner, facet_cell)
     )
-    y_low, y_high = shift_pair(y_last, y_first, "gy")
     y_low = y_tile(y_low, edge - width, edge - 1)
     y_high = y_tile(y_high, 0, 0)
 

time: 72.2 us -> 69.5 us (0.963)
  waiting for transfers between devices: 10.6 us -> 2.9 us
  starting transfers between devices: 24.4 us -> 29.3 us
    ppermute x4, waiting for transfers between devices: 7.69 us -> 0.01 us  [shift_pair(): return (lax.ppermute(last, axis, up), lax.ppermute(leading, axis, down))]
    all_to_all x1, starting transfers between devices: 7.61 us -> 12.6 us  [local(): received = lax.all_to_all(outgoing, 'gx', 0, 0, tiled=True)]
  transfers between devices with their start and end apart: 6 -> 6, of which waited for: 3 -> 2; matrix products, arithmetic and copies ran while one was open for 10% -> 15% of each run, Pallas kernels for 17% -> 18%
where the time goes in v13:
time: 69.5 us; the launch traced here: 69.1 us
  starting transfers between devices  29.3 us (42%)
  Pallas kernels  17.8 us (26%)
  local copies, waits for them, and re-layouts  9.72 us (14%)
  matrix products  5.56 us (8%)
  waiting for transfers between devices  2.9 us (4%)
  other arithmetic  2.81 us (4%)
  between operations  1 us (1%)
    all_to_all x1, starting transfers between devices, local(): received = lax.all_to_all(outgoing, 'gx', 0, 0, tiled=True)  12.6 us
    ppermute x4, starting transfers between devices, shift_pair(): return (lax.ppermute(last, axis, up), lax.ppermute(leading, axis, down))  8.49 us
    all_to_all x1, starting transfers between devices, local(): returned = lax.all_to_all(wall_flux, 'gx', 0, 0, tiled=True)  8.23 us
    pallas_call x1, Pallas kernels, stencil(): pl.pallas_call(stencil_kernel, grid=(levels,), in_specs=[pl.BlockSpec((fi...  6.92 us
    pallas_call x1, Pallas kernels, owner_scatter(): pl.pallas_call(scatter_kernel, grid=(slots // block,), in_specs=[pl.Block...  5.45 us
    pallas_call x1, Pallas kernels, owner_gather(): pl.pallas_call(gather_kernel, grid=(slots // block,), in_specs=[pl.BlockS...  5.44 us
    transpose x3, local copies, waits for them, and re-layouts, x_rows(): jnp.transpose(state[:, :, lo:hi], (1, 0, 2, 3)).reshape(levels, -1, cells_y)  2.28 us
    dot_general x1, matrix products, local(): outgoing = jnp.einsum('cof,fk->cok', spread, rank_hot, precision=exact)  1.94 us
  transfers between devices with their start and end apart: 6, of which 2 were waited for; matrix products, arithmetic and copies ran while one was open for 15% of the time, Pallas kernels for 18%

profile of v13, /device:TPU:1, one launch (start us, length us, event | category | flops | bytes accessed | tf_op | source)
XLA Modules:
  0.0 69.1 jit_solution(12261064410270990092)
XLA Ops:
  0.6 1.1 %fusion.24 = (f32[4,1,2048]{2,1,0:T(1,128)S(1)}, f32[4,1,2048]{2,1,0:T(1,128)S(1)}) fusion(f32[4,8,2048]{2,1,0:T(8,128)} %eu_ref.1), kind=kLoop, calls=%fused_computation.48 | loop fusion | bytes 131072 | tf_op jit(solution)/shard_map/slice | solution.py:282
  1.8 1.8 %slice_bitcast_fusion = (f32[4,4,3,2048]{3,2,0,1:T(4,128)S(1)}, f32[4,4,3,2048]{3,2,0,1:T(4,128)S(1)}) fusion(f32[4,4,8,2048]{3,2,1,0:T(8,128)} %su_ref.1), kind=kLoop, calls=%fused_computation.20 | loop fusion | bytes 1572864 | tf_op jit(solution)/shard_map/transpose | solution.py:281
  3.5 0.3 copy.25
  3.8 0.2 copy.26
  4.0 0.1 pad_maximum_fusion
  4.1 3.1 %collective-permute-start = (f32[4,13,2048]{2,1,0:T(8,128)S(1)}, f32[4,13,2048]{2,1,0:T(8,128)S(1)}, u32[]{:S(2)}, u32[]{:S(2)}) collective-permute-start(f32[4,13,2048]{2,1,0:T(8,128)S(1)} %pad_maximum_fusion), channel_id=1, source_target_pairs={{0,4},{4,8},{8,12},{12,16},{16,20},{20,24},{24,28},{28,32},{32,36}... | collective-permute-start | bytes 1277960 | tf_op jit(solution)/shard_map/ppermute | solution.py:258
  7.2 0.3 copy.27
  7.5 0.0 copy-start.7
  7.5 0.2 copy.28
  7.7 0.1 pad_maximum_fusion.1
  7.8 0.3 collective-permute-start.1
  8.1 0.9 %slice_reduce_fusion = (f32[4,8]{1,0:T(4,128)S(1)}, f32[4,8]{1,0:T(4,128)S(1)}) fusion(f32[4,8,2048]{2,1,0:T(8,128)} %eu_ref.1), kind=kLoop, calls=%fused_computation.40 | loop fusion | bytes 512 | tf_op jit(solution)/shard_map/slice | solution.py:289
  8.9 0.1 reshape.120
  9.0 0.1 reshape.116
  9.1 1.0 %fusion.23 = (f32[4,4,8,3]{3,2,1,0:T(8,128)S(1)}, f32[4,4,8,3]{3,2,1,0:T(8,128)S(1)}) fusion(f32[4,4,8,2048]{3,2,1,0:T(8,128)} %su_ref.1), kind=kLoop, calls=%fused_computation.47 | loop fusion | bytes 6144 | tf_op jit(solution)/shard_map/slice | solution.py:289
  10.1 0.2 reshape.119
  10.3 0.2 reshape.115
  10.5 2.9 %collective-permute-start.2 = (f32[416]{0:T(512)S(1)}, f32[416]{0:T(512)S(1)}, u32[]{:S(2)}, u32[]{:S(2)}) collective-permute-start(f32[416]{0:T(512)S(1)} %get-tuple-element.48), channel_id=1, source_target_pairs={{0,1},{1,2},{2,3},{3,0},{4,5},{5,6},{6,7},{7,4},{8,9},{9,10},{10,1... | collective-permute-start | bytes 5000 | tf_op jit(solution)/shard_map/ppermute | solution.py:258
  13.4 2.2 %collective-permute-start.3 = (f32[416]{0:T(512)S(1)}, f32[416]{0:T(512)S(1)}, u32[]{:S(2)}, u32[]{:S(2)}) collective-permute-start(f32[416]{0:T(512)S(1)} %get-tuple-element.49), channel_id=1, source_target_pairs={{1,0},{2,1},{3,2},{0,3},{5,4},{6,5},{7,6},{4,7},{9,8},{10,9},{11,1... | collective-permute-start | bytes 5000 | tf_op jit(solution)/shard_map/ppermute | solution.py:258
  15.7 0.0 copy-done.7
  15.7 0.0 copy-start.9
  15.7 0.0 copy-start.10
  15.7 1.7 %fusion.10 = f32[2048]{0:T(1024)S(1)} fusion(s32[2048]{0:T(1024)S(1)} %bitcast.49), kind=kOutput, calls=%fused_computation.10 | convolution fusion | flops 541849600 | bytes 16384 | tf_op jit(solution)/shard_map/dot_general | solution.py:316
  17.4 0.0 copy-done.8
  17.4 0.3 convolution_subtract_fusion
  17.7 0.0 copy-done.6
  17.8 1.9 %fusion.7 = f32[7,64,64]{2,1,0:T(8,128)S(1)} fusion(f32[64,2048]{1,0:T(8,128)S(1)} %fusion.16, f32[7,2048]{1,0:T(8,128)S(1)} %pad_maximum_fusion.2, f32[2048]{0:T(1024)S(1)} %fusion.10, f32[64,64]{1,0:T(8,128)S(1)} %convolution_subtract_fusion, f32[7]{0:T(128)S(1)} %compare_convert_fusion), kind=kOutput, calls=%fused_computation.9 | convolution fusion | flops 705748992 | bytes 720924 | tf_op jit(solution)/shard_map/cof,fk->cok/dot_general | solution.py:327
  19.8 0.0 copy-start.5
  19.8 0.2 copy.31
  19.9 0.1 reshape.123
  20.0 0.0 collective-permute-done.3
  20.1 0.1 reshape.133
  20.2 0.0 collective-permute-done.2
  20.2 0.1 reshape.132
  20.3 0.2 reshape.121
  20.5 0.2 reshape.117
  20.7 0.6 select_maximum_fusion.yh_ref
  21.4 0.7 %select_maximum_fusion.1.yl_ref = f32[5,4,8,128]{3,2,1,0:T(8,128)} fusion(f32[1,4,8,1]{3,2,1,0:T(8,128)S(1)} %reshape.132, f32[4,4,8,3]{3,2,1,0:T(8,128)S(1)} %reshape.117), kind=kLoop, calls=%fused_computation.35 | loop fusion | flops 102400 | bytes 83584 | tf_op jit(solution)/shard_map/concatenate | solution.py:296
  22.1 0.0 collective-permute-done.xl_ref
  22.1 0.0 collective-permute-done.1.xh_ref
  22.1 0.0 copy-start.4
  22.1 1.0 %copy.32 = f32[64,1,512]{2,1,0:T(1,128)} copy(f32[64,1,512]{2,0,1:T(8,128)S(1)} %bitcast.42) | data formatting | bytes 262144 | tf_op jit(solution)/shard_map/all_to_all | solution.py:336
  23.1 12.6 %all-to-all-start = ((f32[64,1,512]{2,1,0:T(1,128)}), f32[64,1,512]{2,1,0:T(1,128)S(1)}, u32[]{:S(2)}, u32[]{:S(2)}) async-start(f32[64,1,512]{2,1,0:T(1,128)} %copy.32), calls=%async_computation | async-start | bytes 262144 | tf_op jit(solution)/shard_map/all_to_all | solution.py:336
  35.7 0.0 copy-done.3
  35.7 0.0 copy-done.4
  35.7 6.9 %shard_map.104 = f32[4,4,8,2048]{3,2,1,0:T(8,128)} custom-call(f32[4,4,8,2048]{3,2,1,0:T(8,128)} %su_ref.1, f32[4,4,8,2048]{3,2,1,0:T(8,128)} %su_ref.1, f32[4,4,8,2048]{3,2,1,0:T(8,128)} %su_ref.1, f32[4,8,2048]{2,1,0:T(8,128)} %eu_ref.1, f32[4,8,2048]{2,1,0:T(8,128)} %eu_ref.1, f32[4,8,2048]{2,1,0:T(8,128)} %eu_ref.1, f32[4,13,2048]{2,1,0:T(8,128)} %copy-done.3, ...), custom_call_target="tpu_custom_call" | custom-call | flops 52428800 | bytes 6291456 | tf_op jit(solution)/shard_map/pallas_call | solution.py:120
  42.7 1.5 %all-to-all-done = f32[64,1,512]{2,1,0:T(1,128)S(1)} async-done(((f32[64,1,512]{2,1,0:T(1,128)}), f32[64,1,512]{2,1,0:T(1,128)S(1)}, u32[]{:S(2)}, u32[]{:S(2)}) %all-to-all-start) | async-done | bytes 131104 | tf_op jit(solution)/shard_map/all_to_all | solution.py:336
  44.2 0.1 reshape.125
  44.3 0.1 copy.33
  44.3 0.1 reshape.126.pay_ref
  44.5 0.0 copy-done
  44.5 5.4 %shard_map.105.flux_ref = f32[4,4096]{1,0:T(4,128)S(1)} custom-call(f32[128,2048]{1,0:T(8,128)S(1)} %bitcast.37, f32[8,4096]{1,0:T(8,128)S(1)} %reshape.126.pay_ref), custom_call_target="tpu_custom_call" | custom-call | flops 4294967296 | bytes 1245184 | tf_op jit(solution)/shard_map/pallas_call | solution.py:218
  49.9 0.0 copy-start.1
  49.9 0.0 copy-start.2
  49.9 0.1 reshape.127
  50.1 0.1 copy.45
  50.1 0.1 reshape.128
  50.3 0.7 %copy.35 = f32[64,1,256]{2,1,0:T(1,128)} copy(f32[64,1,256]{2,0,1:T(8,128)S(1)} %bitcast.45) | data formatting | bytes 131072 | tf_op jit(solution)/shard_map/all_to_all | solution.py:344
  51.0 8.2 %all-to-all-start.1 = ((f32[64,1,256]{2,1,0:T(1,128)}), f32[64,1,256]{2,1,0:T(1,128)S(1)}, u32[]{:S(2)}, u32[]{:S(2)}) async-start(f32[64,1,256]{2,1,0:T(1,128)} %copy.35), calls=%async_computation.1 | async-start | bytes 131072 | tf_op jit(solution)/shard_map/all_to_all | solution.py:344
  59.2 5.4 %shard_map.106 = f32[128,2048]{1,0:T(8,128)S(1)} custom-call(f32[8,4096]{1,0:T(8,128)S(1)} %reshape.126.pay_ref, f32[4,4096]{1,0:T(4,128)S(1)} %shard_map.105.flux_ref), custom_call_target="tpu_custom_call" | custom-call | flops 262144 | bytes 1048576 | tf_op jit(solution)/shard_map/pallas_call | solution.py:238
  64.7 1.2 %multiply_add_fusion = f32[4,4,8,2048]{3,2,1,0:T(8,128)} fusion(f32[4,4,8,2048]{3,2,1,0:T(8,128)S(1)} %copy-done.2, f32[4,4,8,2048]{3,2,1,0:T(8,128)S(1)} %copy-done.1, f32[4,4,8,2048]{3,2,1,0:T(8,128)S(1)} %bitcast.38, f32[4,8,2048]{2,1,0:T(8,128)S(1)} %convert_subtract_fusion), kind=kLoop, calls=%fused_computation.12 | loop fusion | flops 1048576 | bytes 4456448 | tf_op jit(solution)/shard_map/add | solution.py:346
  65.9 1.4 %all-to-all-done.1 = f32[64,1,256]{2,1,0:T(1,128)S(1)} async-done(((f32[64,1,256]{2,1,0:T(1,128)}), f32[64,1,256]{2,1,0:T(1,128)S(1)}, u32[]{:S(2)}, u32[]{:S(2)}) %all-to-all-start.1) | async-done | bytes 65568 | tf_op jit(solution)/shard_map/all_to_all | solution.py:344
  67.3 0.1 reshape.130
  67.4 1.7 %fusion.6 = f32[4,2048]{1,0:T(4,128)} fusion(f32[64,2048]{1,0:T(8,128)S(1)} %fusion.16, f32[2048]{0:T(1024)S(1)} %fusion.10, f32[4,64,64]{2,0,1:T(4,128)S(1)} %bitcast.47), kind=kOutput, calls=%fused_computation.8 | convolution fusion | flops 403824640 | bytes 630784 | tf_op jit(solution)/shard_map/cok,fk->cof/dot_general | solution.py:349
  (24 shorter events, 0.2 us)
Async XLA Ops:
  4.1 18.0 %collective-permute-start = (f32[4,13,2048]{2,1,0:T(8,128)S(1)}, f32[4,13,2048]{2,1,0:T(8,128)S(1)}, u32[]{:S(2)}, u32[]{:S(2)}) collective-permute-start(f32[4,13,2048]{2,1,0:T(8,128)S(1)} %pad_maximum_fusion), channel_id=1, source_target_pairs={{0,4},{4,8},{8,12},{12,16},{16,20},{20,24},{24,28},{28,32},{32,36}... | collective-permute-start | bytes 1277960 | tf_op jit(solution)/shard_map/ppermute | solution.py:258
  7.5 8.2 %copy-start.7 = (s32[2048,1]{0,1:T(1,128)S(1)}, s32[2048,1]{0,1:T(1,128)}, u32[]{:S(2)}) copy-start(s32[2048,1]{0,1:T(1,128)} %param.16) | copy-start | bytes 24580
  7.8 14.3 %collective-permute-start.1 = (f32[4,13,2048]{2,1,0:T(8,128)S(1)}, f32[4,13,2048]{2,1,0:T(8,128)S(1)}, u32[]{:S(2)}, u32[]{:S(2)}) collective-permute-start(f32[4,13,2048]{2,1,0:T(8,128)S(1)} %pad_maximum_fusion.1), channel_id=1, source_target_pairs={{4,0},{8,4},{12,8},{16,12},{20,16},{24,20},{28,24},{32,28},{36,32}... | collective-permute-start | bytes 1277960 | tf_op jit(solution)/shard_map/ppermute | solution.py:258
  10.5 9.6 %collective-permute-start.2 = (f32[416]{0:T(512)S(1)}, f32[416]{0:T(512)S(1)}, u32[]{:S(2)}, u32[]{:S(2)}) collective-permute-start(f32[416]{0:T(512)S(1)} %get-tuple-element.48), channel_id=1, source_target_pairs={{0,1},{1,2},{2,3},{3,0},{4,5},{5,6},{6,7},{7,4},{8,9},{9,10},{10,1... | collective-permute-start | bytes 5000 | tf_op jit(solution)/shard_map/ppermute | solution.py:258
  13.4 6.6 %collective-permute-start.3 = (f32[416]{0:T(512)S(1)}, f32[416]{0:T(512)S(1)}, u32[]{:S(2)}, u32[]{:S(2)}) collective-permute-start(f32[416]{0:T(512)S(1)} %get-tuple-element.49), channel_id=1, source_target_pairs={{1,0},{2,1},{3,2},{0,3},{5,4},{6,5},{7,6},{4,7},{9,8},{10,9},{11,1... | collective-permute-start | bytes 5000 | tf_op jit(solution)/shard_map/ppermute | solution.py:258
  15.7 1.8 %copy-start.8 = (s32[2048]{0:T(1024)S(1)}, s32[2048]{0:T(1024)}, u32[]{:S(2)}) copy-start(s32[2048]{0:T(1024)} %param.17) | copy-start | bytes 24580
  15.7 2.0 %copy-start.6 = (f32[4,2048]{1,0:T(4,128)S(1)}, f32[4,2048]{1,0:T(4,128)}, u32[]{:S(2)}) copy-start(f32[4,2048]{1,0:T(4,128)} %param.13) | copy-start | bytes 98308
  15.7 2.0 %copy-start.9 = (f32[2048]{0:T(1024)S(1)}, f32[2048]{0:T(1024)}, u32[]{:S(2)}) copy-start(f32[2048]{0:T(1024)} %param.15) | copy-start | bytes 24580
  15.7 2.0 %copy-start.10 = (f32[2048]{0:T(1024)S(1)}, f32[2048]{0:T(1024)}, u32[]{:S(2)}) copy-start(f32[2048]{0:T(1024)} %param.14) | copy-start | bytes 24580
  19.8 15.9 %copy-start.5 = (s32[4,8,2048]{2,1,0:T(8,128)S(1)}, s32[4,8,2048]{2,1,0:T(8,128)}, u32[]{:S(2)}) copy-start(s32[4,8,2048]{2,1,0:T(8,128)} %param.12) | copy-start | bytes 786436
  22.1 13.6 %copy-start.3 = (f32[4,13,2048]{2,1,0:T(8,128)}, f32[4,13,2048]{2,1,0:T(8,128)S(1)}, u32[]{:S(2)}) copy-start(f32[4,13,2048]{2,1,0:T(8,128)S(1)} %collective-permute-done.xl_ref) | copy-start | bytes 1277956
  22.1 13.6 %copy-start.4 = (f32[4,13,2048]{2,1,0:T(8,128)}, f32[4,13,2048]{2,1,0:T(8,128)S(1)}, u32[]{:S(2)}) copy-start(f32[4,13,2048]{2,1,0:T(8,128)S(1)} %collective-permute-done.1.xh_ref) | copy-start | bytes 1277956
  23.1 21.1 %all-to-all-start = ((f32[64,1,512]{2,1,0:T(1,128)}), f32[64,1,512]{2,1,0:T(1,128)S(1)}, u32[]{:S(2)}, u32[]{:S(2)}) async-start(f32[64,1,512]{2,1,0:T(1,128)} %copy.32), calls=%async_computation | async-start | bytes 262144 | tf_op jit(solution)/shard_map/all_to_all | solution.py:336
  42.7 1.8 %copy-start = (f32[4,4,8,2048]{3,2,1,0:T(8,128)S(1)}, f32[4,4,8,2048]{3,2,1,0:T(8,128)}, u32[]{:S(2)}) copy-start(f32[4,4,8,2048]{3,2,1,0:T(8,128)} %su_ref.1) | copy-start | bytes 3145732
  49.9 14.8 %copy-start.1 = (f32[4,4,8,2048]{3,2,1,0:T(8,128)S(1)}, f32[4,4,8,2048]{3,2,1,0:T(8,128)}, u32[]{:S(2)}) copy-start(f32[4,4,8,2048]{3,2,1,0:T(8,128)} %shard_map.104) | copy-start | bytes 3145732
  49.9 14.8 %copy-start.2 = (f32[4,4,8,2048]{3,2,1,0:T(8,128)S(1)}, f32[4,4,8,2048]{3,2,1,0:T(8,128)}, u32[]{:S(2)}) copy-start(f32[4,4,8,2048]{3,2,1,0:T(8,128)} %param.10) | copy-start | bytes 3145732
  51.0 16.3 %all-to-all-start.1 = ((f32[64,1,256]{2,1,0:T(1,128)}), f32[64,1,256]{2,1,0:T(1,128)S(1)}, u32[]{:S(2)}, u32[]{:S(2)}) async-start(f32[64,1,256]{2,1,0:T(1,128)} %copy.35), calls=%async_computation.1 | async-start | bytes 131072 | tf_op jit(solution)/shard_map/all_to_all | solution.py:344

commit v14 on v6

--- a/solution.py
+++ b/solution.py
@@ -283,11 +283,16 @@
 
     x_last, x_first = x_rows(cells_x - width, cells_x), x_rows(0, width)
     x_low, x_high = shift_pair(x_last, x_first, "gx")
+    _, _, y_state, y_eddy = lax.optimization_barrier((x_last, x_first, state, eddy))
 
     def y_cols(lo, hi):
-        return jnp.concatenate([state[..., lo:hi], eddy[None, ..., lo:hi]], axis=0)
-
-    y_low, y_high = shift_pair(y_cols(cells_y - edge, cells_y), y_cols(0, edge), "gy")
+        return jnp.concatenate([y_state[..., lo:hi], y_eddy[None, ..., lo:hi]], axis=0)
+
+    y_last, y_first = y_cols(cells_y - edge, cells_y), y_cols(0, edge)
+    y_low, y_high = shift_pair(y_last, y_first, "gy")
+    _, _, facet_wall, facet_dist, facet_area, facet_owner, facet_cell = lax.optimization_barrier(
+        (y_last, y_first, facet_wall, facet_dist, facet_area, facet_owner, facet_cell)
+    )
 
     facet_count = facet_cell.shape[0]
     owners_gx = lax.axis_size("gx")

time: 70.8 us -> 71.2 us (level)
  starting transfers between devices: 24.5 us -> 29.7 us
  waiting for transfers between devices: 11.7 us -> 6.94 us
    all_to_all x1, starting transfers between devices: 7.47 us -> 13 us  [local(): received = lax.all_to_all(outgoing, 'gx', 0, 0, tiled=True)]
    ppermute x4, waiting for transfers between devices: 8.79 us -> 4.07 us  [shift_pair(): return (lax.ppermute(last, axis, up), lax.ppermute(leading, axis, down))]
  transfers between devices with their start and end apart: 6 -> 6, of which waited for: 4 -> 3; matrix products, arithmetic and copies ran while one was open for 13% -> 11% of each run, Pallas kernels for 18% -> 17%
where the time goes in v14:
time: 71.2 us; the launch traced here: 70.8 us
  starting transfers between devices  29.7 us (42%)
  Pallas kernels  17.9 us (25%)
  local copies, waits for them, and re-layouts  8.25 us (12%)
  waiting for transfers between devices  6.94 us (10%)
  matrix products  5.56 us (8%)
  other arithmetic  1.45 us (2%)
  between operations  0.95 us (1%)
    all_to_all x1, starting transfers between devices, local(): received = lax.all_to_all(outgoing, 'gx', 0, 0, tiled=True)  13 us
    ppermute x4, starting transfers between devices, shift_pair(): return (lax.ppermute(last, axis, up), lax.ppermute(leading, axis, down))  8.48 us
    all_to_all x1, starting transfers between devices, local(): returned = lax.all_to_all(wall_flux, 'gx', 0, 0, tiled=True)  8.23 us
    pallas_call x1, Pallas kernels, stencil(): pl.pallas_call(stencil_kernel, grid=(levels,), in_specs=[pl.BlockSpec((fi...  6.94 us
    pallas_call x1, Pallas kernels, owner_gather(): pl.pallas_call(gather_kernel, grid=(slots // block,), in_specs=[pl.BlockS...  5.46 us
    pallas_call x1, Pallas kernels, owner_scatter(): pl.pallas_call(scatter_kernel, grid=(slots // block,), in_specs=[pl.Block...  5.44 us
    ppermute x4, waiting for transfers between devices, shift_pair(): return (lax.ppermute(last, axis, up), lax.ppermute(leading, axis, down))  4.07 us
    transpose x3, local copies, waits for them, and re-layouts, x_rows(): jnp.transpose(state[:, :, lo:hi], (1, 0, 2, 3)).reshape(levels, -1, cells_y)  2.28 us
  transfers between devices with their start and end apart: 6, of which 3 were waited for; matrix products, arithmetic and copies ran while one was open for 11% of the time, Pallas kernels for 17%

profile of v14, /device:TPU:1, one launch (start us, length us, event | category | flops | bytes accessed | tf_op | source)
XLA Modules:
  0.0 70.8 jit_solution(14446937623873758213)
XLA Ops:
  0.6 1.1 %fusion.24 = (f32[4,1,2048]{2,1,0:T(1,128)S(1)}, f32[4,1,2048]{2,1,0:T(1,128)S(1)}) fusion(f32[4,8,2048]{2,1,0:T(8,128)} %eu_ref.1), kind=kLoop, calls=%fused_computation.42 | loop fusion | bytes 131072 | tf_op jit(solution)/shard_map/slice | solution.py:282
  1.8 1.8 %slice_bitcast_fusion = (f32[4,4,3,2048]{3,2,0,1:T(4,128)S(1)}, f32[4,4,3,2048]{3,2,0,1:T(4,128)S(1)}) fusion(f32[4,4,8,2048]{3,2,1,0:T(8,128)} %su_ref.1), kind=kLoop, calls=%fused_computation.20 | loop fusion | bytes 1572864 | tf_op jit(solution)/shard_map/transpose | solution.py:281
  3.5 0.3 copy.21
  3.8 0.2 copy.22
  4.0 0.1 pad_maximum_fusion
  4.1 3.1 %collective-permute-start = (f32[4,13,2048]{2,1,0:T(8,128)S(1)}, f32[4,13,2048]{2,1,0:T(8,128)S(1)}, u32[]{:S(2)}, u32[]{:S(2)}) collective-permute-start(f32[4,13,2048]{2,1,0:T(8,128)S(1)} %pad_maximum_fusion), channel_id=1, source_target_pairs={{0,4},{4,8},{8,12},{12,16},{16,20},{20,24},{24,28},{28,32},{32,36}... | collective-permute-start | bytes 1277960 | tf_op jit(solution)/shard_map/ppermute | solution.py:258
  7.2 0.3 copy.23
  7.5 0.2 copy.24
  7.7 0.0 copy-start.7
  7.7 0.1 pad_maximum_fusion.1
  7.8 0.3 collective-permute-start.1
  8.1 0.7 %slice_bitcast_fusion.2 = (f32[1,4,8,128]{3,2,1,0:T(8,128)S(1)}, f32[1,4,8,128]{3,2,1,0:T(8,128)S(1)}) fusion(f32[4,8,2048]{2,1,0:T(8,128)} %eu_ref.1), kind=kLoop, calls=%fused_computation.38 | loop fusion | bytes 65536 | tf_op jit(solution)/shard_map/broadcast_in_dim | solution.py:289
  8.8 0.9 %fusion.23 = (f32[4,4,8,128]{3,2,1,0:T(8,128)S(1)}, f32[4,4,8,128]{3,2,1,0:T(8,128)S(1)}) fusion(f32[4,4,8,2048]{3,2,1,0:T(8,128)} %su_ref.1), kind=kLoop, calls=%fused_computation.41 | loop fusion | bytes 262144 | tf_op jit(solution)/shard_map/slice | solution.py:289
  9.7 2.9 %collective-permute-start.2 = (f32[5,4,8,128]{3,2,1,0:T(8,128)S(1)}, f32[5,4,8,128]{3,2,1,0:T(8,128)}, u32[]{:S(2)}, u32[]{:S(2)}) collective-permute-start(f32[5,4,8,128]{3,2,1,0:T(8,128)S(1)} %pad_maximum_fusion.2), channel_id=1, source_target_pairs={{0,1},{1,2},{2,3},{3,0},{4,5},{5,6},{6,7},{7,4},{8,9},{9,10},{10,1... | collective-permute-start | bytes 245768 | tf_op jit(solution)/shard_map/ppermute | solution.py:258
  12.6 2.2 %collective-permute-start.3 = (f32[5,4,8,128]{3,2,1,0:T(8,128)S(1)}, f32[5,4,8,128]{3,2,1,0:T(8,128)}, u32[]{:S(2)}, u32[]{:S(2)}) collective-permute-start(f32[5,4,8,128]{3,2,1,0:T(8,128)S(1)} %pad_maximum_fusion.3), channel_id=1, source_target_pairs={{1,0},{2,1},{3,2},{0,3},{5,4},{6,5},{7,6},{4,7},{9,8},{10,9},{11,1... | collective-permute-start | bytes 245768 | tf_op jit(solution)/shard_map/ppermute | solution.py:258
  14.8 0.0 copy-done.7
  14.8 0.0 copy-start.8
  14.8 0.0 copy-start.6
  14.8 0.0 copy-start.9
  14.8 0.0 copy-start.10
  14.8 1.7 %fusion.10 = f32[2048]{0:T(1024)S(1)} fusion(s32[2048]{0:T(1024)S(1)} %bitcast.47), kind=kOutput, calls=%fused_computation.10 | convolution fusion | flops 541849600 | bytes 16384 | tf_op jit(solution)/shard_map/dot_general | solution.py:307
  16.6 0.0 copy-done.8
  16.6 0.3 convolution_subtract_fusion
  16.9 0.0 copy-done.6
  16.9 0.0 copy-done.9
  16.9 0.0 copy-done.10
  16.9 1.9 %fusion.7 = f32[7,64,64]{2,1,0:T(8,128)S(1)} fusion(f32[64,2048]{1,0:T(8,128)S(1)} %fusion.16, f32[7,2048]{1,0:T(8,128)S(1)} %pad_maximum_fusion.4, f32[2048]{0:T(1024)S(1)} %fusion.10, f32[64,64]{1,0:T(8,128)S(1)} %convolution_subtract_fusion, f32[7]{0:T(128)S(1)} %compare_convert_fusion), kind=kOutput, calls=%fused_computation.9 | convolution fusion | flops 705748992 | bytes 720924 | tf_op jit(solution)/shard_map/cof,fk->cok/dot_general | solution.py:318
  18.9 0.0 copy-start.5
  18.9 0.2 copy.25
  19.1 0.1 reshape.75
  19.2 4.1 %collective-permute-done.2.yl_ref = f32[5,4,8,128]{3,2,1,0:T(8,128)} collective-permute-done((f32[5,4,8,128]{3,2,1,0:T(8,128)S(1)}, f32[5,4,8,128]{3,2,1,0:T(8,128)}, u32[]{:S(2)}, u32[]{:S(2)}) %collective-permute-start.2) | collective-permute-done | bytes 81952 | tf_op jit(solution)/shard_map/ppermute | solution.py:258
  23.3 0.0 collective-permute-done.3.yh_ref
  23.3 0.0 collective-permute-done.xl_ref
  23.3 0.0 copy-start.3
  23.3 0.0 collective-permute-done.1.xh_ref
  23.3 0.0 copy-start.4
  23.3 1.0 %copy.26 = f32[64,1,512]{2,1,0:T(1,128)} copy(f32[64,1,512]{2,0,1:T(8,128)S(1)} %bitcast.40) | data formatting | bytes 262144 | tf_op jit(solution)/shard_map/all_to_all | solution.py:327
  24.3 13.0 %all-to-all-start = ((f32[64,1,512]{2,1,0:T(1,128)}), f32[64,1,512]{2,1,0:T(1,128)S(1)}, u32[]{:S(2)}, u32[]{:S(2)}) async-start(f32[64,1,512]{2,1,0:T(1,128)} %copy.26), calls=%async_computation | async-start | bytes 262144 | tf_op jit(solution)/shard_map/all_to_all | solution.py:327
  37.3 0.0 copy-done.5
  37.3 0.0 copy-done.3
  37.4 0.0 copy-done.4
  37.4 6.9 %shard_map.104 = f32[4,4,8,2048]{3,2,1,0:T(8,128)} custom-call(f32[4,4,8,2048]{3,2,1,0:T(8,128)} %su_ref.1, f32[4,4,8,2048]{3,2,1,0:T(8,128)} %su_ref.1, f32[4,4,8,2048]{3,2,1,0:T(8,128)} %su_ref.1, f32[4,8,2048]{2,1,0:T(8,128)} %eu_ref.1, f32[4,8,2048]{2,1,0:T(8,128)} %eu_ref.1, f32[4,8,2048]{2,1,0:T(8,128)} %eu_ref.1, f32[4,13,2048]{2,1,0:T(8,128)} %copy-done.3, ...), custom_call_target="tpu_custom_call" | custom-call | flops 52428800 | bytes 6291456 | tf_op jit(solution)/shard_map/pallas_call | solution.py:120
  44.3 0.0 copy-start
  44.3 1.5 %all-to-all-done = f32[64,1,512]{2,1,0:T(1,128)S(1)} async-done(((f32[64,1,512]{2,1,0:T(1,128)}), f32[64,1,512]{2,1,0:T(1,128)S(1)}, u32[]{:S(2)}, u32[]{:S(2)}) %all-to-all-start) | async-done | bytes 131104 | tf_op jit(solution)/shard_map/all_to_all | solution.py:327
  45.8 0.1 reshape.77
  45.9 0.1 copy.27
  46.0 0.1 reshape.78.pay_ref
  46.1 0.0 copy-done
  46.1 5.5 %shard_map.105.flux_ref = f32[4,4096]{1,0:T(4,128)S(1)} custom-call(f32[128,2048]{1,0:T(8,128)S(1)} %bitcast.35, f32[8,4096]{1,0:T(8,128)S(1)} %reshape.78.pay_ref), custom_call_target="tpu_custom_call" | custom-call | flops 4294967296 | bytes 1245184 | tf_op jit(solution)/shard_map/pallas_call | solution.py:218
  51.6 0.0 copy-start.1
  51.6 0.0 copy-start.2
  51.6 0.1 reshape.79
  51.7 0.1 copy.39
  51.8 0.1 reshape.80
  51.9 0.7 copy.29
  52.6 8.2 %all-to-all-start.1 = ((f32[64,1,256]{2,1,0:T(1,128)}), f32[64,1,256]{2,1,0:T(1,128)S(1)}, u32[]{:S(2)}, u32[]{:S(2)}) async-start(f32[64,1,256]{2,1,0:T(1,128)} %copy.29), calls=%async_computation.1 | async-start | bytes 131072 | tf_op jit(solution)/shard_map/all_to_all | solution.py:335
  60.9 5.4 %shard_map.106 = f32[128,2048]{1,0:T(8,128)S(1)} custom-call(f32[8,4096]{1,0:T(8,128)S(1)} %reshape.78.pay_ref, f32[4,4096]{1,0:T(4,128)S(1)} %shard_map.105.flux_ref), custom_call_target="tpu_custom_call" | custom-call | flops 262144 | bytes 1048576 | tf_op jit(solution)/shard_map/pallas_call | solution.py:238
  66.3 0.0 copy-done.1
  66.3 0.0 copy-done.2
  66.4 1.2 %multiply_add_fusion = f32[4,4,8,2048]{3,2,1,0:T(8,128)} fusion(f32[4,4,8,2048]{3,2,1,0:T(8,128)S(1)} %copy-done.2, f32[4,4,8,2048]{3,2,1,0:T(8,128)S(1)} %copy-done.1, f32[4,4,8,2048]{3,2,1,0:T(8,128)S(1)} %bitcast.36, f32[4,8,2048]{2,1,0:T(8,128)S(1)} %convert_subtract_fusion), kind=kLoop, calls=%fused_computation.12 | loop fusion | flops 1048576 | bytes 4456448 | tf_op jit(solution)/shard_map/add | solution.py:337
  67.6 1.4 %all-to-all-done.1 = f32[64,1,256]{2,1,0:T(1,128)S(1)} async-done(((f32[64,1,256]{2,1,0:T(1,128)}), f32[64,1,256]{2,1,0:T(1,128)S(1)}, u32[]{:S(2)}, u32[]{:S(2)}) %all-to-all-start.1) | async-done | bytes 65568 | tf_op jit(solution)/shard_map/all_to_all | solution.py:335
  68.9 0.1 reshape.82
  69.1 1.7 %fusion.6 = f32[4,2048]{1,0:T(4,128)} fusion(f32[64,2048]{1,0:T(8,128)S(1)} %fusion.16, f32[2048]{0:T(1024)S(1)} %fusion.10, f32[4,64,64]{2,0,1:T(4,128)S(1)} %bitcast.45), kind=kOutput, calls=%fused_computation.8 | convolution fusion | flops 403824640 | bytes 630784 | tf_op jit(solution)/shard_map/cok,fk->cof/dot_general | solution.py:340
  (10 shorter events, 0.2 us)
Async XLA Ops:
  4.1 19.2 %collective-permute-start = (f32[4,13,2048]{2,1,0:T(8,128)S(1)}, f32[4,13,2048]{2,1,0:T(8,128)S(1)}, u32[]{:S(2)}, u32[]{:S(2)}) collective-permute-start(f32[4,13,2048]{2,1,0:T(8,128)S(1)} %pad_maximum_fusion), channel_id=1, source_target_pairs={{0,4},{4,8},{8,12},{12,16},{16,20},{20,24},{24,28},{28,32},{32,36}... | collective-permute-start | bytes 1277960 | tf_op jit(solution)/shard_map/ppermute | solution.py:258
  7.7 7.1 %copy-start.7 = (s32[2048,1]{0,1:T(1,128)S(1)}, s32[2048,1]{0,1:T(1,128)}, u32[]{:S(2)}) copy-start(s32[2048,1]{0,1:T(1,128)} %param.16) | copy-start | bytes 24580
  7.8 15.5 %collective-permute-start.1 = (f32[4,13,2048]{2,1,0:T(8,128)S(1)}, f32[4,13,2048]{2,1,0:T(8,128)S(1)}, u32[]{:S(2)}, u32[]{:S(2)}) collective-permute-start(f32[4,13,2048]{2,1,0:T(8,128)S(1)} %pad_maximum_fusion.1), channel_id=1, source_target_pairs={{4,0},{8,4},{12,8},{16,12},{20,16},{24,20},{28,24},{32,28},{36,32}... | collective-permute-start | bytes 1277960 | tf_op jit(solution)/shard_map/ppermute | solution.py:258
  9.7 13.6 %collective-permute-start.2 = (f32[5,4,8,128]{3,2,1,0:T(8,128)S(1)}, f32[5,4,8,128]{3,2,1,0:T(8,128)}, u32[]{:S(2)}, u32[]{:S(2)}) collective-permute-start(f32[5,4,8,128]{3,2,1,0:T(8,128)S(1)} %pad_maximum_fusion.2), channel_id=1, source_target_pairs={{0,1},{1,2},{2,3},{3,0},{4,5},{5,6},{6,7},{7,4},{8,9},{9,10},{10,1... | collective-permute-start | bytes 245768 | tf_op jit(solution)/shard_map/ppermute | solution.py:258
  12.6 10.7 %collective-permute-start.3 = (f32[5,4,8,128]{3,2,1,0:T(8,128)S(1)}, f32[5,4,8,128]{3,2,1,0:T(8,128)}, u32[]{:S(2)}, u32[]{:S(2)}) collective-permute-start(f32[5,4,8,128]{3,2,1,0:T(8,128)S(1)} %pad_maximum_fusion.3), channel_id=1, source_target_pairs={{1,0},{2,1},{3,2},{0,3},{5,4},{6,5},{7,6},{4,7},{9,8},{10,9},{11,1... | collective-permute-start | bytes 245768 | tf_op jit(solution)/shard_map/ppermute | solution.py:258
  14.8 1.7 %copy-start.8 = (s32[2048]{0:T(1024)S(1)}, s32[2048]{0:T(1024)}, u32[]{:S(2)}) copy-start(s32[2048]{0:T(1024)} %param.17) | copy-start | bytes 24580
  14.8 2.0 %copy-start.6 = (f32[4,2048]{1,0:T(4,128)S(1)}, f32[4,2048]{1,0:T(4,128)}, u32[]{:S(2)}) copy-start(f32[4,2048]{1,0:T(4,128)} %param.13) | copy-start | bytes 98308
  14.8 2.0 %copy-start.9 = (f32[2048]{0:T(1024)S(1)}, f32[2048]{0:T(1024)}, u32[]{:S(2)}) copy-start(f32[2048]{0:T(1024)} %param.15) | copy-start | bytes 24580
  14.8 2.1 %copy-start.10 = (f32[2048]{0:T(1024)S(1)}, f32[2048]{0:T(1024)}, u32[]{:S(2)}) copy-start(f32[2048]{0:T(1024)} %param.14) | copy-start | bytes 24580
  18.9 18.4 %copy-start.5 = (s32[4,8,2048]{2,1,0:T(8,128)S(1)}, s32[4,8,2048]{2,1,0:T(8,128)}, u32[]{:S(2)}) copy-start(s32[4,8,2048]{2,1,0:T(8,128)} %param.12) | copy-start | bytes 786436
  23.3 14.1 %copy-start.3 = (f32[4,13,2048]{2,1,0:T(8,128)}, f32[4,13,2048]{2,1,0:T(8,128)S(1)}, u32[]{:S(2)}) copy-start(f32[4,13,2048]{2,1,0:T(8,128)S(1)} %collective-permute-done.xl_ref) | copy-start | bytes 1277956
  23.3 14.1 %copy-start.4 = (f32[4,13,2048]{2,1,0:T(8,128)}, f32[4,13,2048]{2,1,0:T(8,128)S(1)}, u32[]{:S(2)}) copy-start(f32[4,13,2048]{2,1,0:T(8,128)S(1)} %collective-permute-done.1.xh_ref) | copy-start | bytes 1277956
  24.3 21.5 %all-to-all-start = ((f32[64,1,512]{2,1,0:T(1,128)}), f32[64,1,512]{2,1,0:T(1,128)S(1)}, u32[]{:S(2)}, u32[]{:S(2)}) async-start(f32[64,1,512]{2,1,0:T(1,128)} %copy.26), calls=%async_computation | async-start | bytes 262144 | tf_op jit(solution)/shard_map/all_to_all | solution.py:327
  44.3 1.8 %copy-start = (f32[4,4,8,2048]{3,2,1,0:T(8,128)S(1)}, f32[4,4,8,2048]{3,2,1,0:T(8,128)}, u32[]{:S(2)}) copy-start(f32[4,4,8,2048]{3,2,1,0:T(8,128)} %su_ref.1) | copy-start | bytes 3145732
  51.6 14.8 %copy-start.1 = (f32[4,4,8,2048]{3,2,1,0:T(8,128)S(1)}, f32[4,4,8,2048]{3,2,1,0:T(8,128)}, u32[]{:S(2)}) copy-start(f32[4,4,8,2048]{3,2,1,0:T(8,128)} %shard_map.104) | copy-start | bytes 3145732
  51.6 14.8 %copy-start.2 = (f32[4,4,8,2048]{3,2,1,0:T(8,128)S(1)}, f32[4,4,8,2048]{3,2,1,0:T(8,128)}, u32[]{:S(2)}) copy-start(f32[4,4,8,2048]{3,2,1,0:T(8,128)} %param.10) | copy-start | bytes 3145732
  52.6 16.3 %all-to-all-start.1 = ((f32[64,1,256]{2,1,0:T(1,128)}), f32[64,1,256]{2,1,0:T(1,128)S(1)}, u32[]{:S(2)}, u32[]{:S(2)}) async-start(f32[64,1,256]{2,1,0:T(1,128)} %copy.29), calls=%async_computation.1 | async-start | bytes 131072 | tf_op jit(solution)/shard_map/all_to_all | solution.py:335

commit v15 on v13

--- a/solution.py
+++ b/solution.py
@@ -162,24 +162,24 @@
     return jnp.concatenate(hots, axis=0)
 
 
-def gather_kernel(x_ref, pay_ref, flux_ref, pieces_ref, iota_ref):
+def gather_kernel(x_ref, pay_ref, flux_ref, iota_ref):
     rows, cols = x_ref.shape
     fields = 4
     per_field = rows // fields
     block = pay_ref.shape[1]
 
+    rows = rows // 2
+    per_field = rows // fields
+
     @pl.when(pl.program_id(0) == 0)
     def _():
-        parts = _pieces(x_ref[...], 2)
-        for i, p in enumerate(parts):
-            pieces_ref[i * rows:(i + 1) * rows, :] = p
         iota_ref[...] = lax.broadcasted_iota(jnp.int32, iota_ref.shape, 0).astype(jnp.bfloat16)
 
     pay = pay_ref[...]
     cell = (pay[6:7] + 0.5).astype(jnp.int32)
     row = cell // cols
     hot = _one_hot(cell, cols, iota_ref[...])
-    picked = jnp.dot(pieces_ref[...], hot, preferred_element_type=jnp.float32)
+    picked = jnp.dot(x_ref[...], hot, preferred_element_type=jnp.float32)
     value = picked[0:rows] + picked[rows:2 * rows]
     pick_row = lax.broadcasted_iota(jnp.int32, (per_field, block), 0) == row
     gathered = jnp.concatenate(
@@ -224,13 +224,28 @@
         ],
         out_specs=pl.BlockSpec((4, block), lambda j: (0, j)),
         out_shape=jax.ShapeDtypeStruct((4, slots), jnp.float32),
-        scratch_shapes=[pltpu.VMEM((2 * rows, cols), jnp.bfloat16),
-                        pltpu.VMEM((256, block), jnp.bfloat16)],
+        scratch_shapes=[pltpu.VMEM((256, block), jnp.bfloat16)],
         compiler_params=pltpu.CompilerParams(dimension_semantics=("arbitrary",),
                                              vmem_limit_bytes=48 * 1024 * 1024),
-        cost_estimate=pl.CostEstimate(flops=2 * (2 * rows) * cols * slots, transcendentals=0,
-                                      bytes_accessed=4 * (rows * cols + 12 * slots)),
+        cost_estimate=pl.CostEstimate(flops=2 * rows * cols * slots, transcendentals=0,
+                                      bytes_accessed=2 * rows * cols + 48 * slots),
     )(x, pay)
+
+
+def split_kernel(x_ref, out_ref):
+    rows = x_ref.shape[0]
+    parts = _pieces(x_ref[...], 2)
+    for i, p in enumerate(parts):
+        out_ref[i * rows:(i + 1) * rows, :] = p
+
+
+def split_pieces(x):
+    rows, cols = x.shape
+    return pl.pallas_call(
+        split_kernel,
+        out_shape=jax.ShapeDtypeStruct((2 * rows, cols), jnp.bfloat16),
+        cost_estimate=pl.CostEstimate(flops=4 * rows * cols, transcendentals=0, bytes_accessed=8 * rows * cols),
+    )(x)
 
 
 def owner_scatter(pay, flux, rows, cols, block=1024):
@@ -335,9 +350,10 @@
     )
     received = lax.all_to_all(outgoing, "gx", 0, 0, tiled=True)
     tend = stencil(state, eddy, x_low, x_high, y_low, y_high)
-    tend, received = lax.optimization_barrier((tend, received))
+    state_pieces = split_pieces(state.reshape(4 * levels * cells_x, cells_y))
+    tend, state_pieces, received = lax.optimization_barrier((tend, state_pieces, received))
     pay = jnp.transpose(received.reshape(owners_gx, 8, capacity), (1, 0, 2)).reshape(8, slots)
-    flux_slots = owner_gather(state.reshape(4 * levels * cells_x, cells_y), pay)
+    flux_slots = owner_gather(state_pieces, pay)
     wall_flux = jnp.transpose(flux_slots.reshape(4, owners_gx, capacity), (1, 0, 2)).reshape(owners_gx, -1)
     wall_flux, pay, flux_slots = lax.optimization_barrier((wall_flux, pay, flux_slots))
     forcing = owner_scatter(pay, flux_slots, 4 * levels * cells_x, cells_y).reshape(state.shape)

time: 69.5 us -> 69 us (level)
  starting transfers between devices: 29.3 us -> 26.6 us
  Pallas kernels: 17.8 us -> 19.9 us
    all_to_all x1, starting transfers between devices: 12.6 us -> 10.1 us  [local(): received = lax.all_to_all(outgoing, 'gx', 0, 0, tiled=True)]
    pallas_call x0 -> x1, Pallas kernels: none -> 2.39 us  [split_pieces(): pl.pallas_call(split_kernel, out_shape=jax.ShapeDtypeStruct((2 * rows, co...]
  transfers between devices with their start and end apart: 6 -> 6, of which waited for: 2 -> 2; matrix products, arithmetic and copies ran while one was open for 15% -> 15% of each run, Pallas kernels for 18% -> 21%
where the time goes in v15:
time: 69 us; the launch traced here: 68.5 us
  starting transfers between devices  26.6 us (39%)
  Pallas kernels  19.9 us (29%)
  local copies, waits for them, and re-layouts  9.63 us (14%)
  matrix products  5.56 us (8%)
  waiting for transfers between devices  3.08 us (4%)
  other arithmetic  2.82 us (4%)
  between operations  1.01 us (1%)
    all_to_all x1, starting transfers between devices, local(): received = lax.all_to_all(outgoing, 'gx', 0, 0, tiled=True)  10.1 us
    ppermute x4, starting transfers between devices, shift_pair(): return (lax.ppermute(last, axis, up), lax.ppermute(leading, axis, down))  8.4 us
    all_to_all x1, starting transfers between devices, local(): returned = lax.all_to_all(wall_flux, 'gx', 0, 0, tiled=True)  8.06 us
    pallas_call x1, Pallas kernels, stencil(): pl.pallas_call(stencil_kernel, grid=(levels,), in_specs=[pl.BlockSpec((fi...  6.75 us
    pallas_call x1, Pallas kernels, owner_scatter(): pl.pallas_call(scatter_kernel, grid=(slots // block,), in_specs=[pl.Block...  5.44 us
    pallas_call x1, Pallas kernels, owner_gather(): pl.pallas_call(gather_kernel, grid=(slots // block,), in_specs=[pl.BlockS...  5.29 us
    pallas_call x1, Pallas kernels, split_pieces(): pl.pallas_call(split_kernel, out_shape=jax.ShapeDtypeStruct((2 * rows, co...  2.39 us
    transpose x3, local copies, waits for them, and re-layouts, x_rows(): jnp.transpose(state[:, :, lo:hi], (1, 0, 2, 3)).reshape(levels, -1, cells_y)  2.26 us
  transfers between devices with their start and end apart: 6, of which 2 were waited for; matrix products, arithmetic and copies ran while one was open for 15% of the time, Pallas kernels for 21%

profile of v15, /device:TPU:1, one launch (start us, length us, event | category | flops | bytes accessed | tf_op | source)
XLA Modules:
  0.0 68.5 jit_solution(9491176198284051301)
XLA Ops:
  0.6 1.7 %slice_bitcast_fusion = (f32[4,4,3,2048]{3,2,0,1:T(4,128)S(1)}, f32[4,4,3,2048]{3,2,0,1:T(4,128)S(1)}) fusion(f32[4,4,8,2048]{3,2,1,0:T(8,128)} %su_ref.1), kind=kLoop, calls=%fused_computation.20 | loop fusion | bytes 1572864 | tf_op jit(solution)/shard_map/transpose | solution.py:296
  2.4 0.3 copy.25
  2.6 0.2 copy.26
  2.9 1.1 %fusion.24 = (f32[4,1,2048]{2,1,0:T(1,128)S(1)}, f32[4,1,2048]{2,1,0:T(1,128)S(1)}) fusion(f32[4,8,2048]{2,1,0:T(8,128)} %eu_ref.1), kind=kLoop, calls=%fused_computation.48 | loop fusion | bytes 131072 | tf_op jit(solution)/shard_map/slice | solution.py:297
  4.0 0.1 pad_maximum_fusion
  4.0 3.1 %collective-permute-start = (f32[4,13,2048]{2,1,0:T(8,128)S(1)}, f32[4,13,2048]{2,1,0:T(8,128)S(1)}, u32[]{:S(2)}, u32[]{:S(2)}) collective-permute-start(f32[4,13,2048]{2,1,0:T(8,128)S(1)} %pad_maximum_fusion), channel_id=1, source_target_pairs={{0,4},{4,8},{8,12},{12,16},{16,20},{20,24},{24,28},{28,32},{32,36}... | collective-permute-start | bytes 1277960 | tf_op jit(solution)/shard_map/ppermute | solution.py:273
  7.1 0.3 copy.27
  7.4 0.0 copy-start.7
  7.4 0.2 copy.28
  7.6 0.1 pad_maximum_fusion.1
  7.7 0.3 collective-permute-start.1
  8.0 1.0 %fusion.23 = (f32[4,4,8,3]{3,2,1,0:T(8,128)S(1)}, f32[4,4,8,3]{3,2,1,0:T(8,128)S(1)}) fusion(f32[4,4,8,2048]{3,2,1,0:T(8,128)} %su_ref.1), kind=kLoop, calls=%fused_computation.47 | loop fusion | bytes 6144 | tf_op jit(solution)/shard_map/slice | solution.py:304
  8.9 0.2 reshape.119
  9.2 0.2 reshape.115
  9.4 0.9 %slice_reduce_fusion = (f32[4,8]{1,0:T(4,128)S(1)}, f32[4,8]{1,0:T(4,128)S(1)}) fusion(f32[4,8,2048]{2,1,0:T(8,128)} %eu_ref.1), kind=kLoop, calls=%fused_computation.40 | loop fusion | bytes 512 | tf_op jit(solution)/shard_map/slice | solution.py:304
  10.2 0.1 reshape.116
  10.3 0.1 reshape.120
  10.5 5.0 %collective-permute-start.3 = (f32[416]{0:T(512)S(1)}, f32[416]{0:T(512)S(1)}, u32[]{:S(2)}, u32[]{:S(2)}) collective-permute-start(f32[416]{0:T(512)S(1)} %get-tuple-element.51), channel_id=1, source_target_pairs={{1,0},{2,1},{3,2},{0,3},{5,4},{6,5},{7,6},{4,7},{9,8},{10,9},{11,1... | collective-permute-start | bytes 5000 | tf_op jit(solution)/shard_map/ppermute | solution.py:273
  15.5 0.0 collective-permute-start.2
  15.5 0.0 copy-done.7
  15.5 0.0 copy-start.9
  15.5 0.0 copy-start.10
  15.5 1.7 %fusion.10 = f32[2048]{0:T(1024)S(1)} fusion(s32[2048]{0:T(1024)S(1)} %bitcast.49), kind=kOutput, calls=%fused_computation.10 | convolution fusion | flops 541849600 | bytes 16384 | tf_op jit(solution)/shard_map/dot_general | solution.py:331
  17.3 0.3 convolution_subtract_fusion
  17.5 0.0 copy-done.8
  17.6 0.0 copy-done.6
  17.6 0.0 copy-done.9
  17.6 0.0 copy-done.10
  17.6 1.9 %fusion.7 = f32[7,64,64]{2,1,0:T(8,128)S(1)} fusion(f32[64,2048]{1,0:T(8,128)S(1)} %fusion.16, f32[7,2048]{1,0:T(8,128)S(1)} %pad_maximum_fusion.2, f32[2048]{0:T(1024)S(1)} %fusion.10, f32[64,64]{1,0:T(8,128)S(1)} %convolution_subtract_fusion, f32[7]{0:T(128)S(1)} %compare_convert_fusion), kind=kOutput, calls=%fused_computation.9 | convolution fusion | flops 705748992 | bytes 720924 | tf_op jit(solution)/shard_map/cof,fk->cok/dot_general | solution.py:342
  19.6 0.2 copy.31
  19.8 0.1 reshape.123
  19.9 2.4 %shard_map.105.x_ref = bf16[256,2048]{1,0:T(8,128)(2,1)} custom-call(f32[128,2048]{1,0:T(8,128)} %bitcast.38), custom_call_target="tpu_custom_call" | custom-call | flops 1048576 | bytes 2097152 | tf_op jit(solution)/shard_map/pallas_call | solution.py:244
  22.3 0.0 collective-permute-done.3
  22.3 0.2 reshape.121
  22.5 0.1 reshape.133
  22.6 0.0 collective-permute-done.2
  22.6 0.2 reshape.117
  22.8 0.1 reshape.132
  22.9 0.7 select_maximum_fusion.yh_ref
  23.6 0.7 %select_maximum_fusion.1.yl_ref = f32[5,4,8,128]{3,2,1,0:T(8,128)} fusion(f32[1,4,8,1]{3,2,1,0:T(8,128)S(1)} %reshape.132, f32[4,4,8,3]{3,2,1,0:T(8,128)S(1)} %reshape.117), kind=kLoop, calls=%fused_computation.35 | loop fusion | flops 102400 | bytes 83584 | tf_op jit(solution)/shard_map/concatenate | solution.py:311
  24.3 0.0 collective-permute-done.xl_ref
  24.3 0.0 collective-permute-done.1.xh_ref
  24.3 0.0 copy-start.4
  24.3 1.0 %copy.32 = f32[64,1,512]{2,1,0:T(1,128)} copy(f32[64,1,512]{2,0,1:T(8,128)S(1)} %bitcast.42) | data formatting | bytes 262144 | tf_op jit(solution)/shard_map/all_to_all | solution.py:351
  25.3 10.1 %all-to-all-start = ((f32[64,1,512]{2,1,0:T(1,128)}), f32[64,1,512]{2,1,0:T(1,128)S(1)}, u32[]{:S(2)}, u32[]{:S(2)}) async-start(f32[64,1,512]{2,1,0:T(1,128)} %copy.32), calls=%async_computation | async-start | bytes 262144 | tf_op jit(solution)/shard_map/all_to_all | solution.py:351
  35.4 0.0 copy-done.5
  35.5 6.7 %shard_map.104 = f32[4,4,8,2048]{3,2,1,0:T(8,128)} custom-call(f32[4,4,8,2048]{3,2,1,0:T(8,128)} %su_ref.1, f32[4,4,8,2048]{3,2,1,0:T(8,128)} %su_ref.1, f32[4,4,8,2048]{3,2,1,0:T(8,128)} %su_ref.1, f32[4,8,2048]{2,1,0:T(8,128)} %eu_ref.1, f32[4,8,2048]{2,1,0:T(8,128)} %eu_ref.1, f32[4,8,2048]{2,1,0:T(8,128)} %eu_ref.1, f32[4,13,2048]{2,1,0:T(8,128)} %copy-done.3, ...), custom_call_target="tpu_custom_call" | custom-call | flops 52428800 | bytes 6291456 | tf_op jit(solution)/shard_map/pallas_call | solution.py:120
  42.2 1.7 %all-to-all-done = f32[64,1,512]{2,1,0:T(1,128)S(1)} async-done(((f32[64,1,512]{2,1,0:T(1,128)}), f32[64,1,512]{2,1,0:T(1,128)S(1)}, u32[]{:S(2)}, u32[]{:S(2)}) %all-to-all-start) | async-done | bytes 131104 | tf_op jit(solution)/shard_map/all_to_all | solution.py:351
  43.9 0.1 reshape.125
  44.0 0.1 copy.33
  44.1 0.1 reshape.126.pay_ref
  44.2 5.3 %shard_map.106.flux_ref = f32[4,4096]{1,0:T(4,128)S(1)} custom-call(bf16[256,2048]{1,0:T(8,128)(2,1)S(1)} %copy-done, f32[8,4096]{1,0:T(8,128)S(1)} %reshape.126.pay_ref), custom_call_target="tpu_custom_call" | custom-call | flops 4294967296 | bytes 1245184 | tf_op jit(solution)/shard_map/pallas_call | solution.py:218
  49.5 0.0 copy-start.1
  49.5 0.0 copy-start.2
  49.5 0.1 reshape.127
  49.6 0.1 copy.45
  49.7 0.1 reshape.128
  49.9 0.7 %copy.35 = f32[64,1,256]{2,1,0:T(1,128)} copy(f32[64,1,256]{2,0,1:T(8,128)S(1)} %bitcast.45) | data formatting | bytes 131072 | tf_op jit(solution)/shard_map/all_to_all | solution.py:360
  50.6 8.1 %all-to-all-start.1 = ((f32[64,1,256]{2,1,0:T(1,128)}), f32[64,1,256]{2,1,0:T(1,128)S(1)}, u32[]{:S(2)}, u32[]{:S(2)}) async-start(f32[64,1,256]{2,1,0:T(1,128)} %copy.35), calls=%async_computation.1 | async-start | bytes 131072 | tf_op jit(solution)/shard_map/all_to_all | solution.py:360
  58.6 5.4 %shard_map.107 = f32[128,2048]{1,0:T(8,128)S(1)} custom-call(f32[8,4096]{1,0:T(8,128)S(1)} %reshape.126.pay_ref, f32[4,4096]{1,0:T(4,128)S(1)} %shard_map.106.flux_ref), custom_call_target="tpu_custom_call" | custom-call | flops 262144 | bytes 1048576 | tf_op jit(solution)/shard_map/pallas_call | solution.py:253
  64.1 1.2 %multiply_add_fusion = f32[4,4,8,2048]{3,2,1,0:T(8,128)} fusion(f32[4,4,8,2048]{3,2,1,0:T(8,128)S(1)} %copy-done.2, f32[4,4,8,2048]{3,2,1,0:T(8,128)S(1)} %copy-done.1, f32[4,4,8,2048]{3,2,1,0:T(8,128)S(1)} %bitcast.37, f32[4,8,2048]{2,1,0:T(8,128)S(1)} %convert_subtract_fusion), kind=kLoop, calls=%fused_computation.12 | loop fusion | flops 1048576 | bytes 4456448 | tf_op jit(solution)/shard_map/add | solution.py:362
  65.3 1.4 %all-to-all-done.1 = f32[64,1,256]{2,1,0:T(1,128)S(1)} async-done(((f32[64,1,256]{2,1,0:T(1,128)}), f32[64,1,256]{2,1,0:T(1,128)S(1)}, u32[]{:S(2)}, u32[]{:S(2)}) %all-to-all-start.1) | async-done | bytes 65568 | tf_op jit(solution)/shard_map/all_to_all | solution.py:360
  66.7 0.1 reshape.130
  66.8 1.7 %fusion.6 = f32[4,2048]{1,0:T(4,128)} fusion(f32[64,2048]{1,0:T(8,128)S(1)} %fusion.16, f32[2048]{0:T(1024)S(1)} %fusion.10, f32[4,64,64]{2,0,1:T(4,128)S(1)} %bitcast.47), kind=kOutput, calls=%fused_computation.8 | convolution fusion | flops 403824640 | bytes 630784 | tf_op jit(solution)/shard_map/cok,fk->cof/dot_general | solution.py:365
  (25 shorter events, 0.2 us)
Async XLA Ops:
  4.0 20.3 %collective-permute-start = (f32[4,13,2048]{2,1,0:T(8,128)S(1)}, f32[4,13,2048]{2,1,0:T(8,128)S(1)}, u32[]{:S(2)}, u32[]{:S(2)}) collective-permute-start(f32[4,13,2048]{2,1,0:T(8,128)S(1)} %pad_maximum_fusion), channel_id=1, source_target_pairs={{0,4},{4,8},{8,12},{12,16},{16,20},{20,24},{24,28},{28,32},{32,36}... | collective-permute-start | bytes 1277960 | tf_op jit(solution)/shard_map/ppermute | solution.py:273
  7.4 8.1 %copy-start.7 = (s32[2048,1]{0,1:T(1,128)S(1)}, s32[2048,1]{0,1:T(1,128)}, u32[]{:S(2)}) copy-start(s32[2048,1]{0,1:T(1,128)} %param.16) | copy-start | bytes 24580
  7.7 16.6 %collective-permute-start.1 = (f32[4,13,2048]{2,1,0:T(8,128)S(1)}, f32[4,13,2048]{2,1,0:T(8,128)S(1)}, u32[]{:S(2)}, u32[]{:S(2)}) collective-permute-start(f32[4,13,2048]{2,1,0:T(8,128)S(1)} %pad_maximum_fusion.1), channel_id=1, source_target_pairs={{4,0},{8,4},{12,8},{16,12},{20,16},{24,20},{28,24},{32,28},{36,32}... | collective-permute-start | bytes 1277960 | tf_op jit(solution)/shard_map/ppermute | solution.py:273
  10.5 11.8 %collective-permute-start.3 = (f32[416]{0:T(512)S(1)}, f32[416]{0:T(512)S(1)}, u32[]{:S(2)}, u32[]{:S(2)}) collective-permute-start(f32[416]{0:T(512)S(1)} %get-tuple-element.51), channel_id=1, source_target_pairs={{1,0},{2,1},{3,2},{0,3},{5,4},{6,5},{7,6},{4,7},{9,8},{10,9},{11,1... | collective-permute-start | bytes 5000 | tf_op jit(solution)/shard_map/ppermute | solution.py:273
  15.5 7.1 %collective-permute-start.2 = (f32[416]{0:T(512)S(1)}, f32[416]{0:T(512)S(1)}, u32[]{:S(2)}, u32[]{:S(2)}) collective-permute-start(f32[416]{0:T(512)S(1)} %get-tuple-element.50), channel_id=1, source_target_pairs={{0,1},{1,2},{2,3},{3,0},{4,5},{5,6},{6,7},{7,4},{8,9},{9,10},{10,1... | collective-permute-start | bytes 5000 | tf_op jit(solution)/shard_map/ppermute | solution.py:273
  15.5 2.0 %copy-start.8 = (s32[2048]{0:T(1024)S(1)}, s32[2048]{0:T(1024)}, u32[]{:S(2)}) copy-start(s32[2048]{0:T(1024)} %param.17) | copy-start | bytes 24580
  15.5 2.1 %copy-start.6 = (f32[4,2048]{1,0:T(4,128)S(1)}, f32[4,2048]{1,0:T(4,128)}, u32[]{:S(2)}) copy-start(f32[4,2048]{1,0:T(4,128)} %param.13) | copy-start | bytes 98308
  15.5 2.1 %copy-start.9 = (f32[2048]{0:T(1024)S(1)}, f32[2048]{0:T(1024)}, u32[]{:S(2)}) copy-start(f32[2048]{0:T(1024)} %param.15) | copy-start | bytes 24580
  15.5 2.1 %copy-start.10 = (f32[2048]{0:T(1024)S(1)}, f32[2048]{0:T(1024)}, u32[]{:S(2)}) copy-start(f32[2048]{0:T(1024)} %param.14) | copy-start | bytes 24580
  19.9 15.5 %copy-start.5 = (s32[4,8,2048]{2,1,0:T(8,128)S(1)}, s32[4,8,2048]{2,1,0:T(8,128)}, u32[]{:S(2)}) copy-start(s32[4,8,2048]{2,1,0:T(8,128)} %param.12) | copy-start | bytes 786436
  24.3 11.1 %copy-start.3 = (f32[4,13,2048]{2,1,0:T(8,128)}, f32[4,13,2048]{2,1,0:T(8,128)S(1)}, u32[]{:S(2)}) copy-start(f32[4,13,2048]{2,1,0:T(8,128)S(1)} %collective-permute-done.xl_ref) | copy-start | bytes 1277956
  24.3 11.1 %copy-start.4 = (f32[4,13,2048]{2,1,0:T(8,128)}, f32[4,13,2048]{2,1,0:T(8,128)S(1)}, u32[]{:S(2)}) copy-start(f32[4,13,2048]{2,1,0:T(8,128)S(1)} %collective-permute-done.1.xh_ref) | copy-start | bytes 1277956
  25.3 18.6 %all-to-all-start = ((f32[64,1,512]{2,1,0:T(1,128)}), f32[64,1,512]{2,1,0:T(1,128)S(1)}, u32[]{:S(2)}, u32[]{:S(2)}) async-start(f32[64,1,512]{2,1,0:T(1,128)} %copy.32), calls=%async_computation | async-start | bytes 262144 | tf_op jit(solution)/shard_map/all_to_all | solution.py:351
  42.2 2.0 %copy-start = (bf16[256,2048]{1,0:T(8,128)(2,1)S(1)}, bf16[256,2048]{1,0:T(8,128)(2,1)}, u32[]{:S(2)}) copy-start(bf16[256,2048]{1,0:T(8,128)(2,1)} %shard_map.105.x_ref) | copy-start | bytes 3145732
  49.5 14.6 %copy-start.1 = (f32[4,4,8,2048]{3,2,1,0:T(8,128)S(1)}, f32[4,4,8,2048]{3,2,1,0:T(8,128)}, u32[]{:S(2)}) copy-start(f32[4,4,8,2048]{3,2,1,0:T(8,128)} %shard_map.104) | copy-start | bytes 3145732
  49.5 14.6 %copy-start.2 = (f32[4,4,8,2048]{3,2,1,0:T(8,128)S(1)}, f32[4,4,8,2048]{3,2,1,0:T(8,128)}, u32[]{:S(2)}) copy-start(f32[4,4,8,2048]{3,2,1,0:T(8,128)} %param.10) | copy-start | bytes 3145732
  50.6 16.1 %all-to-all-start.1 = ((f32[64,1,256]{2,1,0:T(1,128)}), f32[64,1,256]{2,1,0:T(1,128)S(1)}, u32[]{:S(2)}, u32[]{:S(2)}) async-start(f32[64,1,256]{2,1,0:T(1,128)} %copy.35), calls=%async_computation.1 | async-start | bytes 131072 | tf_op jit(solution)/shard_map/all_to_all | solution.py:360

commit v16 on v15

--- a/solution.py
+++ b/solution.py
@@ -212,7 +212,7 @@
     forcing_ref[...] += added[0:rows] + added[rows:2 * rows]
 
 
-def owner_gather(x, pay, block=1024):
+def owner_gather(x, pay, block=2048):
     rows, cols = x.shape
     slots = pay.shape[1]
     return pl.pallas_call(

time: 69 us -> 68.6 us (level)
  no operation moved by 1% of the time
where the time goes in v16:
time: 68.6 us; the launch traced here: 68.1 us
  starting transfers between devices  26.6 us (39%)
  Pallas kernels  19.5 us (28%)
  local copies, waits for them, and re-layouts  9.63 us (14%)
  matrix products  5.56 us (8%)
  waiting for transfers between devices  3.07 us (4%)
  other arithmetic  2.82 us (4%)
  between operations  1.01 us (1%)
    all_to_all x1, starting transfers between devices, local(): received = lax.all_to_all(outgoing, 'gx', 0, 0, tiled=True)  10.1 us
    ppermute x4, starting transfers between devices, shift_pair(): return (lax.ppermute(last, axis, up), lax.ppermute(leading, axis, down))  8.4 us
    all_to_all x1, starting transfers between devices, local(): returned = lax.all_to_all(wall_flux, 'gx', 0, 0, tiled=True)  8.06 us
    pallas_call x1, Pallas kernels, stencil(): pl.pallas_call(stencil_kernel, grid=(levels,), in_specs=[pl.BlockSpec((fi...  6.75 us
    pallas_call x1, Pallas kernels, owner_scatter(): pl.pallas_call(scatter_kernel, grid=(slots // block,), in_specs=[pl.Block...  5.45 us
    pallas_call x1, Pallas kernels, owner_gather(): pl.pallas_call(gather_kernel, grid=(slots // block,), in_specs=[pl.BlockS...  4.9 us
    pallas_call x1, Pallas kernels, split_pieces(): pl.pallas_call(split_kernel, out_shape=jax.ShapeDtypeStruct((2 * rows, co...  2.39 us
    transpose x3, local copies, waits for them, and re-layouts, x_rows(): jnp.transpose(state[:, :, lo:hi], (1, 0, 2, 3)).reshape(levels, -1, cells_y)  2.26 us
  transfers between devices with their start and end apart: 6, of which 2 were waited for; matrix products, arithmetic and copies ran while one was open for 15% of the time, Pallas kernels for 21%

profile of v16, /device:TPU:1, one launch (start us, length us, event | category | flops | bytes accessed | tf_op | source)
XLA Modules:
  0.0 68.1 jit_solution(16116606383028830421)
XLA Ops:
  0.6 1.7 %slice_bitcast_fusion = (f32[4,4,3,2048]{3,2,0,1:T(4,128)S(1)}, f32[4,4,3,2048]{3,2,0,1:T(4,128)S(1)}) fusion(f32[4,4,8,2048]{3,2,1,0:T(8,128)} %su_ref.1), kind=kLoop, calls=%fused_computation.20 | loop fusion | bytes 1572864 | tf_op jit(solution)/shard_map/transpose | solution.py:296
  2.4 0.3 copy.25
  2.6 0.2 copy.26
  2.9 1.1 %fusion.24 = (f32[4,1,2048]{2,1,0:T(1,128)S(1)}, f32[4,1,2048]{2,1,0:T(1,128)S(1)}) fusion(f32[4,8,2048]{2,1,0:T(8,128)} %eu_ref.1), kind=kLoop, calls=%fused_computation.48 | loop fusion | bytes 131072 | tf_op jit(solution)/shard_map/slice | solution.py:297
  4.0 0.1 pad_maximum_fusion
  4.0 3.1 %collective-permute-start = (f32[4,13,2048]{2,1,0:T(8,128)S(1)}, f32[4,13,2048]{2,1,0:T(8,128)S(1)}, u32[]{:S(2)}, u32[]{:S(2)}) collective-permute-start(f32[4,13,2048]{2,1,0:T(8,128)S(1)} %pad_maximum_fusion), channel_id=1, source_target_pairs={{0,4},{4,8},{8,12},{12,16},{16,20},{20,24},{24,28},{28,32},{32,36}... | collective-permute-start | bytes 1277960 | tf_op jit(solution)/shard_map/ppermute | solution.py:273
  7.1 0.3 copy.27
  7.4 0.0 copy-start.7
  7.4 0.2 copy.28
  7.6 0.1 pad_maximum_fusion.1
  7.7 0.3 collective-permute-start.1
  8.0 1.0 %fusion.23 = (f32[4,4,8,3]{3,2,1,0:T(8,128)S(1)}, f32[4,4,8,3]{3,2,1,0:T(8,128)S(1)}) fusion(f32[4,4,8,2048]{3,2,1,0:T(8,128)} %su_ref.1), kind=kLoop, calls=%fused_computation.47 | loop fusion | bytes 6144 | tf_op jit(solution)/shard_map/slice | solution.py:304
  8.9 0.2 reshape.119
  9.2 0.2 reshape.115
  9.4 0.9 %slice_reduce_fusion = (f32[4,8]{1,0:T(4,128)S(1)}, f32[4,8]{1,0:T(4,128)S(1)}) fusion(f32[4,8,2048]{2,1,0:T(8,128)} %eu_ref.1), kind=kLoop, calls=%fused_computation.40 | loop fusion | bytes 512 | tf_op jit(solution)/shard_map/slice | solution.py:304
  10.2 0.1 reshape.116
  10.3 0.1 reshape.120
  10.5 5.0 %collective-permute-start.3 = (f32[416]{0:T(512)S(1)}, f32[416]{0:T(512)S(1)}, u32[]{:S(2)}, u32[]{:S(2)}) collective-permute-start(f32[416]{0:T(512)S(1)} %get-tuple-element.51), channel_id=1, source_target_pairs={{1,0},{2,1},{3,2},{0,3},{5,4},{6,5},{7,6},{4,7},{9,8},{10,9},{11,1... | collective-permute-start | bytes 5000 | tf_op jit(solution)/shard_map/ppermute | solution.py:273
  15.5 0.0 collective-permute-start.2
  15.5 0.0 copy-done.7
  15.5 0.0 copy-start.9
  15.5 0.0 copy-start.10
  15.5 1.7 %fusion.10 = f32[2048]{0:T(1024)S(1)} fusion(s32[2048]{0:T(1024)S(1)} %bitcast.49), kind=kOutput, calls=%fused_computation.10 | convolution fusion | flops 541849600 | bytes 16384 | tf_op jit(solution)/shard_map/dot_general | solution.py:331
  17.3 0.3 convolution_subtract_fusion
  17.6 0.0 copy-done.6
  17.6 0.0 copy-done.9
  17.6 0.0 copy-done.10
  17.6 1.9 %fusion.7 = f32[7,64,64]{2,1,0:T(8,128)S(1)} fusion(f32[64,2048]{1,0:T(8,128)S(1)} %fusion.16, f32[7,2048]{1,0:T(8,128)S(1)} %pad_maximum_fusion.2, f32[2048]{0:T(1024)S(1)} %fusion.10, f32[64,64]{1,0:T(8,128)S(1)} %convolution_subtract_fusion, f32[7]{0:T(128)S(1)} %compare_convert_fusion), kind=kOutput, calls=%fused_computation.9 | convolution fusion | flops 705748992 | bytes 720924 | tf_op jit(solution)/shard_map/cof,fk->cok/dot_general | solution.py:342
  19.6 0.2 copy.31
  19.8 0.1 reshape.123
  19.9 2.4 %shard_map.105.x_ref = bf16[256,2048]{1,0:T(8,128)(2,1)} custom-call(f32[128,2048]{1,0:T(8,128)} %bitcast.38), custom_call_target="tpu_custom_call" | custom-call | flops 1048576 | bytes 2097152 | tf_op jit(solution)/shard_map/pallas_call | solution.py:244
  22.3 0.0 collective-permute-done.3
  22.3 0.2 reshape.121
  22.5 0.1 reshape.133
  22.6 0.0 collective-permute-done.2
  22.6 0.2 reshape.117
  22.8 0.1 reshape.132
  22.9 0.7 select_maximum_fusion.yh_ref
  23.6 0.7 %select_maximum_fusion.1.yl_ref = f32[5,4,8,128]{3,2,1,0:T(8,128)} fusion(f32[1,4,8,1]{3,2,1,0:T(8,128)S(1)} %reshape.132, f32[4,4,8,3]{3,2,1,0:T(8,128)S(1)} %reshape.117), kind=kLoop, calls=%fused_computation.35 | loop fusion | flops 102400 | bytes 83584 | tf_op jit(solution)/shard_map/concatenate | solution.py:311
  24.3 0.0 collective-permute-done.xl_ref
  24.3 0.0 collective-permute-done.1.xh_ref
  24.3 1.0 %copy.32 = f32[64,1,512]{2,1,0:T(1,128)} copy(f32[64,1,512]{2,0,1:T(8,128)S(1)} %bitcast.42) | data formatting | bytes 262144 | tf_op jit(solution)/shard_map/all_to_all | solution.py:351
  25.3 10.1 %all-to-all-start = ((f32[64,1,512]{2,1,0:T(1,128)}), f32[64,1,512]{2,1,0:T(1,128)S(1)}, u32[]{:S(2)}, u32[]{:S(2)}) async-start(f32[64,1,512]{2,1,0:T(1,128)} %copy.32), calls=%async_computation | async-start | bytes 262144 | tf_op jit(solution)/shard_map/all_to_all | solution.py:351
  35.4 0.0 copy-done.3
  35.5 0.0 copy-done.4
  35.5 6.7 %shard_map.104 = f32[4,4,8,2048]{3,2,1,0:T(8,128)} custom-call(f32[4,4,8,2048]{3,2,1,0:T(8,128)} %su_ref.1, f32[4,4,8,2048]{3,2,1,0:T(8,128)} %su_ref.1, f32[4,4,8,2048]{3,2,1,0:T(8,128)} %su_ref.1, f32[4,8,2048]{2,1,0:T(8,128)} %eu_ref.1, f32[4,8,2048]{2,1,0:T(8,128)} %eu_ref.1, f32[4,8,2048]{2,1,0:T(8,128)} %eu_ref.1, f32[4,13,2048]{2,1,0:T(8,128)} %copy-done.3, ...), custom_call_target="tpu_custom_call" | custom-call | flops 52428800 | bytes 6291456 | tf_op jit(solution)/shard_map/pallas_call | solution.py:120
  42.2 1.7 %all-to-all-done = f32[64,1,512]{2,1,0:T(1,128)S(1)} async-done(((f32[64,1,512]{2,1,0:T(1,128)}), f32[64,1,512]{2,1,0:T(1,128)S(1)}, u32[]{:S(2)}, u32[]{:S(2)}) %all-to-all-start) | async-done | bytes 131104 | tf_op jit(solution)/shard_map/all_to_all | solution.py:351
  43.9 0.1 reshape.125
  44.0 0.1 copy.33
  44.1 0.1 reshape.126.pay_ref
  44.2 0.0 copy-done
  44.2 4.9 %shard_map.106.flux_ref = f32[4,4096]{1,0:T(4,128)S(1)} custom-call(bf16[256,2048]{1,0:T(8,128)(2,1)S(1)} %copy-done, f32[8,4096]{1,0:T(8,128)S(1)} %reshape.126.pay_ref), custom_call_target="tpu_custom_call" | custom-call | flops 4294967296 | bytes 1245184 | tf_op jit(solution)/shard_map/pallas_call | solution.py:218
  49.1 0.0 copy-start.1
  49.1 0.0 copy-start.2
  49.1 0.1 reshape.127
  49.3 0.1 copy.45
  49.3 0.1 reshape.128
  49.5 0.7 %copy.35 = f32[64,1,256]{2,1,0:T(1,128)} copy(f32[64,1,256]{2,0,1:T(8,128)S(1)} %bitcast.45) | data formatting | bytes 131072 | tf_op jit(solution)/shard_map/all_to_all | solution.py:360
  50.2 8.1 %all-to-all-start.1 = ((f32[64,1,256]{2,1,0:T(1,128)}), f32[64,1,256]{2,1,0:T(1,128)S(1)}, u32[]{:S(2)}, u32[]{:S(2)}) async-start(f32[64,1,256]{2,1,0:T(1,128)} %copy.35), calls=%async_computation.1 | async-start | bytes 131072 | tf_op jit(solution)/shard_map/all_to_all | solution.py:360
  58.3 5.4 %shard_map.107 = f32[128,2048]{1,0:T(8,128)S(1)} custom-call(f32[8,4096]{1,0:T(8,128)S(1)} %reshape.126.pay_ref, f32[4,4096]{1,0:T(4,128)S(1)} %shard_map.106.flux_ref), custom_call_target="tpu_custom_call" | custom-call | flops 262144 | bytes 1048576 | tf_op jit(solution)/shard_map/pallas_call | solution.py:253
  63.7 1.2 %multiply_add_fusion = f32[4,4,8,2048]{3,2,1,0:T(8,128)} fusion(f32[4,4,8,2048]{3,2,1,0:T(8,128)S(1)} %copy-done.2, f32[4,4,8,2048]{3,2,1,0:T(8,128)S(1)} %copy-done.1, f32[4,4,8,2048]{3,2,1,0:T(8,128)S(1)} %bitcast.37, f32[4,8,2048]{2,1,0:T(8,128)S(1)} %convert_subtract_fusion), kind=kLoop, calls=%fused_computation.12 | loop fusion | flops 1048576 | bytes 4456448 | tf_op jit(solution)/shard_map/add | solution.py:362
  64.9 1.4 %all-to-all-done.1 = f32[64,1,256]{2,1,0:T(1,128)S(1)} async-done(((f32[64,1,256]{2,1,0:T(1,128)}), f32[64,1,256]{2,1,0:T(1,128)S(1)}, u32[]{:S(2)}, u32[]{:S(2)}) %all-to-all-start.1) | async-done | bytes 65568 | tf_op jit(solution)/shard_map/all_to_all | solution.py:360
  66.3 0.1 reshape.130
  66.4 1.7 %fusion.6 = f32[4,2048]{1,0:T(4,128)} fusion(f32[64,2048]{1,0:T(8,128)S(1)} %fusion.16, f32[2048]{0:T(1024)S(1)} %fusion.10, f32[4,64,64]{2,0,1:T(4,128)S(1)} %bitcast.47), kind=kOutput, calls=%fused_computation.8 | convolution fusion | flops 403824640 | bytes 630784 | tf_op jit(solution)/shard_map/cok,fk->cof/dot_general | solution.py:365
  (25 shorter events, 0.2 us)
Async XLA Ops:
  4.0 20.3 %collective-permute-start = (f32[4,13,2048]{2,1,0:T(8,128)S(1)}, f32[4,13,2048]{2,1,0:T(8,128)S(1)}, u32[]{:S(2)}, u32[]{:S(2)}) collective-permute-start(f32[4,13,2048]{2,1,0:T(8,128)S(1)} %pad_maximum_fusion), channel_id=1, source_target_pairs={{0,4},{4,8},{8,12},{12,16},{16,20},{20,24},{24,28},{28,32},{32,36}... | collective-permute-start | bytes 1277960 | tf_op jit(solution)/shard_map/ppermute | solution.py:273
  7.4 8.1 %copy-start.7 = (s32[2048,1]{0,1:T(1,128)S(1)}, s32[2048,1]{0,1:T(1,128)}, u32[]{:S(2)}) copy-start(s32[2048,1]{0,1:T(1,128)} %param.16) | copy-start | bytes 24580
  7.7 16.6 %collective-permute-start.1 = (f32[4,13,2048]{2,1,0:T(8,128)S(1)}, f32[4,13,2048]{2,1,0:T(8,128)S(1)}, u32[]{:S(2)}, u32[]{:S(2)}) collective-permute-start(f32[4,13,2048]{2,1,0:T(8,128)S(1)} %pad_maximum_fusion.1), channel_id=1, source_target_pairs={{4,0},{8,4},{12,8},{16,12},{20,16},{24,20},{28,24},{32,28},{36,32}... | collective-permute-start | bytes 1277960 | tf_op jit(solution)/shard_map/ppermute | solution.py:273
  10.5 11.8 %collective-permute-start.3 = (f32[416]{0:T(512)S(1)}, f32[416]{0:T(512)S(1)}, u32[]{:S(2)}, u32[]{:S(2)}) collective-permute-start(f32[416]{0:T(512)S(1)} %get-tuple-element.51), channel_id=1, source_target_pairs={{1,0},{2,1},{3,2},{0,3},{5,4},{6,5},{7,6},{4,7},{9,8},{10,9},{11,1... | collective-permute-start | bytes 5000 | tf_op jit(solution)/shard_map/ppermute | solution.py:273
  15.5 7.1 %collective-permute-start.2 = (f32[416]{0:T(512)S(1)}, f32[416]{0:T(512)S(1)}, u32[]{:S(2)}, u32[]{:S(2)}) collective-permute-start(f32[416]{0:T(512)S(1)} %get-tuple-element.50), channel_id=1, source_target_pairs={{0,1},{1,2},{2,3},{3,0},{4,5},{5,6},{6,7},{7,4},{8,9},{9,10},{10,1... | collective-permute-start | bytes 5000 | tf_op jit(solution)/shard_map/ppermute | solution.py:273
  15.5 2.0 %copy-start.8 = (s32[2048]{0:T(1024)S(1)}, s32[2048]{0:T(1024)}, u32[]{:S(2)}) copy-start(s32[2048]{0:T(1024)} %param.17) | copy-start | bytes 24580
  15.5 2.1 %copy-start.6 = (f32[4,2048]{1,0:T(4,128)S(1)}, f32[4,2048]{1,0:T(4,128)}, u32[]{:S(2)}) copy-start(f32[4,2048]{1,0:T(4,128)} %param.13) | copy-start | bytes 98308
  15.5 2.1 %copy-start.9 = (f32[2048]{0:T(1024)S(1)}, f32[2048]{0:T(1024)}, u32[]{:S(2)}) copy-start(f32[2048]{0:T(1024)} %param.15) | copy-start | bytes 24580
  15.5 2.1 %copy-start.10 = (f32[2048]{0:T(1024)S(1)}, f32[2048]{0:T(1024)}, u32[]{:S(2)}) copy-start(f32[2048]{0:T(1024)} %param.14) | copy-start | bytes 24580
  19.9 15.5 %copy-start.5 = (s32[4,8,2048]{2,1,0:T(8,128)S(1)}, s32[4,8,2048]{2,1,0:T(8,128)}, u32[]{:S(2)}) copy-start(s32[4,8,2048]{2,1,0:T(8,128)} %param.12) | copy-start | bytes 786436
  24.3 11.1 %copy-start.3 = (f32[4,13,2048]{2,1,0:T(8,128)}, f32[4,13,2048]{2,1,0:T(8,128)S(1)}, u32[]{:S(2)}) copy-start(f32[4,13,2048]{2,1,0:T(8,128)S(1)} %collective-permute-done.xl_ref) | copy-start | bytes 1277956
  24.3 11.1 %copy-start.4 = (f32[4,13,2048]{2,1,0:T(8,128)}, f32[4,13,2048]{2,1,0:T(8,128)S(1)}, u32[]{:S(2)}) copy-start(f32[4,13,2048]{2,1,0:T(8,128)S(1)} %collective-permute-done.1.xh_ref) | copy-start | bytes 1277956
  25.3 18.6 %all-to-all-start = ((f32[64,1,512]{2,1,0:T(1,128)}), f32[64,1,512]{2,1,0:T(1,128)S(1)}, u32[]{:S(2)}, u32[]{:S(2)}) async-start(f32[64,1,512]{2,1,0:T(1,128)} %copy.32), calls=%async_computation | async-start | bytes 262144 | tf_op jit(solution)/shard_map/all_to_all | solution.py:351
  42.2 2.0 %copy-start = (bf16[256,2048]{1,0:T(8,128)(2,1)S(1)}, bf16[256,2048]{1,0:T(8,128)(2,1)}, u32[]{:S(2)}) copy-start(bf16[256,2048]{1,0:T(8,128)(2,1)} %shard_map.105.x_ref) | copy-start | bytes 3145732
  49.1 14.6 %copy-start.1 = (f32[4,4,8,2048]{3,2,1,0:T(8,128)S(1)}, f32[4,4,8,2048]{3,2,1,0:T(8,128)}, u32[]{:S(2)}) copy-start(f32[4,4,8,2048]{3,2,1,0:T(8,128)} %shard_map.104) | copy-start | bytes 3145732
  49.1 14.6 %copy-start.2 = (f32[4,4,8,2048]{3,2,1,0:T(8,128)S(1)}, f32[4,4,8,2048]{3,2,1,0:T(8,128)}, u32[]{:S(2)}) copy-start(f32[4,4,8,2048]{3,2,1,0:T(8,128)} %param.10) | copy-start | bytes 3145732
  50.2 16.1 %all-to-all-start.1 = ((f32[64,1,256]{2,1,0:T(1,128)}), f32[64,1,256]{2,1,0:T(1,128)S(1)}, u32[]{:S(2)}, u32[]{:S(2)}) async-start(f32[64,1,256]{2,1,0:T(1,128)} %copy.35), calls=%async_computation.1 | async-start | bytes 131072 | tf_op jit(solution)/shard_map/all_to_all | solution.py:360

commit v17 on v16

--- a/solution.py
+++ b/solution.py
@@ -212,7 +212,7 @@
     forcing_ref[...] += added[0:rows] + added[rows:2 * rows]
 
 
-def owner_gather(x, pay, block=2048):
+def owner_gather(x, pay, block=4096):
     rows, cols = x.shape
     slots = pay.shape[1]
     return pl.pallas_call(

time: 68.6 us -> 68.3 us (level)
  no operation moved by 1% of the time
where the time goes in v17:
time: 68.3 us; the launch traced here: 67.8 us
  starting transfers between devices  26.6 us (39%)
  Pallas kernels  19.2 us (28%)
  local copies, waits for them, and re-layouts  9.63 us (14%)
  matrix products  5.56 us (8%)
  waiting for transfers between devices  3.08 us (5%)
  other arithmetic  2.82 us (4%)
  between operations  1.01 us (1%)
    all_to_all x1, starting transfers between devices, local(): received = lax.all_to_all(outgoing, 'gx', 0, 0, tiled=True)  10.1 us
    ppermute x4, starting transfers between devices, shift_pair(): return (lax.ppermute(last, axis, up), lax.ppermute(leading, axis, down))  8.4 us
    all_to_all x1, starting transfers between devices, local(): returned = lax.all_to_all(wall_flux, 'gx', 0, 0, tiled=True)  8.08 us
    pallas_call x1, Pallas kernels, stencil(): pl.pallas_call(stencil_kernel, grid=(levels,), in_specs=[pl.BlockSpec((fi...  6.75 us
    pallas_call x1, Pallas kernels, owner_scatter(): pl.pallas_call(scatter_kernel, grid=(slots // block,), in_specs=[pl.Block...  5.44 us
    pallas_call x1, Pallas kernels, owner_gather(): pl.pallas_call(gather_kernel, grid=(slots // block,), in_specs=[pl.BlockS...  4.6 us
    pallas_call x1, Pallas kernels, split_pieces(): pl.pallas_call(split_kernel, out_shape=jax.ShapeDtypeStruct((2 * rows, co...  2.39 us
    transpose x3, local copies, waits for them, and re-layouts, x_rows(): jnp.transpose(state[:, :, lo:hi], (1, 0, 2, 3)).reshape(levels, -1, cells_y)  2.26 us
  transfers between devices with their start and end apart: 6, of which 2 were waited for; matrix products, arithmetic and copies ran while one was open for 15% of the time, Pallas kernels for 21%

profile of v17, /device:TPU:1, one launch (start us, length us, event | category | flops | bytes accessed | tf_op | source)
XLA Modules:
  0.0 67.8 jit_solution(15897569909753399303)
XLA Ops:
  0.6 1.7 %slice_bitcast_fusion = (f32[4,4,3,2048]{3,2,0,1:T(4,128)S(1)}, f32[4,4,3,2048]{3,2,0,1:T(4,128)S(1)}) fusion(f32[4,4,8,2048]{3,2,1,0:T(8,128)} %su_ref.1), kind=kLoop, calls=%fused_computation.20 | loop fusion | bytes 1572864 | tf_op jit(solution)/shard_map/transpose | solution.py:296
  2.4 0.3 copy.25
  2.6 0.2 copy.26
  2.9 1.1 %fusion.24 = (f32[4,1,2048]{2,1,0:T(1,128)S(1)}, f32[4,1,2048]{2,1,0:T(1,128)S(1)}) fusion(f32[4,8,2048]{2,1,0:T(8,128)} %eu_ref.1), kind=kLoop, calls=%fused_computation.48 | loop fusion | bytes 131072 | tf_op jit(solution)/shard_map/slice | solution.py:297
  4.0 0.1 pad_maximum_fusion
  4.0 3.1 %collective-permute-start = (f32[4,13,2048]{2,1,0:T(8,128)S(1)}, f32[4,13,2048]{2,1,0:T(8,128)S(1)}, u32[]{:S(2)}, u32[]{:S(2)}) collective-permute-start(f32[4,13,2048]{2,1,0:T(8,128)S(1)} %pad_maximum_fusion), channel_id=1, source_target_pairs={{0,4},{4,8},{8,12},{12,16},{16,20},{20,24},{24,28},{28,32},{32,36}... | collective-permute-start | bytes 1277960 | tf_op jit(solution)/shard_map/ppermute | solution.py:273
  7.1 0.3 copy.27
  7.4 0.0 copy-start.7
  7.4 0.2 copy.28
  7.6 0.1 pad_maximum_fusion.1
  7.7 0.3 collective-permute-start.1
  8.0 1.0 %fusion.23 = (f32[4,4,8,3]{3,2,1,0:T(8,128)S(1)}, f32[4,4,8,3]{3,2,1,0:T(8,128)S(1)}) fusion(f32[4,4,8,2048]{3,2,1,0:T(8,128)} %su_ref.1), kind=kLoop, calls=%fused_computation.47 | loop fusion | bytes 6144 | tf_op jit(solution)/shard_map/slice | solution.py:304
  8.9 0.2 reshape.119
  9.2 0.2 reshape.115
  9.4 0.9 %slice_reduce_fusion = (f32[4,8]{1,0:T(4,128)S(1)}, f32[4,8]{1,0:T(4,128)S(1)}) fusion(f32[4,8,2048]{2,1,0:T(8,128)} %eu_ref.1), kind=kLoop, calls=%fused_computation.40 | loop fusion | bytes 512 | tf_op jit(solution)/shard_map/slice | solution.py:304
  10.2 0.1 reshape.116
  10.3 0.1 reshape.120
  10.5 5.0 %collective-permute-start.3 = (f32[416]{0:T(512)S(1)}, f32[416]{0:T(512)S(1)}, u32[]{:S(2)}, u32[]{:S(2)}) collective-permute-start(f32[416]{0:T(512)S(1)} %get-tuple-element.51), channel_id=1, source_target_pairs={{1,0},{2,1},{3,2},{0,3},{5,4},{6,5},{7,6},{4,7},{9,8},{10,9},{11,1... | collective-permute-start | bytes 5000 | tf_op jit(solution)/shard_map/ppermute | solution.py:273
  15.5 0.0 collective-permute-start.2
  15.5 0.0 copy-done.7
  15.5 0.0 copy-start.9
  15.5 0.0 copy-start.10
  15.5 1.7 %fusion.10 = f32[2048]{0:T(1024)S(1)} fusion(s32[2048]{0:T(1024)S(1)} %bitcast.49), kind=kOutput, calls=%fused_computation.10 | convolution fusion | flops 541849600 | bytes 16384 | tf_op jit(solution)/shard_map/dot_general | solution.py:331
  17.3 0.3 convolution_subtract_fusion
  17.5 0.0 copy-done.8
  17.6 0.0 copy-done.6
  17.6 0.0 copy-done.9
  17.6 0.0 copy-done.10
  17.6 1.9 %fusion.7 = f32[7,64,64]{2,1,0:T(8,128)S(1)} fusion(f32[64,2048]{1,0:T(8,128)S(1)} %fusion.16, f32[7,2048]{1,0:T(8,128)S(1)} %pad_maximum_fusion.2, f32[2048]{0:T(1024)S(1)} %fusion.10, f32[64,64]{1,0:T(8,128)S(1)} %convolution_subtract_fusion, f32[7]{0:T(128)S(1)} %compare_convert_fusion), kind=kOutput, calls=%fused_computation.9 | convolution fusion | flops 705748992 | bytes 720924 | tf_op jit(solution)/shard_map/cof,fk->cok/dot_general | solution.py:342
  19.6 0.2 copy.31
  19.8 0.1 reshape.123
  19.9 2.4 %shard_map.105.x_ref = bf16[256,2048]{1,0:T(8,128)(2,1)} custom-call(f32[128,2048]{1,0:T(8,128)} %bitcast.38), custom_call_target="tpu_custom_call" | custom-call | flops 1048576 | bytes 2097152 | tf_op jit(solution)/shard_map/pallas_call | solution.py:244
  22.3 0.0 collective-permute-done.3
  22.3 0.2 reshape.121
  22.5 0.1 reshape.133
  22.6 0.0 collective-permute-done.2
  22.6 0.2 reshape.117
  22.8 0.1 reshape.132
  22.9 0.7 select_maximum_fusion.yh_ref
  23.6 0.7 %select_maximum_fusion.1.yl_ref = f32[5,4,8,128]{3,2,1,0:T(8,128)} fusion(f32[1,4,8,1]{3,2,1,0:T(8,128)S(1)} %reshape.132, f32[4,4,8,3]{3,2,1,0:T(8,128)S(1)} %reshape.117), kind=kLoop, calls=%fused_computation.35 | loop fusion | flops 102400 | bytes 83584 | tf_op jit(solution)/shard_map/concatenate | solution.py:311
  24.3 0.0 collective-permute-done.xl_ref
  24.3 0.0 collective-permute-done.1.xh_ref
  24.3 0.0 copy-start.4
  24.3 1.0 %copy.32 = f32[64,1,512]{2,1,0:T(1,128)} copy(f32[64,1,512]{2,0,1:T(8,128)S(1)} %bitcast.42) | data formatting | bytes 262144 | tf_op jit(solution)/shard_map/all_to_all | solution.py:351
  25.3 10.1 %all-to-all-start = ((f32[64,1,512]{2,1,0:T(1,128)}), f32[64,1,512]{2,1,0:T(1,128)S(1)}, u32[]{:S(2)}, u32[]{:S(2)}) async-start(f32[64,1,512]{2,1,0:T(1,128)} %copy.32), calls=%async_computation | async-start | bytes 262144 | tf_op jit(solution)/shard_map/all_to_all | solution.py:351
  35.4 0.0 copy-done.5
  35.5 6.7 %shard_map.104 = f32[4,4,8,2048]{3,2,1,0:T(8,128)} custom-call(f32[4,4,8,2048]{3,2,1,0:T(8,128)} %su_ref.1, f32[4,4,8,2048]{3,2,1,0:T(8,128)} %su_ref.1, f32[4,4,8,2048]{3,2,1,0:T(8,128)} %su_ref.1, f32[4,8,2048]{2,1,0:T(8,128)} %eu_ref.1, f32[4,8,2048]{2,1,0:T(8,128)} %eu_ref.1, f32[4,8,2048]{2,1,0:T(8,128)} %eu_ref.1, f32[4,13,2048]{2,1,0:T(8,128)} %copy-done.3, ...), custom_call_target="tpu_custom_call" | custom-call | flops 52428800 | bytes 6291456 | tf_op jit(solution)/shard_map/pallas_call | solution.py:120
  42.2 1.7 %all-to-all-done = f32[64,1,512]{2,1,0:T(1,128)S(1)} async-done(((f32[64,1,512]{2,1,0:T(1,128)}), f32[64,1,512]{2,1,0:T(1,128)S(1)}, u32[]{:S(2)}, u32[]{:S(2)}) %all-to-all-start) | async-done | bytes 131104 | tf_op jit(solution)/shard_map/all_to_all | solution.py:351
  43.9 0.1 reshape.125
  44.0 0.1 copy.33
  44.1 0.1 reshape.126.pay_ref
  44.2 4.6 %shard_map.106.flux_ref = f32[4,4096]{1,0:T(4,128)S(1)} custom-call(bf16[256,2048]{1,0:T(8,128)(2,1)S(1)} %copy-done, f32[8,4096]{1,0:T(8,128)S(1)} %reshape.126.pay_ref), custom_call_target="tpu_custom_call" | custom-call | flops 4294967296 | bytes 1245184 | tf_op jit(solution)/shard_map/pallas_call | solution.py:218
  48.8 0.0 copy-start.1
  48.8 0.0 copy-start.2
  48.8 0.1 reshape.127
  49.0 0.1 copy.45
  49.0 0.1 reshape.128
  49.2 0.7 %copy.35 = f32[64,1,256]{2,1,0:T(1,128)} copy(f32[64,1,256]{2,0,1:T(8,128)S(1)} %bitcast.45) | data formatting | bytes 131072 | tf_op jit(solution)/shard_map/all_to_all | solution.py:360
  49.9 8.1 %all-to-all-start.1 = ((f32[64,1,256]{2,1,0:T(1,128)}), f32[64,1,256]{2,1,0:T(1,128)S(1)}, u32[]{:S(2)}, u32[]{:S(2)}) async-start(f32[64,1,256]{2,1,0:T(1,128)} %copy.35), calls=%async_computation.1 | async-start | bytes 131072 | tf_op jit(solution)/shard_map/all_to_all | solution.py:360
  58.0 5.4 %shard_map.107 = f32[128,2048]{1,0:T(8,128)S(1)} custom-call(f32[8,4096]{1,0:T(8,128)S(1)} %reshape.126.pay_ref, f32[4,4096]{1,0:T(4,128)S(1)} %shard_map.106.flux_ref), custom_call_target="tpu_custom_call" | custom-call | flops 262144 | bytes 1048576 | tf_op jit(solution)/shard_map/pallas_call | solution.py:253
  63.4 1.2 %multiply_add_fusion = f32[4,4,8,2048]{3,2,1,0:T(8,128)} fusion(f32[4,4,8,2048]{3,2,1,0:T(8,128)S(1)} %copy-done.2, f32[4,4,8,2048]{3,2,1,0:T(8,128)S(1)} %copy-done.1, f32[4,4,8,2048]{3,2,1,0:T(8,128)S(1)} %bitcast.37, f32[4,8,2048]{2,1,0:T(8,128)S(1)} %convert_subtract_fusion), kind=kLoop, calls=%fused_computation.12 | loop fusion | flops 1048576 | bytes 4456448 | tf_op jit(solution)/shard_map/add | solution.py:362
  64.6 1.4 %all-to-all-done.1 = f32[64,1,256]{2,1,0:T(1,128)S(1)} async-done(((f32[64,1,256]{2,1,0:T(1,128)}), f32[64,1,256]{2,1,0:T(1,128)S(1)}, u32[]{:S(2)}, u32[]{:S(2)}) %all-to-all-start.1) | async-done | bytes 65568 | tf_op jit(solution)/shard_map/all_to_all | solution.py:360
  66.0 0.1 reshape.130
  66.2 1.7 %fusion.6 = f32[4,2048]{1,0:T(4,128)} fusion(f32[64,2048]{1,0:T(8,128)S(1)} %fusion.16, f32[2048]{0:T(1024)S(1)} %fusion.10, f32[4,64,64]{2,0,1:T(4,128)S(1)} %bitcast.47), kind=kOutput, calls=%fused_computation.8 | convolution fusion | flops 403824640 | bytes 630784 | tf_op jit(solution)/shard_map/cok,fk->cof/dot_general | solution.py:365
  (25 shorter events, 0.2 us)
Async XLA Ops:
  4.0 20.3 %collective-permute-start = (f32[4,13,2048]{2,1,0:T(8,128)S(1)}, f32[4,13,2048]{2,1,0:T(8,128)S(1)}, u32[]{:S(2)}, u32[]{:S(2)}) collective-permute-start(f32[4,13,2048]{2,1,0:T(8,128)S(1)} %pad_maximum_fusion), channel_id=1, source_target_pairs={{0,4},{4,8},{8,12},{12,16},{16,20},{20,24},{24,28},{28,32},{32,36}... | collective-permute-start | bytes 1277960 | tf_op jit(solution)/shard_map/ppermute | solution.py:273
  7.4 8.1 %copy-start.7 = (s32[2048,1]{0,1:T(1,128)S(1)}, s32[2048,1]{0,1:T(1,128)}, u32[]{:S(2)}) copy-start(s32[2048,1]{0,1:T(1,128)} %param.16) | copy-start | bytes 24580
  7.7 16.6 %collective-permute-start.1 = (f32[4,13,2048]{2,1,0:T(8,128)S(1)}, f32[4,13,2048]{2,1,0:T(8,128)S(1)}, u32[]{:S(2)}, u32[]{:S(2)}) collective-permute-start(f32[4,13,2048]{2,1,0:T(8,128)S(1)} %pad_maximum_fusion.1), channel_id=1, source_target_pairs={{4,0},{8,4},{12,8},{16,12},{20,16},{24,20},{28,24},{32,28},{36,32}... | collective-permute-start | bytes 1277960 | tf_op jit(solution)/shard_map/ppermute | solution.py:273
  10.5 11.8 %collective-permute-start.3 = (f32[416]{0:T(512)S(1)}, f32[416]{0:T(512)S(1)}, u32[]{:S(2)}, u32[]{:S(2)}) collective-permute-start(f32[416]{0:T(512)S(1)} %get-tuple-element.51), channel_id=1, source_target_pairs={{1,0},{2,1},{3,2},{0,3},{5,4},{6,5},{7,6},{4,7},{9,8},{10,9},{11,1... | collective-permute-start | bytes 5000 | tf_op jit(solution)/shard_map/ppermute | solution.py:273
  15.5 7.1 %collective-permute-start.2 = (f32[416]{0:T(512)S(1)}, f32[416]{0:T(512)S(1)}, u32[]{:S(2)}, u32[]{:S(2)}) collective-permute-start(f32[416]{0:T(512)S(1)} %get-tuple-element.50), channel_id=1, source_target_pairs={{0,1},{1,2},{2,3},{3,0},{4,5},{5,6},{6,7},{7,4},{8,9},{9,10},{10,1... | collective-permute-start | bytes 5000 | tf_op jit(solution)/shard_map/ppermute | solution.py:273
  15.5 2.0 %copy-start.8 = (s32[2048]{0:T(1024)S(1)}, s32[2048]{0:T(1024)}, u32[]{:S(2)}) copy-start(s32[2048]{0:T(1024)} %param.17) | copy-start | bytes 24580
  15.5 2.1 %copy-start.6 = (f32[4,2048]{1,0:T(4,128)S(1)}, f32[4,2048]{1,0:T(4,128)}, u32[]{:S(2)}) copy-start(f32[4,2048]{1,0:T(4,128)} %param.13) | copy-start | bytes 98308
  15.5 2.1 %copy-start.9 = (f32[2048]{0:T(1024)S(1)}, f32[2048]{0:T(1024)}, u32[]{:S(2)}) copy-start(f32[2048]{0:T(1024)} %param.15) | copy-start | bytes 24580
  15.5 2.1 %copy-start.10 = (f32[2048]{0:T(1024)S(1)}, f32[2048]{0:T(1024)}, u32[]{:S(2)}) copy-start(f32[2048]{0:T(1024)} %param.14) | copy-start | bytes 24580
  19.9 15.5 %copy-start.5 = (s32[4,8,2048]{2,1,0:T(8,128)S(1)}, s32[4,8,2048]{2,1,0:T(8,128)}, u32[]{:S(2)}) copy-start(s32[4,8,2048]{2,1,0:T(8,128)} %param.12) | copy-start | bytes 786436
  24.3 11.1 %copy-start.3 = (f32[4,13,2048]{2,1,0:T(8,128)}, f32[4,13,2048]{2,1,0:T(8,128)S(1)}, u32[]{:S(2)}) copy-start(f32[4,13,2048]{2,1,0:T(8,128)S(1)} %collective-permute-done.xl_ref) | copy-start | bytes 1277956
  24.3 11.1 %copy-start.4 = (f32[4,13,2048]{2,1,0:T(8,128)}, f32[4,13,2048]{2,1,0:T(8,128)S(1)}, u32[]{:S(2)}) copy-start(f32[4,13,2048]{2,1,0:T(8,128)S(1)} %collective-permute-done.1.xh_ref) | copy-start | bytes 1277956
  25.3 18.6 %all-to-all-start = ((f32[64,1,512]{2,1,0:T(1,128)}), f32[64,1,512]{2,1,0:T(1,128)S(1)}, u32[]{:S(2)}, u32[]{:S(2)}) async-start(f32[64,1,512]{2,1,0:T(1,128)} %copy.32), calls=%async_computation | async-start | bytes 262144 | tf_op jit(solution)/shard_map/all_to_all | solution.py:351
  42.2 2.0 %copy-start = (bf16[256,2048]{1,0:T(8,128)(2,1)S(1)}, bf16[256,2048]{1,0:T(8,128)(2,1)}, u32[]{:S(2)}) copy-start(bf16[256,2048]{1,0:T(8,128)(2,1)} %shard_map.105.x_ref) | copy-start | bytes 3145732
  48.8 14.6 %copy-start.1 = (f32[4,4,8,2048]{3,2,1,0:T(8,128)S(1)}, f32[4,4,8,2048]{3,2,1,0:T(8,128)}, u32[]{:S(2)}) copy-start(f32[4,4,8,2048]{3,2,1,0:T(8,128)} %shard_map.104) | copy-start | bytes 3145732
  48.8 14.6 %copy-start.2 = (f32[4,4,8,2048]{3,2,1,0:T(8,128)S(1)}, f32[4,4,8,2048]{3,2,1,0:T(8,128)}, u32[]{:S(2)}) copy-start(f32[4,4,8,2048]{3,2,1,0:T(8,128)} %param.10) | copy-start | bytes 3145732
  49.9 16.1 %all-to-all-start.1 = ((f32[64,1,256]{2,1,0:T(1,128)}), f32[64,1,256]{2,1,0:T(1,128)S(1)}, u32[]{:S(2)}, u32[]{:S(2)}) async-start(f32[64,1,256]{2,1,0:T(1,128)} %copy.35), calls=%async_computation.1 | async-start | bytes 131072 | tf_op jit(solution)/shard_map/all_to_all | solution.py:360
